TPU v7x, 32 devices: a whole 2x2x4 slice. The times are simulated.
32 devices in a mesh: ctx: 8 (over z, core), fsdp: 4 (over y, x).
Axes of the slice: x: 2, y: 2, z: 4, core: 2. Of those that a mesh axis runs over, the one named last changes fastest.
Arguments:
- layer_in: bfloat16 [4, 8, 2, 128, 1024], P(None, 'ctx', None, 'fsdp'), may hold values from -6 to 6
- out_grad: bfloat16 [4, 8, 2, 128, 1024], P(None, 'ctx', None, 'fsdp'), may hold values from -6 to 6
- block_pairs: int32 [4, 8], replicated, may hold values from 0 to 7, each once within a row
- attn_gain: bfloat16 [1024], P('fsdp'), may hold values from 0.099609375 to 1.8984375
- attn_shift: bfloat16 [1024], P('fsdp'), may hold values from -3 to 3
- qkv_weight: bfloat16 [1024, 3072], P('fsdp'), may hold values from -0.25 to 0.25
- query_bias: bfloat16 [1024], P('fsdp'), may hold values from -3 to 3
- value_bias: bfloat16 [1024], P('fsdp'), may hold values from -0.29882812 to 0.29882812
- out_weight: bfloat16 [1024, 1024], P('fsdp'), may hold values from -2 to 2
- out_bias: bfloat16 [1024], P('fsdp'), may hold values from -3 to 3
- mlp_gain: bfloat16 [1024], P('fsdp'), may hold values from 0.099609375 to 1.8984375
- mlp_shift: bfloat16 [1024], P('fsdp'), may hold values from -3 to 3
- fc_weight: bfloat16 [1024, 4096], P('fsdp'), may hold values from -0.1875 to 0.1875
- fc_bias: bfloat16 [4096], P('fsdp'), may hold values from -3 to 3
- proj_weight: bfloat16 [4096, 1024], P('fsdp'), may hold values from -0.09375 to 0.09375
- proj_bias: bfloat16 [1024], P('fsdp'), may hold values from -3 to 3
Outputs:
- layer_out: bfloat16 [4, 8, 2, 128, 1024], P(None, 'ctx', None, 'fsdp')
- in_grad: float32 [4, 8, 2, 128, 1024], P(None, 'ctx', None, 'fsdp')
- attn_gain_grad: float32 [1024], P('fsdp')
- attn_shift_grad: float32 [1024], P('fsdp')
- qkv_weight_grad: float32 [1024, 3072], P('fsdp')
- query_bias_grad: float32 [1024], P('fsdp')
- value_bias_grad: float32 [1024], P('fsdp')
- out_weight_grad: float32 [1024, 1024], P('fsdp')
- out_bias_grad: float32 [1024], P('fsdp')
- mlp_gain_grad: float32 [1024], P('fsdp')
- mlp_shift_grad: float32 [1024], P('fsdp')
- fc_weight_grad: float32 [1024, 4096], P('fsdp')
- fc_bias_grad: float32 [4096], P('fsdp')
- proj_weight_grad: float32 [4096, 1024], P('fsdp')
- proj_bias_grad: float32 [1024], P('fsdp')
Inputs may be any that keep to these rules, and one draw needn't show every extreme that they name: `block_pairs`: each row is a permutation: every device of ctx holds exactly one block pair of every sequence.
All inputs are finite; a program needn't handle non-finite values.
Results may differ from a plain program's by a relative error of at most 0.023.
Values may be sent and summed in bfloat16 or wider, within the bound.
No kernel may reach another device: no remote copies, remote signals or barrier semaphores. Data moves between devices by JAX's collectives and lax.ppermute only.
A program may use at most 320 MiB of HBM per device.

v0:
```python
import jax
import jax.numpy as jnp
from jax import lax
from jax.sharding import PartitionSpec as P

HD = 64


norm_eps = 1e-05
masked_score = -1e30


def for_sending(array):
    return jax.tree.map(lambda a: a.astype(jnp.bfloat16) if a.dtype == jnp.float32 else a, array)


def layer_norm(values, gain, shift):
    average = jnp.mean(values, axis=-1, keepdims=True)
    centred = values - average
    spread = jnp.mean(centred * centred, axis=-1, keepdims=True)
    return centred * lax.rsqrt(spread + norm_eps) * gain + shift


def gelu_tanh(values):
    return jax.nn.gelu(values, approximate=True)


def contract_last(left, right):
    return lax.dot_general(
        left, right, (((1,), (1,)), ((), ())), preferred_element_type=jnp.float32
    )


def contract_first(left, right):
    return lax.dot_general(
        left, right, (((0,), (0,)), ((), ())), preferred_element_type=jnp.float32
    )


def head_scores(query, keys, query_places, key_places):
    scores = contract_last(query, keys)
    return jnp.where(key_places[None, :] <= query_places[:, None], scores, masked_score)


def score_grads(query, keys, values, grad_out, summary, row_sum, query_places, key_places):
    scores = head_scores(query, keys, query_places, key_places)
    probs = jnp.exp(scores - summary[:, None])
    grad_probs = contract_last(grad_out, values)
    row_sum = jnp.sum(probs * grad_probs, axis=1)
    grad_scores = (probs * (grad_probs - row_sum[:, None])).astype(jnp.bfloat16)
    return (probs.astype(jnp.bfloat16), grad_scores, row_sum)


def attend_forward(items):
    query, keys, values, query_places, key_places = items
    outputs = []
    summaries = []
    for head_index in range(query.shape[1] // HD):
        columns = slice(head_index * HD, (head_index + 1) * HD)
        scores = head_scores(query[:, columns], keys[:, columns], query_places, key_places)
        row_peak = jnp.max(scores, axis=1, keepdims=True)
        raised = jnp.exp(scores - row_peak)
        row_total = jnp.sum(raised, axis=1, keepdims=True)
        weights = (raised / row_total).astype(jnp.bfloat16)
        outputs.append(
            jnp.dot(weights, values[:, columns], preferred_element_type=jnp.float32).astype(
                jnp.bfloat16
            )
        )
        summaries.append(row_peak[:, 0] + jnp.log(row_total[:, 0]))
    return (jnp.concatenate(outputs, axis=1), jnp.stack(summaries, axis=1))


def attend_backward(items):
    query, keys, values, grad_out, summary, query_places, key_places = items
    query_parts, key_parts, value_parts = ([], [], [])
    for head_index in range(query.shape[1] // HD):
        columns = slice(head_index * HD, (head_index + 1) * HD)
        probs_low, grad_scores, row_sum = score_grads(
            query[:, columns],
            keys[:, columns],
            values[:, columns],
            grad_out[:, columns],
            summary[:, head_index],
            None,
            query_places,
            key_places,
        )
        query_parts.append(
            jnp.dot(grad_scores, keys[:, columns], preferred_element_type=jnp.float32).astype(
                jnp.bfloat16
            )
        )
        key_parts.append(contract_first(grad_scores, query[:, columns]))
        value_parts.append(contract_first(probs_low, grad_out[:, columns]))
    return (
        jnp.concatenate(query_parts, axis=1),
        jnp.concatenate(key_parts, axis=1),
        jnp.concatenate(value_parts, axis=1),
    )


def shards(
    layer_in,
    out_grad,
    block_pairs,
    attn_gain,
    attn_shift,
    qkv_weight,
    query_bias,
    value_bias,
    out_weight,
    out_bias,
    mlp_gain,
    mlp_shift,
    fc_weight,
    fc_bias,
    proj_weight,
    proj_bias,
):
    fsdp_size = lax.axis_size("fsdp")
    ctx_size = lax.axis_size("ctx")
    seq_count = layer_in.shape[0]
    half_rows = layer_in.shape[3]
    model_width = layer_in.shape[4]
    block_len = half_rows * fsdp_size
    pair_len = 2 * block_len
    group_width = model_width // fsdp_size
    gathered = (
        lax.all_gather(qkv_weight, "fsdp", axis=0, tiled=True),
        lax.all_gather(out_weight, "fsdp", axis=0, tiled=True),
        lax.all_gather(fc_weight, "fsdp", axis=0, tiled=True),
        lax.all_gather(proj_weight, "fsdp", axis=0, tiled=True),
        lax.all_gather(attn_gain, "fsdp", axis=0, tiled=True),
        lax.all_gather(attn_shift, "fsdp", axis=0, tiled=True),
        lax.all_gather(query_bias, "fsdp", axis=0, tiled=True),
        lax.all_gather(value_bias, "fsdp", axis=0, tiled=True),
        lax.all_gather(out_bias, "fsdp", axis=0, tiled=True),
        lax.all_gather(mlp_gain, "fsdp", axis=0, tiled=True),
        lax.all_gather(mlp_shift, "fsdp", axis=0, tiled=True),
        lax.all_gather(fc_bias, "fsdp", axis=0, tiled=True),
        lax.all_gather(proj_bias, "fsdp", axis=0, tiled=True),
    )
    qkv_full, out_full, fc_full, proj_full = (gathered[0], gathered[1], gathered[2], gathered[3])
    vectors = [piece.astype(jnp.float32) for piece in gathered[4:]]
    (
        gain_attn,
        shift_attn,
        bias_query,
        bias_value,
        bias_out,
        gain_mlp,
        shift_mlp,
        bias_fc,
        bias_proj,
    ) = vectors
    halves = jnp.stack([block_pairs, 2 * ctx_size - 1 - block_pairs], axis=2)
    key_places = (halves[..., None] * block_len + jnp.arange(block_len, dtype=jnp.int32)).reshape(
        seq_count, ctx_size, pair_len
    )
    query_places = lax.dynamic_slice_in_dim(key_places, lax.axis_index("ctx"), 1, 1).reshape(
        seq_count, pair_len
    )
    key_places = key_places.reshape(seq_count, ctx_size * pair_len)
    inputs = layer_in.reshape(-1, model_width).astype(jnp.float32)
    normed, attn_norm_back = jax.vjp(layer_norm, inputs, gain_attn, shift_attn)
    normed_low = normed.astype(jnp.bfloat16)
    mixed = jnp.dot(normed_low, qkv_full, preferred_element_type=jnp.float32)
    query = ((mixed[:, :model_width] + bias_query) * 0.125).astype(jnp.bfloat16)
    keys = mixed[:, model_width : 2 * model_width].astype(jnp.bfloat16)
    values = (mixed[:, 2 * model_width :] + bias_value).astype(jnp.bfloat16)

    def to_groups(array):
        return array.reshape(seq_count, 2, half_rows, fsdp_size, group_width)

    def to_pairs(array):
        return array.reshape(seq_count, 2, block_len, 1, group_width)

    query_heads, key_heads, value_heads = (
        lax.all_to_all(to_groups(query), "fsdp", split_axis=3, concat_axis=2, tiled=True),
        lax.all_to_all(to_groups(keys), "fsdp", split_axis=3, concat_axis=2, tiled=True),
        lax.all_to_all(to_groups(values), "fsdp", split_axis=3, concat_axis=2, tiled=True),
    )
    query_heads = query_heads.reshape(seq_count, pair_len, group_width)
    own_keys = key_heads.reshape(seq_count, pair_len, group_width)
    own_values = value_heads.reshape(seq_count, pair_len, group_width)
    key_all, value_all = (
        lax.all_gather(
            own_keys.reshape(seq_count, 1, pair_len, group_width), "ctx", axis=1, tiled=True
        ),
        lax.all_gather(
            own_values.reshape(seq_count, 1, pair_len, group_width), "ctx", axis=1, tiled=True
        ),
    )
    key_all = key_all.reshape(seq_count, -1, group_width)
    value_all = value_all.reshape(seq_count, -1, group_width)
    attended, summary = lax.map(
        attend_forward, (query_heads, key_all, value_all, query_places, key_places)
    )
    attended_rows = lax.all_to_all(
        for_sending(to_pairs(attended)), "fsdp", split_axis=2, concat_axis=3, tiled=True
    ).reshape(-1, model_width)
    branch = jnp.dot(attended_rows, out_full, preferred_element_type=jnp.float32) + bias_out
    middle = inputs + branch
    normed_mlp, mlp_norm_back = jax.vjp(layer_norm, middle, gain_mlp, shift_mlp)
    mlp_low = normed_mlp.astype(jnp.bfloat16)
    hidden = jnp.dot(mlp_low, fc_full, preferred_element_type=jnp.float32) + bias_fc
    activated, gelu_back = jax.vjp(gelu_tanh, hidden)
    activated_low = activated.astype(jnp.bfloat16)
    result = (
        middle + jnp.dot(activated_low, proj_full, preferred_element_type=jnp.float32) + bias_proj
    )
    layer_out = result.astype(jnp.bfloat16).reshape(layer_in.shape)
    grad_rows = out_grad.reshape(-1, model_width)
    grad_result = grad_rows.astype(jnp.float32)
    proj_grad = contract_first(activated_low, grad_rows)
    proj_bias_grad = jnp.sum(grad_result, axis=0)
    grad_activated = contract_last(grad_rows, proj_full)
    grad_hidden = gelu_back(grad_activated)[0].astype(jnp.bfloat16)
    fc_grad = contract_first(mlp_low, grad_hidden)
    fc_bias_grad = jnp.sum(grad_hidden.astype(jnp.float32), axis=0)
    grad_middle, mlp_gain_grad, mlp_shift_grad = mlp_norm_back(contract_last(grad_hidden, fc_full))
    grad_middle = grad_middle + grad_result
    grad_branch = grad_middle.astype(jnp.bfloat16)
    out_weight_term = contract_first(attended_rows, grad_branch)
    out_bias_grad = jnp.sum(grad_branch.astype(jnp.float32), axis=0)
    grad_attended = contract_last(grad_branch, out_full).astype(jnp.bfloat16)
    grad_heads = lax.all_to_all(
        to_groups(grad_attended), "fsdp", split_axis=3, concat_axis=2, tiled=True
    ).reshape(seq_count, pair_len, group_width)
    grad_query, grad_keys, grad_values = lax.map(
        attend_backward,
        (query_heads, key_all, value_all, grad_heads, summary, query_places, key_places),
    )
    key_part, value_part = (
        lax.psum_scatter(
            grad_keys.reshape(seq_count, ctx_size, pair_len, group_width).astype(jnp.bfloat16),
            "ctx",
            scatter_dimension=1,
            tiled=True,
        ).astype(jnp.float32),
        lax.psum_scatter(
            grad_values.reshape(seq_count, ctx_size, pair_len, group_width).astype(jnp.bfloat16),
            "ctx",
            scatter_dimension=1,
            tiled=True,
        ).astype(jnp.float32),
    )
    key_grad_low = key_part.astype(jnp.bfloat16)
    value_grad_low = value_part.astype(jnp.bfloat16)
    query_back, key_back, value_back = (
        lax.all_to_all(
            for_sending(to_pairs(grad_query)), "fsdp", split_axis=2, concat_axis=3, tiled=True
        ),
        lax.all_to_all(
            for_sending(to_pairs(key_grad_low)), "fsdp", split_axis=2, concat_axis=3, tiled=True
        ),
        lax.all_to_all(
            for_sending(to_pairs(value_grad_low)), "fsdp", split_axis=2, concat_axis=3, tiled=True
        ),
    )
    grad_mixed = jnp.concatenate(
        [
            query_back.reshape(-1, model_width) * 0.125,
            key_back.reshape(-1, model_width),
            value_back.reshape(-1, model_width),
        ],
        axis=1,
    )
    qkv_grad = contract_first(normed_low, grad_mixed)
    mixed_float = grad_mixed.astype(jnp.float32)
    query_bias_grad = jnp.sum(mixed_float[:, :model_width], axis=0)
    value_bias_grad = jnp.sum(mixed_float[:, 2 * model_width :], axis=0)
    grad_inputs, attn_gain_grad, attn_shift_grad = attn_norm_back(
        contract_last(grad_mixed, qkv_full)
    )
    in_grad = (grad_inputs + grad_middle).reshape(layer_in.shape)
    shares = (
        lax.psum_scatter(
            qkv_grad.astype(jnp.bfloat16), "fsdp", scatter_dimension=0, tiled=True
        ).astype(jnp.float32),
        lax.psum_scatter(
            out_weight_term.astype(jnp.bfloat16), "fsdp", scatter_dimension=0, tiled=True
        ).astype(jnp.float32),
        lax.psum_scatter(
            fc_grad.astype(jnp.bfloat16), "fsdp", scatter_dimension=0, tiled=True
        ).astype(jnp.float32),
        lax.psum_scatter(
            proj_grad.astype(jnp.bfloat16), "fsdp", scatter_dimension=0, tiled=True
        ).astype(jnp.float32),
        lax.psum_scatter(
            attn_gain_grad.astype(jnp.bfloat16), "fsdp", scatter_dimension=0, tiled=True
        ).astype(jnp.float32),
        lax.psum_scatter(
            attn_shift_grad.astype(jnp.bfloat16), "fsdp", scatter_dimension=0, tiled=True
        ).astype(jnp.float32),
        lax.psum_scatter(
            query_bias_grad.astype(jnp.bfloat16), "fsdp", scatter_dimension=0, tiled=True
        ).astype(jnp.float32),
        lax.psum_scatter(
            value_bias_grad.astype(jnp.bfloat16), "fsdp", scatter_dimension=0, tiled=True
        ).astype(jnp.float32),
        lax.psum_scatter(
            out_bias_grad.astype(jnp.bfloat16), "fsdp", scatter_dimension=0, tiled=True
        ).astype(jnp.float32),
        lax.psum_scatter(
            mlp_gain_grad.astype(jnp.bfloat16), "fsdp", scatter_dimension=0, tiled=True
        ).astype(jnp.float32),
        lax.psum_scatter(
            mlp_shift_grad.astype(jnp.bfloat16), "fsdp", scatter_dimension=0, tiled=True
        ).astype(jnp.float32),
        lax.psum_scatter(
            fc_bias_grad.astype(jnp.bfloat16), "fsdp", scatter_dimension=0, tiled=True
        ).astype(jnp.float32),
        lax.psum_scatter(
            proj_bias_grad.astype(jnp.bfloat16), "fsdp", scatter_dimension=0, tiled=True
        ).astype(jnp.float32),
    )
    slices = (
        lax.psum_scatter(
            shares[0].astype(jnp.bfloat16), "ctx", scatter_dimension=0, tiled=True
        ).astype(jnp.float32),
        lax.psum_scatter(
            shares[1].astype(jnp.bfloat16), "ctx", scatter_dimension=0, tiled=True
        ).astype(jnp.float32),
        lax.psum_scatter(
            shares[2].astype(jnp.bfloat16), "ctx", scatter_dimension=0, tiled=True
        ).astype(jnp.float32),
        lax.psum_scatter(
            shares[3].astype(jnp.bfloat16), "ctx", scatter_dimension=0, tiled=True
        ).astype(jnp.float32),
        lax.psum_scatter(
            shares[4].astype(jnp.bfloat16), "ctx", scatter_dimension=0, tiled=True
        ).astype(jnp.float32),
        lax.psum_scatter(
            shares[5].astype(jnp.bfloat16), "ctx", scatter_dimension=0, tiled=True
        ).astype(jnp.float32),
        lax.psum_scatter(
            shares[6].astype(jnp.bfloat16), "ctx", scatter_dimension=0, tiled=True
        ).astype(jnp.float32),
        lax.psum_scatter(
            shares[7].astype(jnp.bfloat16), "ctx", scatter_dimension=0, tiled=True
        ).astype(jnp.float32),
        lax.psum_scatter(
            shares[8].astype(jnp.bfloat16), "ctx", scatter_dimension=0, tiled=True
        ).astype(jnp.float32),
        lax.psum_scatter(
            shares[9].astype(jnp.bfloat16), "ctx", scatter_dimension=0, tiled=True
        ).astype(jnp.float32),
        lax.psum_scatter(
            shares[10].astype(jnp.bfloat16), "ctx", scatter_dimension=0, tiled=True
        ).astype(jnp.float32),
        lax.psum_scatter(
            shares[11].astype(jnp.bfloat16), "ctx", scatter_dimension=0, tiled=True
        ).astype(jnp.float32),
        lax.psum_scatter(
            shares[12].astype(jnp.bfloat16), "ctx", scatter_dimension=0, tiled=True
        ).astype(jnp.float32),
    )
    totals = (
        lax.all_gather(slices[0].astype(jnp.bfloat16), "ctx", axis=0, tiled=True).astype(
            jnp.float32
        ),
        lax.all_gather(slices[1].astype(jnp.bfloat16), "ctx", axis=0, tiled=True).astype(
            jnp.float32
        ),
        lax.all_gather(slices[2].astype(jnp.bfloat16), "ctx", axis=0, tiled=True).astype(
            jnp.float32
        ),
        lax.all_gather(slices[3].astype(jnp.bfloat16), "ctx", axis=0, tiled=True).astype(
            jnp.float32
        ),
        lax.all_gather(slices[4].astype(jnp.bfloat16), "ctx", axis=0, tiled=True).astype(
            jnp.float32
        ),
        lax.all_gather(slices[5].astype(jnp.bfloat16), "ctx", axis=0, tiled=True).astype(
            jnp.float32
        ),
        lax.all_gather(slices[6].astype(jnp.bfloat16), "ctx", axis=0, tiled=True).astype(
            jnp.float32
        ),
        lax.all_gather(slices[7].astype(jnp.bfloat16), "ctx", axis=0, tiled=True).astype(
            jnp.float32
        ),
        lax.all_gather(slices[8].astype(jnp.bfloat16), "ctx", axis=0, tiled=True).astype(
            jnp.float32
        ),
        lax.all_gather(slices[9].astype(jnp.bfloat16), "ctx", axis=0, tiled=True).astype(
            jnp.float32
        ),
        lax.all_gather(slices[10].astype(jnp.bfloat16), "ctx", axis=0, tiled=True).astype(
            jnp.float32
        ),
        lax.all_gather(slices[11].astype(jnp.bfloat16), "ctx", axis=0, tiled=True).astype(
            jnp.float32
        ),
        lax.all_gather(slices[12].astype(jnp.bfloat16), "ctx", axis=0, tiled=True).astype(
            jnp.float32
        ),
    )
    return (
        layer_out,
        in_grad,
        totals[4],
        totals[5],
        totals[0],
        totals[6],
        totals[7],
        totals[1],
        totals[8],
        totals[9],
        totals[10],
        totals[2],
        totals[11],
        totals[3],
        totals[12],
    )


def solution(mesh):
    placed = (
        P(None, "ctx", None, "fsdp", None),
        P(None, "ctx", None, "fsdp", None),
        P(),
        P("fsdp"),
        P("fsdp"),
        P("fsdp", None),
        P("fsdp"),
        P("fsdp"),
        P("fsdp", None),
        P("fsdp"),
        P("fsdp"),
        P("fsdp"),
        P("fsdp", None),
        P("fsdp"),
        P("fsdp", None),
        P("fsdp"),
    )
    return jax.shard_map(
        shards,
        mesh=mesh,
        in_specs=placed,
        out_specs=(
            P(None, "ctx", None, "fsdp", None),
            P(None, "ctx", None, "fsdp", None),
            P("fsdp"),
            P("fsdp"),
            P("fsdp", None),
            P("fsdp"),
            P("fsdp"),
            P("fsdp", None),
            P("fsdp"),
            P("fsdp"),
            P("fsdp"),
            P("fsdp", None),
            P("fsdp"),
            P("fsdp", None),
            P("fsdp"),
        ),
        check_vma=False,
    )
```

profile of v0, /device:TPU:0, one launch (start us, length us, event | category | flops | bytes accessed | tf_op | source)
XLA Modules:
  0.0 1274.3 jit_solution(2730104220366824694)
XLA Ops:
  9.3 9.6 all-gather.1
  18.9 8.2 all-gather
  29.6 53.0 %all-gather.19.cloned.1.call-done = bf16[1024,3072]{1,0:T(8,128)(2,1)} async-done(((bf16[256,3072]{1,0:T(8,128)(2,1)}), bf16[1024,3072]{1,0:T(8,128)(2,1)}) %all-gather.19.cloned.1.call-update) | async-done | bytes 6291472 | tf_op jit(solution)/shard_map/all_gather | solution.py:130
  82.6 4.6 fusion.99
  89.5 11.0 all_to_all.114
  101.5 7.5 all-gather.3
  108.9 7.7 all-gather.2
  116.6 1.8 fusion.79
  118.9 9.6 all_to_all.115
  131.7 7.5 all-gather.6
  139.2 7.7 all-gather.5
  146.8 7.5 all-gather.4
  154.3 7.8 all_gather.96
  163.4 3.8 all-to-all-start
  167.2 6.5 all-to-all-done
  173.8 4.6 copy.99
  178.4 17.3 %all-gather.23.cloned.1.call-done = bf16[4,8,256,256]{3,2,0,1:T(8,128)(2,1)} async-done(((bf16[4,1,256,256]{3,2,0,1:T(8,128)(2,1)}), bf16[4,8,256,256]{3,2,0,1:T(8,128)(2,1)}) %all-gather.23.cloned.1.call-update) | async-done | bytes 4194320 | tf_op jit(solution)/shard_map/all_gather | solution.py:191
  195.7 4.6 copy.102
  200.4 37.8 %while.26 = (s32[]{:T(128)}, bf16[4,256,256]{2,1,0:T(8,128)(2,1)S(1)}, f32[4,256,4]{1,2,0:T(4,128)}, s32[4,2048]{1,0:T(4,128)S(1)}, s32[4,256]{1,0:T(4,128)S(1)}...) while((s32[]{:T(128)}, ...), condition=%wide.region_11.12_spmd, body=%wide.region_2.11_spmd.sunk | while | flops 554240000 | bytes 35092604 | solution.py:197
  200.5 1.7 dynamic-slice_bitcast_fusion.14
  209.9 1.7 dynamic-slice_bitcast_fusion.14
  219.4 1.7 dynamic-slice_bitcast_fusion.14
  239.5 4.1 all-to-all-start.3
  243.7 45.7 %all-gather.29.cloned.1.call-done = bf16[4096,1024]{1,0:T(8,128)(2,1)} async-done(((bf16[1024,1024]{1,0:T(8,128)(2,1)}), bf16[4096,1024]{1,0:T(8,128)(2,1)}) %all-gather.29.cloned.1.call-update) | async-done | bytes 8388624 | tf_op jit(solution)/shard_map/all_gather | solution.py:133
  289.3 7.7 fusion.100
  297.7 28.6 %all-gather.25.cloned.1.call-done = bf16[1024,1024]{1,0:T(8,128)(2,1)} async-done(((bf16[256,1024]{1,0:T(8,128)(2,1)}), bf16[1024,1024]{1,0:T(8,128)(2,1)}) %all-gather.25.cloned.1.call-update) | async-done | bytes 2097168 | tf_op jit(solution)/shard_map/all_gather | solution.py:131
  326.3 2.4 fusion.98
  329.0 86.5 %all-gather.27.cloned.1.call-done = bf16[1024,4096]{1,0:T(8,128)(2,1)} async-done(((bf16[256,4096]{1,0:T(8,128)(2,1)}), bf16[1024,4096]{1,0:T(8,128)(2,1)}) %all-gather.27.cloned.1.call-update) | async-done | bytes 8388624 | tf_op jit(solution)/shard_map/all_gather | solution.py:132
  415.5 12.3 fusion.87
  427.8 3.2 multiply_reduce_fusion.4
  436.1 3.5 all-to-all-start.4
  439.8 7.9 all-to-all-done.4
  449.3 89.8 %while.27 = (s32[]{:T(128)}, bf16[4,256,256]{2,1,0:T(8,128)(2,1)}, bf16[4,2048,256]{2,1,0:T(8,128)(2,1)}, bf16[4,2048,256]{2,1,0:T(8,128)(2,1)}, s32[4,2048]{1,0...) while((s32[]{:T(128)}, bf16[4,256,256]{2,1,0:T(8,128)(2,1)}, ...), condition=%wide.region_21.22_spmd, body=%wide.region_16.21_spmd.sunk | while | flops 1370029056 | bytes 95111440 | solution.py:231
  541.5 3.5 all-to-all-start.5
  545.6 169.3 %all-reduce.34.cloned.1.call-done = (bf16[4,8,256,256]{3,2,1,0:T(8,128)(2,1)}, bf16[4,8,256,256]{3,2,1,0:T(8,128)(2,1)}) async-done(((bf16[4,8,256,256]{3,2,1,0:T(8,128)(2,1)}, bf16[4,8,256,256]{3,2,1,0:T(8,128)(2,1)}), (bf16[4,8,256,256]{3,2,1,0:T(8,128)(2,1)}, bf16[4,8,256,256]{3,2,1,0:T(8,128)(2,1)})) %all-reduce.34.cloned.1.call-update) | async-done | bytes 8388624
  714.8 1.9 constant_dynamic-slice_fusion.4
  718.1 3.9 all-to-all-start.6
  723.3 6.4 all-to-all-done.6
  729.7 3.5 all-to-all-start.7
  734.6 5.6 all-to-all-done.7
  741.3 4.6 convolution_convert_fusion.10
  747.1 7.9 convolution_convert_fusion.9
  756.1 8.4 convolution_convert_fusion.8
  764.6 3.4 convolution_convert_fusion.11
  768.0 47.8 %reduce-scatter.15.cloned.1.call-done = bf16[256,3072]{1,0:T(8,128)(2,1)} async-done(((bf16[1024,3072]{1,0:T(8,128)(2,1)}), bf16[256,3072]{1,0:T(8,128)(2,1)}) %reduce-scatter.15.cloned.1.call-update) | async-done | bytes 1572880 | tf_op jit(solution)/shard_map/reduce_scatter | solution.py:279
  815.9 89.4 %reduce-scatter.23.cloned.1.call-done = bf16[256,4096]{1,0:T(8,128)(2,1)} async-done(((bf16[1024,4096]{1,0:T(8,128)(2,1)}), bf16[256,4096]{1,0:T(8,128)(2,1)}) %reduce-scatter.23.cloned.1.call-update) | async-done | bytes 2097168 | tf_op jit(solution)/shard_map/reduce_scatter | solution.py:285
  905.3 89.2 %reduce-scatter.27.cloned.1.call-done = bf16[1024,1024]{1,0:T(8,128)(2,1)} async-done(((bf16[4096,1024]{1,0:T(8,128)(2,1)}), bf16[1024,1024]{1,0:T(8,128)(2,1)}) %reduce-scatter.27.cloned.1.call-update) | async-done | bytes 2097168 | tf_op jit(solution)/shard_map/reduce_scatter | solution.py:288
  994.6 38.7 %reduce-scatter.19.cloned.1.call-done = bf16[256,1024]{1,0:T(8,128)(2,1)} async-done(((bf16[1024,1024]{1,0:T(8,128)(2,1)}), bf16[256,1024]{1,0:T(8,128)(2,1)}) %reduce-scatter.19.cloned.1.call-update) | async-done | bytes 524304 | tf_op jit(solution)/shard_map/reduce_scatter | solution.py:282
  1033.3 36.3 %reduce-scatter.17.cloned.1.call-done = bf16[32,3072]{1,0:T(8,128)(2,1)} async-done(((bf16[256,3072]{1,0:T(8,128)(2,1)}), bf16[32,3072]{1,0:T(8,128)(2,1)}) %reduce-scatter.17.cloned.1.call-update) | async-done | bytes 196624 | tf_op jit(solution)/shard_map/reduce_scatter | solution.py:320
  1069.7 36.8 %reduce-scatter.25.cloned.1.call-done = bf16[32,4096]{1,0:T(8,128)(2,1)} async-done(((bf16[256,4096]{1,0:T(8,128)(2,1)}), bf16[32,4096]{1,0:T(8,128)(2,1)}) %reduce-scatter.25.cloned.1.call-update) | async-done | bytes 262160 | tf_op jit(solution)/shard_map/reduce_scatter | solution.py:326
  1106.6 36.7 %reduce-scatter.29.cloned.1.call-done = bf16[128,1024]{1,0:T(8,128)(2,1)} async-done(((bf16[1024,1024]{1,0:T(8,128)(2,1)}), bf16[128,1024]{1,0:T(8,128)(2,1)}) %reduce-scatter.29.cloned.1.call-update) | async-done | bytes 262160 | tf_op jit(solution)/shard_map/reduce_scatter | solution.py:329
  1146.6 8.5 all-gather.7
  1155.7 8.2 fusion.78
  1165.4 4.8 fusion.86
  1171.8 15.3 %all-reduce.31 = (bf16[1024]{0:T(1024)(128)(2,1)S(1)}, bf16[1024]{0:T(1024)(128)(2,1)S(1)}, bf16[1024]{0:T(1024)(128)(2,1)S(1)}, bf16[1024]{0:T(1024)(128)(2,1)S...) all-reduce(bf16[1024]{0:T(1024)(128)(2,1)S(1)} %get-tuple-element.2, ...), channel_id=4, replica_groups=mesh['ctx'=8,'fsdp'=4] {'fsdp'}, use_global_device_ids=true, to_apply=%region_27.28.clone | all-reduce | flops 12288 | bytes 49152
  1187.7 14.0 %all-reduce.29 = (bf16[256]{0:T(256)(128)(2,1)S(1)}, bf16[256]{0:T(256)(128)(2,1)S(1)}, bf16[256]{0:T(256)(128)(2,1)S(1)}, bf16[256]{0:T(256)(128)(2,1)S(1)}, bf...) all-reduce(bf16[256]{0:T(256)(128)(2,1)S(1)} %dynamic-slice.13, ...), channel_id=5, replica_groups=mesh['ctx'=8,'fsdp'=4] {'ctx'}, use_global_device_ids=true, to_apply=%region_28.29.clone | all-reduce | flops 2048 | bytes 8192
  1204.0 14.6 %all-reduce.28 = (bf16[256]{0:T(256)(128)(2,1)S(1)}, bf16[256]{0:T(256)(128)(2,1)S(1)}, bf16[256]{0:T(256)(128)(2,1)S(1)}, bf16[256]{0:T(256)(128)(2,1)S(1)}, bf...) all-reduce(bf16[256]{0:T(256)(128)(2,1)S(1)} %dynamic-update-slice,, ...), channel_id=1, replica_groups=mesh['ctx'=8,'fsdp'=4] {'ctx'}, use_global_device_ids=true, to_apply=%add | all-reduce | flops 3072 | bytes 12288
  1223.2 8.5 all-gather.8
  1232.3 2.7 add_add_fusion.2
  1235.0 17.1 %all_gather.104 = bf16[256,1024]{1,0:T(8,128)(2,1)S(1)} all-gather(bf16[32,1024]{1,0:T(8,128)(2,1)} %reduce-scatter.21.cloned.1.call-done), channel_id=1, replica_groups=mesh['ctx'=8,'fsdp'=4] {'ctx'}, dimensions={0}, use_global_device_ids=true | all-gather | bytes 589824 | tf_op jit(solution)/shard_map/all_gather | solution.py:364
  1253.2 3.5 convert_element_type.304
  1256.6 4.1 convert_element_type.318
  1260.7 2.2 all-gather.35.cloned.1.call-done
  1262.9 4.1 convert_element_type.321
  (544 shorter events, 166.3 us)
Async XLA Ops:
  7.2 21.2 %copy-start = (bf16[4,1,2,32,1024]{4,3,2,1,0:T(8,128)(2,1)S(1)}, bf16[4,1,2,32,1024]{4,3,2,1,0:T(8,128)(2,1)}, u32[]{:S(2)}) copy-start(bf16[4,1,2,32,1024]{4,3,2,1,0:T(8,128)(2,1)} %param.20) | copy-start | bytes 1572868
  7.2 75.4 %all-gather.19.cloned.1.call-start = ((), (), s32[]{:S(2)}) async-start(), calls=%async_computation.16 | async-start | bytes 7864320 | tf_op jit(solution)/shard_map/all_gather | solution.py:130
  7.9 165.9 %all-gather.21.cloned.1.call-start = ((), (), s32[]{:S(2)}) async-start(), calls=%async_computation.17 | async-start | bytes 4718592 | tf_op jit(solution)/shard_map/all_gather | solution.py:188
  27.1 55.6 %copy-start.20 = (f32[4,1,256]{2,1,0:T(1,128)}, f32[4,1,256]{2,1,0:T(1,128)S(1)}, u32[]{:S(2)}) copy-start(f32[4,1,256]{2,1,0:T(1,128)S(1)} %convert_element_type.324) | copy-start | bytes 12292
  28.4 54.3 %copy-start.24 = (f32[256]{0:T(256)}, f32[256]{0:T(256)S(1)}, u32[]{:S(2)}) copy-start(f32[256]{0:T(256)S(1)} %div.71) | copy-start | bytes 3076
  29.6 57.6 %copy-start.11 = (bf16[256,1024]{1,0:T(8,128)(2,1)}, bf16[256,1024]{1,0:T(8,128)(2,1)S(1)}, u32[]{:S(2)}) copy-start(bf16[256,1024]{1,0:T(8,128)(2,1)S(1)} %add_convert_fusion.1) | copy-start | bytes 1572868
  89.3 12.1 copy-start.41
  89.4 12.1 copy-start.42
  101.4 94.4 %all-gather.23.cloned.1.call-start = ((), (), s32[]{:S(2)}) async-start(), calls=%async_computation.18 | async-start | bytes 4718592 | tf_op jit(solution)/shard_map/all_gather | solution.py:191
  129.5 2.1 copy-start.43
  129.5 2.1 copy-start.44
  129.5 2.2 copy-start.45
  129.5 24.8 %copy-start.35 = (bf16[1024]{0:T(1024)(128)(2,1)S(1)}, bf16[1024]{0:T(1024)(128)(2,1)}, u32[]{:S(2)}) copy-start(bf16[1024]{0:T(1024)(128)(2,1)} %param.33) | copy-start | bytes 6148
  129.5 159.8 %all-gather.29.cloned.1.call-start = ((), (), s32[]{:S(2)}) async-start(), calls=%async_computation.21 | async-start | bytes 10485760 | tf_op jit(solution)/shard_map/all_gather | solution.py:133
  130.1 196.2 %all-gather.25.cloned.1.call-start = ((), (), s32[]{:S(2)}) async-start(), calls=%async_computation.19 | async-start | bytes 2621440 | tf_op jit(solution)/shard_map/all_gather | solution.py:131
  130.7 284.8 %all-gather.27.cloned.1.call-start = ((), (), s32[]{:S(2)}) async-start(), calls=%async_computation.20 | async-start | bytes 10485760 | tf_op jit(solution)/shard_map/all_gather | solution.py:132
  163.4 10.3 all-to-all-start
  238.2 51.2 %copy-start.8 = (bf16[4,1,2,32,1024]{4,3,2,1,0:T(8,128)(2,1)S(1)}, bf16[4,1,2,32,1024]{4,3,2,1,0:T(8,128)(2,1)}, u32[]{:S(2)}) copy-start(bf16[4,1,2,32,1024]{4,3,2,1,0:T(8,128)(2,1)} %param.21) | copy-start | bytes 1572868
  239.5 57.6 %all-to-all-start.3 = ((bf16[4,2,128,1,256]{4,1,0,3,2:T(2,128)(2,1)}), bf16[4,2,128,1,256]{4,1,0,3,2:T(2,128)(2,1)S(1)}, u32[]{:S(2)}, u32[]{:S(2)}) async-start(bf16[4,2,128,1,256]{4,1,0,3,2:T(2,128)(2,1)} %copy.104), calls=%async_computation.3 | async-start | bytes 1048576 | tf_op jit(solution)/shard_map/all_to_all | solution.py:200
  297.7 31.0 %copy-start.17 = (bf16[32,8,4,256]{3,1,2,0:T(8,128)(2,1)}, bf16[32,8,4,256]{3,1,2,0:T(8,128)(2,1)S(1)}, u32[]{:S(2)}) copy-start(bf16[32,8,4,256]{3,1,2,0:T(8,128)(2,1)S(1)} %copy.154) | copy-start | bytes 1572868
  328.7 102.3 %copy-start.2 = (f32[256,1024]{1,0:T(8,128)}, f32[256,1024]{1,0:T(8,128)S(1)}, u32[]{:S(2)}) copy-start(f32[256,1024]{1,0:T(8,128)S(1)} %get-tuple-element.309) | copy-start | bytes 3145732
  329.0 102.0 %copy-start.22 = (f32[256]{0:T(256)}, f32[256]{0:T(256)S(1)}, u32[]{:S(2)}) copy-start(f32[256]{0:T(256)S(1)} %fusion.84) | copy-start | bytes 3076
  415.5 12.3 copy-start.39
  427.8 3.2 copy-start.14
  431.0 3.0 copy-start.40
  431.5 3.3 copy-start.28
  436.1 11.6 all-to-all-start.4
  439.6 275.3 %all-reduce.34.cloned.1.call-start = ((), (), s32[]{:S(2)}) async-start(), calls=%async_computation.33 | async-start | bytes 16777216
  449.3 3.4 copy-start.6
  449.3 3.4 copy-start.18
  469.5 2.2 copy-start.19
  471.8 3.4 copy-start.6
  471.8 3.4 copy-start.18
  492.0 2.1 copy-start.19
  494.2 3.4 copy-start.6
  494.2 3.4 copy-start.18
  516.7 3.4 copy-start.6
  516.7 3.4 copy-start.18
  536.9 2.1 copy-start.19
  539.1 5.8 copy-start.38
  541.5 176.6 %all-to-all-start.5 = ((bf16[4,2,128,1,256]{4,1,0,3,2:T(2,128)(2,1)}), bf16[4,2,128,1,256]{4,1,0,3,2:T(2,128)(2,1)S(1)}, u32[]{:S(2)}, u32[]{:S(2)}) async-start(bf16[4,2,128,1,256]{4,1,0,3,2:T(2,128)(2,1)} %copy.110), calls=%async_computation.5 | async-start | bytes 1048576 | tf_op jit(solution)/shard_map/all_to_all | solution.py:252
  718.1 11.6 all-to-all-start.6
  729.7 10.5 all-to-all-start.7
  733.2 82.6 %reduce-scatter.15.cloned.1.call-start = ((), (), s32[]{:S(2)}) async-start(), calls=%async_computation.22 | async-start | bytes 7864320 | tf_op jit(solution)/shard_map/reduce_scatter | solution.py:279
  745.9 159.3 %reduce-scatter.23.cloned.1.call-start = ((), (), s32[]{:S(2)}) async-start(), calls=%async_computation.27 | async-start | bytes 10485760 | tf_op jit(solution)/shard_map/reduce_scatter | solution.py:285
  755.1 239.4 %reduce-scatter.27.cloned.1.call-start = ((), (), s32[]{:S(2)}) async-start(), calls=%async_computation.30 | async-start | bytes 10485760 | tf_op jit(solution)/shard_map/reduce_scatter | solution.py:288
  764.6 268.7 %reduce-scatter.19.cloned.1.call-start = ((), (), s32[]{:S(2)}) async-start(), calls=%async_computation.25 | async-start | bytes 2621440 | tf_op jit(solution)/shard_map/reduce_scatter | solution.py:282
  768.0 301.7 %reduce-scatter.17.cloned.1.call-start = ((), (), s32[]{:S(2)}) async-start(), calls=%async_computation.23 | async-start | bytes 1769472 | tf_op jit(solution)/shard_map/reduce_scatter | solution.py:320
  815.8 290.7 %reduce-scatter.25.cloned.1.call-start = ((), (), s32[]{:S(2)}) async-start(), calls=%async_computation.28 | async-start | bytes 2359296 | tf_op jit(solution)/shard_map/reduce_scatter | solution.py:326
  905.3 238.7 %copy-start.47 = (u32[32]{0:T(128)S(1)}, u32[32]{0:T(128)}, u32[]{:S(2)}) copy-start(u32[32]{0:T(128)} %constant.158) | copy-start | bytes 388
  905.3 241.2 %copy-start.46 = (bf16[256]{0:T(256)(128)(2,1)S(1)}, bf16[256]{0:T(256)(128)(2,1)}, u32[]{:S(2)}) copy-start(bf16[256]{0:T(256)(128)(2,1)} %param.35) | copy-start | bytes 1540
  905.3 238.0 %reduce-scatter.29.cloned.1.call-start = ((), (), s32[]{:S(2)}) async-start(), calls=%async_computation.31 | async-start | bytes 2359296 | tf_op jit(solution)/shard_map/reduce_scatter | solution.py:329
  994.5 240.5 %reduce-scatter.21.cloned.1.call-start = ((), (), s32[]{:S(2)}) async-start(), calls=%async_computation.26 | async-start | bytes 589824 | tf_op jit(solution)/shard_map/reduce_scatter | solution.py:323
  1033.3 219.9 %all-gather.31.cloned.1.call-start = ((), (), s32[]{:S(2)}) async-start(), calls=%async_computation.24 | async-start | bytes 1769472 | tf_op jit(solution)/shard_map/all_gather | solution.py:361
  1069.7 187.0 %all-gather.33.cloned.1.call-start = ((), (), s32[]{:S(2)}) async-start(), calls=%async_computation.29 | async-start | bytes 2359296 | tf_op jit(solution)/shard_map/all_gather | solution.py:367
  1106.5 156.4 %all-gather.35.cloned.1.call-start = ((), (), s32[]{:S(2)}) async-start(), calls=%async_computation.32 | async-start | bytes 2359296 | tf_op jit(solution)/shard_map/all_gather | solution.py:370
  1165.4 4.8 copy-start.31
  1165.4 5.8 copy-start.27
  1165.4 6.3 copy-start.32
  1165.4 6.3 copy-start.33
  1165.4 6.3 copy-start.36
  1165.4 6.3 copy-start.37
  1165.4 66.9 %copy-start.29 = (f32[256]{0:T(256)S(1)}, f32[256]{0:T(256)}, u32[]{:S(2)}) copy-start(f32[256]{0:T(256)} %copy-done.28) | copy-start | bytes 3076
  1170.2 62.1 %copy-start.5 = (f32[256,1024]{1,0:T(8,128)S(1)}, f32[256,1024]{1,0:T(8,128)}, u32[]{:S(2)}) copy-start(f32[256,1024]{1,0:T(8,128)} %copy-done.4) | copy-start | bytes 3145732
  (20 other events, 23.0 us)
Sparse Core Ops, SparseCore 0:
  9.8 72.7 all-gather.18
  101.5 46.2 all-gather.20
  150.0 45.6 all-gather.22
  197.4 91.8 all-gather.28
  291.0 35.2 all-gather.24
  328.0 87.4 all-gather.26
  539.2 175.5 all-reduce.33
  746.1 69.7 reduce-scatter.14
  818.9 86.3 reduce-scatter.22
  908.2 86.3 reduce-scatter.26
  998.1 35.1 reduce-scatter.18
  1035.4 34.1 reduce-scatter.16
  1071.9 34.5 reduce-scatter.24
  1108.6 34.5 reduce-scatter.28
  1145.4 29.7 reduce-scatter.20
  1176.7 23.6 all-gather.30
  1201.8 28.6 all-gather.32
  1232.0 30.8 all-gather.34
where the time goes:
time: 1280 us; the launch traced here: 1270 us
  waiting for transfers between devices  806 us (63%)
  blocking collectives  162 us (13%)
  matrix products  139 us (11%)
  local copies, waits for them, and re-layouts  78.4 us (6%)
  other arithmetic  45.8 us (4%)
  starting transfers between devices  23.1 us (2%)
  between operations  19 us (1%)
    unnamed x19, waiting for transfers between devices  172 us
    reduce_scatter x1, waiting for transfers between devices, shards(): lax.psum_scatter(fc_grad.astype(jnp.bfloat16), 'fsdp', scatter_dimension=...  89.4 us
    reduce_scatter x1, waiting for transfers between devices, shards(): lax.psum_scatter(proj_grad.astype(jnp.bfloat16), 'fsdp', scatter_dimensio...  89.2 us
    all_gather x1, waiting for transfers between devices, shards(): lax.all_gather(fc_weight, 'fsdp', axis=0, tiled=True)  86.5 us
    all_gather x1, waiting for transfers between devices, shards(): lax.all_gather(qkv_weight, 'fsdp', axis=0, tiled=True)  53 us
    reduce_scatter x1, waiting for transfers between devices, shards(): lax.psum_scatter(qkv_grad.astype(jnp.bfloat16), 'fsdp', scatter_dimension...  47.8 us
    dot_general x52, matrix products, contract_last(): lax.dot_general(left, right, (((1,), (1,)), ((), ())), preferred_element_...  46.5 us
    all_gather x1, waiting for transfers between devices, shards(): lax.all_gather(proj_weight, 'fsdp', axis=0, tiled=True)  45.7 us
  transfers between devices with their start and end apart: 24, of which 18 were waited for; matrix products, arithmetic and copies ran while one was open for 10% of the time, Pallas kernels for 0%

commit v1 on v0

--- a/solution.py
+++ b/solution.py
@@ -232,20 +232,16 @@
         attend_backward,
         (query_heads, key_all, value_all, grad_heads, summary, query_places, key_places),
     )
-    key_part, value_part = (
-        lax.psum_scatter(
-            grad_keys.reshape(seq_count, ctx_size, pair_len, group_width).astype(jnp.bfloat16),
-            "ctx",
-            scatter_dimension=1,
-            tiled=True,
-        ).astype(jnp.float32),
-        lax.psum_scatter(
-            grad_values.reshape(seq_count, ctx_size, pair_len, group_width).astype(jnp.bfloat16),
-            "ctx",
-            scatter_dimension=1,
-            tiled=True,
-        ).astype(jnp.float32),
-    )
+    kv_grads = jnp.concatenate([grad_keys, grad_values], axis=2).astype(jnp.bfloat16)
+    kv_grads = kv_grads.reshape(seq_count, ctx_size, pair_len, 2 * group_width).transpose(1, 0, 2, 3)
+    kv_part = lax.psum_scatter(
+        kv_grads.reshape(ctx_size * seq_count * pair_len, 2 * group_width),
+        "ctx",
+        scatter_dimension=0,
+        tiled=True,
+    ).reshape(seq_count, pair_len, 2 * group_width)
+    key_part = kv_part[..., :group_width].astype(jnp.float32)
+    value_part = kv_part[..., group_width:].astype(jnp.float32)
     key_grad_low = key_part.astype(jnp.bfloat16)
     value_grad_low = value_part.astype(jnp.bfloat16)
     query_back, key_back, value_back = (

time: 1280 us -> 1200 us (0.938)
  waiting for transfers between devices: 806 us -> 706 us
    unnamed x19 -> x18, waiting for transfers between devices: 172 us -> 2.49 us
    reduce_scatter x0 -> x1, waiting for transfers between devices: none -> 66.3 us  [shards(): lax.psum_scatter(kv_grads.reshape(ctx_size * seq_count * pair_len, 2 * gr...]
    reduce_scatter x1, waiting for transfers between devices: 89.4 us -> 49.4 us  [shards(): lax.psum_scatter(fc_grad.astype(jnp.bfloat16), 'fsdp', scatter_dimension=...]
    reduce_scatter x1, waiting for transfers between devices: 47.8 us -> 72.8 us  [shards(): lax.psum_scatter(qkv_grad.astype(jnp.bfloat16), 'fsdp', scatter_dimension...]
    reduce_scatter x1, waiting for transfers between devices: 0.01 us -> 23.6 us  [shards(): lax.psum_scatter(shares[1].astype(jnp.bfloat16), 'ctx', scatter_dimension...]
    reduce_scatter x1, waiting for transfers between devices: 36.3 us -> 22.2 us  [shards(): lax.psum_scatter(shares[0].astype(jnp.bfloat16), 'ctx', scatter_dimension...]
  transfers between devices with their start and end apart: 24 -> 24, of which waited for: 18 -> 18; matrix products, arithmetic and copies ran while one was open for 10% -> 11% of each run, Pallas kernels for 0% -> 0%
where the time goes in v1:
time: 1200 us; the launch traced here: 1190 us
  waiting for transfers between devices  706 us (59%)
  blocking collectives  162 us (14%)
  matrix products  137 us (11%)
  local copies, waits for them, and re-layouts  88.9 us (7%)
  other arithmetic  53.2 us (4%)
  starting transfers between devices  23.7 us (2%)
  between operations  18.7 us (2%)
    reduce_scatter x1, waiting for transfers between devices, shards(): lax.psum_scatter(proj_grad.astype(jnp.bfloat16), 'fsdp', scatter_dimensio...  89.4 us
    all_gather x1, waiting for transfers between devices, shards(): lax.all_gather(fc_weight, 'fsdp', axis=0, tiled=True)  86.5 us
    reduce_scatter x1, waiting for transfers between devices, shards(): lax.psum_scatter(qkv_grad.astype(jnp.bfloat16), 'fsdp', scatter_dimension...  72.8 us
    reduce_scatter x1, waiting for transfers between devices, shards(): lax.psum_scatter(kv_grads.reshape(ctx_size * seq_count * pair_len, 2 * gr...  66.3 us
    all_gather x1, waiting for transfers between devices, shards(): lax.all_gather(qkv_weight, 'fsdp', axis=0, tiled=True)  53 us
    reduce_scatter x1, waiting for transfers between devices, shards(): lax.psum_scatter(fc_grad.astype(jnp.bfloat16), 'fsdp', scatter_dimension=...  49.4 us
    dot_general x52, matrix products, contract_last(): lax.dot_general(left, right, (((1,), (1,)), ((), ())), preferred_element_...  46.6 us
    all_gather x1, waiting for transfers between devices, shards(): lax.all_gather(proj_weight, 'fsdp', axis=0, tiled=True)  46 us
  transfers between devices with their start and end apart: 24, of which 18 were waited for; matrix products, arithmetic and copies ran while one was open for 11% of the time, Pallas kernels for 0%

profile of v1, /device:TPU:0, one launch (start us, length us, event | category | flops | bytes accessed | tf_op | source)
XLA Modules:
  0.0 1190.1 jit_solution(14960755633067397049)
XLA Ops:
  9.3 9.6 all-gather.1
  18.9 8.2 all-gather
  29.6 53.0 %all-gather.19.cloned.1.call-done = bf16[1024,3072]{1,0:T(8,128)(2,1)} async-done(((bf16[256,3072]{1,0:T(8,128)(2,1)}), bf16[1024,3072]{1,0:T(8,128)(2,1)}) %all-gather.19.cloned.1.call-update) | async-done | bytes 6291472 | tf_op jit(solution)/shard_map/all_gather | solution.py:130
  82.6 4.6 fusion.100
  89.5 11.0 all_to_all.114
  101.5 7.5 all-gather.3
  108.9 7.7 all-gather.2
  116.6 1.8 fusion.79
  118.9 9.6 all_to_all.115
  131.7 7.5 all-gather.6
  139.2 7.7 all-gather.5
  146.8 7.5 all-gather.4
  154.3 7.8 all_gather.96
  163.4 3.6 all-to-all-start
  167.1 6.5 all-to-all-done
  173.7 4.7 copy.99
  178.3 17.4 %all-gather.23.cloned.1.call-done = bf16[4,8,256,256]{3,2,0,1:T(8,128)(2,1)} async-done(((bf16[4,1,256,256]{3,2,0,1:T(8,128)(2,1)}), bf16[4,8,256,256]{3,2,0,1:T(8,128)(2,1)}) %all-gather.23.cloned.1.call-update) | async-done | bytes 4194320 | tf_op jit(solution)/shard_map/all_gather | solution.py:191
  195.7 4.6 copy.102
  200.4 37.8 %while.26 = (s32[]{:T(128)}, bf16[4,256,256]{2,1,0:T(8,128)(2,1)S(1)}, f32[4,256,4]{1,2,0:T(4,128)}, s32[4,2048]{1,0:T(4,128)S(1)}, s32[4,256]{1,0:T(4,128)S(1)}...) while((s32[]{:T(128)}, ...), condition=%wide.region_11.12_spmd, body=%wide.region_2.11_spmd.sunk | while | flops 554240000 | bytes 35092604 | solution.py:197
  200.5 1.7 dynamic-slice_bitcast_fusion.14
  209.9 1.7 dynamic-slice_bitcast_fusion.14
  239.5 3.9 all-to-all-start.3
  243.4 46.0 %all-gather.29.cloned.1.call-done = bf16[4096,1024]{1,0:T(8,128)(2,1)} async-done(((bf16[1024,1024]{1,0:T(8,128)(2,1)}), bf16[4096,1024]{1,0:T(8,128)(2,1)}) %all-gather.29.cloned.1.call-update) | async-done | bytes 8388624 | tf_op jit(solution)/shard_map/all_gather | solution.py:133
  289.4 7.8 fusion.101
  297.8 28.5 %all-gather.25.cloned.1.call-done = bf16[1024,1024]{1,0:T(8,128)(2,1)} async-done(((bf16[256,1024]{1,0:T(8,128)(2,1)}), bf16[1024,1024]{1,0:T(8,128)(2,1)}) %all-gather.25.cloned.1.call-update) | async-done | bytes 2097168 | tf_op jit(solution)/shard_map/all_gather | solution.py:131
  326.3 2.4 fusion.99
  329.0 86.5 %all-gather.27.cloned.1.call-done = bf16[1024,4096]{1,0:T(8,128)(2,1)} async-done(((bf16[256,4096]{1,0:T(8,128)(2,1)}), bf16[1024,4096]{1,0:T(8,128)(2,1)}) %all-gather.27.cloned.1.call-update) | async-done | bytes 8388624 | tf_op jit(solution)/shard_map/all_gather | solution.py:132
  415.5 12.3 %fusion.87 = (bf16[4096]{0:T(1024)(128)(2,1)}, bf16[256,4096]{1,0:T(8,128)(2,1)S(1)}, f32[256,4096]{1,0:T(8,128)}) fusion(f32[256,4096]{1,0:T(8,128)} %fusion.101, f32[4096]{0:T(1024)S(1)} %convert_element_type.277, bf16[1024,4096]{1,0:T(8,128)(2,1)} %all-gather.27.cloned.1.call-done, f32[256,1024]{1,0:T(8,128)S(1)} %get-tuple-element.309, ...), kind=kOutput, calls=%fused_computation.194 | convolution fusion | flops 2171858944 | bytes 19957760 | tf_op jit(solution)/shard_map/dot_general | solution.py:207
  427.8 3.2 multiply_reduce_fusion.4
  436.0 3.5 all-to-all-start.4
  440.0 7.6 all-to-all-done.4
  449.2 89.8 %while.27 = (s32[]{:T(128)}, bf16[4,256,256]{2,1,0:T(8,128)(2,1)}, bf16[4,2048,256]{2,1,0:T(8,128)(2,1)}, bf16[4,2048,256]{2,1,0:T(8,128)(2,1)}, s32[4,2048]{1,0...) while((s32[]{:T(128)}, bf16[4,256,256]{2,1,0:T(8,128)(2,1)}, ...), condition=%wide.region_21.22_spmd, body=%wide.region_16.21_spmd.sunk | while | flops 1370029056 | bytes 95111440 | solution.py:231
  539.1 7.5 maximum_bitcast_fusion.5
  546.6 7.5 copy.115
  556.0 6.1 convolution_convert_fusion.9
  563.1 8.5 convolution_convert_fusion.8
  574.0 3.5 all-to-all-start.5
  577.5 66.3 %reduce-scatter.10.cloned.1.call-done = bf16[1024,512]{1,0:T(8,128)(2,1)} async-done(((bf16[8192,512]{1,0:T(8,128)(2,1)}), bf16[1024,512]{1,0:T(8,128)(2,1)}) %reduce-scatter.10.cloned.1.call-update) | async-done | bytes 1048592 | tf_op jit(solution)/shard_map/reduce_scatter | solution.py:237
  646.4 3.6 all-to-all-start.6
  651.4 11.2 all-to-all-done.6
  662.6 4.1 all-to-all-start.7
  669.9 9.2 all-to-all-done.7
  681.4 4.6 convolution_convert_fusion.10
  686.3 3.3 convolution_convert_fusion.11
  689.6 49.4 %reduce-scatter.20.cloned.1.call-done = bf16[256,4096]{1,0:T(8,128)(2,1)} async-done(((bf16[1024,4096]{1,0:T(8,128)(2,1)}), bf16[256,4096]{1,0:T(8,128)(2,1)}) %reduce-scatter.20.cloned.1.call-update) | async-done | bytes 2097168 | tf_op jit(solution)/shard_map/reduce_scatter | solution.py:281
  739.2 89.4 %reduce-scatter.24.cloned.1.call-done = bf16[1024,1024]{1,0:T(8,128)(2,1)} async-done(((bf16[4096,1024]{1,0:T(8,128)(2,1)}), bf16[1024,1024]{1,0:T(8,128)(2,1)}) %reduce-scatter.24.cloned.1.call-update) | async-done | bytes 2097168 | tf_op jit(solution)/shard_map/reduce_scatter | solution.py:284
  828.6 72.8 %reduce-scatter.12.cloned.1.call-done = bf16[256,3072]{1,0:T(8,128)(2,1)} async-done(((bf16[1024,3072]{1,0:T(8,128)(2,1)}), bf16[256,3072]{1,0:T(8,128)(2,1)}) %reduce-scatter.12.cloned.1.call-update) | async-done | bytes 1572880 | tf_op jit(solution)/shard_map/reduce_scatter | solution.py:275
  901.5 38.7 %reduce-scatter.16.cloned.1.call-done = bf16[256,1024]{1,0:T(8,128)(2,1)} async-done(((bf16[1024,1024]{1,0:T(8,128)(2,1)}), bf16[256,1024]{1,0:T(8,128)(2,1)}) %reduce-scatter.16.cloned.1.call-update) | async-done | bytes 524304 | tf_op jit(solution)/shard_map/reduce_scatter | solution.py:278
  940.3 38.1 %reduce-scatter.22.cloned.1.call-done = bf16[32,4096]{1,0:T(8,128)(2,1)} async-done(((bf16[256,4096]{1,0:T(8,128)(2,1)}), bf16[32,4096]{1,0:T(8,128)(2,1)}) %reduce-scatter.22.cloned.1.call-update) | async-done | bytes 262160 | tf_op jit(solution)/shard_map/reduce_scatter | solution.py:322
  978.5 36.7 %reduce-scatter.26.cloned.1.call-done = bf16[128,1024]{1,0:T(8,128)(2,1)} async-done(((bf16[1024,1024]{1,0:T(8,128)(2,1)}), bf16[128,1024]{1,0:T(8,128)(2,1)}) %reduce-scatter.26.cloned.1.call-update) | async-done | bytes 262160 | tf_op jit(solution)/shard_map/reduce_scatter | solution.py:325
  1019.2 8.2 all-gather.7
  1028.1 22.2 %reduce-scatter.14.cloned.1.call-done = bf16[32,3072]{1,0:T(8,128)(2,1)} async-done(((bf16[256,3072]{1,0:T(8,128)(2,1)}), bf16[32,3072]{1,0:T(8,128)(2,1)}) %reduce-scatter.14.cloned.1.call-update) | async-done | bytes 196624 | tf_op jit(solution)/shard_map/reduce_scatter | solution.py:316
  1050.3 8.2 fusion.78
  1058.5 23.6 %reduce-scatter.18.cloned.1.call-done = bf16[32,1024]{1,0:T(8,128)(2,1)} async-done(((bf16[256,1024]{1,0:T(8,128)(2,1)}), bf16[32,1024]{1,0:T(8,128)(2,1)}) %reduce-scatter.18.cloned.1.call-update) | async-done | bytes 65552 | tf_op jit(solution)/shard_map/reduce_scatter | solution.py:319
  1082.2 16.3 %all_gather.104 = bf16[256,1024]{1,0:T(8,128)(2,1)S(1)} all-gather(bf16[32,1024]{1,0:T(8,128)(2,1)} %reduce-scatter.18.cloned.1.call-done), channel_id=1, replica_groups=mesh['ctx'=8,'fsdp'=4] {'ctx'}, dimensions={0}, use_global_device_ids=true | all-gather | bytes 589824 | tf_op jit(solution)/shard_map/all_gather | solution.py:360
  1101.1 4.8 fusion.86
  1107.4 16.1 %all-reduce.28 = (bf16[1024]{0:T(1024)(128)(2,1)S(1)}, bf16[1024]{0:T(1024)(128)(2,1)S(1)}, bf16[1024]{0:T(1024)(128)(2,1)S(1)}, bf16[1024]{0:T(1024)(128)(2,1)S...) all-reduce(bf16[1024]{0:T(1024)(128)(2,1)S(1)} %get-tuple-element.2, ...), channel_id=3, replica_groups=mesh['ctx'=8,'fsdp'=4] {'fsdp'}, use_global_device_ids=true, to_apply=%region_26.27.clone | all-reduce | flops 12288 | bytes 49152
  1124.1 14.5 %all-reduce.27 = (bf16[256]{0:T(256)(128)(2,1)S(1)}, bf16[256]{0:T(256)(128)(2,1)S(1)}, bf16[256]{0:T(256)(128)(2,1)S(1)}, bf16[256]{0:T(256)(128)(2,1)S(1)}, bf...) all-reduce(bf16[256]{0:T(256)(128)(2,1)S(1)} %dynamic-slice.9, ...), channel_id=4, replica_groups=mesh['ctx'=8,'fsdp'=4] {'ctx'}, use_global_device_ids=true, to_apply=%region_27.28.clone | all-reduce | flops 2048 | bytes 8192
  1140.9 14.0 %all-reduce.26 = (bf16[256]{0:T(256)(128)(2,1)S(1)}, bf16[256]{0:T(256)(128)(2,1)S(1)}, bf16[256]{0:T(256)(128)(2,1)S(1)}, bf16[256]{0:T(256)(128)(2,1)S(1)}, bf...) all-reduce(bf16[256]{0:T(256)(128)(2,1)S(1)} %dynamic-update-slice,, ...), channel_id=1, replica_groups=mesh['ctx'=8,'fsdp'=4] {'ctx'}, use_global_device_ids=true, to_apply=%add | all-reduce | flops 3072 | bytes 12288
  1159.5 8.6 all-gather.8
  1168.7 2.7 add_add_fusion.2
  1171.4 4.1 convert_element_type.304
  1175.5 4.1 convert_element_type.307
  1179.5 3.4 convert_element_type.290
  (552 shorter events, 173.4 us)
Async XLA Ops:
  7.2 21.2 %copy-start = (bf16[4,1,2,32,1024]{4,3,2,1,0:T(8,128)(2,1)S(1)}, bf16[4,1,2,32,1024]{4,3,2,1,0:T(8,128)(2,1)}, u32[]{:S(2)}) copy-start(bf16[4,1,2,32,1024]{4,3,2,1,0:T(8,128)(2,1)} %param.20) | copy-start | bytes 1572868
  7.2 75.4 %all-gather.19.cloned.1.call-start = ((), (), s32[]{:S(2)}) async-start(), calls=%async_computation.17 | async-start | bytes 7864320 | tf_op jit(solution)/shard_map/all_gather | solution.py:130
  7.9 165.7 %all-gather.21.cloned.1.call-start = ((), (), s32[]{:S(2)}) async-start(), calls=%async_computation.18 | async-start | bytes 4718592 | tf_op jit(solution)/shard_map/all_gather | solution.py:188
  27.1 55.6 %copy-start.23 = (f32[4,1,256]{2,1,0:T(1,128)}, f32[4,1,256]{2,1,0:T(1,128)S(1)}, u32[]{:S(2)}) copy-start(f32[4,1,256]{2,1,0:T(1,128)S(1)} %convert_element_type.310) | copy-start | bytes 12292
  28.4 54.3 %copy-start.27 = (f32[256]{0:T(256)}, f32[256]{0:T(256)S(1)}, u32[]{:S(2)}) copy-start(f32[256]{0:T(256)S(1)} %div.71) | copy-start | bytes 3076
  29.6 57.6 %copy-start.11 = (bf16[256,1024]{1,0:T(8,128)(2,1)}, bf16[256,1024]{1,0:T(8,128)(2,1)S(1)}, u32[]{:S(2)}) copy-start(bf16[256,1024]{1,0:T(8,128)(2,1)S(1)} %add_convert_fusion.1) | copy-start | bytes 1572868
  89.3 12.1 %copy-start.44 = (bf16[256]{0:T(256)(128)(2,1)S(1)}, bf16[256]{0:T(256)(128)(2,1)}, u32[]{:S(2)}) copy-start(bf16[256]{0:T(256)(128)(2,1)} %param.26) | copy-start | bytes 1540
  89.4 12.1 %copy-start.45 = (bf16[256]{0:T(256)(128)(2,1)S(1)}, bf16[256]{0:T(256)(128)(2,1)}, u32[]{:S(2)}) copy-start(bf16[256]{0:T(256)(128)(2,1)} %param.27) | copy-start | bytes 1540
  101.4 94.3 %all-gather.23.cloned.1.call-start = ((), (), s32[]{:S(2)}) async-start(), calls=%async_computation.19 | async-start | bytes 4718592 | tf_op jit(solution)/shard_map/all_gather | solution.py:191
  129.5 2.1 copy-start.46
  129.5 2.1 copy-start.47
  129.5 2.2 copy-start.48
  129.5 24.8 %copy-start.38 = (bf16[1024]{0:T(1024)(128)(2,1)S(1)}, bf16[1024]{0:T(1024)(128)(2,1)}, u32[]{:S(2)}) copy-start(bf16[1024]{0:T(1024)(128)(2,1)} %param.33) | copy-start | bytes 6148
  129.5 159.8 %all-gather.29.cloned.1.call-start = ((), (), s32[]{:S(2)}) async-start(), calls=%async_computation.22 | async-start | bytes 10485760 | tf_op jit(solution)/shard_map/all_gather | solution.py:133
  130.1 196.2 %all-gather.25.cloned.1.call-start = ((), (), s32[]{:S(2)}) async-start(), calls=%async_computation.20 | async-start | bytes 2621440 | tf_op jit(solution)/shard_map/all_gather | solution.py:131
  130.7 284.8 %all-gather.27.cloned.1.call-start = ((), (), s32[]{:S(2)}) async-start(), calls=%async_computation.21 | async-start | bytes 10485760 | tf_op jit(solution)/shard_map/all_gather | solution.py:132
  163.4 10.2 all-to-all-start
  238.2 51.2 %copy-start.8 = (bf16[4,1,2,32,1024]{4,3,2,1,0:T(8,128)(2,1)S(1)}, bf16[4,1,2,32,1024]{4,3,2,1,0:T(8,128)(2,1)}, u32[]{:S(2)}) copy-start(bf16[4,1,2,32,1024]{4,3,2,1,0:T(8,128)(2,1)} %param.21) | copy-start | bytes 1572868
  239.5 57.6 %all-to-all-start.3 = ((bf16[4,2,128,1,256]{4,1,0,3,2:T(2,128)(2,1)}), bf16[4,2,128,1,256]{4,1,0,3,2:T(2,128)(2,1)S(1)}, u32[]{:S(2)}, u32[]{:S(2)}) async-start(bf16[4,2,128,1,256]{4,1,0,3,2:T(2,128)(2,1)} %copy.104), calls=%async_computation.3 | async-start | bytes 1048576 | tf_op jit(solution)/shard_map/all_to_all | solution.py:200
  297.7 31.0 %copy-start.20 = (bf16[32,8,4,256]{3,1,2,0:T(8,128)(2,1)}, bf16[32,8,4,256]{3,1,2,0:T(8,128)(2,1)S(1)}, u32[]{:S(2)}) copy-start(bf16[32,8,4,256]{3,1,2,0:T(8,128)(2,1)S(1)} %copy.151) | copy-start | bytes 1572868
  328.7 102.3 %copy-start.2 = (f32[256,1024]{1,0:T(8,128)}, f32[256,1024]{1,0:T(8,128)S(1)}, u32[]{:S(2)}) copy-start(f32[256,1024]{1,0:T(8,128)S(1)} %get-tuple-element.309) | copy-start | bytes 3145732
  329.0 102.0 %copy-start.25 = (f32[256]{0:T(256)}, f32[256]{0:T(256)S(1)}, u32[]{:S(2)}) copy-start(f32[256]{0:T(256)S(1)} %fusion.84) | copy-start | bytes 3076
  415.5 12.3 %copy-start.42 = (bf16[1024,4096]{1,0:T(8,128)(2,1)S(1)}, bf16[1024,4096]{1,0:T(8,128)(2,1)}, u32[]{:S(2)}) copy-start(bf16[1024,4096]{1,0:T(8,128)(2,1)} %all-gather.27.cloned.1.call-done) | copy-start | bytes 25165828
  427.8 3.2 copy-start.14
  431.0 3.0 copy-start.43
  431.4 3.3 copy-start.31
  436.0 11.6 all-to-all-start.4
  439.5 204.3 %reduce-scatter.10.cloned.1.call-start = ((), (), s32[]{:S(2)}) async-start(), calls=%async_computation.23 | async-start | bytes 9437184 | tf_op jit(solution)/shard_map/reduce_scatter | solution.py:237
  449.2 3.4 copy-start.6
  449.2 3.4 copy-start.21
  469.4 2.1 copy-start.22
  471.7 3.4 copy-start.6
  471.7 3.4 copy-start.21
  494.1 3.4 copy-start.6
  494.1 3.4 copy-start.21
  516.6 3.4 copy-start.6
  516.6 3.4 copy-start.21
  536.7 2.2 copy-start.22
  554.1 185.0 %reduce-scatter.20.cloned.1.call-start = ((), (), s32[]{:S(2)}) async-start(), calls=%async_computation.29 | async-start | bytes 10485760 | tf_op jit(solution)/shard_map/reduce_scatter | solution.py:281
  562.1 266.4 %reduce-scatter.24.cloned.1.call-start = ((), (), s32[]{:S(2)}) async-start(), calls=%async_computation.32 | async-start | bytes 10485760 | tf_op jit(solution)/shard_map/reduce_scatter | solution.py:284
  574.0 72.4 %all-to-all-start.5 = ((bf16[4,2,128,1,256]{4,1,0,3,2:T(2,128)(2,1)}), bf16[4,2,128,1,256]{4,1,0,3,2:T(2,128)(2,1)S(1)}, u32[]{:S(2)}, u32[]{:S(2)}) async-start(bf16[4,2,128,1,256]{4,1,0,3,2:T(2,128)(2,1)} %copy.110), calls=%async_computation.5 | async-start | bytes 1048576 | tf_op jit(solution)/shard_map/all_to_all | solution.py:248
  646.4 16.2 %all-to-all-start.6 = ((bf16[4,2,128,1,256]{4,1,0,3,2:T(2,128)(2,1)}), bf16[4,2,128,1,256]{4,1,0,3,2:T(2,128)(2,1)S(1)}, u32[]{:S(2)}, u32[]{:S(2)}) async-start(bf16[4,2,128,1,256]{4,1,0,3,2:T(2,128)(2,1)} %copy.116), calls=%async_computation.7 | async-start | bytes 1048576 | tf_op jit(solution)/shard_map/all_to_all | solution.py:251
  662.6 4.8 copy-start.17
  662.6 16.5 %all-to-all-start.7 = ((bf16[4,2,128,1,256]{4,1,0,3,2:T(2,128)(2,1)}), bf16[4,2,128,1,256]{4,1,0,3,2:T(2,128)(2,1)}, u32[]{:S(2)}, u32[]{:S(2)}) async-start(bf16[4,2,128,1,256]{4,1,0,3,2:T(2,128)(2,1)} %copy.119), calls=%async_computation.8 | async-start | bytes 1048576 | tf_op jit(solution)/shard_map/all_to_all | solution.py:254
  666.7 234.7 %reduce-scatter.12.cloned.1.call-start = ((), (), s32[]{:S(2)}) async-start(), calls=%async_computation.24 | async-start | bytes 7864320 | tf_op jit(solution)/shard_map/reduce_scatter | solution.py:275
  686.0 254.2 %reduce-scatter.16.cloned.1.call-start = ((), (), s32[]{:S(2)}) async-start(), calls=%async_computation.27 | async-start | bytes 2621440 | tf_op jit(solution)/shard_map/reduce_scatter | solution.py:278
  689.6 288.8 %reduce-scatter.22.cloned.1.call-start = ((), (), s32[]{:S(2)}) async-start(), calls=%async_computation.30 | async-start | bytes 2359296 | tf_op jit(solution)/shard_map/reduce_scatter | solution.py:322
  739.1 276.1 %reduce-scatter.26.cloned.1.call-start = ((), (), s32[]{:S(2)}) async-start(), calls=%async_computation.33 | async-start | bytes 2359296 | tf_op jit(solution)/shard_map/reduce_scatter | solution.py:325
  828.5 186.8 %copy-start.50 = (u32[32]{0:T(128)S(1)}, u32[32]{0:T(128)}, u32[]{:S(2)}) copy-start(u32[32]{0:T(128)} %constant.150) | copy-start | bytes 388
  828.5 188.7 %copy-start.41 = (u32[32]{0:T(128)S(1)}, u32[32]{0:T(128)}, u32[]{:S(2)}) copy-start(u32[32]{0:T(128)} %constant.102) | copy-start | bytes 388
  828.5 190.6 %copy-start.49 = (bf16[256]{0:T(256)(128)(2,1)S(1)}, bf16[256]{0:T(256)(128)(2,1)}, u32[]{:S(2)}) copy-start(bf16[256]{0:T(256)(128)(2,1)} %param.35) | copy-start | bytes 1540
  828.5 221.8 %reduce-scatter.14.cloned.1.call-start = ((), (), s32[]{:S(2)}) async-start(), calls=%async_computation.25 | async-start | bytes 1769472 | tf_op jit(solution)/shard_map/reduce_scatter | solution.py:316
  901.5 180.7 %reduce-scatter.18.cloned.1.call-start = ((), (), s32[]{:S(2)}) async-start(), calls=%async_computation.28 | async-start | bytes 589824 | tf_op jit(solution)/shard_map/reduce_scatter | solution.py:319
  940.2 231.1 %all-gather.33.cloned.1.call-start = ((), (), s32[]{:S(2)}) async-start(), calls=%async_computation.31 | async-start | bytes 2359296 | tf_op jit(solution)/shard_map/all_gather | solution.py:363
  978.5 197.0 %all-gather.35.cloned.1.call-start = ((), (), s32[]{:S(2)}) async-start(), calls=%async_computation.34 | async-start | bytes 2359296 | tf_op jit(solution)/shard_map/all_gather | solution.py:366
  1015.3 164.3 %all-gather.31.cloned.1.call-start = ((), (), s32[]{:S(2)}) async-start(), calls=%async_computation.26 | async-start | bytes 1769472 | tf_op jit(solution)/shard_map/all_gather | solution.py:357
  1101.0 4.9 copy-start.34
  1101.0 5.8 copy-start.30
  1101.0 6.4 copy-start.35
  1101.0 6.4 copy-start.36
  1101.0 6.4 copy-start.39
  1101.0 6.4 copy-start.40
  1101.0 67.6 %copy-start.32 = (f32[256]{0:T(256)S(1)}, f32[256]{0:T(256)}, u32[]{:S(2)}) copy-start(f32[256]{0:T(256)} %copy-done.31) | copy-start | bytes 3076
  1105.9 62.8 %copy-start.5 = (f32[256,1024]{1,0:T(8,128)S(1)}, f32[256,1024]{1,0:T(8,128)}, u32[]{:S(2)}) copy-start(f32[256,1024]{1,0:T(8,128)} %copy-done.4) | copy-start | bytes 3145732
  (23 other events, 29.5 us)
Sparse Core Ops, SparseCore 0:
  9.8 72.7 all-gather.18
  101.5 46.2 all-gather.20
  150.0 45.6 all-gather.22
  197.4 91.9 all-gather.28
  291.0 35.2 all-gather.24
  328.0 87.4 all-gather.26
  554.2 89.5 reduce-scatter.9
  646.9 92.1 reduce-scatter.19
  742.2 86.3 reduce-scatter.23
  831.3 70.0 reduce-scatter.11
  905.0 35.1 reduce-scatter.15
  942.4 36.0 reduce-scatter.21
  980.7 34.4 reduce-scatter.25
  1017.4 32.8 reduce-scatter.13
  1052.4 29.7 reduce-scatter.17
  1083.6 27.7 all-gather.32
  1112.8 29.6 all-gather.34
  1144.1 24.6 all-gather.30

commit v2 on v1

--- a/solution.py
+++ b/solution.py
@@ -100,6 +100,33 @@
     )
 
 
+CTX = ("zc", "core")
+
+
+def gather_weight(shard):
+    half = shard.shape[0] // 2
+    piece = lax.dynamic_slice_in_dim(shard, lax.axis_index("core") * half, half, 0)
+    pieces = lax.all_gather(piece, "fsdp", axis=0, tiled=False)
+    whole = lax.all_gather(pieces, "core", axis=1, tiled=True)
+    return whole.reshape(-1, shard.shape[1])
+
+
+def core_major(rows, fsdp_size):
+    count, width = rows.shape
+    return rows.reshape(count, fsdp_size, 2, width // (2 * fsdp_size)).transpose(0, 2, 1, 3).reshape(
+        count, width
+    )
+
+
+def reduce_weight_grad(grad):
+    grad = lax.psum_scatter(grad.astype(jnp.bfloat16), "core", scatter_dimension=0, tiled=True)
+    grad = lax.psum_scatter(grad, "fsdp", scatter_dimension=0, tiled=True)
+    grad = lax.psum_scatter(grad, "zc", scatter_dimension=0, tiled=True)
+    grad = lax.all_gather(grad, "zc", axis=0, tiled=True)
+    grad = lax.all_gather(grad, "core", axis=0, tiled=True)
+    return grad.astype(jnp.float32)
+
+
 def shards(
     layer_in,
     out_grad,
@@ -119,7 +146,7 @@
     proj_bias,
 ):
     fsdp_size = lax.axis_size("fsdp")
-    ctx_size = lax.axis_size("ctx")
+    ctx_size = lax.axis_size("zc") * lax.axis_size("core")
     seq_count = layer_in.shape[0]
     half_rows = layer_in.shape[3]
     model_width = layer_in.shape[4]
@@ -127,10 +154,10 @@
     pair_len = 2 * block_len
     group_width = model_width // fsdp_size
     gathered = (
-        lax.all_gather(qkv_weight, "fsdp", axis=0, tiled=True),
-        lax.all_gather(out_weight, "fsdp", axis=0, tiled=True),
-        lax.all_gather(fc_weight, "fsdp", axis=0, tiled=True),
-        lax.all_gather(proj_weight, "fsdp", axis=0, tiled=True),
+        gather_weight(qkv_weight),
+        gather_weight(out_weight),
+        gather_weight(fc_weight),
+        gather_weight(proj_weight),
         lax.all_gather(attn_gain, "fsdp", axis=0, tiled=True),
         lax.all_gather(attn_shift, "fsdp", axis=0, tiled=True),
         lax.all_gather(query_bias, "fsdp", axis=0, tiled=True),
@@ -158,7 +185,7 @@
     key_places = (halves[..., None] * block_len + jnp.arange(block_len, dtype=jnp.int32)).reshape(
         seq_count, ctx_size, pair_len
     )
-    query_places = lax.dynamic_slice_in_dim(key_places, lax.axis_index("ctx"), 1, 1).reshape(
+    query_places = lax.dynamic_slice_in_dim(key_places, lax.axis_index(CTX), 1, 1).reshape(
         seq_count, pair_len
     )
     key_places = key_places.reshape(seq_count, ctx_size * pair_len)
@@ -186,10 +213,10 @@
     own_values = value_heads.reshape(seq_count, pair_len, group_width)
     key_all, value_all = (
         lax.all_gather(
-            own_keys.reshape(seq_count, 1, pair_len, group_width), "ctx", axis=1, tiled=True
+            own_keys.reshape(seq_count, 1, pair_len, group_width), CTX, axis=1, tiled=True
         ),
         lax.all_gather(
-            own_values.reshape(seq_count, 1, pair_len, group_width), "ctx", axis=1, tiled=True
+            own_values.reshape(seq_count, 1, pair_len, group_width), CTX, axis=1, tiled=True
         ),
     )
     key_all = key_all.reshape(seq_count, -1, group_width)
@@ -213,16 +240,16 @@
     layer_out = result.astype(jnp.bfloat16).reshape(layer_in.shape)
     grad_rows = out_grad.reshape(-1, model_width)
     grad_result = grad_rows.astype(jnp.float32)
-    proj_grad = contract_first(activated_low, grad_rows)
+    proj_grad = contract_first(core_major(activated_low, fsdp_size), grad_rows)
     proj_bias_grad = jnp.sum(grad_result, axis=0)
     grad_activated = contract_last(grad_rows, proj_full)
     grad_hidden = gelu_back(grad_activated)[0].astype(jnp.bfloat16)
-    fc_grad = contract_first(mlp_low, grad_hidden)
+    fc_grad = contract_first(core_major(mlp_low, fsdp_size), grad_hidden)
     fc_bias_grad = jnp.sum(grad_hidden.astype(jnp.float32), axis=0)
     grad_middle, mlp_gain_grad, mlp_shift_grad = mlp_norm_back(contract_last(grad_hidden, fc_full))
     grad_middle = grad_middle + grad_result
     grad_branch = grad_middle.astype(jnp.bfloat16)
-    out_weight_term = contract_first(attended_rows, grad_branch)
+    out_weight_term = contract_first(core_major(attended_rows, fsdp_size), grad_branch)
     out_bias_grad = jnp.sum(grad_branch.astype(jnp.float32), axis=0)
     grad_attended = contract_last(grad_branch, out_full).astype(jnp.bfloat16)
     grad_heads = lax.all_to_all(
@@ -236,7 +263,7 @@
     kv_grads = kv_grads.reshape(seq_count, ctx_size, pair_len, 2 * group_width).transpose(1, 0, 2, 3)
     kv_part = lax.psum_scatter(
         kv_grads.reshape(ctx_size * seq_count * pair_len, 2 * group_width),
-        "ctx",
+        CTX,
         scatter_dimension=0,
         tiled=True,
     ).reshape(seq_count, pair_len, 2 * group_width)
@@ -263,7 +290,7 @@
         ],
         axis=1,
     )
-    qkv_grad = contract_first(normed_low, grad_mixed)
+    qkv_grad = contract_first(core_major(normed_low, fsdp_size), grad_mixed)
     mixed_float = grad_mixed.astype(jnp.float32)
     query_bias_grad = jnp.sum(mixed_float[:, :model_width], axis=0)
     value_bias_grad = jnp.sum(mixed_float[:, 2 * model_width :], axis=0)
@@ -271,129 +298,25 @@
         contract_last(grad_mixed, qkv_full)
     )
     in_grad = (grad_inputs + grad_middle).reshape(layer_in.shape)
-    shares = (
-        lax.psum_scatter(
-            qkv_grad.astype(jnp.bfloat16), "fsdp", scatter_dimension=0, tiled=True
-        ).astype(jnp.float32),
-        lax.psum_scatter(
-            out_weight_term.astype(jnp.bfloat16), "fsdp", scatter_dimension=0, tiled=True
-        ).astype(jnp.float32),
-        lax.psum_scatter(
-            fc_grad.astype(jnp.bfloat16), "fsdp", scatter_dimension=0, tiled=True
-        ).astype(jnp.float32),
-        lax.psum_scatter(
-            proj_grad.astype(jnp.bfloat16), "fsdp", scatter_dimension=0, tiled=True
-        ).astype(jnp.float32),
-        lax.psum_scatter(
-            attn_gain_grad.astype(jnp.bfloat16), "fsdp", scatter_dimension=0, tiled=True
-        ).astype(jnp.float32),
-        lax.psum_scatter(
-            attn_shift_grad.astype(jnp.bfloat16), "fsdp", scatter_dimension=0, tiled=True
-        ).astype(jnp.float32),
-        lax.psum_scatter(
-            query_bias_grad.astype(jnp.bfloat16), "fsdp", scatter_dimension=0, tiled=True
-        ).astype(jnp.float32),
-        lax.psum_scatter(
-            value_bias_grad.astype(jnp.bfloat16), "fsdp", scatter_dimension=0, tiled=True
-        ).astype(jnp.float32),
-        lax.psum_scatter(
-            out_bias_grad.astype(jnp.bfloat16), "fsdp", scatter_dimension=0, tiled=True
-        ).astype(jnp.float32),
-        lax.psum_scatter(
-            mlp_gain_grad.astype(jnp.bfloat16), "fsdp", scatter_dimension=0, tiled=True
-        ).astype(jnp.float32),
-        lax.psum_scatter(
-            mlp_shift_grad.astype(jnp.bfloat16), "fsdp", scatter_dimension=0, tiled=True
-        ).astype(jnp.float32),
-        lax.psum_scatter(
-            fc_bias_grad.astype(jnp.bfloat16), "fsdp", scatter_dimension=0, tiled=True
-        ).astype(jnp.float32),
-        lax.psum_scatter(
-            proj_bias_grad.astype(jnp.bfloat16), "fsdp", scatter_dimension=0, tiled=True
-        ).astype(jnp.float32),
-    )
-    slices = (
-        lax.psum_scatter(
-            shares[0].astype(jnp.bfloat16), "ctx", scatter_dimension=0, tiled=True
-        ).astype(jnp.float32),
-        lax.psum_scatter(
-            shares[1].astype(jnp.bfloat16), "ctx", scatter_dimension=0, tiled=True
-        ).astype(jnp.float32),
-        lax.psum_scatter(
-            shares[2].astype(jnp.bfloat16), "ctx", scatter_dimension=0, tiled=True
-        ).astype(jnp.float32),
-        lax.psum_scatter(
-            shares[3].astype(jnp.bfloat16), "ctx", scatter_dimension=0, tiled=True
-        ).astype(jnp.float32),
-        lax.psum_scatter(
-            shares[4].astype(jnp.bfloat16), "ctx", scatter_dimension=0, tiled=True
-        ).astype(jnp.float32),
-        lax.psum_scatter(
-            shares[5].astype(jnp.bfloat16), "ctx", scatter_dimension=0, tiled=True
-        ).astype(jnp.float32),
-        lax.psum_scatter(
-            shares[6].astype(jnp.bfloat16), "ctx", scatter_dimension=0, tiled=True
-        ).astype(jnp.float32),
-        lax.psum_scatter(
-            shares[7].astype(jnp.bfloat16), "ctx", scatter_dimension=0, tiled=True
-        ).astype(jnp.float32),
-        lax.psum_scatter(
-            shares[8].astype(jnp.bfloat16), "ctx", scatter_dimension=0, tiled=True
-        ).astype(jnp.float32),
-        lax.psum_scatter(
-            shares[9].astype(jnp.bfloat16), "ctx", scatter_dimension=0, tiled=True
-        ).astype(jnp.float32),
-        lax.psum_scatter(
-            shares[10].astype(jnp.bfloat16), "ctx", scatter_dimension=0, tiled=True
-        ).astype(jnp.float32),
-        lax.psum_scatter(
-            shares[11].astype(jnp.bfloat16), "ctx", scatter_dimension=0, tiled=True
-        ).astype(jnp.float32),
-        lax.psum_scatter(
-            shares[12].astype(jnp.bfloat16), "ctx", scatter_dimension=0, tiled=True
-        ).astype(jnp.float32),
-    )
-    totals = (
-        lax.all_gather(slices[0].astype(jnp.bfloat16), "ctx", axis=0, tiled=True).astype(
-            jnp.float32
-        ),
-        lax.all_gather(slices[1].astype(jnp.bfloat16), "ctx", axis=0, tiled=True).astype(
-            jnp.float32
-        ),
-        lax.all_gather(slices[2].astype(jnp.bfloat16), "ctx", axis=0, tiled=True).astype(
-            jnp.float32
-        ),
-        lax.all_gather(slices[3].astype(jnp.bfloat16), "ctx", axis=0, tiled=True).astype(
-            jnp.float32
-        ),
-        lax.all_gather(slices[4].astype(jnp.bfloat16), "ctx", axis=0, tiled=True).astype(
-            jnp.float32
-        ),
-        lax.all_gather(slices[5].astype(jnp.bfloat16), "ctx", axis=0, tiled=True).astype(
-            jnp.float32
-        ),
-        lax.all_gather(slices[6].astype(jnp.bfloat16), "ctx", axis=0, tiled=True).astype(
-            jnp.float32
-        ),
-        lax.all_gather(slices[7].astype(jnp.bfloat16), "ctx", axis=0, tiled=True).astype(
-            jnp.float32
-        ),
-        lax.all_gather(slices[8].astype(jnp.bfloat16), "ctx", axis=0, tiled=True).astype(
-            jnp.float32
-        ),
-        lax.all_gather(slices[9].astype(jnp.bfloat16), "ctx", axis=0, tiled=True).astype(
-            jnp.float32
-        ),
-        lax.all_gather(slices[10].astype(jnp.bfloat16), "ctx", axis=0, tiled=True).astype(
-            jnp.float32
-        ),
-        lax.all_gather(slices[11].astype(jnp.bfloat16), "ctx", axis=0, tiled=True).astype(
-            jnp.float32
-        ),
-        lax.all_gather(slices[12].astype(jnp.bfloat16), "ctx", axis=0, tiled=True).astype(
-            jnp.float32
-        ),
-    )
+    weight_totals = tuple(
+        reduce_weight_grad(grad) for grad in (qkv_grad, out_weight_term, fc_grad, proj_grad)
+    )
+    vector_totals = []
+    for grad in (
+        attn_gain_grad,
+        attn_shift_grad,
+        query_bias_grad,
+        value_bias_grad,
+        out_bias_grad,
+        mlp_gain_grad,
+        mlp_shift_grad,
+        fc_bias_grad,
+        proj_bias_grad,
+    ):
+        share = lax.psum_scatter(grad.astype(jnp.bfloat16), "fsdp", scatter_dimension=0, tiled=True)
+        piece = lax.psum_scatter(share, CTX, scatter_dimension=0, tiled=True)
+        vector_totals.append(lax.all_gather(piece, CTX, axis=0, tiled=True).astype(jnp.float32))
+    totals = weight_totals + tuple(vector_totals)
     return (
         layer_out,
         in_grad,
@@ -414,9 +337,13 @@
 
 
 def solution(mesh):
+    ctx_count, fsdp_count = mesh.devices.shape
+    mesh = jax.sharding.Mesh(
+        mesh.devices.reshape(ctx_count // 2, 2, fsdp_count), ("zc", "core", "fsdp")
+    )
     placed = (
-        P(None, "ctx", None, "fsdp", None),
-        P(None, "ctx", None, "fsdp", None),
+        P(None, CTX, None, "fsdp", None),
+        P(None, CTX, None, "fsdp", None),
         P(),
         P("fsdp"),
         P("fsdp"),
@@ -437,8 +364,8 @@
         mesh=mesh,
         in_specs=placed,
         out_specs=(
-            P(None, "ctx", None, "fsdp", None),
-            P(None, "ctx", None, "fsdp", None),
+            P(None, CTX, None, "fsdp", None),
+            P(None, CTX, None, "fsdp", None),
             P("fsdp"),
             P("fsdp"),
             P("fsdp", None),

time: 1200 us -> 1190 us (level)
  waiting for transfers between devices: 706 us -> 621 us
  local copies, waits for them, and re-layouts: 88.9 us -> 144 us
  blocking collectives: 162 us -> 190 us
    reduce_scatter x8 -> x12, waiting for transfers between devices: 371 us -> 235 us  [the longest x4 135 us: reduce_weight_grad(): grad = lax.psum_scatter(grad, 'fsdp', scatter_dimension=0, tiled=True)]
    all_gather x9 -> x15, waiting for transfers between devices: 231 us -> 282 us  [the longest x4 132 us: gather_weight(): pieces = lax.all_gather(piece, 'fsdp', axis=0, tiled=False)]
    all_gather x2 -> x4, blocking collectives: 24.9 us -> 46.4 us  [the longest x2 35.6 us: reduce_weight_grad(): grad = lax.all_gather(grad, 'zc', axis=0, tiled=True)]
    while x32 -> x136, local copies, waits for them, and re-layouts: 0.66 us -> 20.5 us
    reduce_scatter x1, waiting for transfers between devices: 66.3 us -> 81.8 us  [shards(): lax.psum_scatter(kv_grads.reshape(ctx_size * seq_count * pair_len, 2 * gr...]
  transfers between devices with their start and end apart: 24 -> 34, of which waited for: 18 -> 19; matrix products, arithmetic and copies ran while one was open for 11% -> 23% of each run, Pallas kernels for 0% -> 0%
where the time goes in v2:
time: 1190 us
  waiting for transfers between devices  621 us (52%)
  blocking collectives  190 us (16%)
  local copies, waits for them, and re-layouts  144 us (12%)
  matrix products  136 us (11%)
  other arithmetic  50.6 us (4%)
  starting transfers between devices  24.6 us (2%)
  between operations  19.1 us (2%)
    reduce_scatter x4, waiting for transfers between devices, reduce_weight_grad(): grad = lax.psum_scatter(grad, 'fsdp', scatter_dimension=0, tiled=True)  135 us
    all_gather x4, waiting for transfers between devices, gather_weight(): pieces = lax.all_gather(piece, 'fsdp', axis=0, tiled=False)  132 us
    reduce_scatter x1, waiting for transfers between devices, shards(): lax.psum_scatter(kv_grads.reshape(ctx_size * seq_count * pair_len, 2 * gr...  81.8 us
    reduce_scatter x4, waiting for transfers between devices, reduce_weight_grad(): grad = lax.psum_scatter(grad, 'zc', scatter_dimension=0, tiled=True)  69.7 us
    all_gather x2, waiting for transfers between devices, reduce_weight_grad(): grad = lax.all_gather(grad, 'zc', axis=0, tiled=True)  58.4 us
    dot_general x52, matrix products, contract_last(): lax.dot_general(left, right, (((1,), (1,)), ((), ())), preferred_element_...  57.1 us
    all_gather x1, waiting for transfers between devices, shards(): lax.all_gather(own_keys.reshape(seq_count, 1, pair_len, group_width), CTX...  48.8 us
    unnamed x3, blocking collectives  43.7 us
  transfers between devices with their start and end apart: 34, of which 19 were waited for; matrix products, arithmetic and copies ran while one was open for 23% of the time, Pallas kernels for 0%

profile of v2, /device:TPU:0, one launch (start us, length us, event | category | flops | bytes accessed | tf_op | source)
XLA Modules:
  0.0 1187.7 jit_solution(8331422857436750790)
XLA Ops:
  9.5 47.5 %all-gather.51.cloned.1.call-done = bf16[512,3072]{1,0:T(8,128)(2,1)} async-done(((bf16[128,3072]{1,0:T(8,128)(2,1)}), bf16[512,3072]{1,0:T(8,128)(2,1)}) %all-gather.51.cloned.1.call-update) | async-done | bytes 3145744 | tf_op jit(solution)/shard_map/all_gather | solution.py:109
  61.5 8.0 all-gather.5
  69.6 7.1 all-gather.4
  78.1 4.6 fusion.101
  84.9 12.8 %all_to_all.114 = bf16[4,2,32,4,256]{4,2,1,0,3:T(8,128)(2,1)S(1)} all-to-all(bf16[4,2,32,4,256]{4,2,1,0,3:T(8,128)(2,1)S(1)} %copy.117), channel_id=1, replica_groups=mesh['zc'=4,'core'=2,'fsdp'=4] {'fsdp'}, dimensions={3} | all-to-all | bytes 1048576 | tf_op jit(solution)/shard_map/all_to_all | solution.py:208
  98.6 7.7 all-gather.7
  106.3 7.7 all-gather.6
  116.2 14.6 %all_to_all.115 = bf16[4,2,32,4,256]{4,2,1,0,3:T(8,128)(2,1)S(1)} all-to-all(bf16[4,2,32,4,256]{4,2,1,0,3:T(8,128)(2,1)S(1)} %copy.120), channel_id=1, replica_groups=mesh['zc'=4,'core'=2,'fsdp'=4] {'fsdp'}, dimensions={3} | all-to-all | bytes 1048576 | tf_op jit(solution)/shard_map/all_to_all | solution.py:209
  132.5 34.5 %all-gather.55.cloned.1.call-done = bf16[512,4096]{1,0:T(8,128)(2,1)} async-done(((bf16[128,4096]{1,0:T(8,128)(2,1)}), bf16[512,4096]{1,0:T(8,128)(2,1)}) %all-gather.55.cloned.1.call-update) | async-done | bytes 4194320 | tf_op jit(solution)/shard_map/all_gather | solution.py:109
  169.3 3.5 all-to-all-start
  173.0 49.7 %all-gather.57.cloned.1.call-done = bf16[2048,1024]{1,0:T(8,128)(2,1)} async-done(((bf16[512,1024]{1,0:T(8,128)(2,1)}), bf16[2048,1024]{1,0:T(8,128)(2,1)}) %all-gather.57.cloned.1.call-update) | async-done | bytes 4194320 | tf_op jit(solution)/shard_map/all_gather | solution.py:109
  222.8 48.8 %all-gather.31.cloned.1.call-done = bf16[4,8,256,256]{3,2,0,1:T(8,128)(2,1)} async-done(((bf16[4,1,256,256]{3,2,0,1:T(8,128)(2,1)}), bf16[4,8,256,256]{3,2,0,1:T(8,128)(2,1)}) %all-gather.31.cloned.1.call-update) | async-done | bytes 4194320 | tf_op jit(solution)/shard_map/all_gather | solution.py:215
  271.6 4.6 copy.119
  276.2 43.2 %all-gather.33.cloned.1.call-done = bf16[4,8,256,256]{3,2,0,1:T(8,128)(2,1)} async-done(((bf16[4,1,256,256]{3,2,0,1:T(8,128)(2,1)}), bf16[4,8,256,256]{3,2,0,1:T(8,128)(2,1)}) %all-gather.33.cloned.1.call-update) | async-done | bytes 4194320 | tf_op jit(solution)/shard_map/all_gather | solution.py:218
  319.5 4.6 copy.122
  324.2 38.2 %while.26 = (s32[]{:T(128)}, bf16[4,256,256]{2,1,0:T(8,128)(2,1)S(1)}, f32[4,256,4]{1,2,0:T(4,128)}, s32[4,2048]{1,0:T(4,128)S(1)}, s32[4,256]{1,0:T(4,128)S(1)}...) while((s32[]{:T(128)}, ...), condition=%wide.region_11.12_spmd, body=%wide.region_2.11_spmd.sunk | while | flops 554240000 | bytes 35092604 | solution.py:224
  363.7 3.6 all-to-all-start.3
  367.5 10.0 all-gather.8
  377.5 8.7 all_gather.138
  386.2 8.0 all-gather.10
  394.2 7.4 all-gather.9
  403.9 2.6 fusion.99
  408.7 9.5 multiply_convert_fusion.4
  418.1 12.4 %fusion.100 = (bf16[4096]{0:T(1024)(128)(2,1)}, bf16[256,4096]{1,0:T(8,128)(2,1)S(1)}) fusion(f32[256,4096]{1,0:T(8,128)} %get-tuple-element.313, bf16[4096,1024]{1,0:T(8,128)(2,1)} %bitcast.353, bf16[256,1024]{1,0:T(8,128)(2,1)S(1)} %bitcast.272), kind=kOutput, calls=%fused_computation.212 | convolution fusion | flops 2169499648 | bytes 15212544 | tf_op jit(solution)/shard_map/dot_general | solution.py:29
  431.9 5.6 convolution_convert_fusion.9
  437.6 7.3 multiply_reduce_fusion.4
  453.8 4.1 all-to-all-start.4
  458.1 2.8 reshape.418
  460.9 4.7 copy.150
  465.5 5.7 convolution_convert_fusion.8
  473.2 115.3 %while.27 = (s32[]{:T(128)}, bf16[4,256,256]{2,1,0:T(8,128)(2,1)}, bf16[4,2048,256]{2,1,0:T(8,128)(2,1)}, bf16[4,2048,256]{2,1,0:T(8,128)(2,1)}, s32[4,2048]{1,0...) while((s32[]{:T(128)}, bf16[4,256,256]{2,1,0:T(8,128)(2,1)}, ...), condition=%wide.region_21.22_spmd, body=%wide.region_16.21_spmd.sunk | while | flops 1370029056 | bytes 170609328 | solution.py:258
  588.5 7.5 maximum_bitcast_fusion.5
  596.0 7.5 copy.135
  606.6 4.3 all-to-all-start.5
  610.9 81.8 %reduce-scatter.14.cloned.1.call-done = bf16[1024,512]{1,0:T(8,128)(2,1)} async-done(((bf16[8192,512]{1,0:T(8,128)(2,1)}), bf16[1024,512]{1,0:T(8,128)(2,1)}) %reduce-scatter.14.cloned.1.call-update) | async-done | bytes 1048592 | tf_op jit(solution)/shard_map/reduce_scatter | solution.py:264
  695.4 3.6 all-to-all-start.6
  700.3 11.3 all-to-all-done.6
  711.6 4.2 all-to-all-start.7
  719.6 8.6 all-to-all-done.7
  730.1 5.7 fusion.88
  738.9 4.5 convolution_convert_fusion.10
  747.6 3.1 convolution_convert_fusion.11
  750.7 3.6 reduce-scatter.30.cloned.1.call-done
  754.4 55.4 %reduce-scatter.36.cloned.1.call-done = bf16[512,1024]{1,0:T(8,128)(2,1)} async-done(((bf16[2048,1024]{1,0:T(8,128)(2,1)}), bf16[512,1024]{1,0:T(8,128)(2,1)}) %reduce-scatter.36.cloned.1.call-update) | async-done | bytes 1048592 | tf_op jit(solution)/shard_map/reduce_scatter | solution.py:123
  809.9 16.1 %reduce-scatter.16.cloned.1.call-done = bf16[512,3072]{1,0:T(8,128)(2,1)} async-done(((bf16[1024,3072]{1,0:T(8,128)(2,1)}), bf16[512,3072]{1,0:T(8,128)(2,1)}) %reduce-scatter.16.cloned.1.call-update) | async-done | bytes 3145744 | tf_op jit(solution)/shard_map/reduce_scatter | solution.py:122
  826.1 14.4 %reduce-scatter.22.cloned.1.call-done = bf16[512,1024]{1,0:T(8,128)(2,1)} async-done(((bf16[1024,1024]{1,0:T(8,128)(2,1)}), bf16[512,1024]{1,0:T(8,128)(2,1)}) %reduce-scatter.22.cloned.1.call-update) | async-done | bytes 1048592 | tf_op jit(solution)/shard_map/reduce_scatter | solution.py:122
  840.6 30.7 %reduce-scatter.32.cloned.1.call-done = bf16[32,4096]{1,0:T(8,128)(2,1)} async-done(((bf16[128,4096]{1,0:T(8,128)(2,1)}), bf16[32,4096]{1,0:T(8,128)(2,1)}) %reduce-scatter.32.cloned.1.call-update) | async-done | bytes 262160 | tf_op jit(solution)/shard_map/reduce_scatter | solution.py:124
  871.3 28.1 %reduce-scatter.38.cloned.1.call-done = bf16[128,1024]{1,0:T(8,128)(2,1)} async-done(((bf16[512,1024]{1,0:T(8,128)(2,1)}), bf16[128,1024]{1,0:T(8,128)(2,1)}) %reduce-scatter.38.cloned.1.call-update) | async-done | bytes 262160 | tf_op jit(solution)/shard_map/reduce_scatter | solution.py:124
  899.5 45.2 %reduce-scatter.18.cloned.1.call-done = bf16[128,3072]{1,0:T(8,128)(2,1)} async-done(((bf16[512,3072]{1,0:T(8,128)(2,1)}), bf16[128,3072]{1,0:T(8,128)(2,1)}) %reduce-scatter.18.cloned.1.call-update) | async-done | bytes 786448 | tf_op jit(solution)/shard_map/reduce_scatter | solution.py:123
  944.7 30.8 %reduce-scatter.24.cloned.1.call-done = bf16[128,1024]{1,0:T(8,128)(2,1)} async-done(((bf16[512,1024]{1,0:T(8,128)(2,1)}), bf16[128,1024]{1,0:T(8,128)(2,1)}) %reduce-scatter.24.cloned.1.call-update) | async-done | bytes 262160 | tf_op jit(solution)/shard_map/reduce_scatter | solution.py:123
  975.6 29.5 %all-gather.43.cloned.1.call-done = bf16[128,4096]{1,0:T(8,128)(2,1)} async-done(((bf16[32,4096]{1,0:T(8,128)(2,1)}), bf16[128,4096]{1,0:T(8,128)(2,1)}) %all-gather.43.cloned.1.call-update) | async-done | bytes 1048592 | tf_op jit(solution)/shard_map/all_gather | solution.py:125
  1005.2 28.9 %all-gather.47.cloned.1.call-done = bf16[512,1024]{1,0:T(8,128)(2,1)} async-done(((bf16[128,1024]{1,0:T(8,128)(2,1)}), bf16[512,1024]{1,0:T(8,128)(2,1)}) %all-gather.47.cloned.1.call-update) | async-done | bytes 1048592 | tf_op jit(solution)/shard_map/all_gather | solution.py:125
  1034.2 8.0 all-gather.11
  1047.8 11.0 reduce-scatter.20.cloned.1.call-done
  1058.8 21.0 %all_gather.145 = bf16[128,3072]{1,0:T(8,128)(2,1)} all-gather(bf16[32,3072]{1,0:T(8,128)(2,1)} %reduce-scatter.20.cloned.1.call-done), channel_id=1, replica_groups=mesh['zc'=4,'core'=2,'fsdp'=4] {'zc'}, dimensions={0}, use_global_device_ids=true | all-gather | bytes 983040 | tf_op jit(solution)/shard_map/all_gather | solution.py:125
  1079.8 7.2 fusion.78
  1087.0 14.7 %all_gather.149 = bf16[128,1024]{1,0:T(8,128)(2,1)S(1)} all-gather(bf16[32,1024]{1,0:T(8,128)(2,1)} %reduce-scatter.26.cloned.1.call-done), channel_id=1, replica_groups=mesh['zc'=4,'core'=2,'fsdp'=4] {'zc'}, dimensions={0}, use_global_device_ids=true | all-gather | bytes 327680 | tf_op jit(solution)/shard_map/all_gather | solution.py:125
  1106.9 16.3 %all-reduce.28 = (bf16[1024]{0:T(1024)(128)(2,1)S(1)}, bf16[1024]{0:T(1024)(128)(2,1)S(1)}, bf16[1024]{0:T(1024)(128)(2,1)S(1)}, bf16[1024]{0:T(1024)(128)(2,1)S...) all-reduce(bf16[1024]{0:T(1024)(128)(2,1)S(1)} %get-tuple-element.2, ...), channel_id=7, replica_groups=mesh['zc'=4,'core'=2,'fsdp'=4] {'fsdp'}, use_global_device_ids=true, to_apply=%region_26.27.clone | all-reduce | flops 12288 | bytes 49152
  1123.7 13.6 %all-reduce.27 = (bf16[256]{0:T(256)(128)(2,1)S(1)}, bf16[256]{0:T(256)(128)(2,1)S(1)}, bf16[256]{0:T(256)(128)(2,1)S(1)}, bf16[256]{0:T(256)(128)(2,1)S(1)}, bf...) all-reduce(bf16[256]{0:T(256)(128)(2,1)S(1)} %dynamic-slice.9, ...), channel_id=8, replica_groups=mesh['zc'=4,'core'=2,'fsdp'=4] {'zc','core'}, use_global_device_ids=true, to_apply=%region_27.28.clone | all-reduce | flops 2048 | bytes 8192
  1139.7 13.9 %all-reduce.26 = (bf16[256]{0:T(256)(128)(2,1)S(1)}, bf16[256]{0:T(256)(128)(2,1)S(1)}, bf16[256]{0:T(256)(128)(2,1)S(1)}, bf16[256]{0:T(256)(128)(2,1)S(1)}, bf...) all-reduce(bf16[256]{0:T(256)(128)(2,1)S(1)} %dynamic-update-slice,, ...), channel_id=1, replica_groups=mesh['zc'=4,'core'=2,'fsdp'=4] {'zc','core'}, use_global_device_ids=true, to_apply=%add | all-reduce | flops 3072 | bytes 12288
  1157.6 8.4 all-gather.12
  1168.7 4.1 convert_element_type.269
  1172.8 4.2 convert_element_type.272
  1177.0 3.4 convert_element_type.255
  (711 shorter events, 224.8 us)
Async XLA Ops:
  7.2 50.7 %copy-start = (bf16[256,4096]{1,0:T(8,128)(2,1)S(1)}, bf16[256,4096]{1,0:T(8,128)(2,1)}, u32[]{:S(2)}) copy-start(bf16[256,4096]{1,0:T(8,128)(2,1)} %param.32) | copy-start | bytes 6291460
  7.2 49.8 %all-gather.51.cloned.1.call-start = ((), (), s32[]{:S(2)}) async-start(), calls=%async_computation.45 | async-start | bytes 3932160 | tf_op jit(solution)/shard_map/all_gather | solution.py:109
  9.5 47.6 %copy-start.42 = (bf16[256,1024]{1,0:T(8,128)(2,1)S(1)}, bf16[256,1024]{1,0:T(8,128)(2,1)}, u32[]{:S(2)}) copy-start(bf16[256,1024]{1,0:T(8,128)(2,1)} %param.28) | copy-start | bytes 1572868
  9.5 68.6 %all-gather.29.cloned.1.call-start = ((), (), s32[]{:S(2)}) async-start(), calls=%async_computation.21 | async-start | bytes 9437184 | tf_op jit(solution)/shard_map/all_gather | solution.py:110
  57.0 74.7 %all-gather.53.cloned.1.call-start = ((), (), s32[]{:S(2)}) async-start(), calls=%async_computation.46 | async-start | bytes 1310720 | tf_op jit(solution)/shard_map/all_gather | solution.py:109
  57.9 109.1 %all-gather.55.cloned.1.call-start = ((), (), s32[]{:S(2)}) async-start(), calls=%async_computation.47 | async-start | bytes 5242880 | tf_op jit(solution)/shard_map/all_gather | solution.py:109
  59.0 10.6 copy-start.60
  59.0 17.7 %copy-start.13 = (bf16[4,1,2,32,1024]{4,3,2,1,0:T(8,128)(2,1)S(1)}, bf16[4,1,2,32,1024]{4,3,2,1,0:T(8,128)(2,1)}, u32[]{:S(2)}) copy-start(bf16[4,1,2,32,1024]{4,3,2,1,0:T(8,128)(2,1)} %param.20) | copy-start | bytes 1572868
  59.0 163.7 %all-gather.57.cloned.1.call-start = ((), (), s32[]{:S(2)}) async-start(), calls=%async_computation.48 | async-start | bytes 5242880 | tf_op jit(solution)/shard_map/all_gather | solution.py:109
  61.4 210.2 %all-gather.31.cloned.1.call-start = ((), (), s32[]{:S(2)}) async-start(), calls=%async_computation.22 | async-start | bytes 4718592 | tf_op jit(solution)/shard_map/all_gather | solution.py:215
  69.5 8.2 copy-start.47
  84.8 13.8 %copy-start.61 = (bf16[256]{0:T(256)(128)(2,1)S(1)}, bf16[256]{0:T(256)(128)(2,1)}, u32[]{:S(2)}) copy-start(bf16[256]{0:T(256)(128)(2,1)} %param.27) | copy-start | bytes 1540
  84.8 21.5 %copy-start.62 = (bf16[256]{0:T(256)(128)(2,1)S(1)}, bf16[256]{0:T(256)(128)(2,1)}, u32[]{:S(2)}) copy-start(bf16[256]{0:T(256)(128)(2,1)} %param.26) | copy-start | bytes 1540
  98.5 221.0 %all-gather.33.cloned.1.call-start = ((), (), s32[]{:S(2)}) async-start(), calls=%async_computation.23 | async-start | bytes 4718592 | tf_op jit(solution)/shard_map/all_gather | solution.py:218
  131.7 272.2 %all-gather.35.cloned.1.call-start = ((), (), s32[]{:S(2)}) async-start(), calls=%async_computation.24 | async-start | bytes 3145728 | tf_op jit(solution)/shard_map/all_gather | solution.py:110
  132.4 276.2 %all-gather.37.cloned.1.call-start = ((), (), s32[]{:S(2)}) async-start(), calls=%async_computation.25 | async-start | bytes 12582912 | tf_op jit(solution)/shard_map/all_gather | solution.py:110
  169.3 53.5 %all-to-all-start = ((bf16[4,2,32,4,256]{4,2,1,0,3:T(8,128)(2,1)}), bf16[4,2,32,4,256]{4,2,1,0,3:T(8,128)(2,1)S(1)}, u32[]{:S(2)}, u32[]{:S(2)}) async-start(bf16[4,2,32,4,256]{4,2,1,0,3:T(8,128)(2,1)} %copy.115), calls=%async_computation | async-start | bytes 1048576 | tf_op jit(solution)/shard_map/all_to_all | solution.py:207
  172.7 245.4 %all-gather.39.cloned.1.call-start = ((), (), s32[]{:S(2)}) async-start(), calls=%async_computation.26 | async-start | bytes 12582912 | tf_op jit(solution)/shard_map/all_gather | solution.py:110
  362.4 5.1 copy-start.63
  362.4 15.1 %copy-start.55 = (bf16[1024]{0:T(1024)(128)(2,1)S(1)}, bf16[1024]{0:T(1024)(128)(2,1)}, u32[]{:S(2)}) copy-start(bf16[1024]{0:T(1024)(128)(2,1)} %param.33) | copy-start | bytes 6148
  362.4 23.8 %copy-start.64 = (bf16[256]{0:T(256)(128)(2,1)S(1)}, bf16[256]{0:T(256)(128)(2,1)}, u32[]{:S(2)}) copy-start(bf16[256]{0:T(256)(128)(2,1)} %param.31) | copy-start | bytes 1540
  362.4 31.8 %copy-start.65 = (bf16[256]{0:T(256)(128)(2,1)S(1)}, bf16[256]{0:T(256)(128)(2,1)}, u32[]{:S(2)}) copy-start(bf16[256]{0:T(256)(128)(2,1)} %param.30) | copy-start | bytes 1540
  363.7 37.9 %all-to-all-start.3 = ((bf16[4,2,128,1,256]{4,1,0,3,2:T(2,128)(2,1)}), bf16[4,2,128,1,256]{4,1,0,3,2:T(2,128)(2,1)S(1)}, u32[]{:S(2)}, u32[]{:S(2)}) async-start(bf16[4,2,128,1,256]{4,1,0,3,2:T(2,128)(2,1)} %copy.124), calls=%async_computation.3 | async-start | bytes 1048576 | tf_op jit(solution)/shard_map/all_to_all | solution.py:227
  367.3 236.3 %reduce-scatter.28.cloned.1.call-start = ((), (), s32[]{:S(2)}) async-start(), calls=%async_computation.35 | async-start | bytes 12582912 | tf_op jit(solution)/shard_map/reduce_scatter | solution.py:122
  406.5 38.4 %copy-start.15 = (f32[256,1024]{1,0:T(8,128)}, f32[256,1024]{1,0:T(8,128)S(1)}, u32[]{:S(2)}) copy-start(f32[256,1024]{1,0:T(8,128)S(1)} %get-tuple-element.311) | copy-start | bytes 3145732
  408.7 9.5 copy-start.19
  418.1 13.8 %copy-start.39 = (bf16[256,4,2,128]{0,3,1,2:T(8,128)(2,1)S(1)}, bf16[256,4,2,128]{0,3,1,2:T(8,128)(2,1)}, u32[]{:S(2)}) copy-start(bf16[256,4,2,128]{0,3,1,2:T(8,128)(2,1)} %copy.149) | copy-start | bytes 1572868
  449.5 8.6 copy-start.30
  453.8 17.4 %all-to-all-start.4 = ((bf16[4,2,32,4,256]{4,2,1,0,3:T(8,128)(2,1)}), bf16[4,2,32,4,256]{4,2,1,0,3:T(8,128)(2,1)}, u32[]{:S(2)}, u32[]{:S(2)}) async-start(bf16[4,2,32,4,256]{4,2,1,0,3:T(8,128)(2,1)} %copy.127), calls=%async_computation.4 | async-start | bytes 1048576 | tf_op jit(solution)/shard_map/all_to_all | solution.py:255
  458.0 146.2 %reduce-scatter.34.cloned.1.call-start = ((), (), s32[]{:S(2)}) async-start(), calls=%async_computation.40 | async-start | bytes 12582912 | tf_op jit(solution)/shard_map/reduce_scatter | solution.py:122
  471.2 221.5 %reduce-scatter.14.cloned.1.call-start = ((), (), s32[]{:S(2)}) async-start(), calls=%async_computation.27 | async-start | bytes 9437184 | tf_op jit(solution)/shard_map/reduce_scatter | solution.py:264
  603.6 150.8 %reduce-scatter.30.cloned.1.call-start = ((), (), s32[]{:S(2)}) async-start(), calls=%async_computation.36 | async-start | bytes 5242880 | tf_op jit(solution)/shard_map/reduce_scatter | solution.py:123
  604.1 205.7 %reduce-scatter.36.cloned.1.call-start = ((), (), s32[]{:S(2)}) async-start(), calls=%async_computation.41 | async-start | bytes 5242880 | tf_op jit(solution)/shard_map/reduce_scatter | solution.py:123
  606.6 88.8 %all-to-all-start.5 = ((bf16[4,2,128,1,256]{4,1,0,3,2:T(2,128)(2,1)}), bf16[4,2,128,1,256]{4,1,0,3,2:T(2,128)(2,1)S(1)}, u32[]{:S(2)}, u32[]{:S(2)}) async-start(bf16[4,2,128,1,256]{4,1,0,3,2:T(2,128)(2,1)} %copy.130), calls=%async_computation.5 | async-start | bytes 1048576 | tf_op jit(solution)/shard_map/all_to_all | solution.py:275
  694.0 21.9 %copy-start.46 = (f32[4,2,32]{2,1,0:T(2,128)S(1)}, f32[4,2,32]{2,1,0:T(2,128)}, u32[]{:S(2)}) copy-start(f32[4,2,32]{2,1,0:T(2,128)} %copy-done.45) | copy-start | bytes 3076
  694.0 21.9 %copy-start.14 = (bf16[4,1,2,32,1024]{4,3,2,1,0:T(8,128)(2,1)S(1)}, bf16[4,1,2,32,1024]{4,3,2,1,0:T(8,128)(2,1)}, u32[]{:S(2)}) copy-start(bf16[4,1,2,32,1024]{4,3,2,1,0:T(8,128)(2,1)} %param.20) | copy-start | bytes 1572868
  695.4 16.3 %all-to-all-start.6 = ((bf16[4,2,128,1,256]{4,1,0,3,2:T(2,128)(2,1)}), bf16[4,2,128,1,256]{4,1,0,3,2:T(2,128)(2,1)S(1)}, u32[]{:S(2)}, u32[]{:S(2)}) async-start(bf16[4,2,128,1,256]{4,1,0,3,2:T(2,128)(2,1)} %copy.136), calls=%async_computation.7 | async-start | bytes 1048576 | tf_op jit(solution)/shard_map/all_to_all | solution.py:278
  699.0 18.0 %copy-start.49 = (f32[4,2,32]{2,1,0:T(2,128)S(1)}, f32[4,2,32]{2,1,0:T(2,128)}, u32[]{:S(2)}) copy-start(f32[4,2,32]{2,1,0:T(2,128)} %get-tuple-element.304) | copy-start | bytes 3076
  711.6 4.2 copy-start.33
  711.6 16.5 %all-to-all-start.7 = ((bf16[4,2,128,1,256]{4,1,0,3,2:T(2,128)(2,1)}), bf16[4,2,128,1,256]{4,1,0,3,2:T(2,128)(2,1)}, u32[]{:S(2)}, u32[]{:S(2)}) async-start(bf16[4,2,128,1,256]{4,1,0,3,2:T(2,128)(2,1)} %copy.139), calls=%async_computation.8 | async-start | bytes 1048576 | tf_op jit(solution)/shard_map/all_to_all | solution.py:281
  715.8 110.2 %reduce-scatter.16.cloned.1.call-start = ((), (), s32[]{:S(2)}) async-start(), calls=%async_computation.28 | async-start | bytes 9437184 | tf_op jit(solution)/shard_map/reduce_scatter | solution.py:122
  730.1 5.7 copy-start.48
  743.4 4.2 copy-start.32
  743.5 97.0 %reduce-scatter.22.cloned.1.call-start = ((), (), s32[]{:S(2)}) async-start(), calls=%async_computation.32 | async-start | bytes 3145728 | tf_op jit(solution)/shard_map/reduce_scatter | solution.py:122
  750.7 120.6 %reduce-scatter.32.cloned.1.call-start = ((), (), s32[]{:S(2)}) async-start(), calls=%async_computation.37 | async-start | bytes 1310720 | tf_op jit(solution)/shard_map/reduce_scatter | solution.py:124
  754.4 145.0 %reduce-scatter.38.cloned.1.call-start = ((), (), s32[]{:S(2)}) async-start(), calls=%async_computation.42 | async-start | bytes 1310720 | tf_op jit(solution)/shard_map/reduce_scatter | solution.py:124
  809.8 134.8 %reduce-scatter.18.cloned.1.call-start = ((), (), s32[]{:S(2)}) async-start(), calls=%async_computation.29 | async-start | bytes 3932160 | tf_op jit(solution)/shard_map/reduce_scatter | solution.py:123
  826.0 149.5 %reduce-scatter.24.cloned.1.call-start = ((), (), s32[]{:S(2)}) async-start(), calls=%async_computation.33 | async-start | bytes 1310720 | tf_op jit(solution)/shard_map/reduce_scatter | solution.py:123
  840.5 193.6 %copy-start.66 = (bf16[256]{0:T(256)(128)(2,1)S(1)}, bf16[256]{0:T(256)(128)(2,1)}, u32[]{:S(2)}) copy-start(bf16[256]{0:T(256)(128)(2,1)} %param.35) | copy-start | bytes 1540
  840.5 164.6 %all-gather.43.cloned.1.call-start = ((), (), s32[]{:S(2)}) async-start(), calls=%async_computation.38 | async-start | bytes 1310720 | tf_op jit(solution)/shard_map/all_gather | solution.py:125
  871.3 172.1 %copy-start.67 = (u32[32]{0:T(128)S(1)}, u32[32]{0:T(128)}, u32[]{:S(2)}) copy-start(u32[32]{0:T(128)} %constant.163) | copy-start | bytes 388
  871.3 172.7 %copy-start.58 = (u32[32]{0:T(128)S(1)}, u32[32]{0:T(128)}, u32[]{:S(2)}) copy-start(u32[32]{0:T(128)} %constant.115) | copy-start | bytes 388
  871.3 162.8 %all-gather.47.cloned.1.call-start = ((), (), s32[]{:S(2)}) async-start(), calls=%async_computation.43 | async-start | bytes 1310720 | tf_op jit(solution)/shard_map/all_gather | solution.py:125
  899.4 159.4 %reduce-scatter.20.cloned.1.call-start = ((), (), s32[]{:S(2)}) async-start(), calls=%async_computation.30 | async-start | bytes 983040 | tf_op jit(solution)/shard_map/reduce_scatter | solution.py:124
  944.7 142.3 %reduce-scatter.26.cloned.1.call-start = ((), (), s32[]{:S(2)}) async-start(), calls=%async_computation.34 | async-start | bytes 327680 | tf_op jit(solution)/shard_map/reduce_scatter | solution.py:124
  975.5 193.1 %all-gather.45.cloned.1.call-start = ((), (), s32[]{:S(2)}) async-start(), calls=%async_computation.39 | async-start | bytes 3145728 | tf_op jit(solution)/shard_map/all_gather | solution.py:126
  1005.1 74.7 %copy-start.16 = (f32[256,1024]{1,0:T(8,128)S(1)}, f32[256,1024]{1,0:T(8,128)}, u32[]{:S(2)}) copy-start(f32[256,1024]{1,0:T(8,128)} %copy-done.15) | copy-start | bytes 3145732
  1005.1 167.7 %all-gather.49.cloned.1.call-start = ((), (), s32[]{:S(2)}) async-start(), calls=%async_computation.44 | async-start | bytes 3145728 | tf_op jit(solution)/shard_map/all_gather | solution.py:126
  1034.1 142.9 %all-gather.41.cloned.1.call-start = ((), (), s32[]{:S(2)}) async-start(), calls=%async_computation.31 | async-start | bytes 2359296 | tf_op jit(solution)/shard_map/all_gather | solution.py:126
  1105.5 61.7 %copy-start.18 = (f32[256,1024]{1,0:T(8,128)S(1)}, f32[256,1024]{1,0:T(8,128)}, u32[]{:S(2)}) copy-start(f32[256,1024]{1,0:T(8,128)} %copy-done.17) | copy-start | bytes 3145732
  1105.5 61.7 %copy-start.20 = (bf16[4,1,2,32,1024]{4,3,2,1,0:T(8,128)(2,1)S(1)}, bf16[4,1,2,32,1024]{4,3,2,1,0:T(8,128)(2,1)}, u32[]{:S(2)}) copy-start(bf16[4,1,2,32,1024]{4,3,2,1,0:T(8,128)(2,1)} %param.21) | copy-start | bytes 1572868
  1105.5 61.7 %copy-start.26 = (f32[256,1024]{1,0:T(8,128)S(1)}, f32[256,1024]{1,0:T(8,128)}, u32[]{:S(2)}) copy-start(f32[256,1024]{1,0:T(8,128)} %get-tuple-element.315) | copy-start | bytes 3145732
  1105.5 61.7 %copy-start.51 = (f32[256]{0:T(256)S(1)}, f32[256]{0:T(256)}, u32[]{:S(2)}) copy-start(f32[256]{0:T(256)} %copy-done.50) | copy-start | bytes 3076
  1172.8 7.7 copy-start.1
  (89 other events, 160.6 us)
Sparse Core Ops, SparseCore 0:
  10.4 46.5 all-gather.50
  58.6 16.7 all-gather.28
  77.8 31.9 all-gather.52
  112.1 54.8 all-gather.54
  169.2 53.4 all-gather.56
  224.7 46.8 all-gather.30
  273.8 45.6 all-gather.32
  321.0 9.3 all-gather.34
  332.0 21.0 all-gather.36
  354.4 21.1 all-gather.38
  437.7 14.3 reduce-scatter.27
  471.3 15.8 reduce-scatter.33
  603.7 89.0 reduce-scatter.13
  695.6 58.7 reduce-scatter.29
  757.2 52.5 reduce-scatter.35
  812.0 14.0 reduce-scatter.15
  828.7 11.7 reduce-scatter.21
  842.6 28.5 reduce-scatter.31
  873.5 25.7 reduce-scatter.37
  902.2 42.3 reduce-scatter.17
  947.5 27.9 reduce-scatter.23
  977.1 27.9 all-gather.42
  1006.7 27.3 all-gather.46
  1036.2 22.5 reduce-scatter.19
  1061.1 20.7 reduce-scatter.25
  1083.3 9.0 all-gather.44
  1093.7 11.7 all-gather.48
  1107.0 10.9 all-gather.40

commit v3 on v2

--- a/solution.py
+++ b/solution.py
@@ -106,7 +106,14 @@
 def gather_weight(shard):
     half = shard.shape[0] // 2
     piece = lax.dynamic_slice_in_dim(shard, lax.axis_index("core") * half, half, 0)
-    pieces = lax.all_gather(piece, "fsdp", axis=0, tiled=False)
+    fsdp_size = lax.axis_size("fsdp")
+    pieces = lax.all_to_all(
+        jnp.broadcast_to(piece[None], (fsdp_size,) + piece.shape),
+        "fsdp",
+        split_axis=0,
+        concat_axis=0,
+        tiled=True,
+    )
     whole = lax.all_gather(pieces, "core", axis=1, tiled=True)
     return whole.reshape(-1, shard.shape[1])
 

time: 1190 us -> 1130 us (0.950)
  waiting for transfers between devices: 621 us -> 501 us
  blocking collectives: 190 us -> 224 us
  starting transfers between devices: 24.6 us -> 38.5 us
    all_gather x4 -> x0, waiting for transfers between devices: 132 us -> none  [gather_weight(): pieces = lax.all_gather(piece, 'fsdp', axis=0, tiled=False)]
    all_to_all x0 -> x3, waiting for transfers between devices: none -> 93.9 us  [gather_weight(): lax.all_to_all(jnp.broadcast_to(piece[None], (fsdp_size,) + piece.shape),...]
    all_gather x1, waiting for transfers between devices: 48.8 us -> 0.02 us  [shards(): lax.all_gather(own_keys.reshape(seq_count, 1, pair_len, group_width), CTX...]
    all_gather x1, waiting for transfers between devices: 43.2 us -> 0.01 us  [shards(): lax.all_gather(own_values.reshape(seq_count, 1, pair_len, group_width), C...]
    all_to_all x0 -> x1, blocking collectives: none -> 41.7 us  [gather_weight(): lax.all_to_all(jnp.broadcast_to(piece[None], (fsdp_size,) + piece.shape),...]
    all_to_all x0 -> x3, starting transfers between devices: none -> 14.1 us  [gather_weight(): lax.all_to_all(jnp.broadcast_to(piece[None], (fsdp_size,) + piece.shape),...]
  transfers between devices with their start and end apart: 34 -> 33, of which waited for: 19 -> 18; matrix products, arithmetic and copies ran while one was open for 23% -> 25% of each run, Pallas kernels for 0% -> 0%
where the time goes in v3:
time: 1130 us
  waiting for transfers between devices  501 us (44%)
  blocking collectives  224 us (20%)
  local copies, waits for them, and re-layouts  153 us (14%)
  matrix products  136 us (12%)
  other arithmetic  51.6 us (5%)
  starting transfers between devices  38.5 us (3%)
  between operations  19.1 us (2%)
    reduce_scatter x4, waiting for transfers between devices, reduce_weight_grad(): grad = lax.psum_scatter(grad, 'fsdp', scatter_dimension=0, tiled=True)  135 us
    all_to_all x3, waiting for transfers between devices, gather_weight(): lax.all_to_all(jnp.broadcast_to(piece[None], (fsdp_size,) + piece.shape),...  93.9 us
    reduce_scatter x1, waiting for transfers between devices, shards(): lax.psum_scatter(kv_grads.reshape(ctx_size * seq_count * pair_len, 2 * gr...  84.2 us
    reduce_scatter x4, waiting for transfers between devices, reduce_weight_grad(): grad = lax.psum_scatter(grad, 'zc', scatter_dimension=0, tiled=True)  69.5 us
    all_gather x2, waiting for transfers between devices, reduce_weight_grad(): grad = lax.all_gather(grad, 'zc', axis=0, tiled=True)  58.3 us
    dot_general x52, matrix products, contract_last(): lax.dot_general(left, right, (((1,), (1,)), ((), ())), preferred_element_...  57.1 us
    unnamed x3, blocking collectives  43.5 us
    all_to_all x1, blocking collectives, gather_weight(): lax.all_to_all(jnp.broadcast_to(piece[None], (fsdp_size,) + piece.shape),...  41.7 us
  transfers between devices with their start and end apart: 33, of which 18 were waited for; matrix products, arithmetic and copies ran while one was open for 25% of the time, Pallas kernels for 0%

profile of v3, /device:TPU:0, one launch (start us, length us, event | category | flops | bytes accessed | tf_op | source)
XLA Modules:
  0.0 1125.5 jit_solution(17647504080420708333)
XLA Ops:
  9.0 41.7 %all_to_all.134 = bf16[4,128,3072]{2,1,0:T(8,128)(2,1)} all-to-all(bf16[4,128,3072]{2,1,0:T(8,128)(2,1)S(1)} %broadcast_in_dim.65), channel_id=1, replica_groups=mesh['zc'=4,'core'=2,'fsdp'=4] {'fsdp'}, dimensions={0} | all-to-all | bytes 6291456 | tf_op jit(solution)/shard_map/all_to_all | solution.py:110
  51.3 7.5 all-gather.1
  58.8 7.7 all-gather
  67.9 4.6 fusion.101
  76.6 12.1 %all_to_all.135 = bf16[4,2,32,4,256]{4,2,1,0,3:T(8,128)(2,1)S(1)} all-to-all(bf16[4,2,32,4,256]{4,2,1,0,3:T(8,128)(2,1)S(1)} %copy.117), channel_id=1, replica_groups=mesh['zc'=4,'core'=2,'fsdp'=4] {'fsdp'}, dimensions={3} | all-to-all | bytes 1048576 | tf_op jit(solution)/shard_map/all_to_all | solution.py:215
  89.6 7.5 all-gather.3
  97.2 7.7 all-gather.2
  109.2 9.8 all_to_all.136
  121.0 4.2 all-to-all-start.5
  126.3 8.4 all-to-all-done.5
  134.7 3.8 broadcast_in_dim.67
  138.5 4.8 all-to-all-start.6
  143.9 40.2 %all-to-all-done.6 = bf16[4,128,4096]{2,1,0:T(8,128)(2,1)} async-done(((bf16[4,128,4096]{2,1,0:T(8,128)(2,1)}), bf16[4,128,4096]{2,1,0:T(8,128)(2,1)}, u32[]{:S(2)}, u32[]{:S(2)}) %all-to-all-start.6) | async-done | bytes 4194336 | tf_op jit(solution)/shard_map/all_to_all | solution.py:110
  188.4 5.1 all-to-all-start.7
  195.2 45.3 %all-to-all-done.7 = bf16[4,512,1024]{2,1,0:T(8,128)(2,1)} async-done(((bf16[4,512,1024]{2,1,0:T(8,128)(2,1)}), bf16[4,512,1024]{2,1,0:T(8,128)(2,1)}, u32[]{:S(2)}, u32[]{:S(2)}) %all-to-all-start.7) | async-done | bytes 4194336 | tf_op jit(solution)/shard_map/all_to_all | solution.py:110
  240.4 3.5 all-to-all-start.1
  244.5 6.9 all-to-all-done.1
  251.5 4.8 copy.119
  256.3 5.4 copy.122
  261.8 38.4 %while.26 = (s32[]{:T(128)}, bf16[4,256,256]{2,1,0:T(8,128)(2,1)S(1)}, f32[4,256,4]{1,2,0:T(4,128)}, s32[4,2048]{1,0:T(4,128)S(1)}, s32[4,256]{1,0:T(4,128)S(1)}...) while((s32[]{:T(128)}, ...), condition=%wide.region_11.12_spmd, body=%wide.region_2.11_spmd.sunk | while | flops 554240000 | bytes 35092604 | solution.py:231
  301.6 3.5 all-to-all-start.4
  305.2 8.6 all-gather.4
  313.9 8.0 all_gather.108
  321.9 8.0 all-gather.6
  330.0 7.4 all-gather.5
  344.4 9.5 multiply_convert_fusion.4
  353.8 12.5 %fusion.100 = (bf16[4096]{0:T(1024)(128)(2,1)}, bf16[256,4096]{1,0:T(8,128)(2,1)S(1)}) fusion(f32[256,4096]{1,0:T(8,128)} %get-tuple-element.313, bf16[4096,1024]{1,0:T(8,128)(2,1)} %bitcast.345, bf16[256,1024]{1,0:T(8,128)(2,1)S(1)} %bitcast.268), kind=kOutput, calls=%fused_computation.212 | convolution fusion | flops 2169499648 | bytes 15212544 | tf_op jit(solution)/shard_map/dot_general | solution.py:29
  367.7 5.6 convolution_convert_fusion.9
  373.3 7.2 multiply_reduce_fusion.4
  389.7 4.2 all-to-all-start.8
  396.7 4.7 copy.150
  401.4 5.7 convolution_convert_fusion.8
  409.0 115.4 %while.27 = (s32[]{:T(128)}, bf16[4,256,256]{2,1,0:T(8,128)(2,1)}, bf16[4,2048,256]{2,1,0:T(8,128)(2,1)}, bf16[4,2048,256]{2,1,0:T(8,128)(2,1)}, s32[4,2048]{1,0...) while((s32[]{:T(128)}, bf16[4,256,256]{2,1,0:T(8,128)(2,1)}, ...), condition=%wide.region_21.22_spmd, body=%wide.region_16.21_spmd.sunk | while | flops 1370029056 | bytes 170609328 | solution.py:265
  524.4 7.6 maximum_bitcast_fusion.5
  532.0 7.5 copy.135
  542.6 4.3 all-to-all-start.9
  546.9 84.2 %reduce-scatter.14.cloned.1.call-done = bf16[1024,512]{1,0:T(8,128)(2,1)} async-done(((bf16[8192,512]{1,0:T(8,128)(2,1)}), bf16[1024,512]{1,0:T(8,128)(2,1)}) %reduce-scatter.14.cloned.1.call-update) | async-done | bytes 1048592 | tf_op jit(solution)/shard_map/reduce_scatter | solution.py:271
  633.7 3.6 all-to-all-start.10
  638.7 11.3 %all-to-all-done.10 = bf16[4,2,128,1,256]{4,1,0,3,2:T(2,128)(2,1)S(1)} async-done(((bf16[4,2,128,1,256]{4,1,0,3,2:T(2,128)(2,1)}), bf16[4,2,128,1,256]{4,1,0,3,2:T(2,128)(2,1)S(1)}, u32[]{:S(2)}, u32[]{:S(2)}) %all-to-all-start.10) | async-done | bytes 524320 | tf_op jit(solution)/shard_map/all_to_all | solution.py:285
  650.0 4.2 all-to-all-start.11
  657.9 8.6 all-to-all-done.11
  668.4 5.7 fusion.88
  677.3 4.5 convolution_convert_fusion.10
  689.1 3.6 reduce-scatter.30.cloned.1.call-done
  692.8 55.5 %reduce-scatter.36.cloned.1.call-done = bf16[512,1024]{1,0:T(8,128)(2,1)} async-done(((bf16[2048,1024]{1,0:T(8,128)(2,1)}), bf16[512,1024]{1,0:T(8,128)(2,1)}) %reduce-scatter.36.cloned.1.call-update) | async-done | bytes 1048592 | tf_op jit(solution)/shard_map/reduce_scatter | solution.py:130
  748.4 16.1 %reduce-scatter.16.cloned.1.call-done = bf16[512,3072]{1,0:T(8,128)(2,1)} async-done(((bf16[1024,3072]{1,0:T(8,128)(2,1)}), bf16[512,3072]{1,0:T(8,128)(2,1)}) %reduce-scatter.16.cloned.1.call-update) | async-done | bytes 3145744 | tf_op jit(solution)/shard_map/reduce_scatter | solution.py:129
  764.6 14.6 %reduce-scatter.22.cloned.1.call-done = bf16[512,1024]{1,0:T(8,128)(2,1)} async-done(((bf16[1024,1024]{1,0:T(8,128)(2,1)}), bf16[512,1024]{1,0:T(8,128)(2,1)}) %reduce-scatter.22.cloned.1.call-update) | async-done | bytes 1048592 | tf_op jit(solution)/shard_map/reduce_scatter | solution.py:129
  779.2 30.7 %reduce-scatter.32.cloned.1.call-done = bf16[32,4096]{1,0:T(8,128)(2,1)} async-done(((bf16[128,4096]{1,0:T(8,128)(2,1)}), bf16[32,4096]{1,0:T(8,128)(2,1)}) %reduce-scatter.32.cloned.1.call-update) | async-done | bytes 262160 | tf_op jit(solution)/shard_map/reduce_scatter | solution.py:131
  810.0 27.9 %reduce-scatter.38.cloned.1.call-done = bf16[128,1024]{1,0:T(8,128)(2,1)} async-done(((bf16[512,1024]{1,0:T(8,128)(2,1)}), bf16[128,1024]{1,0:T(8,128)(2,1)}) %reduce-scatter.38.cloned.1.call-update) | async-done | bytes 262160 | tf_op jit(solution)/shard_map/reduce_scatter | solution.py:131
  837.9 45.2 %reduce-scatter.18.cloned.1.call-done = bf16[128,3072]{1,0:T(8,128)(2,1)} async-done(((bf16[512,3072]{1,0:T(8,128)(2,1)}), bf16[128,3072]{1,0:T(8,128)(2,1)}) %reduce-scatter.18.cloned.1.call-update) | async-done | bytes 786448 | tf_op jit(solution)/shard_map/reduce_scatter | solution.py:130
  883.2 30.7 %reduce-scatter.24.cloned.1.call-done = bf16[128,1024]{1,0:T(8,128)(2,1)} async-done(((bf16[512,1024]{1,0:T(8,128)(2,1)}), bf16[128,1024]{1,0:T(8,128)(2,1)}) %reduce-scatter.24.cloned.1.call-update) | async-done | bytes 262160 | tf_op jit(solution)/shard_map/reduce_scatter | solution.py:130
  913.9 29.4 %all-gather.35.cloned.1.call-done = bf16[128,4096]{1,0:T(8,128)(2,1)} async-done(((bf16[32,4096]{1,0:T(8,128)(2,1)}), bf16[128,4096]{1,0:T(8,128)(2,1)}) %all-gather.35.cloned.1.call-update) | async-done | bytes 1048592 | tf_op jit(solution)/shard_map/all_gather | solution.py:132
  943.4 28.9 %all-gather.39.cloned.1.call-done = bf16[512,1024]{1,0:T(8,128)(2,1)} async-done(((bf16[128,1024]{1,0:T(8,128)(2,1)}), bf16[512,1024]{1,0:T(8,128)(2,1)}) %all-gather.39.cloned.1.call-update) | async-done | bytes 1048592 | tf_op jit(solution)/shard_map/all_gather | solution.py:132
  972.4 8.0 all-gather.7
  986.0 11.0 reduce-scatter.20.cloned.1.call-done
  997.0 21.0 %all_gather.113 = bf16[128,3072]{1,0:T(8,128)(2,1)} all-gather(bf16[32,3072]{1,0:T(8,128)(2,1)} %reduce-scatter.20.cloned.1.call-done), channel_id=1, replica_groups=mesh['zc'=4,'core'=2,'fsdp'=4] {'zc'}, dimensions={0}, use_global_device_ids=true | all-gather | bytes 983040 | tf_op jit(solution)/shard_map/all_gather | solution.py:132
  1018.0 7.2 fusion.78
  1025.2 14.6 %all_gather.117 = bf16[128,1024]{1,0:T(8,128)(2,1)S(1)} all-gather(bf16[32,1024]{1,0:T(8,128)(2,1)} %reduce-scatter.26.cloned.1.call-done), channel_id=1, replica_groups=mesh['zc'=4,'core'=2,'fsdp'=4] {'zc'}, dimensions={0}, use_global_device_ids=true | all-gather | bytes 327680 | tf_op jit(solution)/shard_map/all_gather | solution.py:132
  1044.9 16.0 %all-reduce.28 = (bf16[1024]{0:T(1024)(128)(2,1)S(1)}, bf16[1024]{0:T(1024)(128)(2,1)S(1)}, bf16[1024]{0:T(1024)(128)(2,1)S(1)}, bf16[1024]{0:T(1024)(128)(2,1)S...) all-reduce(bf16[1024]{0:T(1024)(128)(2,1)S(1)} %get-tuple-element.2, ...), channel_id=3, replica_groups=mesh['zc'=4,'core'=2,'fsdp'=4] {'fsdp'}, use_global_device_ids=true, to_apply=%region_26.27.clone | all-reduce | flops 12288 | bytes 49152
  1061.6 13.6 %all-reduce.27 = (bf16[256]{0:T(256)(128)(2,1)S(1)}, bf16[256]{0:T(256)(128)(2,1)S(1)}, bf16[256]{0:T(256)(128)(2,1)S(1)}, bf16[256]{0:T(256)(128)(2,1)S(1)}, bf...) all-reduce(bf16[256]{0:T(256)(128)(2,1)S(1)} %dynamic-slice.9, ...), channel_id=4, replica_groups=mesh['zc'=4,'core'=2,'fsdp'=4] {'zc','core'}, use_global_device_ids=true, to_apply=%region_27.28.clone | all-reduce | flops 2048 | bytes 8192
  1077.5 13.9 %all-reduce.26 = (bf16[256]{0:T(256)(128)(2,1)S(1)}, bf16[256]{0:T(256)(128)(2,1)S(1)}, bf16[256]{0:T(256)(128)(2,1)S(1)}, bf16[256]{0:T(256)(128)(2,1)S(1)}, bf...) all-reduce(bf16[256]{0:T(256)(128)(2,1)S(1)} %dynamic-update-slice,, ...), channel_id=1, replica_groups=mesh['zc'=4,'core'=2,'fsdp'=4] {'zc','core'}, use_global_device_ids=true, to_apply=%add | all-reduce | flops 3072 | bytes 12288
  1095.4 8.4 all-gather.8
  1106.5 4.1 convert_element_type.269
  1110.6 4.2 convert_element_type.272
  (714 shorter events, 242.7 us)
Async XLA Ops:
  7.2 118.0 %copy-start = (bf16[256,4096]{1,0:T(8,128)(2,1)S(1)}, bf16[256,4096]{1,0:T(8,128)(2,1)}, u32[]{:S(2)}) copy-start(bf16[256,4096]{1,0:T(8,128)(2,1)} %param.32) | copy-start | bytes 6291460
  7.2 60.7 %all-gather.21.cloned.1.call-start = ((), (), s32[]{:S(2)}) async-start(), calls=%async_computation.25 | async-start | bytes 9437184 | tf_op jit(solution)/shard_map/all_gather | solution.py:117
  50.7 8.1 copy-start.62
  50.7 15.9 %copy-start.13 = (bf16[4,1,2,32,1024]{4,3,2,1,0:T(8,128)(2,1)S(1)}, bf16[4,1,2,32,1024]{4,3,2,1,0:T(8,128)(2,1)}, u32[]{:S(2)}) copy-start(bf16[4,1,2,32,1024]{4,3,2,1,0:T(8,128)(2,1)} %param.20) | copy-start | bytes 1572868
  50.7 200.8 %all-gather.23.cloned.1.call-start = ((), (), s32[]{:S(2)}) async-start(), calls=%async_computation.26 | async-start | bytes 4718592 | tf_op jit(solution)/shard_map/all_gather | solution.py:222
  58.8 8.8 copy-start.49
  76.5 13.1 %copy-start.63 = (bf16[256]{0:T(256)(128)(2,1)S(1)}, bf16[256]{0:T(256)(128)(2,1)}, u32[]{:S(2)}) copy-start(bf16[256]{0:T(256)(128)(2,1)} %param.27) | copy-start | bytes 1540
  76.5 20.6 %copy-start.64 = (bf16[256]{0:T(256)(128)(2,1)S(1)}, bf16[256]{0:T(256)(128)(2,1)}, u32[]{:S(2)}) copy-start(bf16[256]{0:T(256)(128)(2,1)} %param.26) | copy-start | bytes 1540
  89.6 166.8 %all-gather.25.cloned.1.call-start = ((), (), s32[]{:S(2)}) async-start(), calls=%async_computation.27 | async-start | bytes 4718592 | tf_op jit(solution)/shard_map/all_gather | solution.py:225
  109.2 10.6 copy-start.44
  121.0 13.7 %all-to-all-start.5 = ((bf16[4,128,1024]{2,1,0:T(8,128)(2,1)}), bf16[4,128,1024]{2,1,0:T(8,128)(2,1)}, u32[]{:S(2)}, u32[]{:S(2)}) async-start(bf16[4,128,1024]{2,1,0:T(8,128)(2,1)} %broadcast_in_dim.66), calls=%async_computation.5 | async-start | bytes 2097152 | tf_op jit(solution)/shard_map/all_to_all | solution.py:110
  138.5 45.7 %all-to-all-start.6 = ((bf16[4,128,4096]{2,1,0:T(8,128)(2,1)}), bf16[4,128,4096]{2,1,0:T(8,128)(2,1)}, u32[]{:S(2)}, u32[]{:S(2)}) async-start(bf16[4,128,4096]{2,1,0:T(8,128)(2,1)} %broadcast_in_dim.67), calls=%async_computation.6 | async-start | bytes 8388608 | tf_op jit(solution)/shard_map/all_to_all | solution.py:110
  143.3 196.3 %all-gather.27.cloned.1.call-start = ((), (), s32[]{:S(2)}) async-start(), calls=%async_computation.28 | async-start | bytes 3145728 | tf_op jit(solution)/shard_map/all_gather | solution.py:117
  143.9 200.5 %all-gather.29.cloned.1.call-start = ((), (), s32[]{:S(2)}) async-start(), calls=%async_computation.29 | async-start | bytes 12582912 | tf_op jit(solution)/shard_map/all_gather | solution.py:117
  188.4 5.1 copy-start.56
  188.4 5.5 copy-start.38
  188.4 52.0 %all-to-all-start.7 = ((bf16[4,512,1024]{2,1,0:T(8,128)(2,1)}), bf16[4,512,1024]{2,1,0:T(8,128)(2,1)}, u32[]{:S(2)}, u32[]{:S(2)}) async-start(bf16[4,512,1024]{2,1,0:T(8,128)(2,1)} %broadcast_in_dim.68), calls=%async_computation.7 | async-start | bytes 8388608 | tf_op jit(solution)/shard_map/all_to_all | solution.py:110
  240.4 11.0 all-to-all-start.1
  243.9 109.9 %all-gather.31.cloned.1.call-start = ((), (), s32[]{:S(2)}) async-start(), calls=%async_computation.30 | async-start | bytes 12582912 | tf_op jit(solution)/shard_map/all_gather | solution.py:117
  300.2 5.0 copy-start.65
  300.2 13.6 %copy-start.57 = (bf16[1024]{0:T(1024)(128)(2,1)S(1)}, bf16[1024]{0:T(1024)(128)(2,1)}, u32[]{:S(2)}) copy-start(bf16[1024]{0:T(1024)(128)(2,1)} %param.33) | copy-start | bytes 6148
  300.2 21.7 %copy-start.66 = (bf16[256]{0:T(256)(128)(2,1)S(1)}, bf16[256]{0:T(256)(128)(2,1)}, u32[]{:S(2)}) copy-start(bf16[256]{0:T(256)(128)(2,1)} %param.31) | copy-start | bytes 1540
  300.2 29.7 %copy-start.67 = (bf16[256]{0:T(256)(128)(2,1)S(1)}, bf16[256]{0:T(256)(128)(2,1)}, u32[]{:S(2)}) copy-start(bf16[256]{0:T(256)(128)(2,1)} %param.30) | copy-start | bytes 1540
  301.6 35.8 %all-to-all-start.4 = ((bf16[4,2,128,1,256]{4,1,0,3,2:T(2,128)(2,1)}), bf16[4,2,128,1,256]{4,1,0,3,2:T(2,128)(2,1)S(1)}, u32[]{:S(2)}, u32[]{:S(2)}) async-start(bf16[4,2,128,1,256]{4,1,0,3,2:T(2,128)(2,1)} %copy.124), calls=%async_computation.4 | async-start | bytes 1048576 | tf_op jit(solution)/shard_map/all_to_all | solution.py:234
  305.0 234.5 %reduce-scatter.28.cloned.1.call-start = ((), (), s32[]{:S(2)}) async-start(), calls=%async_computation.39 | async-start | bytes 12582912 | tf_op jit(solution)/shard_map/reduce_scatter | solution.py:129
  342.2 38.4 %copy-start.15 = (f32[256,1024]{1,0:T(8,128)}, f32[256,1024]{1,0:T(8,128)S(1)}, u32[]{:S(2)}) copy-start(f32[256,1024]{1,0:T(8,128)S(1)} %get-tuple-element.311) | copy-start | bytes 3145732
  344.4 9.5 copy-start.19
  353.8 13.8 %copy-start.40 = (bf16[256,4,2,128]{0,3,1,2:T(8,128)(2,1)S(1)}, bf16[256,4,2,128]{0,3,1,2:T(8,128)(2,1)}, u32[]{:S(2)}) copy-start(bf16[256,4,2,128]{0,3,1,2:T(8,128)(2,1)} %copy.149) | copy-start | bytes 1572868
  385.1 8.8 copy-start.30
  389.7 17.4 %all-to-all-start.8 = ((bf16[4,2,32,4,256]{4,2,1,0,3:T(8,128)(2,1)}), bf16[4,2,32,4,256]{4,2,1,0,3:T(8,128)(2,1)}, u32[]{:S(2)}, u32[]{:S(2)}) async-start(bf16[4,2,32,4,256]{4,2,1,0,3:T(8,128)(2,1)} %copy.127), calls=%async_computation.8 | async-start | bytes 1048576 | tf_op jit(solution)/shard_map/all_to_all | solution.py:262
  393.9 146.3 %reduce-scatter.34.cloned.1.call-start = ((), (), s32[]{:S(2)}) async-start(), calls=%async_computation.44 | async-start | bytes 12582912 | tf_op jit(solution)/shard_map/reduce_scatter | solution.py:129
  407.1 224.0 %reduce-scatter.14.cloned.1.call-start = ((), (), s32[]{:S(2)}) async-start(), calls=%async_computation.31 | async-start | bytes 9437184 | tf_op jit(solution)/shard_map/reduce_scatter | solution.py:271
  539.5 153.2 %reduce-scatter.30.cloned.1.call-start = ((), (), s32[]{:S(2)}) async-start(), calls=%async_computation.40 | async-start | bytes 5242880 | tf_op jit(solution)/shard_map/reduce_scatter | solution.py:130
  540.1 208.2 %reduce-scatter.36.cloned.1.call-start = ((), (), s32[]{:S(2)}) async-start(), calls=%async_computation.45 | async-start | bytes 5242880 | tf_op jit(solution)/shard_map/reduce_scatter | solution.py:130
  542.6 91.1 %all-to-all-start.9 = ((bf16[4,2,128,1,256]{4,1,0,3,2:T(2,128)(2,1)}), bf16[4,2,128,1,256]{4,1,0,3,2:T(2,128)(2,1)S(1)}, u32[]{:S(2)}, u32[]{:S(2)}) async-start(bf16[4,2,128,1,256]{4,1,0,3,2:T(2,128)(2,1)} %copy.130), calls=%async_computation.9 | async-start | bytes 1048576 | tf_op jit(solution)/shard_map/all_to_all | solution.py:282
  632.3 21.9 %copy-start.48 = (f32[4,2,32]{2,1,0:T(2,128)S(1)}, f32[4,2,32]{2,1,0:T(2,128)}, u32[]{:S(2)}) copy-start(f32[4,2,32]{2,1,0:T(2,128)} %copy-done.47) | copy-start | bytes 3076
  632.3 22.0 %copy-start.14 = (bf16[4,1,2,32,1024]{4,3,2,1,0:T(8,128)(2,1)S(1)}, bf16[4,1,2,32,1024]{4,3,2,1,0:T(8,128)(2,1)}, u32[]{:S(2)}) copy-start(bf16[4,1,2,32,1024]{4,3,2,1,0:T(8,128)(2,1)} %param.20) | copy-start | bytes 1572868
  633.7 16.3 %all-to-all-start.10 = ((bf16[4,2,128,1,256]{4,1,0,3,2:T(2,128)(2,1)}), bf16[4,2,128,1,256]{4,1,0,3,2:T(2,128)(2,1)S(1)}, u32[]{:S(2)}, u32[]{:S(2)}) async-start(bf16[4,2,128,1,256]{4,1,0,3,2:T(2,128)(2,1)} %copy.136), calls=%async_computation.11 | async-start | bytes 1048576 | tf_op jit(solution)/shard_map/all_to_all | solution.py:285
  637.3 18.0 %copy-start.51 = (f32[4,2,32]{2,1,0:T(2,128)S(1)}, f32[4,2,32]{2,1,0:T(2,128)}, u32[]{:S(2)}) copy-start(f32[4,2,32]{2,1,0:T(2,128)} %get-tuple-element.304) | copy-start | bytes 3076
  650.0 4.3 copy-start.33
  650.0 16.6 %all-to-all-start.11 = ((bf16[4,2,128,1,256]{4,1,0,3,2:T(2,128)(2,1)}), bf16[4,2,128,1,256]{4,1,0,3,2:T(2,128)(2,1)}, u32[]{:S(2)}, u32[]{:S(2)}) async-start(bf16[4,2,128,1,256]{4,1,0,3,2:T(2,128)(2,1)} %copy.139), calls=%async_computation.12 | async-start | bytes 1048576 | tf_op jit(solution)/shard_map/all_to_all | solution.py:288
  654.2 110.3 %reduce-scatter.16.cloned.1.call-start = ((), (), s32[]{:S(2)}) async-start(), calls=%async_computation.32 | async-start | bytes 9437184 | tf_op jit(solution)/shard_map/reduce_scatter | solution.py:129
  668.4 5.7 copy-start.50
  681.8 97.3 %reduce-scatter.22.cloned.1.call-start = ((), (), s32[]{:S(2)}) async-start(), calls=%async_computation.36 | async-start | bytes 3145728 | tf_op jit(solution)/shard_map/reduce_scatter | solution.py:129
  689.1 120.8 %reduce-scatter.32.cloned.1.call-start = ((), (), s32[]{:S(2)}) async-start(), calls=%async_computation.41 | async-start | bytes 1310720 | tf_op jit(solution)/shard_map/reduce_scatter | solution.py:131
  692.7 145.1 %reduce-scatter.38.cloned.1.call-start = ((), (), s32[]{:S(2)}) async-start(), calls=%async_computation.46 | async-start | bytes 1310720 | tf_op jit(solution)/shard_map/reduce_scatter | solution.py:131
  748.3 134.8 %reduce-scatter.18.cloned.1.call-start = ((), (), s32[]{:S(2)}) async-start(), calls=%async_computation.33 | async-start | bytes 3932160 | tf_op jit(solution)/shard_map/reduce_scatter | solution.py:130
  764.5 149.3 %reduce-scatter.24.cloned.1.call-start = ((), (), s32[]{:S(2)}) async-start(), calls=%async_computation.37 | async-start | bytes 1310720 | tf_op jit(solution)/shard_map/reduce_scatter | solution.py:130
  779.2 193.2 %copy-start.68 = (bf16[256]{0:T(256)(128)(2,1)S(1)}, bf16[256]{0:T(256)(128)(2,1)}, u32[]{:S(2)}) copy-start(bf16[256]{0:T(256)(128)(2,1)} %param.35) | copy-start | bytes 1540
  779.2 164.1 %all-gather.35.cloned.1.call-start = ((), (), s32[]{:S(2)}) async-start(), calls=%async_computation.42 | async-start | bytes 1310720 | tf_op jit(solution)/shard_map/all_gather | solution.py:132
  809.9 171.7 %copy-start.69 = (u32[32]{0:T(128)S(1)}, u32[32]{0:T(128)}, u32[]{:S(2)}) copy-start(u32[32]{0:T(128)} %constant.163) | copy-start | bytes 388
  809.9 172.3 %copy-start.60 = (u32[32]{0:T(128)S(1)}, u32[32]{0:T(128)}, u32[]{:S(2)}) copy-start(u32[32]{0:T(128)} %constant.115) | copy-start | bytes 388
  809.9 162.3 %all-gather.39.cloned.1.call-start = ((), (), s32[]{:S(2)}) async-start(), calls=%async_computation.47 | async-start | bytes 1310720 | tf_op jit(solution)/shard_map/all_gather | solution.py:132
  837.9 159.1 %reduce-scatter.20.cloned.1.call-start = ((), (), s32[]{:S(2)}) async-start(), calls=%async_computation.34 | async-start | bytes 983040 | tf_op jit(solution)/shard_map/reduce_scatter | solution.py:131
  883.1 142.0 %reduce-scatter.26.cloned.1.call-start = ((), (), s32[]{:S(2)}) async-start(), calls=%async_computation.38 | async-start | bytes 327680 | tf_op jit(solution)/shard_map/reduce_scatter | solution.py:131
  913.9 192.6 %all-gather.37.cloned.1.call-start = ((), (), s32[]{:S(2)}) async-start(), calls=%async_computation.43 | async-start | bytes 3145728 | tf_op jit(solution)/shard_map/all_gather | solution.py:133
  943.3 74.7 %copy-start.16 = (f32[256,1024]{1,0:T(8,128)S(1)}, f32[256,1024]{1,0:T(8,128)}, u32[]{:S(2)}) copy-start(f32[256,1024]{1,0:T(8,128)} %copy-done.15) | copy-start | bytes 3145732
  943.3 167.3 %all-gather.41.cloned.1.call-start = ((), (), s32[]{:S(2)}) async-start(), calls=%async_computation.48 | async-start | bytes 3145728 | tf_op jit(solution)/shard_map/all_gather | solution.py:133
  972.3 142.5 %all-gather.33.cloned.1.call-start = ((), (), s32[]{:S(2)}) async-start(), calls=%async_computation.35 | async-start | bytes 2359296 | tf_op jit(solution)/shard_map/all_gather | solution.py:133
  1043.5 61.5 %copy-start.18 = (f32[256,1024]{1,0:T(8,128)S(1)}, f32[256,1024]{1,0:T(8,128)}, u32[]{:S(2)}) copy-start(f32[256,1024]{1,0:T(8,128)} %copy-done.17) | copy-start | bytes 3145732
  1043.5 61.5 %copy-start.20 = (bf16[4,1,2,32,1024]{4,3,2,1,0:T(8,128)(2,1)S(1)}, bf16[4,1,2,32,1024]{4,3,2,1,0:T(8,128)(2,1)}, u32[]{:S(2)}) copy-start(bf16[4,1,2,32,1024]{4,3,2,1,0:T(8,128)(2,1)} %param.21) | copy-start | bytes 1572868
  1043.5 61.5 %copy-start.26 = (f32[256,1024]{1,0:T(8,128)S(1)}, f32[256,1024]{1,0:T(8,128)}, u32[]{:S(2)}) copy-start(f32[256,1024]{1,0:T(8,128)} %get-tuple-element.315) | copy-start | bytes 3145732
  1043.6 61.5 %copy-start.53 = (f32[256]{0:T(256)S(1)}, f32[256]{0:T(256)}, u32[]{:S(2)}) copy-start(f32[256]{0:T(256)} %copy-done.52) | copy-start | bytes 3076
  1110.6 7.7 copy-start.1
  (90 other events, 163.8 us)
Sparse Core Ops, SparseCore 0:
  50.8 16.4 all-gather.20
  89.7 46.2 all-gather.22
  138.2 45.6 all-gather.24
  185.3 9.3 all-gather.26
  196.1 21.0 all-gather.28
  246.0 21.7 all-gather.30
  373.5 16.8 reduce-scatter.27
  407.2 18.1 reduce-scatter.33
  539.6 91.3 reduce-scatter.13
  633.9 58.7 reduce-scatter.29
  695.7 52.5 reduce-scatter.35
  750.5 13.9 reduce-scatter.15
  767.3 11.7 reduce-scatter.21
  781.3 28.5 reduce-scatter.31
  812.0 25.7 reduce-scatter.37
  840.7 42.3 reduce-scatter.17
  885.9 27.9 reduce-scatter.23
  915.3 27.9 all-gather.34
  944.9 27.3 all-gather.38
  974.4 22.5 reduce-scatter.19
  999.2 20.7 reduce-scatter.25
  1021.6 9.0 all-gather.36
  1032.2 11.7 all-gather.40
  1045.4 10.9 all-gather.32

commit v4 on v3

--- a/solution.py
+++ b/solution.py
@@ -127,7 +127,11 @@
 
 def reduce_weight_grad(grad):
     grad = lax.psum_scatter(grad.astype(jnp.bfloat16), "core", scatter_dimension=0, tiled=True)
-    grad = lax.psum_scatter(grad, "fsdp", scatter_dimension=0, tiled=True)
+    fsdp_size = lax.axis_size("fsdp")
+    blocks = lax.all_to_all(
+        grad.reshape((fsdp_size, -1) + grad.shape[1:]), "fsdp", split_axis=0, concat_axis=0, tiled=True
+    )
+    grad = jnp.sum(blocks.astype(jnp.float32), axis=0).astype(jnp.bfloat16)
     grad = lax.psum_scatter(grad, "zc", scatter_dimension=0, tiled=True)
     grad = lax.all_gather(grad, "zc", axis=0, tiled=True)
     grad = lax.all_gather(grad, "core", axis=0, tiled=True)

time: 1130 us -> 1030 us (0.912)
  waiting for transfers between devices: 501 us -> 303 us
  blocking collectives: 224 us -> 294 us
  other arithmetic: 51.6 us -> 64.9 us
    reduce_scatter x4 -> x0, waiting for transfers between devices: 135 us -> none  [reduce_weight_grad(): grad = lax.psum_scatter(grad, 'fsdp', scatter_dimension=0, tiled=True)]
    all_to_all x0 -> x2, blocking collectives: none -> 70.5 us  [reduce_weight_grad(): lax.all_to_all(grad.reshape((fsdp_size, -1) + grad.shape[1:]), 'fsdp', sp...]
    all_to_all x0 -> x2, waiting for transfers between devices: none -> 66.3 us  [reduce_weight_grad(): lax.all_to_all(grad.reshape((fsdp_size, -1) + grad.shape[1:]), 'fsdp', sp...]
    reduce_scatter x4, waiting for transfers between devices: 69.5 us -> 26.3 us  [reduce_weight_grad(): grad = lax.psum_scatter(grad, 'zc', scatter_dimension=0, tiled=True)]
    all_gather x2, waiting for transfers between devices: 58.3 us -> 29.1 us  [reduce_weight_grad(): grad = lax.all_gather(grad, 'zc', axis=0, tiled=True)]
    reduce_scatter x1, waiting for transfers between devices: 84.2 us -> 61.7 us  [shards(): lax.psum_scatter(kv_grads.reshape(ctx_size * seq_count * pair_len, 2 * gr...]
    reduce_scatter x4, waiting for transfers between devices: 30.7 us -> 11 us  [reduce_weight_grad(): lax.psum_scatter(grad.astype(jnp.bfloat16), 'core', scatter_dimension=0,...]
    reduce_sum x0 -> x4, other arithmetic: none -> 13.3 us  [reduce_weight_grad(): grad = jnp.sum(blocks.astype(jnp.float32), axis=0).astype(jnp.bfloat16)]
  transfers between devices with their start and end apart: 33 -> 31, of which waited for: 18 -> 13; matrix products, arithmetic and copies ran while one was open for 25% -> 17% of each run, Pallas kernels for 0% -> 0%
where the time goes in v4:
time: 1030 us; the launch traced here: 1020 us
  waiting for transfers between devices  303 us (29%)
  blocking collectives  294 us (29%)
  local copies, waits for them, and re-layouts  157 us (15%)
  matrix products  131 us (13%)
  other arithmetic  64.9 us (6%)
  starting transfers between devices  47.4 us (5%)
  between operations  18.9 us (2%)
    all_to_all x3, waiting for transfers between devices, gather_weight(): lax.all_to_all(jnp.broadcast_to(piece[None], (fsdp_size,) + piece.shape),...  93.9 us
    all_to_all x2, blocking collectives, reduce_weight_grad(): lax.all_to_all(grad.reshape((fsdp_size, -1) + grad.shape[1:]), 'fsdp', sp...  70.5 us
    all_to_all x2, waiting for transfers between devices, reduce_weight_grad(): lax.all_to_all(grad.reshape((fsdp_size, -1) + grad.shape[1:]), 'fsdp', sp...  66.3 us
    reduce_scatter x1, waiting for transfers between devices, shards(): lax.psum_scatter(kv_grads.reshape(ctx_size * seq_count * pair_len, 2 * gr...  61.7 us
    dot_general x52, matrix products, contract_last(): lax.dot_general(left, right, (((1,), (1,)), ((), ())), preferred_element_...  51.8 us
    unnamed x3, blocking collectives  43.8 us
    all_to_all x1, blocking collectives, gather_weight(): lax.all_to_all(jnp.broadcast_to(piece[None], (fsdp_size,) + piece.shape),...  41.7 us
    dot_general x36, matrix products, contract_first(): lax.dot_general(left, right, (((0,), (0,)), ((), ())), preferred_element_...  35.7 us
  transfers between devices with their start and end apart: 31, of which 13 were waited for; matrix products, arithmetic and copies ran while one was open for 17% of the time, Pallas kernels for 0%

profile of v4, /device:TPU:0, one launch (start us, length us, event | category | flops | bytes accessed | tf_op | source)
XLA Modules:
  0.0 1018.1 jit_solution(12323205183428236896)
XLA Ops:
  9.0 41.7 %all_to_all.154 = bf16[4,128,3072]{2,1,0:T(8,128)(2,1)} all-to-all(bf16[4,128,3072]{2,1,0:T(8,128)(2,1)S(1)} %broadcast_in_dim.65), channel_id=1, replica_groups=mesh['zc'=4,'core'=2,'fsdp'=4] {'fsdp'}, dimensions={0} | all-to-all | bytes 6291456 | tf_op jit(solution)/shard_map/all_to_all | solution.py:110
  51.3 7.5 all-gather.1
  58.8 7.7 all-gather
  67.9 4.6 fusion.101
  76.6 12.1 %all_to_all.155 = bf16[4,2,32,4,256]{4,2,1,0,3:T(8,128)(2,1)S(1)} all-to-all(bf16[4,2,32,4,256]{4,2,1,0,3:T(8,128)(2,1)S(1)} %copy.117), channel_id=1, replica_groups=mesh['zc'=4,'core'=2,'fsdp'=4] {'fsdp'}, dimensions={3} | all-to-all | bytes 1048576 | tf_op jit(solution)/shard_map/all_to_all | solution.py:219
  89.6 7.5 all-gather.3
  97.2 7.7 all-gather.2
  109.2 9.8 all_to_all.156
  121.0 4.3 all-to-all-start.5
  126.3 8.4 all-to-all-done.5
  134.7 3.8 broadcast_in_dim.67
  138.5 4.9 all-to-all-start.6
  144.0 40.2 %all-to-all-done.6 = bf16[4,128,4096]{2,1,0:T(8,128)(2,1)} async-done(((bf16[4,128,4096]{2,1,0:T(8,128)(2,1)}), bf16[4,128,4096]{2,1,0:T(8,128)(2,1)}, u32[]{:S(2)}, u32[]{:S(2)}) %all-to-all-start.6) | async-done | bytes 4194336 | tf_op jit(solution)/shard_map/all_to_all | solution.py:110
  188.5 5.1 all-to-all-start.7
  195.3 45.3 %all-to-all-done.7 = bf16[4,512,1024]{2,1,0:T(8,128)(2,1)} async-done(((bf16[4,512,1024]{2,1,0:T(8,128)(2,1)}), bf16[4,512,1024]{2,1,0:T(8,128)(2,1)}, u32[]{:S(2)}, u32[]{:S(2)}) %all-to-all-start.7) | async-done | bytes 4194336 | tf_op jit(solution)/shard_map/all_to_all | solution.py:110
  240.5 3.5 all-to-all-start.1
  244.6 6.9 all-to-all-done.1
  252.3 5.3 copy.119
  257.7 6.1 copy.122
  263.8 41.3 %while.26 = (s32[]{:T(128)}, bf16[4,256,256]{2,1,0:T(8,128)(2,1)S(1)}, f32[4,256,4]{1,2,0:T(4,128)}, s32[4,2048]{1,0:T(4,128)S(1)}, s32[4,256]{1,0:T(4,128)S(1)}...) while((s32[]{:T(128)}, ...), condition=%wide.region_11.12_spmd, body=%wide.region_2.11_spmd.sunk | while | flops 554240000 | bytes 35092604 | solution.py:235
  306.4 3.5 all-to-all-start.4
  310.1 8.7 all-gather.4
  318.7 8.0 all_gather.108
  326.8 8.0 all-gather.6
  334.8 7.7 all-gather.5
  347.0 9.6 multiply_convert_fusion.4
  356.6 12.1 %fusion.100 = (bf16[4096]{0:T(1024)(128)(2,1)}, bf16[256,4096]{1,0:T(8,128)(2,1)S(1)}) fusion(f32[256,4096]{1,0:T(8,128)} %get-tuple-element.313, bf16[4096,1024]{1,0:T(8,128)(2,1)} %bitcast.352, bf16[256,1024]{1,0:T(8,128)(2,1)S(1)} %bitcast.272), kind=kOutput, calls=%fused_computation.212 | convolution fusion | flops 2169499648 | bytes 15212544 | tf_op jit(solution)/shard_map/dot_general | solution.py:29
  376.9 3.5 all-to-all-start.8
  380.6 6.3 all-to-all-done.8
  387.8 117.9 %while.27 = (s32[]{:T(128)}, bf16[4,256,256]{2,1,0:T(8,128)(2,1)}, bf16[4,2048,256]{2,1,0:T(8,128)(2,1)}, bf16[4,2048,256]{2,1,0:T(8,128)(2,1)}, s32[4,2048]{1,0...) while((s32[]{:T(128)}, bf16[4,256,256]{2,1,0:T(8,128)(2,1)}, ...), condition=%wide.region_21.22_spmd, body=%wide.region_16.21_spmd.sunk | while | flops 1370029056 | bytes 166414960 | solution.py:269
  505.7 7.5 maximum_bitcast_fusion.5
  513.2 7.6 copy.135
  522.8 5.9 convolution_convert_fusion.9
  533.0 4.7 copy.150
  537.8 5.6 convolution_convert_fusion.8
  545.8 3.5 all-to-all-start.9
  549.2 61.7 %reduce-scatter.10.cloned.1.call-done = bf16[1024,512]{1,0:T(8,128)(2,1)} async-done(((bf16[8192,512]{1,0:T(8,128)(2,1)}), bf16[1024,512]{1,0:T(8,128)(2,1)}) %reduce-scatter.10.cloned.1.call-update) | async-done | bytes 1048592 | tf_op jit(solution)/shard_map/reduce_scatter | solution.py:275
  613.6 3.7 all-to-all-start.10
  617.2 10.9 %reduce-scatter.20.cloned.1.call-done = bf16[512,4096]{1,0:T(8,128)(2,1)} async-done(((bf16[1024,4096]{1,0:T(8,128)(2,1)}), bf16[512,4096]{1,0:T(8,128)(2,1)}) %reduce-scatter.20.cloned.1.call-update) | async-done | bytes 4194320 | tf_op jit(solution)/shard_map/reduce_scatter | solution.py:129
  628.9 4.9 all-to-all-start.14
  635.2 46.8 %all-to-all-done.14 = bf16[4,128,4096]{2,1,0:T(8,128)(2,1)} async-done(((bf16[4,128,4096]{2,1,0:T(8,128)(2,1)}), bf16[4,128,4096]{2,1,0:T(8,128)(2,1)}, u32[]{:S(2)}, u32[]{:S(2)}) %all-to-all-start.14) | async-done | bytes 4194336 | tf_op jit(solution)/shard_map/all_to_all | solution.py:131
  682.0 4.1 all-to-all-start.11
  687.4 4.2 reduce_sum.331
  696.5 5.6 fusion.88
  705.3 4.5 convolution_convert_fusion.10
  709.9 53.5 %all_to_all.157 = bf16[4,512,1024]{2,1,0:T(8,128)(2,1)} all-to-all(bf16[4,512,1024]{2,1,0:T(8,128)(2,1)} %bitcast.284), channel_id=1, replica_groups=mesh['zc'=4,'core'=2,'fsdp'=4] {'fsdp'}, dimensions={0} | all-to-all | bytes 8388608 | tf_op jit(solution)/shard_map/all_to_all | solution.py:131
  763.4 4.4 reduce_sum.333
  774.7 4.7 all-to-all-start.12
  779.4 15.3 %reduce-scatter.26.cloned.1.call-done = bf16[128,1024]{1,0:T(8,128)(2,1)} async-done(((bf16[512,1024]{1,0:T(8,128)(2,1)}), bf16[128,1024]{1,0:T(8,128)(2,1)}) %reduce-scatter.26.cloned.1.call-update) | async-done | bytes 262160 | tf_op jit(solution)/shard_map/reduce_scatter | solution.py:135
  794.8 19.5 %all-to-all-done.12 = bf16[4,128,3072]{2,1,0:T(8,128)(2,1)} async-done(((bf16[4,128,3072]{2,1,0:T(8,128)(2,1)}), bf16[4,128,3072]{2,1,0:T(8,128)(2,1)}, u32[]{:S(2)}, u32[]{:S(2)}) %all-to-all-start.12) | async-done | bytes 3145760 | tf_op jit(solution)/shard_map/all_to_all | solution.py:131
  814.3 3.7 reduce_sum.324
  818.0 17.0 %all_to_all.158 = bf16[4,128,1024]{2,1,0:T(8,128)(2,1)S(1)} all-to-all(bf16[4,128,1024]{2,1,0:T(8,128)(2,1)} %bitcast.315), channel_id=1, replica_groups=mesh['zc'=4,'core'=2,'fsdp'=4] {'fsdp'}, dimensions={0} | all-to-all | bytes 2097152 | tf_op jit(solution)/shard_map/all_to_all | solution.py:131
  836.7 28.7 %all-gather.39.cloned.1.call-done = bf16[512,1024]{1,0:T(8,128)(2,1)} async-done(((bf16[128,1024]{1,0:T(8,128)(2,1)}), bf16[512,1024]{1,0:T(8,128)(2,1)}) %all-gather.39.cloned.1.call-update) | async-done | bytes 1048592 | tf_op jit(solution)/shard_map/all_gather | solution.py:136
  865.4 8.0 all-gather.7
  879.1 11.0 %reduce-scatter.14.cloned.1.call-done = bf16[32,3072]{1,0:T(8,128)(2,1)} async-done(((bf16[128,3072]{1,0:T(8,128)(2,1)}), bf16[32,3072]{1,0:T(8,128)(2,1)}) %reduce-scatter.14.cloned.1.call-update) | async-done | bytes 196624 | tf_op jit(solution)/shard_map/reduce_scatter | solution.py:135
  890.1 20.4 %all_gather.113 = bf16[128,3072]{1,0:T(8,128)(2,1)} all-gather(bf16[32,3072]{1,0:T(8,128)(2,1)} %reduce-scatter.14.cloned.1.call-done), channel_id=1, replica_groups=mesh['zc'=4,'core'=2,'fsdp'=4] {'zc'}, dimensions={0}, use_global_device_ids=true | all-gather | bytes 983040 | tf_op jit(solution)/shard_map/all_gather | solution.py:136
  910.5 7.2 fusion.78
  917.7 14.6 %all_gather.117 = bf16[128,1024]{1,0:T(8,128)(2,1)S(1)} all-gather(bf16[32,1024]{1,0:T(8,128)(2,1)} %reduce-scatter.18.cloned.1.call-done), channel_id=1, replica_groups=mesh['zc'=4,'core'=2,'fsdp'=4] {'zc'}, dimensions={0}, use_global_device_ids=true | all-gather | bytes 327680 | tf_op jit(solution)/shard_map/all_gather | solution.py:136
  937.4 16.4 %all-reduce.28 = (bf16[1024]{0:T(1024)(128)(2,1)S(1)}, bf16[1024]{0:T(1024)(128)(2,1)S(1)}, bf16[1024]{0:T(1024)(128)(2,1)S(1)}, bf16[1024]{0:T(1024)(128)(2,1)S...) all-reduce(bf16[1024]{0:T(1024)(128)(2,1)S(1)} %get-tuple-element.2, ...), channel_id=3, replica_groups=mesh['zc'=4,'core'=2,'fsdp'=4] {'fsdp'}, use_global_device_ids=true, to_apply=%region_26.27.clone | all-reduce | flops 12288 | bytes 49152
  954.4 13.6 %all-reduce.27 = (bf16[256]{0:T(256)(128)(2,1)S(1)}, bf16[256]{0:T(256)(128)(2,1)S(1)}, bf16[256]{0:T(256)(128)(2,1)S(1)}, bf16[256]{0:T(256)(128)(2,1)S(1)}, bf...) all-reduce(bf16[256]{0:T(256)(128)(2,1)S(1)} %dynamic-slice.9, ...), channel_id=4, replica_groups=mesh['zc'=4,'core'=2,'fsdp'=4] {'zc','core'}, use_global_device_ids=true, to_apply=%region_27.28.clone | all-reduce | flops 2048 | bytes 8192
  970.3 13.9 %all-reduce.26 = (bf16[256]{0:T(256)(128)(2,1)S(1)}, bf16[256]{0:T(256)(128)(2,1)S(1)}, bf16[256]{0:T(256)(128)(2,1)S(1)}, bf16[256]{0:T(256)(128)(2,1)S(1)}, bf...) all-reduce(bf16[256]{0:T(256)(128)(2,1)S(1)} %dynamic-update-slice,, ...), channel_id=1, replica_groups=mesh['zc'=4,'core'=2,'fsdp'=4] {'zc','core'}, use_global_device_ids=true, to_apply=%add | all-reduce | flops 3072 | bytes 12288
  988.2 8.4 all-gather.8
  999.3 4.1 convert_element_type.277
  1003.4 4.2 convert_element_type.280
  (704 shorter events, 248.3 us)
Async XLA Ops:
  7.2 118.1 %copy-start = (bf16[256,4096]{1,0:T(8,128)(2,1)S(1)}, bf16[256,4096]{1,0:T(8,128)(2,1)}, u32[]{:S(2)}) copy-start(bf16[256,4096]{1,0:T(8,128)(2,1)} %param.32) | copy-start | bytes 6291460
  7.2 60.7 %all-gather.21.cloned.1.call-start = ((), (), s32[]{:S(2)}) async-start(), calls=%async_computation.25 | async-start | bytes 9437184 | tf_op jit(solution)/shard_map/all_gather | solution.py:117
  50.7 8.1 copy-start.64
  50.7 15.9 %copy-start.13 = (bf16[4,1,2,32,1024]{4,3,2,1,0:T(8,128)(2,1)S(1)}, bf16[4,1,2,32,1024]{4,3,2,1,0:T(8,128)(2,1)}, u32[]{:S(2)}) copy-start(bf16[4,1,2,32,1024]{4,3,2,1,0:T(8,128)(2,1)} %param.20) | copy-start | bytes 1572868
  50.7 201.6 %all-gather.23.cloned.1.call-start = ((), (), s32[]{:S(2)}) async-start(), calls=%async_computation.26 | async-start | bytes 4718592 | tf_op jit(solution)/shard_map/all_gather | solution.py:226
  58.8 8.8 copy-start.50
  76.5 13.1 %copy-start.65 = (bf16[256]{0:T(256)(128)(2,1)S(1)}, bf16[256]{0:T(256)(128)(2,1)}, u32[]{:S(2)}) copy-start(bf16[256]{0:T(256)(128)(2,1)} %param.27) | copy-start | bytes 1540
  76.5 20.6 %copy-start.66 = (bf16[256]{0:T(256)(128)(2,1)S(1)}, bf16[256]{0:T(256)(128)(2,1)}, u32[]{:S(2)}) copy-start(bf16[256]{0:T(256)(128)(2,1)} %param.26) | copy-start | bytes 1540
  89.6 168.1 %all-gather.25.cloned.1.call-start = ((), (), s32[]{:S(2)}) async-start(), calls=%async_computation.27 | async-start | bytes 4718592 | tf_op jit(solution)/shard_map/all_gather | solution.py:229
  109.2 10.6 %copy-start.45 = (bf16[256,1024]{1,0:T(8,128)(2,1)S(1)}, bf16[256,1024]{1,0:T(8,128)(2,1)}, u32[]{:S(2)}) copy-start(bf16[256,1024]{1,0:T(8,128)(2,1)} %param.28) | copy-start | bytes 1572868
  121.0 13.8 %all-to-all-start.5 = ((bf16[4,128,1024]{2,1,0:T(8,128)(2,1)}), bf16[4,128,1024]{2,1,0:T(8,128)(2,1)}, u32[]{:S(2)}, u32[]{:S(2)}) async-start(bf16[4,128,1024]{2,1,0:T(8,128)(2,1)} %broadcast_in_dim.66), calls=%async_computation.5 | async-start | bytes 2097152 | tf_op jit(solution)/shard_map/all_to_all | solution.py:110
  138.5 45.7 %all-to-all-start.6 = ((bf16[4,128,4096]{2,1,0:T(8,128)(2,1)}), bf16[4,128,4096]{2,1,0:T(8,128)(2,1)}, u32[]{:S(2)}, u32[]{:S(2)}) async-start(bf16[4,128,4096]{2,1,0:T(8,128)(2,1)} %broadcast_in_dim.67), calls=%async_computation.6 | async-start | bytes 8388608 | tf_op jit(solution)/shard_map/all_to_all | solution.py:110
  143.4 200.6 %all-gather.27.cloned.1.call-start = ((), (), s32[]{:S(2)}) async-start(), calls=%async_computation.28 | async-start | bytes 3145728 | tf_op jit(solution)/shard_map/all_gather | solution.py:117
  144.0 203.0 %all-gather.29.cloned.1.call-start = ((), (), s32[]{:S(2)}) async-start(), calls=%async_computation.29 | async-start | bytes 12582912 | tf_op jit(solution)/shard_map/all_gather | solution.py:117
  188.5 5.1 copy-start.57
  188.5 5.5 copy-start.39
  188.5 52.0 %all-to-all-start.7 = ((bf16[4,512,1024]{2,1,0:T(8,128)(2,1)}), bf16[4,512,1024]{2,1,0:T(8,128)(2,1)}, u32[]{:S(2)}, u32[]{:S(2)}) async-start(bf16[4,512,1024]{2,1,0:T(8,128)(2,1)} %broadcast_in_dim.68), calls=%async_computation.7 | async-start | bytes 8388608 | tf_op jit(solution)/shard_map/all_to_all | solution.py:110
  240.5 11.0 %all-to-all-start.1 = ((bf16[4,2,32,4,256]{4,2,1,0,3:T(8,128)(2,1)}), bf16[4,2,32,4,256]{4,2,1,0,3:T(8,128)(2,1)S(1)}, u32[]{:S(2)}, u32[]{:S(2)}) async-start(bf16[4,2,32,4,256]{4,2,1,0,3:T(8,128)(2,1)} %copy.115), calls=%async_computation.1 | async-start | bytes 1048576 | tf_op jit(solution)/shard_map/all_to_all | solution.py:218
  244.0 112.6 %all-gather.31.cloned.1.call-start = ((), (), s32[]{:S(2)}) async-start(), calls=%async_computation.30 | async-start | bytes 12582912 | tf_op jit(solution)/shard_map/all_gather | solution.py:117
  305.1 4.9 copy-start.67
  305.1 13.6 %copy-start.58 = (bf16[1024]{0:T(1024)(128)(2,1)S(1)}, bf16[1024]{0:T(1024)(128)(2,1)}, u32[]{:S(2)}) copy-start(bf16[1024]{0:T(1024)(128)(2,1)} %param.33) | copy-start | bytes 6148
  305.1 21.7 %copy-start.68 = (bf16[256]{0:T(256)(128)(2,1)S(1)}, bf16[256]{0:T(256)(128)(2,1)}, u32[]{:S(2)}) copy-start(bf16[256]{0:T(256)(128)(2,1)} %param.31) | copy-start | bytes 1540
  305.1 29.7 %copy-start.69 = (bf16[256]{0:T(256)(128)(2,1)S(1)}, bf16[256]{0:T(256)(128)(2,1)}, u32[]{:S(2)}) copy-start(bf16[256]{0:T(256)(128)(2,1)} %param.30) | copy-start | bytes 1540
  306.4 36.1 %all-to-all-start.4 = ((bf16[4,2,128,1,256]{4,1,0,3,2:T(2,128)(2,1)}), bf16[4,2,128,1,256]{4,1,0,3,2:T(2,128)(2,1)S(1)}, u32[]{:S(2)}, u32[]{:S(2)}) async-start(bf16[4,2,128,1,256]{4,1,0,3,2:T(2,128)(2,1)} %copy.124), calls=%async_computation.4 | async-start | bytes 1048576 | tf_op jit(solution)/shard_map/all_to_all | solution.py:238
  346.4 25.5 %copy-start.15 = (f32[256,1024]{1,0:T(8,128)}, f32[256,1024]{1,0:T(8,128)S(1)}, u32[]{:S(2)}) copy-start(f32[256,1024]{1,0:T(8,128)S(1)} %get-tuple-element.311) | copy-start | bytes 3145732
  346.9 9.6 copy-start.32
  347.0 9.6 copy-start.19
  356.6 12.1 %copy-start.62 = (bf16[4,256,4096]{2,1,0:T(8,128)(2,1)S(1)}, bf16[4,256,4096]{2,1,0:T(8,128)(2,1)}, u32[]{:S(2)}) copy-start(bf16[4,256,4096]{2,1,0:T(8,128)(2,1)} %all-gather.29.cloned.1.call-done) | copy-start | bytes 25165828
  376.9 10.0 all-to-all-start.8
  380.4 230.6 %reduce-scatter.10.cloned.1.call-start = ((), (), s32[]{:S(2)}) async-start(), calls=%async_computation.31 | async-start | bytes 9437184 | tf_op jit(solution)/shard_map/reduce_scatter | solution.py:275
  446.8 4.1 copy-start.43
  520.8 107.3 %reduce-scatter.20.cloned.1.call-start = ((), (), s32[]{:S(2)}) async-start(), calls=%async_computation.37 | async-start | bytes 12582912 | tf_op jit(solution)/shard_map/reduce_scatter | solution.py:129
  528.7 181.2 %reduce-scatter.24.cloned.1.call-start = ((), (), s32[]{:S(2)}) async-start(), calls=%async_computation.41 | async-start | bytes 12582912 | tf_op jit(solution)/shard_map/reduce_scatter | solution.py:129
  533.0 4.8 copy-start.20
  545.8 67.8 %all-to-all-start.9 = ((bf16[4,2,128,1,256]{4,1,0,3,2:T(2,128)(2,1)}), bf16[4,2,128,1,256]{4,1,0,3,2:T(2,128)(2,1)S(1)}, u32[]{:S(2)}, u32[]{:S(2)}) async-start(bf16[4,2,128,1,256]{4,1,0,3,2:T(2,128)(2,1)} %copy.130), calls=%async_computation.9 | async-start | bytes 1048576 | tf_op jit(solution)/shard_map/all_to_all | solution.py:286
  613.6 14.6 %all-to-all-start.10 = ((bf16[4,2,128,1,256]{4,1,0,3,2:T(2,128)(2,1)}), bf16[4,2,128,1,256]{4,1,0,3,2:T(2,128)(2,1)S(1)}, u32[]{:S(2)}, u32[]{:S(2)}) async-start(bf16[4,2,128,1,256]{4,1,0,3,2:T(2,128)(2,1)} %copy.136), calls=%async_computation.11 | async-start | bytes 1048576 | tf_op jit(solution)/shard_map/all_to_all | solution.py:289
  628.9 53.1 %all-to-all-start.14 = ((bf16[4,128,4096]{2,1,0:T(8,128)(2,1)}), bf16[4,128,4096]{2,1,0:T(8,128)(2,1)}, u32[]{:S(2)}, u32[]{:S(2)}) async-start(bf16[4,128,4096]{2,1,0:T(8,128)(2,1)} %bitcast.285), calls=%async_computation.20 | async-start | bytes 8388608 | tf_op jit(solution)/shard_map/all_to_all | solution.py:131
  633.8 52.4 %copy-start.49 = (f32[4,2,32]{2,1,0:T(2,128)S(1)}, f32[4,2,32]{2,1,0:T(2,128)}, u32[]{:S(2)}) copy-start(f32[4,2,32]{2,1,0:T(2,128)} %copy-done.48) | copy-start | bytes 3076
  633.8 52.5 %copy-start.14 = (bf16[4,1,2,32,1024]{4,3,2,1,0:T(8,128)(2,1)S(1)}, bf16[4,1,2,32,1024]{4,3,2,1,0:T(8,128)(2,1)}, u32[]{:S(2)}) copy-start(bf16[4,1,2,32,1024]{4,3,2,1,0:T(8,128)(2,1)} %param.20) | copy-start | bytes 1572868
  633.8 53.5 %copy-start.52 = (f32[4,2,32]{2,1,0:T(2,128)S(1)}, f32[4,2,32]{2,1,0:T(2,128)}, u32[]{:S(2)}) copy-start(f32[4,2,32]{2,1,0:T(2,128)} %get-tuple-element.304) | copy-start | bytes 3076
  682.0 12.6 %all-to-all-start.11 = ((bf16[4,2,128,1,256]{4,1,0,3,2:T(2,128)(2,1)}), bf16[4,2,128,1,256]{4,1,0,3,2:T(2,128)(2,1)}, u32[]{:S(2)}, u32[]{:S(2)}) async-start(bf16[4,2,128,1,256]{4,1,0,3,2:T(2,128)(2,1)} %copy.139), calls=%async_computation.12 | async-start | bytes 1048576 | tf_op jit(solution)/shard_map/all_to_all | solution.py:292
  686.2 88.0 %reduce-scatter.22.cloned.1.call-start = ((), (), s32[]{:S(2)}) async-start(), calls=%async_computation.38 | async-start | bytes 1310720 | tf_op jit(solution)/shard_map/reduce_scatter | solution.py:135
  691.7 83.0 %reduce-scatter.12.cloned.1.call-start = ((), (), s32[]{:S(2)}) async-start(), calls=%async_computation.32 | async-start | bytes 9437184 | tf_op jit(solution)/shard_map/reduce_scatter | solution.py:129
  696.5 5.7 copy-start.51
  709.8 84.9 %reduce-scatter.26.cloned.1.call-start = ((), (), s32[]{:S(2)}) async-start(), calls=%async_computation.42 | async-start | bytes 1310720 | tf_op jit(solution)/shard_map/reduce_scatter | solution.py:135
  763.4 4.5 copy-start.23
  767.8 50.2 %reduce-scatter.16.cloned.1.call-start = ((), (), s32[]{:S(2)}) async-start(), calls=%async_computation.35 | async-start | bytes 3145728 | tf_op jit(solution)/shard_map/reduce_scatter | solution.py:129
  774.1 62.4 %all-gather.35.cloned.1.call-start = ((), (), s32[]{:S(2)}) async-start(), calls=%async_computation.39 | async-start | bytes 1310720 | tf_op jit(solution)/shard_map/all_gather | solution.py:136
  774.7 39.6 %all-to-all-start.12 = ((bf16[4,128,3072]{2,1,0:T(8,128)(2,1)}), bf16[4,128,3072]{2,1,0:T(8,128)(2,1)}, u32[]{:S(2)}, u32[]{:S(2)}) async-start(bf16[4,128,3072]{2,1,0:T(8,128)(2,1)} %bitcast.289), calls=%async_computation.14 | async-start | bytes 6291456 | tf_op jit(solution)/shard_map/all_to_all | solution.py:131
  779.4 85.9 %all-gather.39.cloned.1.call-start = ((), (), s32[]{:S(2)}) async-start(), calls=%async_computation.43 | async-start | bytes 1310720 | tf_op jit(solution)/shard_map/all_gather | solution.py:136
  794.7 95.3 %reduce-scatter.14.cloned.1.call-start = ((), (), s32[]{:S(2)}) async-start(), calls=%async_computation.33 | async-start | bytes 983040 | tf_op jit(solution)/shard_map/reduce_scatter | solution.py:135
  818.0 99.7 %reduce-scatter.18.cloned.1.call-start = ((), (), s32[]{:S(2)}) async-start(), calls=%async_computation.36 | async-start | bytes 327680 | tf_op jit(solution)/shard_map/reduce_scatter | solution.py:135
  835.1 30.3 %copy-start.70 = (bf16[256]{0:T(256)(128)(2,1)S(1)}, bf16[256]{0:T(256)(128)(2,1)}, u32[]{:S(2)}) copy-start(bf16[256]{0:T(256)(128)(2,1)} %param.35) | copy-start | bytes 1540
  835.1 39.6 %copy-start.71 = (u32[32]{0:T(128)S(1)}, u32[32]{0:T(128)}, u32[]{:S(2)}) copy-start(u32[32]{0:T(128)} %constant.167) | copy-start | bytes 388
  835.1 40.1 %copy-start.61 = (u32[32]{0:T(128)S(1)}, u32[32]{0:T(128)}, u32[]{:S(2)}) copy-start(u32[32]{0:T(128)} %constant.119) | copy-start | bytes 388
  836.1 163.2 %all-gather.37.cloned.1.call-start = ((), (), s32[]{:S(2)}) async-start(), calls=%async_computation.40 | async-start | bytes 3145728 | tf_op jit(solution)/shard_map/all_gather | solution.py:137
  836.5 74.0 %copy-start.16 = (f32[256,1024]{1,0:T(8,128)S(1)}, f32[256,1024]{1,0:T(8,128)}, u32[]{:S(2)}) copy-start(f32[256,1024]{1,0:T(8,128)} %copy-done.15) | copy-start | bytes 3145732
  836.6 166.7 %all-gather.41.cloned.1.call-start = ((), (), s32[]{:S(2)}) async-start(), calls=%async_computation.44 | async-start | bytes 3145728 | tf_op jit(solution)/shard_map/all_gather | solution.py:137
  865.4 142.2 %all-gather.33.cloned.1.call-start = ((), (), s32[]{:S(2)}) async-start(), calls=%async_computation.34 | async-start | bytes 2359296 | tf_op jit(solution)/shard_map/all_gather | solution.py:137
  936.0 61.8 %copy-start.18 = (f32[256,1024]{1,0:T(8,128)S(1)}, f32[256,1024]{1,0:T(8,128)}, u32[]{:S(2)}) copy-start(f32[256,1024]{1,0:T(8,128)} %copy-done.17) | copy-start | bytes 3145732
  936.0 61.8 %copy-start.21 = (bf16[4,1,2,32,1024]{4,3,2,1,0:T(8,128)(2,1)S(1)}, bf16[4,1,2,32,1024]{4,3,2,1,0:T(8,128)(2,1)}, u32[]{:S(2)}) copy-start(bf16[4,1,2,32,1024]{4,3,2,1,0:T(8,128)(2,1)} %param.21) | copy-start | bytes 1572868
  936.0 61.8 %copy-start.25 = (f32[256,1024]{1,0:T(8,128)S(1)}, f32[256,1024]{1,0:T(8,128)}, u32[]{:S(2)}) copy-start(f32[256,1024]{1,0:T(8,128)} %get-tuple-element.315) | copy-start | bytes 3145732
  936.0 61.8 %copy-start.54 = (f32[256]{0:T(256)S(1)}, f32[256]{0:T(256)}, u32[]{:S(2)}) copy-start(f32[256]{0:T(256)} %copy-done.53) | copy-start | bytes 3076
  1003.4 7.7 copy-start.1
  (84 other events, 149.8 us)
Sparse Core Ops, SparseCore 0:
  50.8 16.4 all-gather.20
  89.7 46.2 all-gather.22
  138.2 45.6 all-gather.24
  185.3 9.3 all-gather.26
  196.1 21.0 all-gather.28
  246.0 21.6 all-gather.30
  520.9 89.9 reduce-scatter.9
  613.3 14.8 reduce-scatter.19
  630.4 17.6 reduce-scatter.23
  691.8 28.8 reduce-scatter.21
  723.0 12.5 reduce-scatter.11
  768.0 26.7 reduce-scatter.25
  797.5 8.2 reduce-scatter.15
  807.2 29.2 all-gather.34
  837.9 27.3 all-gather.38
  867.5 22.5 reduce-scatter.13
  892.7 20.6 reduce-scatter.17
  914.9 9.0 all-gather.36
  925.5 11.7 all-gather.40
  938.7 10.9 all-gather.32

commit v5 on v4

--- a/solution.py
+++ b/solution.py
@@ -223,12 +223,10 @@
     own_keys = key_heads.reshape(seq_count, pair_len, group_width)
     own_values = value_heads.reshape(seq_count, pair_len, group_width)
     key_all, value_all = (
-        lax.all_gather(
-            own_keys.reshape(seq_count, 1, pair_len, group_width), CTX, axis=1, tiled=True
-        ),
-        lax.all_gather(
-            own_values.reshape(seq_count, 1, pair_len, group_width), CTX, axis=1, tiled=True
-        ),
+        lax.all_to_all(
+            jnp.broadcast_to(own[None], (ctx_size,) + own.shape), CTX, split_axis=0, concat_axis=0, tiled=True
+        ).transpose(1, 0, 2, 3)
+        for own in (own_keys, own_values)
     )
     key_all = key_all.reshape(seq_count, -1, group_width)
     value_all = value_all.reshape(seq_count, -1, group_width)
@@ -272,12 +270,10 @@
     )
     kv_grads = jnp.concatenate([grad_keys, grad_values], axis=2).astype(jnp.bfloat16)
     kv_grads = kv_grads.reshape(seq_count, ctx_size, pair_len, 2 * group_width).transpose(1, 0, 2, 3)
-    kv_part = lax.psum_scatter(
-        kv_grads.reshape(ctx_size * seq_count * pair_len, 2 * group_width),
-        CTX,
-        scatter_dimension=0,
-        tiled=True,
-    ).reshape(seq_count, pair_len, 2 * group_width)
+    kv_part = jnp.sum(
+        lax.all_to_all(kv_grads, CTX, split_axis=0, concat_axis=0, tiled=True).astype(jnp.float32),
+        axis=0,
+    ).astype(jnp.bfloat16)
     key_part = kv_part[..., :group_width].astype(jnp.float32)
     value_part = kv_part[..., group_width:].astype(jnp.float32)
     key_grad_low = key_part.astype(jnp.bfloat16)

time: 1030 us -> 1330 us (1.29)
  waiting for transfers between devices: 303 us -> 550 us
  blocking collectives: 294 us -> 325 us
  starting transfers between devices: 47.4 us -> 65.1 us
    all_to_all x1 -> x5, waiting for transfers between devices: 0.01 us -> 362 us  [the longest x2 180 us: shards(): lax.all_to_all(jnp.broadcast_to(own[None], (ctx_size,) + own.shape), CTX,...]
    reduce_scatter x1 -> x0, waiting for transfers between devices: 61.7 us -> none  [shards(): lax.psum_scatter(kv_grads.reshape(ctx_size * seq_count * pair_len, 2 * gr...]
    all_gather x1, blocking collectives: 7.48 us -> 48.4 us  [shards(): lax.all_gather(attn_shift, 'fsdp', axis=0, tiled=True)]
    all_to_all x3, waiting for transfers between devices: 93.9 us -> 59.2 us  [gather_weight(): lax.all_to_all(jnp.broadcast_to(piece[None], (fsdp_size,) + piece.shape),...]
    all_to_all x1 -> x5, starting transfers between devices: 3.67 us -> 21.6 us  [the longest x2 9.6 us: shards(): lax.all_to_all(jnp.broadcast_to(own[None], (ctx_size,) + own.shape), CTX,...]
  transfers between devices with their start and end apart: 31 -> 32, of which waited for: 13 -> 15; matrix products, arithmetic and copies ran while one was open for 17% -> 23% of each run, Pallas kernels for 0% -> 0%
where the time goes in v5:
time: 1330 us; the launch traced here: 1320 us
  waiting for transfers between devices  550 us (41%)
  blocking collectives  325 us (24%)
  local copies, waits for them, and re-layouts  155 us (12%)
  matrix products  133 us (10%)
  other arithmetic  67.1 us (5%)
  starting transfers between devices  65.1 us (5%)
  between operations  18.7 us (1%)
    all_to_all x2, waiting for transfers between devices, shards(): lax.all_to_all(jnp.broadcast_to(own[None], (ctx_size,) + own.shape), CTX,...  180 us
    all_to_all x1, waiting for transfers between devices, shards(): lax.all_to_all(kv_grads, CTX, split_axis=0, concat_axis=0, tiled=True)  168 us
    all_to_all x2, blocking collectives, reduce_weight_grad(): lax.all_to_all(grad.reshape((fsdp_size, -1) + grad.shape[1:]), 'fsdp', sp...  70 us
    all_to_all x2, waiting for transfers between devices, reduce_weight_grad(): lax.all_to_all(grad.reshape((fsdp_size, -1) + grad.shape[1:]), 'fsdp', sp...  62.4 us
    all_to_all x3, waiting for transfers between devices, gather_weight(): lax.all_to_all(jnp.broadcast_to(piece[None], (fsdp_size,) + piece.shape),...  59.2 us
    dot_general x52, matrix products, contract_last(): lax.dot_general(left, right, (((1,), (1,)), ((), ())), preferred_element_...  52.2 us
    all_gather x1, blocking collectives, shards(): lax.all_gather(attn_shift, 'fsdp', axis=0, tiled=True)  48.4 us
    unnamed x3, blocking collectives  43.7 us
  transfers between devices with their start and end apart: 32, of which 15 were waited for; matrix products, arithmetic and copies ran while one was open for 23% of the time, Pallas kernels for 0%

profile of v5, /device:TPU:0, one launch (start us, length us, event | category | flops | bytes accessed | tf_op | source)
XLA Modules:
  0.0 1316.1 jit_solution(6242690358229896090)
XLA Ops:
  9.0 41.7 %all_to_all.169 = bf16[4,128,3072]{2,1,0:T(8,128)(2,1)} all-to-all(bf16[4,128,3072]{2,1,0:T(8,128)(2,1)S(1)} %broadcast_in_dim.73), channel_id=1, replica_groups=mesh['zc'=4,'core'=2,'fsdp'=4] {'fsdp'}, dimensions={0} | all-to-all | bytes 6291456 | tf_op jit(solution)/shard_map/all_to_all | solution.py:110
  52.8 4.2 all-to-all-start.7
  57.2 12.4 all-to-all-done.7
  72.2 5.0 all-to-all-start.8
  77.3 46.8 %all-to-all-done.8 = bf16[4,128,4096]{2,1,0:T(8,128)(2,1)} async-done(((bf16[4,128,4096]{2,1,0:T(8,128)(2,1)}), bf16[4,128,4096]{2,1,0:T(8,128)(2,1)}, u32[]{:S(2)}, u32[]{:S(2)}) %all-to-all-start.8) | async-done | bytes 4194336 | tf_op jit(solution)/shard_map/all_to_all | solution.py:110
  126.7 5.0 all-to-all-start.9
  131.7 48.4 %all-gather.1 = bf16[4,1,256]{2,1,0:T(2,128)(2,1)S(1)} all-gather(bf16[1,1,256]{2,1,0:T(2,128)(2,1)S(1)} %reshape.462), channel_id=1, replica_groups=mesh['zc'=4,'core'=2,'fsdp'=4] {'fsdp'}, dimensions={0}, use_global_device_ids=true | all-gather | bytes 2560 | tf_op jit(solution)/shard_map/all_gather | solution.py:173
  180.2 8.7 all-gather
  188.9 8.0 all-gather.3
  196.9 7.1 all-gather.2
  205.5 4.6 fusion.101
  213.3 3.5 all-to-all-start.1
  219.3 6.7 all-to-all-done.1
  230.8 7.3 all-to-all-done.2
  241.6 6.5 all-to-all-done.4
  250.6 4.9 all-to-all-start.3
  257.0 92.6 %all-to-all-done.3 = bf16[8,4,256,256]{3,2,1,0:T(8,128)(2,1)} async-done(((bf16[8,4,256,256]{3,2,1,0:T(8,128)(2,1)}), bf16[8,4,256,256]{3,2,1,0:T(8,128)(2,1)}, u32[]{:S(2)}, u32[]{:S(2)}) %all-to-all-start.3) | async-done | bytes 4194336 | tf_op jit(solution)/shard_map/all_to_all | solution.py:226
  352.0 4.7 all-to-all-start.5
  358.3 4.6 copy.112
  362.9 87.9 %all-to-all-done.5 = bf16[8,4,256,256]{3,2,1,0:T(8,128)(2,1)} async-done(((bf16[8,4,256,256]{3,2,1,0:T(8,128)(2,1)}), bf16[8,4,256,256]{3,2,1,0:T(8,128)(2,1)}, u32[]{:S(2)}, u32[]{:S(2)}) %all-to-all-start.5) | async-done | bytes 4194336 | tf_op jit(solution)/shard_map/all_to_all | solution.py:226
  450.8 4.6 copy.115
  455.4 41.4 %while.26 = (s32[]{:T(128)}, bf16[4,256,256]{2,1,0:T(8,128)(2,1)S(1)}, f32[4,256,4]{1,2,0:T(4,128)}, s32[4,2048]{1,0:T(4,128)S(1)}, s32[4,256]{1,0:T(4,128)S(1)}...) while((s32[]{:T(128)}, ...), condition=%wide.region_11.12_spmd, body=%wide.region_2.11_spmd.sunk | while | flops 554240000 | bytes 35092604 | solution.py:233
  501.8 9.6 all-gather.4
  511.3 8.5 all_gather.100
  519.9 8.0 all-gather.6
  527.9 7.2 all-gather.5
  539.9 9.5 multiply_convert_fusion.4
  549.4 12.3 fusion.100
  574.0 7.2 convolution_convert_fusion.9
  582.1 118.3 %while.27 = (s32[]{:T(128)}, bf16[4,256,256]{2,1,0:T(8,128)(2,1)}, bf16[4,2048,256]{2,1,0:T(8,128)(2,1)}, bf16[4,2048,256]{2,1,0:T(8,128)(2,1)}, s32[4,2048]{1,0...) while((s32[]{:T(128)}, bf16[4,256,256]{2,1,0:T(8,128)(2,1)}, ...), condition=%wide.region_21.22_spmd, body=%wide.region_16.21_spmd.sunk | while | flops 1370029056 | bytes 166414960 | solution.py:267
  700.5 7.6 maximum_bitcast_fusion.5
  708.0 12.1 copy.128
  720.1 5.1 all-to-all-start.12
  728.2 4.7 copy.144
  733.0 5.6 convolution_convert_fusion.8
  741.0 168.1 %all-to-all-done.12 = bf16[8,4,256,512]{2,3,1,0:T(8,128)(2,1)} async-done(((bf16[8,4,256,512]{2,3,1,0:T(8,128)(2,1)}), bf16[8,4,256,512]{2,3,1,0:T(8,128)(2,1)}, u32[]{:S(2)}, u32[]{:S(2)}) %all-to-all-start.12) | async-done | bytes 8388640 | tf_op jit(solution)/shard_map/all_to_all | solution.py:274
  909.1 4.1 all-to-all-start.11
  913.2 4.7 reduce_sum.332
  920.9 10.5 all_to_all.170
  931.4 4.8 all-to-all-start.17
  938.2 42.9 %all-to-all-done.17 = bf16[4,128,4096]{2,1,0:T(8,128)(2,1)} async-done(((bf16[4,128,4096]{2,1,0:T(8,128)(2,1)}), bf16[4,128,4096]{2,1,0:T(8,128)(2,1)}, u32[]{:S(2)}, u32[]{:S(2)}) %all-to-all-start.17) | async-done | bytes 4194336 | tf_op jit(solution)/shard_map/all_to_all | solution.py:131
  981.2 4.1 all-to-all-start.14
  986.6 4.3 reduce_sum.344
  995.5 5.8 fusion.88
  1004.4 4.5 convolution_convert_fusion.10
  1009.0 52.9 %all_to_all.171 = bf16[4,512,1024]{2,1,0:T(8,128)(2,1)} all-to-all(bf16[4,512,1024]{2,1,0:T(8,128)(2,1)} %bitcast.288), channel_id=1, replica_groups=mesh['zc'=4,'core'=2,'fsdp'=4] {'fsdp'}, dimensions={0} | all-to-all | bytes 8388608 | tf_op jit(solution)/shard_map/all_to_all | solution.py:131
  1061.9 4.4 reduce_sum.346
  1073.4 4.7 all-to-all-start.15
  1078.2 14.6 %reduce-scatter.23.cloned.1.call-done = bf16[128,1024]{1,0:T(8,128)(2,1)} async-done(((bf16[512,1024]{1,0:T(8,128)(2,1)}), bf16[128,1024]{1,0:T(8,128)(2,1)}) %reduce-scatter.23.cloned.1.call-update) | async-done | bytes 262160 | tf_op jit(solution)/shard_map/reduce_scatter | solution.py:135
  1092.9 19.5 %all-to-all-done.15 = bf16[4,128,3072]{2,1,0:T(8,128)(2,1)} async-done(((bf16[4,128,3072]{2,1,0:T(8,128)(2,1)}), bf16[4,128,3072]{2,1,0:T(8,128)(2,1)}, u32[]{:S(2)}, u32[]{:S(2)}) %all-to-all-start.15) | async-done | bytes 3145760 | tf_op jit(solution)/shard_map/all_to_all | solution.py:131
  1112.3 3.7 reduce_sum.337
  1116.1 17.0 %all_to_all.172 = bf16[4,128,1024]{2,1,0:T(8,128)(2,1)S(1)} all-to-all(bf16[4,128,1024]{2,1,0:T(8,128)(2,1)} %bitcast.316), channel_id=1, replica_groups=mesh['zc'=4,'core'=2,'fsdp'=4] {'fsdp'}, dimensions={0} | all-to-all | bytes 2097152 | tf_op jit(solution)/shard_map/all_to_all | solution.py:131
  1134.8 28.7 %all-gather.33.cloned.1.call-done = bf16[512,1024]{1,0:T(8,128)(2,1)} async-done(((bf16[128,1024]{1,0:T(8,128)(2,1)}), bf16[512,1024]{1,0:T(8,128)(2,1)}) %all-gather.33.cloned.1.call-update) | async-done | bytes 1048592 | tf_op jit(solution)/shard_map/all_gather | solution.py:136
  1163.5 8.0 all-gather.7
  1177.2 11.1 reduce-scatter.11.cloned.1.call-done
  1188.3 20.7 %all_gather.105 = bf16[128,3072]{1,0:T(8,128)(2,1)} all-gather(bf16[32,3072]{1,0:T(8,128)(2,1)} %reduce-scatter.11.cloned.1.call-done), channel_id=1, replica_groups=mesh['zc'=4,'core'=2,'fsdp'=4] {'zc'}, dimensions={0}, use_global_device_ids=true | all-gather | bytes 983040 | tf_op jit(solution)/shard_map/all_gather | solution.py:136
  1209.0 7.2 fusion.78
  1216.2 14.5 %all_gather.109 = bf16[128,1024]{1,0:T(8,128)(2,1)S(1)} all-gather(bf16[32,1024]{1,0:T(8,128)(2,1)} %reduce-scatter.15.cloned.1.call-done), channel_id=1, replica_groups=mesh['zc'=4,'core'=2,'fsdp'=4] {'zc'}, dimensions={0}, use_global_device_ids=true | all-gather | bytes 327680 | tf_op jit(solution)/shard_map/all_gather | solution.py:136
  1235.8 16.2 %all-reduce.28 = (bf16[1024]{0:T(1024)(128)(2,1)S(1)}, bf16[1024]{0:T(1024)(128)(2,1)S(1)}, bf16[1024]{0:T(1024)(128)(2,1)S(1)}, bf16[1024]{0:T(1024)(128)(2,1)S...) all-reduce(bf16[1024]{0:T(1024)(128)(2,1)S(1)} %get-tuple-element.2, ...), channel_id=2, replica_groups=mesh['zc'=4,'core'=2,'fsdp'=4] {'fsdp'}, use_global_device_ids=true, to_apply=%region_26.27.clone | all-reduce | flops 12288 | bytes 49152
  1252.6 13.6 %all-reduce.27 = (bf16[256]{0:T(256)(128)(2,1)S(1)}, bf16[256]{0:T(256)(128)(2,1)S(1)}, bf16[256]{0:T(256)(128)(2,1)S(1)}, bf16[256]{0:T(256)(128)(2,1)S(1)}, bf...) all-reduce(bf16[256]{0:T(256)(128)(2,1)S(1)} %dynamic-slice.9, ...), channel_id=3, replica_groups=mesh['zc'=4,'core'=2,'fsdp'=4] {'zc','core'}, use_global_device_ids=true, to_apply=%region_27.28.clone | all-reduce | flops 2048 | bytes 8192
  1268.5 13.9 %all-reduce.26 = (bf16[256]{0:T(256)(128)(2,1)S(1)}, bf16[256]{0:T(256)(128)(2,1)S(1)}, bf16[256]{0:T(256)(128)(2,1)S(1)}, bf16[256]{0:T(256)(128)(2,1)S(1)}, bf...) all-reduce(bf16[256]{0:T(256)(128)(2,1)S(1)} %dynamic-update-slice,, ...), channel_id=1, replica_groups=mesh['zc'=4,'core'=2,'fsdp'=4] {'zc','core'}, use_global_device_ids=true, to_apply=%add | all-reduce | flops 3072 | bytes 12288
  1286.5 8.4 all-gather.8
  1297.5 4.1 convert_element_type.279
  1301.6 4.2 convert_element_type.282
  (697 shorter events, 261.5 us)
Async XLA Ops:
  7.2 49.9 %copy-start = (bf16[256,4096]{1,0:T(8,128)(2,1)S(1)}, bf16[256,4096]{1,0:T(8,128)(2,1)}, u32[]{:S(2)}) copy-start(bf16[256,4096]{1,0:T(8,128)(2,1)} %param.32) | copy-start | bytes 6291460
  7.2 198.3 %all-gather.19.cloned.1.call-start = ((), (), s32[]{:S(2)}) async-start(), calls=%async_computation.27 | async-start | bytes 9437184 | tf_op jit(solution)/shard_map/all_gather | solution.py:117
  52.8 16.7 %all-to-all-start.7 = ((bf16[4,128,1024]{2,1,0:T(8,128)(2,1)}), bf16[4,128,1024]{2,1,0:T(8,128)(2,1)}, u32[]{:S(2)}, u32[]{:S(2)}) async-start(bf16[4,128,1024]{2,1,0:T(8,128)(2,1)} %broadcast_in_dim.78), calls=%async_computation.7 | async-start | bytes 2097152 | tf_op jit(solution)/shard_map/all_to_all | solution.py:110
  72.2 5.0 copy-start.37
  72.2 51.9 %all-to-all-start.8 = ((bf16[4,128,4096]{2,1,0:T(8,128)(2,1)}), bf16[4,128,4096]{2,1,0:T(8,128)(2,1)}, u32[]{:S(2)}, u32[]{:S(2)}) async-start(bf16[4,128,4096]{2,1,0:T(8,128)(2,1)} %broadcast_in_dim.79), calls=%async_computation.8 | async-start | bytes 8388608 | tf_op jit(solution)/shard_map/all_to_all | solution.py:110
  126.6 5.0 copy-start.58
  126.6 53.5 %copy-start.59 = (bf16[256]{0:T(256)(128)(2,1)S(1)}, bf16[256]{0:T(256)(128)(2,1)}, u32[]{:S(2)}) copy-start(bf16[256]{0:T(256)(128)(2,1)} %param.23) | copy-start | bytes 1540
  126.6 62.2 %copy-start.60 = (bf16[256]{0:T(256)(128)(2,1)S(1)}, bf16[256]{0:T(256)(128)(2,1)}, u32[]{:S(2)}) copy-start(bf16[256]{0:T(256)(128)(2,1)} %param.27) | copy-start | bytes 1540
  126.6 70.3 %copy-start.61 = (bf16[256]{0:T(256)(128)(2,1)S(1)}, bf16[256]{0:T(256)(128)(2,1)}, u32[]{:S(2)}) copy-start(bf16[256]{0:T(256)(128)(2,1)} %param.26) | copy-start | bytes 1540
  126.7 77.4 %copy-start.13 = (bf16[4,1,2,32,1024]{4,3,2,1,0:T(8,128)(2,1)S(1)}, bf16[4,1,2,32,1024]{4,3,2,1,0:T(8,128)(2,1)}, u32[]{:S(2)}) copy-start(bf16[4,1,2,32,1024]{4,3,2,1,0:T(8,128)(2,1)} %param.20) | copy-start | bytes 1572868
  126.7 86.6 %all-to-all-start.9 = ((bf16[4,512,1024]{2,1,0:T(8,128)(2,1)}), bf16[4,512,1024]{2,1,0:T(8,128)(2,1)}, u32[]{:S(2)}, u32[]{:S(2)}) async-start(bf16[4,512,1024]{2,1,0:T(8,128)(2,1)} %broadcast_in_dim.80), calls=%async_computation.9 | async-start | bytes 8388608 | tf_op jit(solution)/shard_map/all_to_all | solution.py:110
  180.1 25.0 %copy-start.45 = (f32[4,1,256]{2,1,0:T(1,128)}, f32[4,1,256]{2,1,0:T(1,128)S(1)}, u32[]{:S(2)}) copy-start(f32[4,1,256]{2,1,0:T(1,128)S(1)} %convert_element_type.287) | copy-start | bytes 12292
  188.8 16.3 %copy-start.41 = (f32[4,1,256]{2,1,0:T(1,128)}, f32[4,1,256]{2,1,0:T(1,128)S(1)}, u32[]{:S(2)}) copy-start(f32[4,1,256]{2,1,0:T(1,128)S(1)} %convert_element_type.286) | copy-start | bytes 12292
  213.3 12.8 all-to-all-start.1
  226.1 12.0 all-to-all-start.2
  238.1 10.0 all-to-all-start.4
  250.6 99.0 %all-to-all-start.3 = ((bf16[8,4,256,256]{3,2,1,0:T(8,128)(2,1)}), bf16[8,4,256,256]{3,2,1,0:T(8,128)(2,1)}, u32[]{:S(2)}, u32[]{:S(2)}) async-start(bf16[8,4,256,256]{3,2,1,0:T(8,128)(2,1)} %broadcast_in_dim.75), calls=%async_computation.3 | async-start | bytes 8388608 | tf_op jit(solution)/shard_map/all_to_all | solution.py:226
  255.5 281.1 %all-gather.21.cloned.1.call-start = ((), (), s32[]{:S(2)}) async-start(), calls=%async_computation.28 | async-start | bytes 3145728 | tf_op jit(solution)/shard_map/all_gather | solution.py:117
  256.2 283.7 %all-gather.23.cloned.1.call-start = ((), (), s32[]{:S(2)}) async-start(), calls=%async_computation.29 | async-start | bytes 12582912 | tf_op jit(solution)/shard_map/all_gather | solution.py:117
  352.0 5.0 copy-start.52
  352.0 98.7 %all-to-all-start.5 = ((bf16[8,4,256,256]{3,2,1,0:T(8,128)(2,1)}), bf16[8,4,256,256]{3,2,1,0:T(8,128)(2,1)}, u32[]{:S(2)}, u32[]{:S(2)}) async-start(bf16[8,4,256,256]{3,2,1,0:T(8,128)(2,1)} %broadcast_in_dim.77), calls=%async_computation.5 | async-start | bytes 8388608 | tf_op jit(solution)/shard_map/all_to_all | solution.py:226
  356.8 192.6 %all-gather.25.cloned.1.call-start = ((), (), s32[]{:S(2)}) async-start(), calls=%async_computation.30 | async-start | bytes 12582912 | tf_op jit(solution)/shard_map/all_gather | solution.py:117
  496.8 5.0 copy-start.62
  496.8 14.5 %copy-start.53 = (bf16[1024]{0:T(1024)(128)(2,1)S(1)}, bf16[1024]{0:T(1024)(128)(2,1)}, u32[]{:S(2)}) copy-start(bf16[1024]{0:T(1024)(128)(2,1)} %param.33) | copy-start | bytes 6148
  496.8 23.1 %copy-start.63 = (bf16[256]{0:T(256)(128)(2,1)S(1)}, bf16[256]{0:T(256)(128)(2,1)}, u32[]{:S(2)}) copy-start(bf16[256]{0:T(256)(128)(2,1)} %param.31) | copy-start | bytes 1540
  496.8 31.1 %copy-start.64 = (bf16[256]{0:T(256)(128)(2,1)S(1)}, bf16[256]{0:T(256)(128)(2,1)}, u32[]{:S(2)}) copy-start(bf16[256]{0:T(256)(128)(2,1)} %param.30) | copy-start | bytes 1540
  498.1 37.0 %all-to-all-start.6 = ((bf16[4,2,128,1,256]{4,1,0,3,2:T(2,128)(2,1)}), bf16[4,2,128,1,256]{4,1,0,3,2:T(2,128)(2,1)S(1)}, u32[]{:S(2)}, u32[]{:S(2)}) async-start(bf16[4,2,128,1,256]{4,1,0,3,2:T(2,128)(2,1)} %copy.117), calls=%async_computation.6 | async-start | bytes 1048576 | tf_op jit(solution)/shard_map/all_to_all | solution.py:236
  538.9 25.9 %copy-start.15 = (f32[256,1024]{1,0:T(8,128)}, f32[256,1024]{1,0:T(8,128)S(1)}, u32[]{:S(2)}) copy-start(f32[256,1024]{1,0:T(8,128)S(1)} %get-tuple-element.311) | copy-start | bytes 3145732
  539.9 9.5 copy-start.19
  549.4 12.3 copy-start.57
  569.9 11.3 all-to-all-start.10
  573.4 358.0 %reduce-scatter.17.cloned.1.call-start = ((), (), s32[]{:S(2)}) async-start(), calls=%async_computation.36 | async-start | bytes 12582912 | tf_op jit(solution)/shard_map/reduce_scatter | solution.py:129
  720.1 5.2 copy-start.29
  720.1 189.0 %all-to-all-start.12 = ((bf16[8,4,256,512]{2,3,1,0:T(8,128)(2,1)}), bf16[8,4,256,512]{2,3,1,0:T(8,128)(2,1)}, u32[]{:S(2)}, u32[]{:S(2)}) async-start(bf16[8,4,256,512]{2,3,1,0:T(8,128)(2,1)} %copy.128), calls=%async_computation.12 | async-start | bytes 16777216 | tf_op jit(solution)/shard_map/all_to_all | solution.py:274
  725.2 283.8 %reduce-scatter.21.cloned.1.call-start = ((), (), s32[]{:S(2)}) async-start(), calls=%async_computation.40 | async-start | bytes 12582912 | tf_op jit(solution)/shard_map/reduce_scatter | solution.py:129
  728.2 4.7 copy-start.20
  909.1 11.8 all-to-all-start.11
  931.4 49.7 %all-to-all-start.17 = ((bf16[4,128,4096]{2,1,0:T(8,128)(2,1)}), bf16[4,128,4096]{2,1,0:T(8,128)(2,1)}, u32[]{:S(2)}, u32[]{:S(2)}) async-start(bf16[4,128,4096]{2,1,0:T(8,128)(2,1)} %bitcast.287), calls=%async_computation.22 | async-start | bytes 8388608 | tf_op jit(solution)/shard_map/all_to_all | solution.py:131
  936.3 49.0 %copy-start.44 = (f32[4,2,32]{2,1,0:T(2,128)S(1)}, f32[4,2,32]{2,1,0:T(2,128)}, u32[]{:S(2)}) copy-start(f32[4,2,32]{2,1,0:T(2,128)} %copy-done.43) | copy-start | bytes 3076
  936.3 49.1 %copy-start.14 = (bf16[4,1,2,32,1024]{4,3,2,1,0:T(8,128)(2,1)S(1)}, bf16[4,1,2,32,1024]{4,3,2,1,0:T(8,128)(2,1)}, u32[]{:S(2)}) copy-start(bf16[4,1,2,32,1024]{4,3,2,1,0:T(8,128)(2,1)} %param.20) | copy-start | bytes 1572868
  936.5 50.0 %copy-start.47 = (f32[4,2,32]{2,1,0:T(2,128)S(1)}, f32[4,2,32]{2,1,0:T(2,128)}, u32[]{:S(2)}) copy-start(f32[4,2,32]{2,1,0:T(2,128)} %get-tuple-element.304) | copy-start | bytes 3076
  981.2 12.4 all-to-all-start.14
  985.3 87.4 %reduce-scatter.19.cloned.1.call-start = ((), (), s32[]{:S(2)}) async-start(), calls=%async_computation.37 | async-start | bytes 1310720 | tf_op jit(solution)/shard_map/reduce_scatter | solution.py:135
  990.9 82.6 %reduce-scatter.9.cloned.1.call-start = ((), (), s32[]{:S(2)}) async-start(), calls=%async_computation.31 | async-start | bytes 9437184 | tf_op jit(solution)/shard_map/reduce_scatter | solution.py:129
  995.5 5.8 copy-start.46
  1008.9 83.9 %reduce-scatter.23.cloned.1.call-start = ((), (), s32[]{:S(2)}) async-start(), calls=%async_computation.41 | async-start | bytes 1310720 | tf_op jit(solution)/shard_map/reduce_scatter | solution.py:135
  1066.4 49.7 %reduce-scatter.13.cloned.1.call-start = ((), (), s32[]{:S(2)}) async-start(), calls=%async_computation.34 | async-start | bytes 3145728 | tf_op jit(solution)/shard_map/reduce_scatter | solution.py:129
  1072.7 62.0 %all-gather.29.cloned.1.call-start = ((), (), s32[]{:S(2)}) async-start(), calls=%async_computation.38 | async-start | bytes 1310720 | tf_op jit(solution)/shard_map/all_gather | solution.py:136
  1073.4 38.9 %all-to-all-start.15 = ((bf16[4,128,3072]{2,1,0:T(8,128)(2,1)}), bf16[4,128,3072]{2,1,0:T(8,128)(2,1)}, u32[]{:S(2)}, u32[]{:S(2)}) async-start(bf16[4,128,3072]{2,1,0:T(8,128)(2,1)} %bitcast.292), calls=%async_computation.16 | async-start | bytes 6291456 | tf_op jit(solution)/shard_map/all_to_all | solution.py:131
  1078.1 85.3 %all-gather.33.cloned.1.call-start = ((), (), s32[]{:S(2)}) async-start(), calls=%async_computation.42 | async-start | bytes 1310720 | tf_op jit(solution)/shard_map/all_gather | solution.py:136
  1092.8 95.5 %reduce-scatter.11.cloned.1.call-start = ((), (), s32[]{:S(2)}) async-start(), calls=%async_computation.32 | async-start | bytes 983040 | tf_op jit(solution)/shard_map/reduce_scatter | solution.py:135
  1116.0 100.2 %reduce-scatter.15.cloned.1.call-start = ((), (), s32[]{:S(2)}) async-start(), calls=%async_computation.35 | async-start | bytes 327680 | tf_op jit(solution)/shard_map/reduce_scatter | solution.py:135
  1133.2 30.4 %copy-start.65 = (bf16[256]{0:T(256)(128)(2,1)S(1)}, bf16[256]{0:T(256)(128)(2,1)}, u32[]{:S(2)}) copy-start(bf16[256]{0:T(256)(128)(2,1)} %param.35) | copy-start | bytes 1540
  1133.2 39.6 %copy-start.66 = (u32[32]{0:T(128)S(1)}, u32[32]{0:T(128)}, u32[]{:S(2)}) copy-start(u32[32]{0:T(128)} %constant.168) | copy-start | bytes 388
  1133.2 40.2 %copy-start.56 = (u32[32]{0:T(128)S(1)}, u32[32]{0:T(128)}, u32[]{:S(2)}) copy-start(u32[32]{0:T(128)} %constant.120) | copy-start | bytes 388
  1134.1 163.4 %all-gather.31.cloned.1.call-start = ((), (), s32[]{:S(2)}) async-start(), calls=%async_computation.39 | async-start | bytes 3145728 | tf_op jit(solution)/shard_map/all_gather | solution.py:137
  1134.6 74.4 %copy-start.16 = (f32[256,1024]{1,0:T(8,128)S(1)}, f32[256,1024]{1,0:T(8,128)}, u32[]{:S(2)}) copy-start(f32[256,1024]{1,0:T(8,128)} %copy-done.15) | copy-start | bytes 3145732
  1134.7 166.9 %all-gather.35.cloned.1.call-start = ((), (), s32[]{:S(2)}) async-start(), calls=%async_computation.43 | async-start | bytes 3145728 | tf_op jit(solution)/shard_map/all_gather | solution.py:137
  1163.5 142.4 %all-gather.27.cloned.1.call-start = ((), (), s32[]{:S(2)}) async-start(), calls=%async_computation.33 | async-start | bytes 2359296 | tf_op jit(solution)/shard_map/all_gather | solution.py:137
  1234.4 61.6 %copy-start.18 = (f32[256,1024]{1,0:T(8,128)S(1)}, f32[256,1024]{1,0:T(8,128)}, u32[]{:S(2)}) copy-start(f32[256,1024]{1,0:T(8,128)} %copy-done.17) | copy-start | bytes 3145732
  1234.4 61.6 %copy-start.21 = (bf16[4,1,2,32,1024]{4,3,2,1,0:T(8,128)(2,1)S(1)}, bf16[4,1,2,32,1024]{4,3,2,1,0:T(8,128)(2,1)}, u32[]{:S(2)}) copy-start(bf16[4,1,2,32,1024]{4,3,2,1,0:T(8,128)(2,1)} %param.21) | copy-start | bytes 1572868
  1234.4 61.6 %copy-start.25 = (f32[256,1024]{1,0:T(8,128)S(1)}, f32[256,1024]{1,0:T(8,128)}, u32[]{:S(2)}) copy-start(f32[256,1024]{1,0:T(8,128)} %get-tuple-element.315) | copy-start | bytes 3145732
  1234.4 61.6 %copy-start.49 = (f32[256]{0:T(256)S(1)}, f32[256]{0:T(256)}, u32[]{:S(2)}) copy-start(f32[256]{0:T(256)} %copy-done.48) | copy-start | bytes 3076
  1301.6 7.7 copy-start.1
  (80 other events, 152.4 us)
Sparse Core Ops, SparseCore 0:
  50.8 16.4 all-gather.18
  257.8 11.0 all-gather.20
  270.5 21.0 all-gather.22
  358.8 20.2 all-gather.24
  581.3 16.1 reduce-scatter.16
  738.8 18.0 reduce-scatter.20
  991.0 28.1 reduce-scatter.18
  1021.5 12.5 reduce-scatter.8
  1066.5 26.2 reduce-scatter.22
  1095.5 8.2 reduce-scatter.12
  1105.3 29.2 all-gather.28
  1136.0 27.3 all-gather.32
  1165.7 22.5 reduce-scatter.10
  1191.0 20.7 reduce-scatter.14
  1213.2 9.0 all-gather.30
  1223.6 11.7 all-gather.34
  1236.8 10.9 all-gather.26

commit v6 on v4

--- a/solution.py
+++ b/solution.py
@@ -312,8 +312,7 @@
     weight_totals = tuple(
         reduce_weight_grad(grad) for grad in (qkv_grad, out_weight_term, fc_grad, proj_grad)
     )
-    vector_totals = []
-    for grad in (
+    vector_grads = (
         attn_gain_grad,
         attn_shift_grad,
         query_bias_grad,
@@ -323,10 +322,19 @@
         mlp_shift_grad,
         fc_bias_grad,
         proj_bias_grad,
-    ):
-        share = lax.psum_scatter(grad.astype(jnp.bfloat16), "fsdp", scatter_dimension=0, tiled=True)
-        piece = lax.psum_scatter(share, CTX, scatter_dimension=0, tiled=True)
-        vector_totals.append(lax.all_gather(piece, CTX, axis=0, tiled=True).astype(jnp.float32))
+    )
+    packed = jnp.concatenate(
+        [grad.astype(jnp.bfloat16).reshape(fsdp_size, -1) for grad in vector_grads], axis=1
+    )
+    packed = lax.psum_scatter(packed, "fsdp", scatter_dimension=0, tiled=True).reshape(-1)
+    packed = lax.psum_scatter(packed, CTX, scatter_dimension=0, tiled=True)
+    packed = lax.all_gather(packed, CTX, axis=0, tiled=True).astype(jnp.float32)
+    vector_totals = []
+    offset = 0
+    for grad in vector_grads:
+        width = grad.shape[0] // fsdp_size
+        vector_totals.append(packed[offset : offset + width])
+        offset += width
     totals = weight_totals + tuple(vector_totals)
     return (
         layer_out,

time: 1030 us -> 934 us (0.907)
  waiting for transfers between devices: 303 us -> 199 us
  blocking collectives: 294 us -> 320 us
    all_to_all x2 -> x1, waiting for transfers between devices: 66.3 us -> 16.1 us  [reduce_weight_grad(): lax.all_to_all(grad.reshape((fsdp_size, -1) + grad.shape[1:]), 'fsdp', sp...]
    reduce_scatter x1, waiting for transfers between devices: 61.7 us -> 19.8 us  [shards(): lax.psum_scatter(kv_grads.reshape(ctx_size * seq_count * pair_len, 2 * gr...]
    all_to_all x2 -> x3, blocking collectives: 70.5 us -> 107 us  [reduce_weight_grad(): lax.all_to_all(grad.reshape((fsdp_size, -1) + grad.shape[1:]), 'fsdp', sp...]
    unnamed x3 -> x2, blocking collectives: 43.8 us -> 30.2 us
    reduce_scatter x4, waiting for transfers between devices: 11 us -> 0.06 us  [reduce_weight_grad(): lax.psum_scatter(grad.astype(jnp.bfloat16), 'core', scatter_dimension=0,...]
  transfers between devices with their start and end apart: 31 -> 30, of which waited for: 13 -> 13; matrix products, arithmetic and copies ran while one was open for 17% -> 31% of each run, Pallas kernels for 0% -> 0%
where the time goes in v6:
time: 934 us; the launch traced here: 925 us
  blocking collectives  320 us (34%)
  waiting for transfers between devices  199 us (21%)
  local copies, waits for them, and re-layouts  151 us (16%)
  matrix products  132 us (14%)
  other arithmetic  63.1 us (7%)
  starting transfers between devices  41.9 us (4%)
  between operations  16.6 us (2%)
    all_to_all x3, blocking collectives, reduce_weight_grad(): lax.all_to_all(grad.reshape((fsdp_size, -1) + grad.shape[1:]), 'fsdp', sp...  107 us
    all_to_all x3, waiting for transfers between devices, gather_weight(): lax.all_to_all(jnp.broadcast_to(piece[None], (fsdp_size,) + piece.shape),...  93.9 us
    dot_general x52, matrix products, contract_last(): lax.dot_general(left, right, (((1,), (1,)), ((), ())), preferred_element_...  52.4 us
    all_to_all x1, blocking collectives, gather_weight(): lax.all_to_all(jnp.broadcast_to(piece[None], (fsdp_size,) + piece.shape),...  41.7 us
    dot_general x36, matrix products, contract_first(): lax.dot_general(left, right, (((0,), (0,)), ((), ())), preferred_element_...  36 us
    all_gather x2, waiting for transfers between devices, reduce_weight_grad(): grad = lax.all_gather(grad, 'zc', axis=0, tiled=True)  35.8 us
    all_gather x2, blocking collectives, reduce_weight_grad(): grad = lax.all_gather(grad, 'zc', axis=0, tiled=True)  33.7 us
    unnamed x2, blocking collectives  30.2 us
  transfers between devices with their start and end apart: 30, of which 13 were waited for; matrix products, arithmetic and copies ran while one was open for 31% of the time, Pallas kernels for 0%

profile of v6, /device:TPU:0, one launch (start us, length us, event | category | flops | bytes accessed | tf_op | source)
XLA Modules:
  0.0 924.9 jit_solution(17985691420127177629)
XLA Ops:
  9.0 41.7 %all_to_all.154 = bf16[4,128,3072]{2,1,0:T(8,128)(2,1)} all-to-all(bf16[4,128,3072]{2,1,0:T(8,128)(2,1)S(1)} %broadcast_in_dim.65), channel_id=1, replica_groups=mesh['zc'=4,'core'=2,'fsdp'=4] {'fsdp'}, dimensions={0} | all-to-all | bytes 6291456 | tf_op jit(solution)/shard_map/all_to_all | solution.py:110
  51.3 7.5 all-gather.1
  58.8 7.7 all-gather
  67.9 4.6 fusion.101
  76.6 12.1 %all_to_all.155 = bf16[4,2,32,4,256]{4,2,1,0,3:T(8,128)(2,1)S(1)} all-to-all(bf16[4,2,32,4,256]{4,2,1,0,3:T(8,128)(2,1)S(1)} %copy.117), channel_id=1, replica_groups=mesh['zc'=4,'core'=2,'fsdp'=4] {'fsdp'}, dimensions={3} | all-to-all | bytes 1048576 | tf_op jit(solution)/shard_map/all_to_all | solution.py:219
  89.6 7.5 all-gather.3
  97.1 7.7 all-gather.2
  109.2 9.8 %all_to_all.156 = bf16[4,2,32,4,256]{4,2,1,0,3:T(8,128)(2,1)S(1)} all-to-all(bf16[4,2,32,4,256]{4,2,1,0,3:T(8,128)(2,1)S(1)} %copy.120), channel_id=1, replica_groups=mesh['zc'=4,'core'=2,'fsdp'=4] {'fsdp'}, dimensions={3} | all-to-all | bytes 1048576 | tf_op jit(solution)/shard_map/all_to_all | solution.py:220
  121.0 4.3 all-to-all-start.5
  126.3 8.4 all-to-all-done.5
  134.7 3.8 broadcast_in_dim.67
  138.5 4.9 all-to-all-start.6
  144.0 40.2 %all-to-all-done.6 = bf16[4,128,4096]{2,1,0:T(8,128)(2,1)} async-done(((bf16[4,128,4096]{2,1,0:T(8,128)(2,1)}), bf16[4,128,4096]{2,1,0:T(8,128)(2,1)}, u32[]{:S(2)}, u32[]{:S(2)}) %all-to-all-start.6) | async-done | bytes 4194336 | tf_op jit(solution)/shard_map/all_to_all | solution.py:110
  188.5 5.1 all-to-all-start.7
  195.3 45.2 %all-to-all-done.7 = bf16[4,512,1024]{2,1,0:T(8,128)(2,1)} async-done(((bf16[4,512,1024]{2,1,0:T(8,128)(2,1)}), bf16[4,512,1024]{2,1,0:T(8,128)(2,1)}, u32[]{:S(2)}, u32[]{:S(2)}) %all-to-all-start.7) | async-done | bytes 4194336 | tf_op jit(solution)/shard_map/all_to_all | solution.py:110
  240.5 3.5 all-to-all-start.1
  244.6 6.9 all-to-all-done.1
  252.3 5.3 copy.119
  257.7 6.1 copy.122
  263.7 41.4 %while.26 = (s32[]{:T(128)}, bf16[4,256,256]{2,1,0:T(8,128)(2,1)S(1)}, f32[4,256,4]{1,2,0:T(4,128)}, s32[4,2048]{1,0:T(4,128)S(1)}, s32[4,256]{1,0:T(4,128)S(1)}...) while((s32[]{:T(128)}, ...), condition=%wide.region_11.12_spmd, body=%wide.region_2.11_spmd.sunk | while | flops 554240000 | bytes 35092604 | solution.py:235
  306.5 3.5 all-to-all-start.4
  310.1 8.7 all-gather.4
  318.8 8.0 all_gather.84
  326.8 8.0 all-gather.6
  334.8 7.2 all-gather.5
  346.8 9.5 %multiply_convert_fusion.4 = (bf16[256,4096]{1,0:T(8,128)(2,1)}, f32[256,4096]{1,0:T(8,128)}) fusion(f32[4096]{0:T(1024)S(1)} %convert_element_type.247, bf16[256,1024]{1,0:T(8,128)(2,1)S(1)} %add_convert_fusion.1, bf16[1024,4096]{1,0:T(8,128)(2,1)} %bitcast.352), kind=kOutput, calls=%fused_computation.141 | convolution fusion | flops 2157969408 | bytes 15220736 | tf_op jit(solution)/shard_map/dot_general | solution.py:245
  356.3 12.5 %fusion.100 = (bf16[4096]{0:T(1024)(128)(2,1)}, bf16[256,4096]{1,0:T(8,128)(2,1)S(1)}) fusion(f32[256,4096]{1,0:T(8,128)} %get-tuple-element.293, bf16[4096,1024]{1,0:T(8,128)(2,1)} %bitcast.350, bf16[256,1024]{1,0:T(8,128)(2,1)S(1)} %bitcast.269), kind=kOutput, calls=%fused_computation.221 | convolution fusion | flops 2169499648 | bytes 15212544 | tf_op jit(solution)/shard_map/dot_general | solution.py:29
  368.8 3.2 multiply_reduce_fusion.4
  377.0 3.5 all-to-all-start.8
  381.1 7.2 convolution_convert_fusion.9
  389.3 118.0 %while.27 = (s32[]{:T(128)}, bf16[4,256,256]{2,1,0:T(8,128)(2,1)}, bf16[4,2048,256]{2,1,0:T(8,128)(2,1)}, bf16[4,2048,256]{2,1,0:T(8,128)(2,1)}, s32[4,2048]{1,0...) while((s32[]{:T(128)}, bf16[4,256,256]{2,1,0:T(8,128)(2,1)}, ...), condition=%wide.region_21.22_spmd, body=%wide.region_16.21_spmd.sunk | while | flops 1370029056 | bytes 166414960 | solution.py:269
  507.3 7.6 maximum_bitcast_fusion.5
  514.8 7.5 copy.135
  523.9 2.9 reshape.471
  526.9 4.8 copy.150
  531.7 5.6 convolution_convert_fusion.8
  537.5 44.4 %all_to_all.158 = bf16[4,128,4096]{2,1,0:T(8,128)(2,1)} all-to-all(bf16[4,128,4096]{2,1,0:T(8,128)(2,1)} %bitcast.281), channel_id=1, replica_groups=mesh['zc'=4,'core'=2,'fsdp'=4] {'fsdp'}, dimensions={0} | all-to-all | bytes 8388608 | tf_op jit(solution)/shard_map/all_to_all | solution.py:131
  581.9 4.3 reduce_sum.333
  590.7 3.5 all-to-all-start.9
  594.1 19.8 %reduce-scatter.10.cloned.1.call-done = bf16[1024,512]{1,0:T(8,128)(2,1)} async-done(((bf16[8192,512]{1,0:T(8,128)(2,1)}), bf16[1024,512]{1,0:T(8,128)(2,1)}) %reduce-scatter.10.cloned.1.call-update) | async-done | bytes 1048592 | tf_op jit(solution)/shard_map/reduce_scatter | solution.py:275
  616.6 3.6 all-to-all-start.10
  621.6 5.2 all-to-all-done.10
  626.8 4.2 all-to-all-start.11
  639.5 5.8 fusion.88
  648.5 4.5 convolution_convert_fusion.10
  653.1 49.4 %all_to_all.159 = bf16[4,512,1024]{2,1,0:T(8,128)(2,1)} all-to-all(bf16[4,512,1024]{2,1,0:T(8,128)(2,1)} %bitcast.282), channel_id=1, replica_groups=mesh['zc'=4,'core'=2,'fsdp'=4] {'fsdp'}, dimensions={0} | all-to-all | bytes 8388608 | tf_op jit(solution)/shard_map/all_to_all | solution.py:131
  702.5 4.4 reduce_sum.334
  707.6 13.4 %all_to_all.157 = bf16[4,128,1024]{2,1,0:T(8,128)(2,1)S(1)} all-to-all(bf16[4,128,1024]{2,1,0:T(8,128)(2,1)} %bitcast.312), channel_id=1, replica_groups=mesh['zc'=4,'core'=2,'fsdp'=4] {'fsdp'}, dimensions={0} | all-to-all | bytes 2097152 | tf_op jit(solution)/shard_map/all_to_all | solution.py:131
  721.0 4.7 all-to-all-start.12
  725.7 12.3 %reduce-scatter.26.cloned.1.call-done = bf16[128,1024]{1,0:T(8,128)(2,1)} async-done(((bf16[512,1024]{1,0:T(8,128)(2,1)}), bf16[128,1024]{1,0:T(8,128)(2,1)}) %reduce-scatter.26.cloned.1.call-update) | async-done | bytes 262160 | tf_op jit(solution)/shard_map/reduce_scatter | solution.py:135
  739.1 16.1 %all-to-all-done.12 = bf16[4,128,3072]{2,1,0:T(8,128)(2,1)} async-done(((bf16[4,128,3072]{2,1,0:T(8,128)(2,1)}), bf16[4,128,3072]{2,1,0:T(8,128)(2,1)}, u32[]{:S(2)}, u32[]{:S(2)}) %all-to-all-start.12) | async-done | bytes 3145760 | tf_op jit(solution)/shard_map/all_to_all | solution.py:131
  755.2 3.6 reduce_sum.331
  758.9 7.1 all-gather.35.cloned.1.call-done
  766.1 28.7 %all-gather.39.cloned.1.call-done = bf16[512,1024]{1,0:T(8,128)(2,1)} async-done(((bf16[128,1024]{1,0:T(8,128)(2,1)}), bf16[512,1024]{1,0:T(8,128)(2,1)}) %all-gather.39.cloned.1.call-update) | async-done | bytes 1048592 | tf_op jit(solution)/shard_map/all_gather | solution.py:136
  794.9 8.3 all-gather.7
  806.3 7.2 fusion.78
  816.3 15.5 %all_gather.90 = bf16[128,1024]{1,0:T(8,128)(2,1)S(1)} all-gather(bf16[32,1024]{1,0:T(8,128)(2,1)} %reduce-scatter.18.cloned.1.call-done), channel_id=1, replica_groups=mesh['zc'=4,'core'=2,'fsdp'=4] {'zc'}, dimensions={0}, use_global_device_ids=true | all-gather | bytes 327680 | tf_op jit(solution)/shard_map/all_gather | solution.py:136
  841.1 18.2 %all_gather.88 = bf16[128,3072]{1,0:T(8,128)(2,1)} all-gather(bf16[32,3072]{1,0:T(8,128)(2,1)} %reduce-scatter.14.cloned.1.call-done), channel_id=1, replica_groups=mesh['zc'=4,'core'=2,'fsdp'=4] {'zc'}, dimensions={0}, use_global_device_ids=true | all-gather | bytes 983040 | tf_op jit(solution)/shard_map/all_gather | solution.py:136
  859.4 16.3 %all-reduce = bf16[4,3072]{1,0:T(4,128)(2,1)S(1)} all-reduce(bf16[4,3072]{1,0:T(4,128)(2,1)S(1)} %constant_dynamic-update-slice_fusion.7), channel_id=3, replica_groups=mesh['zc'=4,'core'=2,'fsdp'=4] {'fsdp'}, use_global_device_ids=true, to_apply=%region_34.35.clone | all-reduce | flops 12288 | bytes 49152
  876.4 13.8 %all-reduce.1 = bf16[3072]{0:T(1024)(128)(2,1)S(1)} all-reduce(bf16[3072]{0:T(1024)(128)(2,1)S(1)} %dynamic-slice_reduce_fusion), channel_id=4, replica_groups=mesh['zc'=4,'core'=2,'fsdp'=4] {'zc','core'}, use_global_device_ids=true, to_apply=%region_35.36.clone | all-reduce | flops 3072 | bytes 12288
  890.4 12.7 %all-gather.8 = bf16[8,1,384]{2,1,0:T(2,128)(2,1)S(1)} all-gather(bf16[1,1,384]{2,1,0:T(2,128)(2,1)S(1)} %reshape.492), channel_id=1, replica_groups=mesh['zc'=4,'core'=2,'fsdp'=4] {'zc','core'}, dimensions={0}, use_global_device_ids=true | all-gather | bytes 6912 | tf_op jit(solution)/shard_map/all_gather | solution.py:331
  905.8 4.1 convert_element_type.277
  909.9 4.2 convert_element_type.279
  914.2 3.4 convert_element_type.273
  (677 shorter events, 235.8 us)
Async XLA Ops:
  7.2 118.1 %copy-start = (bf16[256,4096]{1,0:T(8,128)(2,1)S(1)}, bf16[256,4096]{1,0:T(8,128)(2,1)}, u32[]{:S(2)}) copy-start(bf16[256,4096]{1,0:T(8,128)(2,1)} %param.32) | copy-start | bytes 6291460
  7.2 60.7 %all-gather.21.cloned.1.call-start = ((), (), s32[]{:S(2)}) async-start(), calls=%async_computation.25 | async-start | bytes 9437184 | tf_op jit(solution)/shard_map/all_gather | solution.py:117
  50.7 8.1 copy-start.60
  50.7 15.9 %copy-start.13 = (bf16[4,1,2,32,1024]{4,3,2,1,0:T(8,128)(2,1)S(1)}, bf16[4,1,2,32,1024]{4,3,2,1,0:T(8,128)(2,1)}, u32[]{:S(2)}) copy-start(bf16[4,1,2,32,1024]{4,3,2,1,0:T(8,128)(2,1)} %param.20) | copy-start | bytes 1572868
  50.7 201.6 %all-gather.23.cloned.1.call-start = ((), (), s32[]{:S(2)}) async-start(), calls=%async_computation.26 | async-start | bytes 4718592 | tf_op jit(solution)/shard_map/all_gather | solution.py:226
  58.8 8.8 copy-start.47
  76.5 13.1 %copy-start.61 = (bf16[256]{0:T(256)(128)(2,1)S(1)}, bf16[256]{0:T(256)(128)(2,1)}, u32[]{:S(2)}) copy-start(bf16[256]{0:T(256)(128)(2,1)} %param.27) | copy-start | bytes 1540
  76.5 20.6 %copy-start.62 = (bf16[256]{0:T(256)(128)(2,1)S(1)}, bf16[256]{0:T(256)(128)(2,1)}, u32[]{:S(2)}) copy-start(bf16[256]{0:T(256)(128)(2,1)} %param.26) | copy-start | bytes 1540
  89.6 168.1 %all-gather.25.cloned.1.call-start = ((), (), s32[]{:S(2)}) async-start(), calls=%async_computation.27 | async-start | bytes 4718592 | tf_op jit(solution)/shard_map/all_gather | solution.py:229
  109.2 10.6 %copy-start.42 = (bf16[256,1024]{1,0:T(8,128)(2,1)S(1)}, bf16[256,1024]{1,0:T(8,128)(2,1)}, u32[]{:S(2)}) copy-start(bf16[256,1024]{1,0:T(8,128)(2,1)} %param.28) | copy-start | bytes 1572868
  121.0 13.8 %all-to-all-start.5 = ((bf16[4,128,1024]{2,1,0:T(8,128)(2,1)}), bf16[4,128,1024]{2,1,0:T(8,128)(2,1)}, u32[]{:S(2)}, u32[]{:S(2)}) async-start(bf16[4,128,1024]{2,1,0:T(8,128)(2,1)} %broadcast_in_dim.66), calls=%async_computation.5 | async-start | bytes 2097152 | tf_op jit(solution)/shard_map/all_to_all | solution.py:110
  138.5 45.7 %all-to-all-start.6 = ((bf16[4,128,4096]{2,1,0:T(8,128)(2,1)}), bf16[4,128,4096]{2,1,0:T(8,128)(2,1)}, u32[]{:S(2)}, u32[]{:S(2)}) async-start(bf16[4,128,4096]{2,1,0:T(8,128)(2,1)} %broadcast_in_dim.67), calls=%async_computation.6 | async-start | bytes 8388608 | tf_op jit(solution)/shard_map/all_to_all | solution.py:110
  143.4 200.1 %all-gather.27.cloned.1.call-start = ((), (), s32[]{:S(2)}) async-start(), calls=%async_computation.28 | async-start | bytes 3145728 | tf_op jit(solution)/shard_map/all_gather | solution.py:117
  144.0 202.9 %all-gather.29.cloned.1.call-start = ((), (), s32[]{:S(2)}) async-start(), calls=%async_computation.29 | async-start | bytes 12582912 | tf_op jit(solution)/shard_map/all_gather | solution.py:117
  188.5 5.1 copy-start.54
  188.5 5.5 copy-start.37
  188.5 52.0 %all-to-all-start.7 = ((bf16[4,512,1024]{2,1,0:T(8,128)(2,1)}), bf16[4,512,1024]{2,1,0:T(8,128)(2,1)}, u32[]{:S(2)}, u32[]{:S(2)}) async-start(bf16[4,512,1024]{2,1,0:T(8,128)(2,1)} %broadcast_in_dim.68), calls=%async_computation.7 | async-start | bytes 8388608 | tf_op jit(solution)/shard_map/all_to_all | solution.py:110
  240.5 11.0 %all-to-all-start.1 = ((bf16[4,2,32,4,256]{4,2,1,0,3:T(8,128)(2,1)}), bf16[4,2,32,4,256]{4,2,1,0,3:T(8,128)(2,1)S(1)}, u32[]{:S(2)}, u32[]{:S(2)}) async-start(bf16[4,2,32,4,256]{4,2,1,0,3:T(8,128)(2,1)} %copy.115), calls=%async_computation.1 | async-start | bytes 1048576 | tf_op jit(solution)/shard_map/all_to_all | solution.py:218
  244.0 112.3 %all-gather.31.cloned.1.call-start = ((), (), s32[]{:S(2)}) async-start(), calls=%async_computation.30 | async-start | bytes 12582912 | tf_op jit(solution)/shard_map/all_gather | solution.py:117
  305.1 5.0 copy-start.63
  305.1 13.7 %copy-start.55 = (bf16[1024]{0:T(1024)(128)(2,1)S(1)}, bf16[1024]{0:T(1024)(128)(2,1)}, u32[]{:S(2)}) copy-start(bf16[1024]{0:T(1024)(128)(2,1)} %param.33) | copy-start | bytes 6148
  305.1 21.7 %copy-start.64 = (bf16[256]{0:T(256)(128)(2,1)S(1)}, bf16[256]{0:T(256)(128)(2,1)}, u32[]{:S(2)}) copy-start(bf16[256]{0:T(256)(128)(2,1)} %param.31) | copy-start | bytes 1540
  305.1 29.7 %copy-start.65 = (bf16[256]{0:T(256)(128)(2,1)S(1)}, bf16[256]{0:T(256)(128)(2,1)}, u32[]{:S(2)}) copy-start(bf16[256]{0:T(256)(128)(2,1)} %param.30) | copy-start | bytes 1540
  306.5 35.6 %all-to-all-start.4 = ((bf16[4,2,128,1,256]{4,1,0,3,2:T(2,128)(2,1)}), bf16[4,2,128,1,256]{4,1,0,3,2:T(2,128)(2,1)S(1)}, u32[]{:S(2)}, u32[]{:S(2)}) async-start(bf16[4,2,128,1,256]{4,1,0,3,2:T(2,128)(2,1)} %copy.124), calls=%async_computation.4 | async-start | bytes 1048576 | tf_op jit(solution)/shard_map/all_to_all | solution.py:238
  345.9 26.1 %copy-start.15 = (f32[256,1024]{1,0:T(8,128)}, f32[256,1024]{1,0:T(8,128)S(1)}, u32[]{:S(2)}) copy-start(f32[256,1024]{1,0:T(8,128)S(1)} %get-tuple-element.291) | copy-start | bytes 3145732
  346.8 9.5 %copy-start.19 = (bf16[4,1,2,32,1024]{4,3,2,1,0:T(8,128)(2,1)S(1)}, bf16[4,1,2,32,1024]{4,3,2,1,0:T(8,128)(2,1)}, u32[]{:S(2)}) copy-start(bf16[4,1,2,32,1024]{4,3,2,1,0:T(8,128)(2,1)} %param.21) | copy-start | bytes 1572868
  356.3 12.5 %copy-start.58 = (bf16[4,256,4096]{2,1,0:T(8,128)(2,1)S(1)}, bf16[4,256,4096]{2,1,0:T(8,128)(2,1)}, u32[]{:S(2)}) copy-start(bf16[4,256,4096]{2,1,0:T(8,128)(2,1)} %all-gather.29.cloned.1.call-done) | copy-start | bytes 25165828
  377.0 11.3 %all-to-all-start.8 = ((bf16[4,2,32,4,256]{4,2,1,0,3:T(8,128)(2,1)}), bf16[4,2,32,4,256]{4,2,1,0,3:T(8,128)(2,1)S(1)}, u32[]{:S(2)}, u32[]{:S(2)}) async-start(bf16[4,2,32,4,256]{4,2,1,0,3:T(8,128)(2,1)} %copy.127), calls=%async_computation.8 | async-start | bytes 1048576 | tf_op jit(solution)/shard_map/all_to_all | solution.py:266
  380.5 157.0 %reduce-scatter.20.cloned.1.call-start = ((), (), s32[]{:S(2)}) async-start(), calls=%async_computation.37 | async-start | bytes 12582912 | tf_op jit(solution)/shard_map/reduce_scatter | solution.py:129
  388.3 225.6 %reduce-scatter.10.cloned.1.call-start = ((), (), s32[]{:S(2)}) async-start(), calls=%async_computation.31 | async-start | bytes 9437184 | tf_op jit(solution)/shard_map/reduce_scatter | solution.py:275
  522.4 130.7 %reduce-scatter.24.cloned.1.call-start = ((), (), s32[]{:S(2)}) async-start(), calls=%async_computation.41 | async-start | bytes 12582912 | tf_op jit(solution)/shard_map/reduce_scatter | solution.py:129
  526.9 4.8 copy-start.20
  537.4 169.6 %reduce-scatter.22.cloned.1.call-start = ((), (), s32[]{:S(2)}) async-start(), calls=%async_computation.38 | async-start | bytes 1310720 | tf_op jit(solution)/shard_map/reduce_scatter | solution.py:135
  586.2 121.3 %reduce-scatter.16.cloned.1.call-start = ((), (), s32[]{:S(2)}) async-start(), calls=%async_computation.35 | async-start | bytes 3145728 | tf_op jit(solution)/shard_map/reduce_scatter | solution.py:129
  590.7 25.9 %all-to-all-start.9 = ((bf16[4,2,128,1,256]{4,1,0,3,2:T(2,128)(2,1)}), bf16[4,2,128,1,256]{4,1,0,3,2:T(2,128)(2,1)S(1)}, u32[]{:S(2)}, u32[]{:S(2)}) async-start(bf16[4,2,128,1,256]{4,1,0,3,2:T(2,128)(2,1)} %copy.130), calls=%async_computation.9 | async-start | bytes 1048576 | tf_op jit(solution)/shard_map/all_to_all | solution.py:286
  615.2 16.1 %copy-start.46 = (f32[4,2,32]{2,1,0:T(2,128)S(1)}, f32[4,2,32]{2,1,0:T(2,128)}, u32[]{:S(2)}) copy-start(f32[4,2,32]{2,1,0:T(2,128)} %copy-done.45) | copy-start | bytes 3076
  615.2 16.1 %copy-start.14 = (bf16[4,1,2,32,1024]{4,3,2,1,0:T(8,128)(2,1)S(1)}, bf16[4,1,2,32,1024]{4,3,2,1,0:T(8,128)(2,1)}, u32[]{:S(2)}) copy-start(bf16[4,1,2,32,1024]{4,3,2,1,0:T(8,128)(2,1)} %param.20) | copy-start | bytes 1572868
  616.6 10.2 %all-to-all-start.10 = ((bf16[4,2,128,1,256]{4,1,0,3,2:T(2,128)(2,1)}), bf16[4,2,128,1,256]{4,1,0,3,2:T(2,128)(2,1)S(1)}, u32[]{:S(2)}, u32[]{:S(2)}) async-start(bf16[4,2,128,1,256]{4,1,0,3,2:T(2,128)(2,1)} %copy.136), calls=%async_computation.11 | async-start | bytes 1048576 | tf_op jit(solution)/shard_map/all_to_all | solution.py:289
  620.2 12.2 %copy-start.49 = (f32[4,2,32]{2,1,0:T(2,128)S(1)}, f32[4,2,32]{2,1,0:T(2,128)}, u32[]{:S(2)}) copy-start(f32[4,2,32]{2,1,0:T(2,128)} %get-tuple-element.286) | copy-start | bytes 3076
  626.8 10.8 %all-to-all-start.11 = ((bf16[4,2,128,1,256]{4,1,0,3,2:T(2,128)(2,1)}), bf16[4,2,128,1,256]{4,1,0,3,2:T(2,128)(2,1)}, u32[]{:S(2)}, u32[]{:S(2)}) async-start(bf16[4,2,128,1,256]{4,1,0,3,2:T(2,128)(2,1)} %copy.139), calls=%async_computation.12 | async-start | bytes 1048576 | tf_op jit(solution)/shard_map/all_to_all | solution.py:292
  631.0 90.0 %reduce-scatter.12.cloned.1.call-start = ((), (), s32[]{:S(2)}) async-start(), calls=%async_computation.32 | async-start | bytes 9437184 | tf_op jit(solution)/shard_map/reduce_scatter | solution.py:129
  639.5 5.8 copy-start.48
  653.0 85.0 %reduce-scatter.26.cloned.1.call-start = ((), (), s32[]{:S(2)}) async-start(), calls=%async_computation.42 | async-start | bytes 1310720 | tf_op jit(solution)/shard_map/reduce_scatter | solution.py:135
  706.9 59.0 %all-gather.35.cloned.1.call-start = ((), (), s32[]{:S(2)}) async-start(), calls=%async_computation.39 | async-start | bytes 1310720 | tf_op jit(solution)/shard_map/all_gather | solution.py:136
  721.0 34.2 %all-to-all-start.12 = ((bf16[4,128,3072]{2,1,0:T(8,128)(2,1)}), bf16[4,128,3072]{2,1,0:T(8,128)(2,1)}, u32[]{:S(2)}, u32[]{:S(2)}) async-start(bf16[4,128,3072]{2,1,0:T(8,128)(2,1)} %bitcast.286), calls=%async_computation.14 | async-start | bytes 6291456 | tf_op jit(solution)/shard_map/all_to_all | solution.py:131
  725.7 69.1 %all-gather.39.cloned.1.call-start = ((), (), s32[]{:S(2)}) async-start(), calls=%async_computation.43 | async-start | bytes 1310720 | tf_op jit(solution)/shard_map/all_gather | solution.py:136
  738.1 78.3 %reduce-scatter.18.cloned.1.call-start = ((), (), s32[]{:S(2)}) async-start(), calls=%async_computation.36 | async-start | bytes 327680 | tf_op jit(solution)/shard_map/reduce_scatter | solution.py:135
  739.1 102.1 %reduce-scatter.14.cloned.1.call-start = ((), (), s32[]{:S(2)}) async-start(), calls=%async_computation.33 | async-start | bytes 983040 | tf_op jit(solution)/shard_map/reduce_scatter | solution.py:135
  758.8 36.1 %copy-start.66 = (bf16[256]{0:T(256)(128)(2,1)S(1)}, bf16[256]{0:T(256)(128)(2,1)}, u32[]{:S(2)}) copy-start(bf16[256]{0:T(256)(128)(2,1)} %param.35) | copy-start | bytes 1540
  758.8 45.6 %copy-start.68 = (u32[32]{0:T(128)S(1)}, u32[32]{0:T(128)}, u32[]{:S(2)}) copy-start(u32[32]{0:T(128)} %constant.119) | copy-start | bytes 388
  758.8 46.2 %copy-start.67 = (u32[32]{0:T(128)S(1)}, u32[32]{0:T(128)}, u32[]{:S(2)}) copy-start(u32[32]{0:T(128)} %constant.123) | copy-start | bytes 388
  758.8 47.4 %copy-start.52 = (bf16[1024]{0:T(1024)(128)(2,1)S(1)}, bf16[1024]{0:T(1024)(128)(2,1)}, u32[]{:S(2)}) copy-start(bf16[1024]{0:T(1024)(128)(2,1)} %get-tuple-element.244) | copy-start | bytes 6148
  758.8 47.5 %copy-start.57 = (bf16[1024]{0:T(1024)(128)(2,1)S(1)}, bf16[1024]{0:T(1024)(128)(2,1)}, u32[]{:S(2)}) copy-start(bf16[1024]{0:T(1024)(128)(2,1)} %get-tuple-element.199) | copy-start | bytes 6148
  758.8 47.5 %copy-start.56 = (bf16[1024]{0:T(1024)(128)(2,1)S(1)}, bf16[1024]{0:T(1024)(128)(2,1)}, u32[]{:S(2)}) copy-start(bf16[1024]{0:T(1024)(128)(2,1)} %get-tuple-element.203) | copy-start | bytes 6148
  758.8 47.5 %copy-start.53 = (bf16[4096]{0:T(1024)(128)(2,1)S(1)}, bf16[4096]{0:T(1024)(128)(2,1)}, u32[]{:S(2)}) copy-start(bf16[4096]{0:T(1024)(128)(2,1)} %get-tuple-element.296) | copy-start | bytes 24580
  758.8 47.5 %copy-start.16 = (f32[256,1024]{1,0:T(8,128)S(1)}, f32[256,1024]{1,0:T(8,128)}, u32[]{:S(2)}) copy-start(f32[256,1024]{1,0:T(8,128)} %copy-done.15) | copy-start | bytes 3145732
  758.9 147.0 %all-gather.37.cloned.1.call-start = ((), (), s32[]{:S(2)}) async-start(), calls=%async_computation.40 | async-start | bytes 3145728 | tf_op jit(solution)/shard_map/all_gather | solution.py:137
  766.0 143.9 %all-gather.41.cloned.1.call-start = ((), (), s32[]{:S(2)}) async-start(), calls=%async_computation.44 | async-start | bytes 3145728 | tf_op jit(solution)/shard_map/all_gather | solution.py:137
  794.8 119.3 %all-gather.33.cloned.1.call-start = ((), (), s32[]{:S(2)}) async-start(), calls=%async_computation.34 | async-start | bytes 2359296 | tf_op jit(solution)/shard_map/all_gather | solution.py:137
  837.7 66.7 %copy-start.18 = (f32[256,1024]{1,0:T(8,128)S(1)}, f32[256,1024]{1,0:T(8,128)}, u32[]{:S(2)}) copy-start(f32[256,1024]{1,0:T(8,128)} %copy-done.17) | copy-start | bytes 3145732
  837.7 66.7 %copy-start.21 = (bf16[4,1,2,32,1024]{4,3,2,1,0:T(8,128)(2,1)S(1)}, bf16[4,1,2,32,1024]{4,3,2,1,0:T(8,128)(2,1)}, u32[]{:S(2)}) copy-start(bf16[4,1,2,32,1024]{4,3,2,1,0:T(8,128)(2,1)} %param.21) | copy-start | bytes 1572868
  837.7 66.7 %copy-start.25 = (f32[256,1024]{1,0:T(8,128)S(1)}, f32[256,1024]{1,0:T(8,128)}, u32[]{:S(2)}) copy-start(f32[256,1024]{1,0:T(8,128)} %get-tuple-element.295) | copy-start | bytes 3145732
  837.7 66.7 %copy-start.51 = (f32[256]{0:T(256)S(1)}, f32[256]{0:T(256)}, u32[]{:S(2)}) copy-start(f32[256]{0:T(256)} %copy-done.50) | copy-start | bytes 3076
  909.9 7.7 copy-start.1
  (80 other events, 154.6 us)
Sparse Core Ops, SparseCore 0:
  50.8 16.4 all-gather.20
  89.7 46.2 all-gather.22
  138.2 45.6 all-gather.24
  185.3 9.3 all-gather.26
  196.1 21.0 all-gather.28
  246.1 21.6 all-gather.30
  388.4 18.2 reduce-scatter.19
  522.5 91.3 reduce-scatter.9
  616.2 14.8 reduce-scatter.23
  633.2 28.5 reduce-scatter.21
  664.7 8.2 reduce-scatter.15
  675.1 15.3 reduce-scatter.11
  707.1 30.9 reduce-scatter.25
  739.5 26.4 all-gather.34
  767.4 27.3 all-gather.38
  796.9 19.3 reduce-scatter.17
  819.0 22.0 reduce-scatter.13
  842.5 10.1 all-gather.36
  854.2 11.7 all-gather.40
  867.4 10.9 all-gather.32

commit v7 on v6

--- a/solution.py
+++ b/solution.py
@@ -131,11 +131,21 @@
     blocks = lax.all_to_all(
         grad.reshape((fsdp_size, -1) + grad.shape[1:]), "fsdp", split_axis=0, concat_axis=0, tiled=True
     )
-    grad = jnp.sum(blocks.astype(jnp.float32), axis=0).astype(jnp.bfloat16)
-    grad = lax.psum_scatter(grad, "zc", scatter_dimension=0, tiled=True)
-    grad = lax.all_gather(grad, "zc", axis=0, tiled=True)
-    grad = lax.all_gather(grad, "core", axis=0, tiled=True)
-    return grad.astype(jnp.float32)
+    return jnp.sum(blocks.astype(jnp.float32), axis=0).astype(jnp.bfloat16)
+
+
+def finish_weight_grads(grads):
+    packed = jnp.concatenate([grad.reshape(-1, 512) for grad in grads])
+    packed = lax.psum_scatter(packed, "zc", scatter_dimension=0, tiled=True)
+    packed = lax.all_gather(packed, "zc", axis=0, tiled=True).reshape(-1)
+    packed = lax.all_gather(packed, "core", axis=0, tiled=False).astype(jnp.float32)
+    totals = []
+    offset = 0
+    for grad in grads:
+        size = grad.size
+        totals.append(packed[:, offset : offset + size].reshape((-1,) + grad.shape[1:]))
+        offset += size
+    return tuple(totals)
 
 
 def shards(
@@ -309,8 +319,8 @@
         contract_last(grad_mixed, qkv_full)
     )
     in_grad = (grad_inputs + grad_middle).reshape(layer_in.shape)
-    weight_totals = tuple(
-        reduce_weight_grad(grad) for grad in (qkv_grad, out_weight_term, fc_grad, proj_grad)
+    weight_totals = finish_weight_grads(
+        tuple(reduce_weight_grad(grad) for grad in (qkv_grad, out_weight_term, fc_grad, proj_grad))
     )
     vector_grads = (
         attn_gain_grad,

time: 934 us -> 1090 us (1.17)
  waiting for transfers between devices: 199 us -> 371 us
  blocking collectives: 320 us -> 243 us
  local copies, waits for them, and re-layouts: 151 us -> 214 us
    reduce_scatter x4 -> x1, waiting for transfers between devices: 16.6 us -> 69.5 us  [finish_weight_grads(): packed = lax.psum_scatter(packed, 'zc', scatter_dimension=0, tiled=True)]
    all_to_all x1 -> x2, waiting for transfers between devices: 16.1 us -> 60.8 us  [reduce_weight_grad(): lax.all_to_all(grad.reshape((fsdp_size, -1) + grad.shape[1:]), 'fsdp', sp...]
    all_to_all x3 -> x2, blocking collectives: 107 us -> 66.5 us  [reduce_weight_grad(): lax.all_to_all(grad.reshape((fsdp_size, -1) + grad.shape[1:]), 'fsdp', sp...]
    reduce_scatter x1, waiting for transfers between devices: 19.8 us -> 59.8 us  [shards(): lax.psum_scatter(kv_grads.reshape(ctx_size * seq_count * pair_len, 2 * gr...]
    all_gather x3 -> x0, blocking collectives: 35.9 us -> none  [the longest x2 33.7 us: reduce_weight_grad(): grad = lax.all_gather(grad, 'zc', axis=0, tiled=True)]
    reshape x0 -> x8, local copies, waits for them, and re-layouts: none -> 30.4 us  [the longest x4 23.2 us: finish_weight_grads(): packed[:, offset:offset + size].reshape((-1,) + grad.shape[1:])]
    all_gather x5 -> x2, waiting for transfers between devices: 35.8 us -> 64.9 us  [the longest x1 64.9 us: finish_weight_grads(): packed = lax.all_gather(packed, 'zc', axis=0, tiled=True).reshape(-1)]
    unnamed x134 -> x142, local copies, waits for them, and re-layouts: 11.5 us -> 39.7 us
  transfers between devices with their start and end apart: 30 -> 25, of which waited for: 13 -> 12; matrix products, arithmetic and copies ran while one was open for 31% -> 15% of each run, Pallas kernels for 0% -> 0%
where the time goes in v7:
time: 1090 us; the launch traced here: 1080 us
  waiting for transfers between devices  371 us (34%)
  blocking collectives  243 us (22%)
  local copies, waits for them, and re-layouts  214 us (20%)
  matrix products  133 us (12%)
  other arithmetic  53.2 us (5%)
  starting transfers between devices  47.5 us (4%)
  between operations  16.2 us (1%)
    all_to_all x3, waiting for transfers between devices, gather_weight(): lax.all_to_all(jnp.broadcast_to(piece[None], (fsdp_size,) + piece.shape),...  93.9 us
    reduce_scatter x1, waiting for transfers between devices, finish_weight_grads(): packed = lax.psum_scatter(packed, 'zc', scatter_dimension=0, tiled=True)  69.5 us
    all_to_all x2, blocking collectives, reduce_weight_grad(): lax.all_to_all(grad.reshape((fsdp_size, -1) + grad.shape[1:]), 'fsdp', sp...  66.5 us
    all_gather x1, waiting for transfers between devices, finish_weight_grads(): packed = lax.all_gather(packed, 'zc', axis=0, tiled=True).reshape(-1)  64.9 us
    all_to_all x2, waiting for transfers between devices, reduce_weight_grad(): lax.all_to_all(grad.reshape((fsdp_size, -1) + grad.shape[1:]), 'fsdp', sp...  60.8 us
    reduce_scatter x1, waiting for transfers between devices, shards(): lax.psum_scatter(kv_grads.reshape(ctx_size * seq_count * pair_len, 2 * gr...  59.8 us
    dot_general x52, matrix products, contract_last(): lax.dot_general(left, right, (((1,), (1,)), ((), ())), preferred_element_...  53.2 us
    all_to_all x1, blocking collectives, gather_weight(): lax.all_to_all(jnp.broadcast_to(piece[None], (fsdp_size,) + piece.shape),...  41.7 us
  transfers between devices with their start and end apart: 25, of which 12 were waited for; matrix products, arithmetic and copies ran while one was open for 15% of the time, Pallas kernels for 0%

profile of v7, /device:TPU:0, one launch (start us, length us, event | category | flops | bytes accessed | tf_op | source)
XLA Modules:
  0.0 1079.5 jit_solution(1300968559425384114)
XLA Ops:
  9.0 41.7 %all_to_all.154 = bf16[4,128,3072]{2,1,0:T(8,128)(2,1)} all-to-all(bf16[4,128,3072]{2,1,0:T(8,128)(2,1)S(1)} %broadcast_in_dim.65), channel_id=1, replica_groups=mesh['zc'=4,'core'=2,'fsdp'=4] {'fsdp'}, dimensions={0} | all-to-all | bytes 6291456 | tf_op jit(solution)/shard_map/all_to_all | solution.py:110
  51.3 7.5 all-gather.1
  58.8 7.7 all-gather
  67.9 4.6 fusion.102
  76.6 12.1 %all_to_all.155 = bf16[4,2,32,4,256]{4,2,1,0,3:T(8,128)(2,1)S(1)} all-to-all(bf16[4,2,32,4,256]{4,2,1,0,3:T(8,128)(2,1)S(1)} %copy.117), channel_id=1, replica_groups=mesh['zc'=4,'core'=2,'fsdp'=4] {'fsdp'}, dimensions={3} | all-to-all | bytes 1048576 | tf_op jit(solution)/shard_map/all_to_all | solution.py:229
  89.6 7.5 all-gather.3
  97.1 7.7 all-gather.2
  109.2 9.8 all_to_all.156
  120.9 4.2 all-to-all-start.5
  126.2 8.4 all-to-all-done.5
  134.7 3.8 broadcast_in_dim.67
  138.4 4.9 all-to-all-start.6
  143.9 40.2 %all-to-all-done.6 = bf16[4,128,4096]{2,1,0:T(8,128)(2,1)} async-done(((bf16[4,128,4096]{2,1,0:T(8,128)(2,1)}), bf16[4,128,4096]{2,1,0:T(8,128)(2,1)}, u32[]{:S(2)}, u32[]{:S(2)}) %all-to-all-start.6) | async-done | bytes 4194336 | tf_op jit(solution)/shard_map/all_to_all | solution.py:110
  188.5 5.1 all-to-all-start.7
  195.2 45.3 %all-to-all-done.7 = bf16[4,512,1024]{2,1,0:T(8,128)(2,1)} async-done(((bf16[4,512,1024]{2,1,0:T(8,128)(2,1)}), bf16[4,512,1024]{2,1,0:T(8,128)(2,1)}, u32[]{:S(2)}, u32[]{:S(2)}) %all-to-all-start.7) | async-done | bytes 4194336 | tf_op jit(solution)/shard_map/all_to_all | solution.py:110
  240.5 3.5 all-to-all-start.1
  244.6 6.9 all-to-all-done.1
  252.3 5.3 copy.119
  257.6 6.1 copy.122
  263.7 41.4 %while.26 = (s32[]{:T(128)}, bf16[4,256,256]{2,1,0:T(8,128)(2,1)S(1)}, f32[4,256,4]{1,2,0:T(4,128)}, s32[4,2048]{1,0:T(4,128)S(1)}, s32[4,256]{1,0:T(4,128)S(1)}...) while((s32[]{:T(128)}, ...), condition=%wide.region_11.12_spmd, body=%wide.region_2.11_spmd.sunk | while | flops 554240000 | bytes 35092604 | solution.py:245
  306.4 3.5 all-to-all-start.4
  310.0 8.7 all-gather.4
  318.7 8.0 all_gather.66
  326.8 8.0 all-gather.6
  334.8 7.4 all-gather.5
  346.6 9.5 multiply_convert_fusion.4
  356.2 12.1 %fusion.101 = (bf16[4096]{0:T(1024)(128)(2,1)}, bf16[256,4096]{1,0:T(8,128)(2,1)S(1)}) fusion(f32[256,4096]{1,0:T(8,128)} %get-tuple-element.295, bf16[4096,1024]{1,0:T(8,128)(2,1)} %bitcast.356, bf16[256,1024]{1,0:T(8,128)(2,1)S(1)} %bitcast.275), kind=kOutput, calls=%fused_computation.224 | convolution fusion | flops 2169499648 | bytes 15212544 | tf_op jit(solution)/shard_map/dot_general | solution.py:29
  376.5 3.5 all-to-all-start.8
  380.3 6.3 all-to-all-done.8
  387.4 117.8 %while.27 = (s32[]{:T(128)}, bf16[4,256,256]{2,1,0:T(8,128)(2,1)}, bf16[4,2048,256]{2,1,0:T(8,128)(2,1)}, bf16[4,2048,256]{2,1,0:T(8,128)(2,1)}, s32[4,2048]{1,0...) while((s32[]{:T(128)}, bf16[4,256,256]{2,1,0:T(8,128)(2,1)}, ...), condition=%wide.region_21.22_spmd, body=%wide.region_16.21_spmd.sunk | while | flops 1370029056 | bytes 166414960 | solution.py:279
  505.2 7.5 maximum_bitcast_fusion.5
  512.8 7.6 copy.135
  526.9 4.8 copy.150
  531.7 5.6 convolution_convert_fusion.8
  539.3 5.6 convolution_convert_fusion.9
  547.3 3.5 all-to-all-start.9
  550.8 59.8 %reduce-scatter.7.cloned.1.call-done = bf16[1024,512]{1,0:T(8,128)(2,1)} async-done(((bf16[8192,512]{1,0:T(8,128)(2,1)}), bf16[1024,512]{1,0:T(8,128)(2,1)}) %reduce-scatter.7.cloned.1.call-update) | async-done | bytes 1048592 | tf_op jit(solution)/shard_map/reduce_scatter | solution.py:285
  613.2 3.7 all-to-all-start.10
  618.2 5.2 all-to-all-done.10
  623.4 4.1 all-to-all-start.11
  636.3 7.1 fusion.88
  646.5 4.4 convolution_convert_fusion.10
  651.0 13.5 %all_to_all.157 = bf16[4,128,1024]{2,1,0:T(8,128)(2,1)S(1)} all-to-all(bf16[4,128,1024]{2,1,0:T(8,128)(2,1)} %bitcast.318), channel_id=1, replica_groups=mesh['zc'=4,'core'=2,'fsdp'=4] {'fsdp'}, dimensions={0} | all-to-all | bytes 2097152 | tf_op jit(solution)/shard_map/all_to_all | solution.py:131
  664.5 4.8 all-to-all-start.15
  669.4 41.2 %all-to-all-done.15 = bf16[4,512,1024]{2,1,0:T(8,128)(2,1)} async-done(((bf16[4,512,1024]{2,1,0:T(8,128)(2,1)}), bf16[4,512,1024]{2,1,0:T(8,128)(2,1)}, u32[]{:S(2)}, u32[]{:S(2)}) %all-to-all-start.15) | async-done | bytes 4194336 | tf_op jit(solution)/shard_map/all_to_all | solution.py:131
  710.5 53.1 %all_to_all.158 = bf16[4,128,4096]{2,1,0:T(8,128)(2,1)} all-to-all(bf16[4,128,4096]{2,1,0:T(8,128)(2,1)} %bitcast.288), channel_id=1, replica_groups=mesh['zc'=4,'core'=2,'fsdp'=4] {'fsdp'}, dimensions={0} | all-to-all | bytes 8388608 | tf_op jit(solution)/shard_map/all_to_all | solution.py:131
  763.6 4.7 all-to-all-start.12
  770.5 4.4 reduce_sum.334
  776.3 4.2 reduce_sum.333
  782.9 19.7 %all-to-all-done.12 = bf16[4,128,3072]{2,1,0:T(8,128)(2,1)} async-done(((bf16[4,128,3072]{2,1,0:T(8,128)(2,1)}), bf16[4,128,3072]{2,1,0:T(8,128)(2,1)}, u32[]{:S(2)}, u32[]{:S(2)}) %all-to-all-start.12) | async-done | bytes 3145760 | tf_op jit(solution)/shard_map/all_to_all | solution.py:131
  802.6 3.5 reduce_sum.331
  811.6 69.5 %reduce-scatter.17.cloned.1.call-done = bf16[768,512]{1,0:T(8,128)(2,1)} async-done(((bf16[3072,512]{1,0:T(8,128)(2,1)}), bf16[768,512]{1,0:T(8,128)(2,1)}) %reduce-scatter.17.cloned.1.call-update) | async-done | bytes 786448 | tf_op jit(solution)/shard_map/reduce_scatter | solution.py:139
  881.2 64.9 %all-gather.31.cloned.1.call-done = bf16[3072,512]{1,0:T(8,128)(2,1)} async-done(((bf16[768,512]{1,0:T(8,128)(2,1)}), bf16[3072,512]{1,0:T(8,128)(2,1)}) %all-gather.31.cloned.1.call-update) | async-done | bytes 3145744 | tf_op jit(solution)/shard_map/all_gather | solution.py:140
  946.0 6.1 reshape.526
  952.8 8.0 all-gather.7
  964.1 9.2 fusion.78
  977.9 15.3 %all-reduce = bf16[4,3072]{1,0:T(4,128)(2,1)S(1)} all-reduce(bf16[4,3072]{1,0:T(4,128)(2,1)S(1)} %constant_dynamic-update-slice_fusion.7), channel_id=3, replica_groups=mesh['zc'=4,'core'=2,'fsdp'=4] {'fsdp'}, use_global_device_ids=true, to_apply=%region_34.35.clone | all-reduce | flops 12288 | bytes 49152
  993.9 13.9 %all-reduce.1 = bf16[3072]{0:T(1024)(128)(2,1)S(1)} all-reduce(bf16[3072]{0:T(1024)(128)(2,1)S(1)} %dynamic-slice_reduce_fusion), channel_id=4, replica_groups=mesh['zc'=4,'core'=2,'fsdp'=4] {'zc','core'}, use_global_device_ids=true, to_apply=%region_35.36.clone | all-reduce | flops 3072 | bytes 12288
  1007.9 12.7 %all-gather.8 = bf16[8,1,384]{2,1,0:T(2,128)(2,1)S(1)} all-gather(bf16[1,1,384]{2,1,0:T(2,128)(2,1)S(1)} %reshape.524), channel_id=1, replica_groups=mesh['zc'=4,'core'=2,'fsdp'=4] {'zc','core'}, dimensions={0}, use_global_device_ids=true | all-gather | bytes 6912 | tf_op jit(solution)/shard_map/all_gather | solution.py:341
  1023.3 20.9 %copy.196 = f32[2,1,1572864]{2,0,1:T(2,128)S(1)} copy(bf16[2,1,1572864]{2,1,0:T(2,128)(2,1)} %all-gather.33.cloned.1.call-done) | data formatting | bytes 18874368
  1045.5 3.8 fusion.97
  1049.3 4.4 reshape.502
  1056.8 7.8 reshape.504
  1064.6 7.9 reshape.505
  (673 shorter events, 250.2 us)
Async XLA Ops:
  7.2 118.0 %copy-start = (bf16[256,4096]{1,0:T(8,128)(2,1)S(1)}, bf16[256,4096]{1,0:T(8,128)(2,1)}, u32[]{:S(2)}) copy-start(bf16[256,4096]{1,0:T(8,128)(2,1)} %param.32) | copy-start | bytes 6291460
  7.2 60.7 %all-gather.19.cloned.1.call-start = ((), (), s32[]{:S(2)}) async-start(), calls=%async_computation.22 | async-start | bytes 9437184 | tf_op jit(solution)/shard_map/all_gather | solution.py:117
  50.7 8.1 copy-start.63
  50.7 15.9 %copy-start.13 = (bf16[4,1,2,32,1024]{4,3,2,1,0:T(8,128)(2,1)S(1)}, bf16[4,1,2,32,1024]{4,3,2,1,0:T(8,128)(2,1)}, u32[]{:S(2)}) copy-start(bf16[4,1,2,32,1024]{4,3,2,1,0:T(8,128)(2,1)} %param.20) | copy-start | bytes 1572868
  50.7 201.6 %all-gather.21.cloned.1.call-start = ((), (), s32[]{:S(2)}) async-start(), calls=%async_computation.23 | async-start | bytes 4718592 | tf_op jit(solution)/shard_map/all_gather | solution.py:236
  58.8 8.8 copy-start.50
  76.5 13.1 %copy-start.64 = (bf16[256]{0:T(256)(128)(2,1)S(1)}, bf16[256]{0:T(256)(128)(2,1)}, u32[]{:S(2)}) copy-start(bf16[256]{0:T(256)(128)(2,1)} %param.27) | copy-start | bytes 1540
  76.5 20.6 %copy-start.65 = (bf16[256]{0:T(256)(128)(2,1)S(1)}, bf16[256]{0:T(256)(128)(2,1)}, u32[]{:S(2)}) copy-start(bf16[256]{0:T(256)(128)(2,1)} %param.26) | copy-start | bytes 1540
  89.5 168.1 %all-gather.23.cloned.1.call-start = ((), (), s32[]{:S(2)}) async-start(), calls=%async_computation.24 | async-start | bytes 4718592 | tf_op jit(solution)/shard_map/all_gather | solution.py:239
  109.2 10.6 copy-start.45
  120.9 13.7 %all-to-all-start.5 = ((bf16[4,128,1024]{2,1,0:T(8,128)(2,1)}), bf16[4,128,1024]{2,1,0:T(8,128)(2,1)}, u32[]{:S(2)}, u32[]{:S(2)}) async-start(bf16[4,128,1024]{2,1,0:T(8,128)(2,1)} %broadcast_in_dim.66), calls=%async_computation.5 | async-start | bytes 2097152 | tf_op jit(solution)/shard_map/all_to_all | solution.py:110
  138.4 45.7 %all-to-all-start.6 = ((bf16[4,128,4096]{2,1,0:T(8,128)(2,1)}), bf16[4,128,4096]{2,1,0:T(8,128)(2,1)}, u32[]{:S(2)}, u32[]{:S(2)}) async-start(bf16[4,128,4096]{2,1,0:T(8,128)(2,1)} %broadcast_in_dim.67), calls=%async_computation.6 | async-start | bytes 8388608 | tf_op jit(solution)/shard_map/all_to_all | solution.py:110
  143.3 200.3 %all-gather.25.cloned.1.call-start = ((), (), s32[]{:S(2)}) async-start(), calls=%async_computation.25 | async-start | bytes 3145728 | tf_op jit(solution)/shard_map/all_gather | solution.py:117
  143.9 202.7 %all-gather.27.cloned.1.call-start = ((), (), s32[]{:S(2)}) async-start(), calls=%async_computation.26 | async-start | bytes 12582912 | tf_op jit(solution)/shard_map/all_gather | solution.py:117
  188.4 5.2 copy-start.57
  188.5 5.5 copy-start.39
  188.5 52.0 %all-to-all-start.7 = ((bf16[4,512,1024]{2,1,0:T(8,128)(2,1)}), bf16[4,512,1024]{2,1,0:T(8,128)(2,1)}, u32[]{:S(2)}, u32[]{:S(2)}) async-start(bf16[4,512,1024]{2,1,0:T(8,128)(2,1)} %broadcast_in_dim.68), calls=%async_computation.7 | async-start | bytes 8388608 | tf_op jit(solution)/shard_map/all_to_all | solution.py:110
  240.5 11.0 %all-to-all-start.1 = ((bf16[4,2,32,4,256]{4,2,1,0,3:T(8,128)(2,1)}), bf16[4,2,32,4,256]{4,2,1,0,3:T(8,128)(2,1)S(1)}, u32[]{:S(2)}, u32[]{:S(2)}) async-start(bf16[4,2,32,4,256]{4,2,1,0,3:T(8,128)(2,1)} %copy.115), calls=%async_computation.1 | async-start | bytes 1048576 | tf_op jit(solution)/shard_map/all_to_all | solution.py:228
  244.0 112.2 %all-gather.29.cloned.1.call-start = ((), (), s32[]{:S(2)}) async-start(), calls=%async_computation.27 | async-start | bytes 12582912 | tf_op jit(solution)/shard_map/all_gather | solution.py:117
  305.1 4.9 copy-start.66
  305.1 13.6 %copy-start.58 = (bf16[1024]{0:T(1024)(128)(2,1)S(1)}, bf16[1024]{0:T(1024)(128)(2,1)}, u32[]{:S(2)}) copy-start(bf16[1024]{0:T(1024)(128)(2,1)} %param.33) | copy-start | bytes 6148
  305.1 21.7 %copy-start.67 = (bf16[256]{0:T(256)(128)(2,1)S(1)}, bf16[256]{0:T(256)(128)(2,1)}, u32[]{:S(2)}) copy-start(bf16[256]{0:T(256)(128)(2,1)} %param.31) | copy-start | bytes 1540
  305.1 29.7 %copy-start.68 = (bf16[256]{0:T(256)(128)(2,1)S(1)}, bf16[256]{0:T(256)(128)(2,1)}, u32[]{:S(2)}) copy-start(bf16[256]{0:T(256)(128)(2,1)} %param.30) | copy-start | bytes 1540
  306.4 35.7 %all-to-all-start.4 = ((bf16[4,2,128,1,256]{4,1,0,3,2:T(2,128)(2,1)}), bf16[4,2,128,1,256]{4,1,0,3,2:T(2,128)(2,1)S(1)}, u32[]{:S(2)}, u32[]{:S(2)}) async-start(bf16[4,2,128,1,256]{4,1,0,3,2:T(2,128)(2,1)} %copy.124), calls=%async_computation.4 | async-start | bytes 1048576 | tf_op jit(solution)/shard_map/all_to_all | solution.py:248
  346.0 25.4 %copy-start.15 = (f32[256,1024]{1,0:T(8,128)}, f32[256,1024]{1,0:T(8,128)S(1)}, u32[]{:S(2)}) copy-start(f32[256,1024]{1,0:T(8,128)S(1)} %get-tuple-element.293) | copy-start | bytes 3145732
  346.6 9.6 copy-start.30
  346.6 9.6 copy-start.19
  356.2 12.1 %copy-start.61 = (bf16[4,256,4096]{2,1,0:T(8,128)(2,1)S(1)}, bf16[4,256,4096]{2,1,0:T(8,128)(2,1)}, u32[]{:S(2)}) copy-start(bf16[4,256,4096]{2,1,0:T(8,128)(2,1)} %all-gather.27.cloned.1.call-done) | copy-start | bytes 25165828
  376.5 10.0 all-to-all-start.8
  380.0 230.6 %reduce-scatter.7.cloned.1.call-start = ((), (), s32[]{:S(2)}) async-start(), calls=%async_computation.28 | async-start | bytes 9437184 | tf_op jit(solution)/shard_map/reduce_scatter | solution.py:285
  387.4 4.1 copy-start.43
  416.9 4.0 copy-start.43
  446.3 4.0 copy-start.43
  475.7 4.1 copy-start.43
  520.4 130.6 %reduce-scatter.11.cloned.1.call-start = ((), (), s32[]{:S(2)}) async-start(), calls=%async_computation.30 | async-start | bytes 3145728 | tf_op jit(solution)/shard_map/reduce_scatter | solution.py:129
  524.1 140.4 %reduce-scatter.15.cloned.1.call-start = ((), (), s32[]{:S(2)}) async-start(), calls=%async_computation.32 | async-start | bytes 12582912 | tf_op jit(solution)/shard_map/reduce_scatter | solution.py:129
  526.9 4.8 copy-start.20
  537.4 132.0 %reduce-scatter.13.cloned.1.call-start = ((), (), s32[]{:S(2)}) async-start(), calls=%async_computation.31 | async-start | bytes 12582912 | tf_op jit(solution)/shard_map/reduce_scatter | solution.py:129
  547.3 65.9 %all-to-all-start.9 = ((bf16[4,2,128,1,256]{4,1,0,3,2:T(2,128)(2,1)}), bf16[4,2,128,1,256]{4,1,0,3,2:T(2,128)(2,1)S(1)}, u32[]{:S(2)}, u32[]{:S(2)}) async-start(bf16[4,2,128,1,256]{4,1,0,3,2:T(2,128)(2,1)} %copy.130), calls=%async_computation.9 | async-start | bytes 1048576 | tf_op jit(solution)/shard_map/all_to_all | solution.py:296
  611.8 16.0 %copy-start.49 = (f32[4,2,32]{2,1,0:T(2,128)S(1)}, f32[4,2,32]{2,1,0:T(2,128)}, u32[]{:S(2)}) copy-start(f32[4,2,32]{2,1,0:T(2,128)} %copy-done.48) | copy-start | bytes 3076
  611.8 16.1 %copy-start.14 = (bf16[4,1,2,32,1024]{4,3,2,1,0:T(8,128)(2,1)S(1)}, bf16[4,1,2,32,1024]{4,3,2,1,0:T(8,128)(2,1)}, u32[]{:S(2)}) copy-start(bf16[4,1,2,32,1024]{4,3,2,1,0:T(8,128)(2,1)} %param.20) | copy-start | bytes 1572868
  613.2 10.2 all-to-all-start.10
  616.9 12.1 %copy-start.52 = (f32[4,2,32]{2,1,0:T(2,128)S(1)}, f32[4,2,32]{2,1,0:T(2,128)}, u32[]{:S(2)}) copy-start(f32[4,2,32]{2,1,0:T(2,128)} %get-tuple-element.288) | copy-start | bytes 3076
  623.4 4.4 copy-start.34
  623.4 10.8 all-to-all-start.11
  627.6 136.0 %reduce-scatter.9.cloned.1.call-start = ((), (), s32[]{:S(2)}) async-start(), calls=%async_computation.29 | async-start | bytes 9437184 | tf_op jit(solution)/shard_map/reduce_scatter | solution.py:129
  636.3 7.1 copy-start.51
  664.5 46.1 %all-to-all-start.15 = ((bf16[4,512,1024]{2,1,0:T(8,128)(2,1)}), bf16[4,512,1024]{2,1,0:T(8,128)(2,1)}, u32[]{:S(2)}, u32[]{:S(2)}) async-start(bf16[4,512,1024]{2,1,0:T(8,128)(2,1)} %bitcast.287), calls=%async_computation.20 | async-start | bytes 8388608 | tf_op jit(solution)/shard_map/all_to_all | solution.py:131
  763.6 39.0 %all-to-all-start.12 = ((bf16[4,128,3072]{2,1,0:T(8,128)(2,1)}), bf16[4,128,3072]{2,1,0:T(8,128)(2,1)}, u32[]{:S(2)}, u32[]{:S(2)}) async-start(bf16[4,128,3072]{2,1,0:T(8,128)(2,1)} %bitcast.292), calls=%async_computation.14 | async-start | bytes 6291456 | tf_op jit(solution)/shard_map/all_to_all | solution.py:131
  768.3 112.8 %reduce-scatter.17.cloned.1.call-start = ((), (), s32[]{:S(2)}) async-start(), calls=%async_computation.33 | async-start | bytes 3932160 | tf_op jit(solution)/shard_map/reduce_scatter | solution.py:139
  811.5 134.5 %all-gather.31.cloned.1.call-start = ((), (), s32[]{:S(2)}) async-start(), calls=%async_computation.34 | async-start | bytes 3932160 | tf_op jit(solution)/shard_map/all_gather | solution.py:140
  881.1 142.2 %all-gather.33.cloned.1.call-start = ((), (), s32[]{:S(2)}) async-start(), calls=%async_computation.35 | async-start | bytes 18874368 | tf_op jit(solution)/shard_map/all_gather | solution.py:141
  952.1 10.0 copy-start.71
  952.1 10.6 copy-start.70
  952.1 11.9 %copy-start.55 = (bf16[1024]{0:T(1024)(128)(2,1)S(1)}, bf16[1024]{0:T(1024)(128)(2,1)}, u32[]{:S(2)}) copy-start(bf16[1024]{0:T(1024)(128)(2,1)} %get-tuple-element.244) | copy-start | bytes 6148
  952.1 11.9 %copy-start.60 = (bf16[1024]{0:T(1024)(128)(2,1)S(1)}, bf16[1024]{0:T(1024)(128)(2,1)}, u32[]{:S(2)}) copy-start(bf16[1024]{0:T(1024)(128)(2,1)} %get-tuple-element.199) | copy-start | bytes 6148
  952.1 11.9 %copy-start.59 = (bf16[1024]{0:T(1024)(128)(2,1)S(1)}, bf16[1024]{0:T(1024)(128)(2,1)}, u32[]{:S(2)}) copy-start(bf16[1024]{0:T(1024)(128)(2,1)} %get-tuple-element.203) | copy-start | bytes 6148
  952.1 11.9 %copy-start.56 = (bf16[4096]{0:T(1024)(128)(2,1)S(1)}, bf16[4096]{0:T(1024)(128)(2,1)}, u32[]{:S(2)}) copy-start(bf16[4096]{0:T(1024)(128)(2,1)} %get-tuple-element.298) | copy-start | bytes 24580
  952.1 11.9 %copy-start.16 = (f32[256,1024]{1,0:T(8,128)S(1)}, f32[256,1024]{1,0:T(8,128)}, u32[]{:S(2)}) copy-start(f32[256,1024]{1,0:T(8,128)} %copy-done.15) | copy-start | bytes 3145732
  975.2 46.6 %copy-start.18 = (f32[256,1024]{1,0:T(8,128)S(1)}, f32[256,1024]{1,0:T(8,128)}, u32[]{:S(2)}) copy-start(f32[256,1024]{1,0:T(8,128)} %copy-done.17) | copy-start | bytes 3145732
  975.2 46.6 %copy-start.21 = (bf16[4,1,2,32,1024]{4,3,2,1,0:T(8,128)(2,1)S(1)}, bf16[4,1,2,32,1024]{4,3,2,1,0:T(8,128)(2,1)}, u32[]{:S(2)}) copy-start(bf16[4,1,2,32,1024]{4,3,2,1,0:T(8,128)(2,1)} %param.21) | copy-start | bytes 1572868
  975.3 46.6 %copy-start.25 = (f32[256,1024]{1,0:T(8,128)S(1)}, f32[256,1024]{1,0:T(8,128)}, u32[]{:S(2)}) copy-start(f32[256,1024]{1,0:T(8,128)} %get-tuple-element.297) | copy-start | bytes 3145732
  975.3 46.6 %copy-start.54 = (f32[256]{0:T(256)S(1)}, f32[256]{0:T(256)}, u32[]{:S(2)}) copy-start(f32[256]{0:T(256)} %copy-done.53) | copy-start | bytes 3076
  1064.6 7.9 copy-start.1
  (78 other events, 132.9 us)
Sparse Core Ops, SparseCore 0:
  50.8 16.4 all-gather.18
  89.7 46.2 all-gather.20
  138.2 45.6 all-gather.22
  185.3 9.3 all-gather.24
  196.1 21.0 all-gather.26
  246.0 21.6 all-gather.28
  520.5 90.0 reduce-scatter.6
  613.4 8.2 reduce-scatter.10
  623.9 17.6 reduce-scatter.14
  643.8 17.6 reduce-scatter.12
  663.8 15.3 reduce-scatter.8
  811.6 69.4 reduce-scatter.16
  882.6 63.3 all-gather.30
  952.3 23.3 all-gather.32

commit v8 on v6

--- a/solution.py
+++ b/solution.py
@@ -169,18 +169,25 @@
         gather_weight(out_weight),
         gather_weight(fc_weight),
         gather_weight(proj_weight),
-        lax.all_gather(attn_gain, "fsdp", axis=0, tiled=True),
-        lax.all_gather(attn_shift, "fsdp", axis=0, tiled=True),
-        lax.all_gather(query_bias, "fsdp", axis=0, tiled=True),
-        lax.all_gather(value_bias, "fsdp", axis=0, tiled=True),
-        lax.all_gather(out_bias, "fsdp", axis=0, tiled=True),
-        lax.all_gather(mlp_gain, "fsdp", axis=0, tiled=True),
-        lax.all_gather(mlp_shift, "fsdp", axis=0, tiled=True),
-        lax.all_gather(fc_bias, "fsdp", axis=0, tiled=True),
-        lax.all_gather(proj_bias, "fsdp", axis=0, tiled=True),
     )
     qkv_full, out_full, fc_full, proj_full = (gathered[0], gathered[1], gathered[2], gathered[3])
-    vectors = [piece.astype(jnp.float32) for piece in gathered[4:]]
+    vector_shards = (
+        attn_gain,
+        attn_shift,
+        query_bias,
+        value_bias,
+        out_bias,
+        mlp_gain,
+        mlp_shift,
+        fc_bias,
+        proj_bias,
+    )
+    vector_pieces = lax.all_gather(jnp.concatenate(vector_shards), "fsdp", axis=0, tiled=False)
+    vectors = []
+    start = 0
+    for shard in vector_shards:
+        vectors.append(vector_pieces[:, start : start + shard.shape[0]].reshape(-1).astype(jnp.float32))
+        start += shard.shape[0]
     (
         gain_attn,
         shift_attn,

time: 934 us -> 903 us (0.967)
  blocking collectives: 320 us -> 264 us
  waiting for transfers between devices: 199 us -> 220 us
    all_gather x9 -> x1, blocking collectives: 70.5 us -> 7.58 us  [shards(): lax.all_gather(jnp.concatenate(vector_shards), 'fsdp', axis=0, tiled=False)]
  transfers between devices with their start and end apart: 30 -> 30, of which waited for: 13 -> 15; matrix products, arithmetic and copies ran while one was open for 31% -> 32% of each run, Pallas kernels for 0% -> 0%
where the time goes in v8:
time: 903 us; the launch traced here: 893 us
  blocking collectives  264 us (29%)
  waiting for transfers between devices  220 us (24%)
  local copies, waits for them, and re-layouts  153 us (17%)
  matrix products  132 us (15%)
  other arithmetic  63.6 us (7%)
  starting transfers between devices  42.3 us (5%)
  between operations  16.6 us (2%)
    all_to_all x3, blocking collectives, reduce_weight_grad(): lax.all_to_all(grad.reshape((fsdp_size, -1) + grad.shape[1:]), 'fsdp', sp...  113 us
    all_to_all x3, waiting for transfers between devices, gather_weight(): lax.all_to_all(jnp.broadcast_to(piece[None], (fsdp_size,) + piece.shape),...  102 us
    dot_general x52, matrix products, contract_last(): lax.dot_general(left, right, (((1,), (1,)), ((), ())), preferred_element_...  52.4 us
    all_to_all x1, blocking collectives, gather_weight(): lax.all_to_all(jnp.broadcast_to(piece[None], (fsdp_size,) + piece.shape),...  41.7 us
    dot_general x36, matrix products, contract_first(): lax.dot_general(left, right, (((0,), (0,)), ((), ())), preferred_element_...  36 us
    all_gather x2, waiting for transfers between devices, reduce_weight_grad(): grad = lax.all_gather(grad, 'zc', axis=0, tiled=True)  35.8 us
    all_gather x2, blocking collectives, reduce_weight_grad(): grad = lax.all_gather(grad, 'zc', axis=0, tiled=True)  33.7 us
    unnamed x2, blocking collectives  30.1 us
  transfers between devices with their start and end apart: 30, of which 15 were waited for; matrix products, arithmetic and copies ran while one was open for 32% of the time, Pallas kernels for 0%

profile of v8, /device:TPU:0, one launch (start us, length us, event | category | flops | bytes accessed | tf_op | source)
XLA Modules:
  0.0 892.8 jit_solution(979832411230011779)
XLA Ops:
  9.0 41.7 %all_to_all.154 = bf16[4,128,3072]{2,1,0:T(8,128)(2,1)} all-to-all(bf16[4,128,3072]{2,1,0:T(8,128)(2,1)S(1)} %broadcast_in_dim.65), channel_id=1, replica_groups=mesh['zc'=4,'core'=2,'fsdp'=4] {'fsdp'}, dimensions={0} | all-to-all | bytes 6291456 | tf_op jit(solution)/shard_map/all_to_all | solution.py:110
  53.2 7.6 all-gather
  62.8 4.6 all-gather.14.cloned.1.call-done
  67.4 4.6 fusion.103
  76.1 12.7 %all_to_all.155 = bf16[4,2,32,4,256]{4,2,1,0,3:T(8,128)(2,1)S(1)} all-to-all(bf16[4,2,32,4,256]{4,2,1,0,3:T(8,128)(2,1)S(1)} %copy.111), channel_id=1, replica_groups=mesh['zc'=4,'core'=2,'fsdp'=4] {'fsdp'}, dimensions={3} | all-to-all | bytes 1048576 | tf_op jit(solution)/shard_map/all_to_all | solution.py:226
  89.7 2.8 fusion.79
  94.0 10.3 %all_to_all.156 = bf16[4,2,32,4,256]{4,2,1,0,3:T(8,128)(2,1)S(1)} all-to-all(bf16[4,2,32,4,256]{4,2,1,0,3:T(8,128)(2,1)S(1)} %copy.114), channel_id=1, replica_groups=mesh['zc'=4,'core'=2,'fsdp'=4] {'fsdp'}, dimensions={3} | all-to-all | bytes 1048576 | tf_op jit(solution)/shard_map/all_to_all | solution.py:227
  106.3 4.3 all-to-all-start.5
  111.7 10.8 %all-to-all-done.5 = bf16[4,128,1024]{2,1,0:T(8,128)(2,1)} async-done(((bf16[4,128,1024]{2,1,0:T(8,128)(2,1)}), bf16[4,128,1024]{2,1,0:T(8,128)(2,1)}, u32[]{:S(2)}, u32[]{:S(2)}) %all-to-all-start.5) | async-done | bytes 1048608 | tf_op jit(solution)/shard_map/all_to_all | solution.py:110
  122.5 3.8 broadcast_in_dim.67
  126.2 4.9 all-to-all-start.6
  131.7 46.3 %all-to-all-done.6 = bf16[4,128,4096]{2,1,0:T(8,128)(2,1)} async-done(((bf16[4,128,4096]{2,1,0:T(8,128)(2,1)}), bf16[4,128,4096]{2,1,0:T(8,128)(2,1)}, u32[]{:S(2)}, u32[]{:S(2)}) %all-to-all-start.6) | async-done | bytes 4194336 | tf_op jit(solution)/shard_map/all_to_all | solution.py:110
  179.7 2.6 broadcast_in_dim.68
  182.3 5.0 all-to-all-start.7
  189.0 45.2 %all-to-all-done.7 = bf16[4,512,1024]{2,1,0:T(8,128)(2,1)} async-done(((bf16[4,512,1024]{2,1,0:T(8,128)(2,1)}), bf16[4,512,1024]{2,1,0:T(8,128)(2,1)}, u32[]{:S(2)}, u32[]{:S(2)}) %all-to-all-start.7) | async-done | bytes 4194336 | tf_op jit(solution)/shard_map/all_to_all | solution.py:110
  234.2 3.5 all-to-all-start.1
  238.3 6.9 all-to-all-done.1
  246.0 5.6 copy.113
  251.6 5.7 copy.116
  257.3 41.4 %while.26 = (s32[]{:T(128)}, bf16[4,256,256]{2,1,0:T(8,128)(2,1)S(1)}, f32[4,256,4]{1,2,0:T(4,128)}, s32[4,2048]{1,0:T(4,128)S(1)}, s32[4,256]{1,0:T(4,128)S(1)}...) while((s32[]{:T(128)}, ...), condition=%wide.region_11.12_spmd, body=%wide.region_2.11_spmd.sunk | while | flops 554240000 | bytes 35092604 | solution.py:242
  300.0 3.7 all-to-all-start.4
  303.9 6.3 all-to-all-done.4
  315.1 9.5 %multiply_convert_fusion.4 = (bf16[256,4096]{1,0:T(8,128)(2,1)}, f32[256,4096]{1,0:T(8,128)}) fusion(f32[4096]{0:T(1024)S(1)} %bitcast.365, bf16[256,1024]{1,0:T(8,128)(2,1)S(1)} %add_convert_fusion.1, bf16[1024,4096]{1,0:T(8,128)(2,1)} %bitcast.370), kind=kOutput, calls=%fused_computation.141 | convolution fusion | flops 2157969408 | bytes 15220736 | tf_op jit(solution)/shard_map/dot_general | solution.py:252
  324.6 12.5 %fusion.102 = (bf16[4096]{0:T(1024)(128)(2,1)}, bf16[256,4096]{1,0:T(8,128)(2,1)S(1)}) fusion(f32[256,4096]{1,0:T(8,128)} %get-tuple-element.303, bf16[4096,1024]{1,0:T(8,128)(2,1)} %bitcast.368, bf16[256,1024]{1,0:T(8,128)(2,1)S(1)} %bitcast.288), kind=kOutput, calls=%fused_computation.233 | convolution fusion | flops 2169499648 | bytes 15212544 | tf_op jit(solution)/shard_map/dot_general | solution.py:29
  337.1 3.2 multiply_reduce_fusion.4
  345.3 3.5 all-to-all-start.8
  349.4 7.2 convolution_convert_fusion.9
  357.5 118.0 %while.27 = (s32[]{:T(128)}, bf16[4,256,256]{2,1,0:T(8,128)(2,1)}, bf16[4,2048,256]{2,1,0:T(8,128)(2,1)}, bf16[4,2048,256]{2,1,0:T(8,128)(2,1)}, s32[4,2048]{1,0...) while((s32[]{:T(128)}, bf16[4,256,256]{2,1,0:T(8,128)(2,1)}, ...), condition=%wide.region_21.22_spmd, body=%wide.region_16.21_spmd.sunk | while | flops 1370029056 | bytes 166414960 | solution.py:276
  380.3 2.4 constant_dynamic-update-slice_fusion.22
  468.6 2.5 constant_dynamic-update-slice_fusion.22
  475.6 7.6 maximum_bitcast_fusion.5
  483.1 7.5 copy.129
  492.2 2.9 reshape.542
  495.2 4.8 copy.140
  500.0 5.6 convolution_convert_fusion.8
  505.7 50.3 %all_to_all.158 = bf16[4,128,4096]{2,1,0:T(8,128)(2,1)} all-to-all(bf16[4,128,4096]{2,1,0:T(8,128)(2,1)} %bitcast.300), channel_id=1, replica_groups=mesh['zc'=4,'core'=2,'fsdp'=4] {'fsdp'}, dimensions={0} | all-to-all | bytes 8388608 | tf_op jit(solution)/shard_map/all_to_all | solution.py:131
  556.1 4.3 reduce_sum.333
  564.8 3.5 all-to-all-start.9
  568.3 13.5 %reduce-scatter.10.cloned.1.call-done = bf16[1024,512]{1,0:T(8,128)(2,1)} async-done(((bf16[8192,512]{1,0:T(8,128)(2,1)}), bf16[1024,512]{1,0:T(8,128)(2,1)}) %reduce-scatter.10.cloned.1.call-update) | async-done | bytes 1048592 | tf_op jit(solution)/shard_map/reduce_scatter | solution.py:282
  584.5 3.6 all-to-all-start.10
  589.5 5.2 all-to-all-done.10
  594.7 4.2 all-to-all-start.11
  602.9 2.6 all-to-all-done.11
  607.4 5.8 fusion.90
  616.4 4.5 convolution_convert_fusion.10
  621.0 49.4 %all_to_all.159 = bf16[4,512,1024]{2,1,0:T(8,128)(2,1)} all-to-all(bf16[4,512,1024]{2,1,0:T(8,128)(2,1)} %bitcast.301), channel_id=1, replica_groups=mesh['zc'=4,'core'=2,'fsdp'=4] {'fsdp'}, dimensions={0} | all-to-all | bytes 8388608 | tf_op jit(solution)/shard_map/all_to_all | solution.py:131
  670.4 4.4 reduce_sum.334
  675.4 13.4 %all_to_all.157 = bf16[4,128,1024]{2,1,0:T(8,128)(2,1)S(1)} all-to-all(bf16[4,128,1024]{2,1,0:T(8,128)(2,1)} %bitcast.331), channel_id=1, replica_groups=mesh['zc'=4,'core'=2,'fsdp'=4] {'fsdp'}, dimensions={0} | all-to-all | bytes 2097152 | tf_op jit(solution)/shard_map/all_to_all | solution.py:131
  688.9 4.7 all-to-all-start.12
  693.6 12.3 %reduce-scatter.26.cloned.1.call-done = bf16[128,1024]{1,0:T(8,128)(2,1)} async-done(((bf16[512,1024]{1,0:T(8,128)(2,1)}), bf16[128,1024]{1,0:T(8,128)(2,1)}) %reduce-scatter.26.cloned.1.call-update) | async-done | bytes 262160 | tf_op jit(solution)/shard_map/reduce_scatter | solution.py:135
  707.0 16.1 %all-to-all-done.12 = bf16[4,128,3072]{2,1,0:T(8,128)(2,1)} async-done(((bf16[4,128,3072]{2,1,0:T(8,128)(2,1)}), bf16[4,128,3072]{2,1,0:T(8,128)(2,1)}, u32[]{:S(2)}, u32[]{:S(2)}) %all-to-all-start.12) | async-done | bytes 3145760 | tf_op jit(solution)/shard_map/all_to_all | solution.py:131
  723.1 3.6 reduce_sum.331
  726.8 7.1 all-gather.28.cloned.1.call-done
  733.9 28.7 %all-gather.32.cloned.1.call-done = bf16[512,1024]{1,0:T(8,128)(2,1)} async-done(((bf16[128,1024]{1,0:T(8,128)(2,1)}), bf16[512,1024]{1,0:T(8,128)(2,1)}) %all-gather.32.cloned.1.call-update) | async-done | bytes 1048592 | tf_op jit(solution)/shard_map/all_gather | solution.py:136
  766.2 7.2 fusion.78
  773.3 10.9 %reduce-scatter.18.cloned.1.call-done = bf16[32,1024]{1,0:T(8,128)(2,1)} async-done(((bf16[128,1024]{1,0:T(8,128)(2,1)}), bf16[32,1024]{1,0:T(8,128)(2,1)}) %reduce-scatter.18.cloned.1.call-update) | async-done | bytes 65552 | tf_op jit(solution)/shard_map/reduce_scatter | solution.py:135
  784.2 15.5 %all_gather.62 = bf16[128,1024]{1,0:T(8,128)(2,1)S(1)} all-gather(bf16[32,1024]{1,0:T(8,128)(2,1)} %reduce-scatter.18.cloned.1.call-done), channel_id=1, replica_groups=mesh['zc'=4,'core'=2,'fsdp'=4] {'zc'}, dimensions={0}, use_global_device_ids=true | all-gather | bytes 327680 | tf_op jit(solution)/shard_map/all_gather | solution.py:136
  809.0 18.2 %all_gather.60 = bf16[128,3072]{1,0:T(8,128)(2,1)} all-gather(bf16[32,3072]{1,0:T(8,128)(2,1)} %reduce-scatter.14.cloned.1.call-done), channel_id=1, replica_groups=mesh['zc'=4,'core'=2,'fsdp'=4] {'zc'}, dimensions={0}, use_global_device_ids=true | all-gather | bytes 983040 | tf_op jit(solution)/shard_map/all_gather | solution.py:136
  827.3 16.3 %all-reduce = bf16[4,3072]{1,0:T(4,128)(2,1)S(1)} all-reduce(bf16[4,3072]{1,0:T(4,128)(2,1)S(1)} %constant_dynamic-update-slice_fusion.7), channel_id=4, replica_groups=mesh['zc'=4,'core'=2,'fsdp'=4] {'fsdp'}, use_global_device_ids=true, to_apply=%region_34.35.clone | all-reduce | flops 12288 | bytes 49152
  844.3 13.8 %all-reduce.1 = bf16[3072]{0:T(1024)(128)(2,1)S(1)} all-reduce(bf16[3072]{0:T(1024)(128)(2,1)S(1)} %dynamic-slice_reduce_fusion), channel_id=5, replica_groups=mesh['zc'=4,'core'=2,'fsdp'=4] {'zc','core'}, use_global_device_ids=true, to_apply=%region_35.36.clone | all-reduce | flops 3072 | bytes 12288
  858.3 12.7 %all-gather.1 = bf16[8,1,384]{2,1,0:T(2,128)(2,1)S(1)} all-gather(bf16[1,1,384]{2,1,0:T(2,128)(2,1)S(1)} %reshape.559), channel_id=1, replica_groups=mesh['zc'=4,'core'=2,'fsdp'=4] {'zc','core'}, dimensions={0}, use_global_device_ids=true | all-gather | bytes 6912 | tf_op jit(solution)/shard_map/all_gather | solution.py:338
  873.7 4.1 convert_element_type.365
  877.8 4.2 convert_element_type.367
  882.0 3.4 convert_element_type.361
  (678 shorter events, 222.7 us)
Async XLA Ops:
  7.2 103.4 %copy-start = (bf16[256,4096]{1,0:T(8,128)(2,1)S(1)}, bf16[256,4096]{1,0:T(8,128)(2,1)}, u32[]{:S(2)}) copy-start(bf16[256,4096]{1,0:T(8,128)(2,1)} %param.32) | copy-start | bytes 6291460
  7.2 60.2 %all-gather.14.cloned.1.call-start = ((), (), s32[]{:S(2)}) async-start(), calls=%async_computation.25 | async-start | bytes 9437184 | tf_op jit(solution)/shard_map/all_gather | solution.py:117
  50.7 10.7 %copy-start.13 = (bf16[4,1,2,32,1024]{4,3,2,1,0:T(8,128)(2,1)S(1)}, bf16[4,1,2,32,1024]{4,3,2,1,0:T(8,128)(2,1)}, u32[]{:S(2)}) copy-start(bf16[4,1,2,32,1024]{4,3,2,1,0:T(8,128)(2,1)} %param.20) | copy-start | bytes 1572868
  50.8 195.3 %all-gather.16.cloned.1.call-start = ((), (), s32[]{:S(2)}) async-start(), calls=%async_computation.26 | async-start | bytes 4718592 | tf_op jit(solution)/shard_map/all_gather | solution.py:233
  89.7 161.9 %all-gather.18.cloned.1.call-start = ((), (), s32[]{:S(2)}) async-start(), calls=%async_computation.27 | async-start | bytes 4718592 | tf_op jit(solution)/shard_map/all_gather | solution.py:236
  94.0 11.2 %copy-start.42 = (bf16[256,1024]{1,0:T(8,128)(2,1)S(1)}, bf16[256,1024]{1,0:T(8,128)(2,1)}, u32[]{:S(2)}) copy-start(bf16[256,1024]{1,0:T(8,128)(2,1)} %param.28) | copy-start | bytes 1572868
  106.3 16.1 %all-to-all-start.5 = ((bf16[4,128,1024]{2,1,0:T(8,128)(2,1)}), bf16[4,128,1024]{2,1,0:T(8,128)(2,1)}, u32[]{:S(2)}, u32[]{:S(2)}) async-start(bf16[4,128,1024]{2,1,0:T(8,128)(2,1)} %broadcast_in_dim.66), calls=%async_computation.5 | async-start | bytes 2097152 | tf_op jit(solution)/shard_map/all_to_all | solution.py:110
  126.2 51.8 %all-to-all-start.6 = ((bf16[4,128,4096]{2,1,0:T(8,128)(2,1)}), bf16[4,128,4096]{2,1,0:T(8,128)(2,1)}, u32[]{:S(2)}, u32[]{:S(2)}) async-start(bf16[4,128,4096]{2,1,0:T(8,128)(2,1)} %broadcast_in_dim.67), calls=%async_computation.6 | async-start | bytes 8388608 | tf_op jit(solution)/shard_map/all_to_all | solution.py:110
  131.1 180.6 %all-gather.20.cloned.1.call-start = ((), (), s32[]{:S(2)}) async-start(), calls=%async_computation.28 | async-start | bytes 3145728 | tf_op jit(solution)/shard_map/all_gather | solution.py:117
  131.7 183.4 %all-gather.22.cloned.1.call-start = ((), (), s32[]{:S(2)}) async-start(), calls=%async_computation.29 | async-start | bytes 12582912 | tf_op jit(solution)/shard_map/all_gather | solution.py:117
  182.3 5.0 copy-start.55
  182.3 5.4 copy-start.37
  182.3 51.9 %all-to-all-start.7 = ((bf16[4,512,1024]{2,1,0:T(8,128)(2,1)}), bf16[4,512,1024]{2,1,0:T(8,128)(2,1)}, u32[]{:S(2)}, u32[]{:S(2)}) async-start(bf16[4,512,1024]{2,1,0:T(8,128)(2,1)} %broadcast_in_dim.68), calls=%async_computation.7 | async-start | bytes 8388608 | tf_op jit(solution)/shard_map/all_to_all | solution.py:110
  234.2 11.0 %all-to-all-start.1 = ((bf16[4,2,32,4,256]{4,2,1,0,3:T(8,128)(2,1)}), bf16[4,2,32,4,256]{4,2,1,0,3:T(8,128)(2,1)S(1)}, u32[]{:S(2)}, u32[]{:S(2)}) async-start(bf16[4,2,32,4,256]{4,2,1,0,3:T(8,128)(2,1)} %copy.109), calls=%async_computation.1 | async-start | bytes 1048576 | tf_op jit(solution)/shard_map/all_to_all | solution.py:225
  237.7 86.9 %all-gather.24.cloned.1.call-start = ((), (), s32[]{:S(2)}) async-start(), calls=%async_computation.30 | async-start | bytes 12582912 | tf_op jit(solution)/shard_map/all_gather | solution.py:117
  300.0 10.3 %all-to-all-start.4 = ((bf16[4,2,128,1,256]{4,1,0,3,2:T(2,128)(2,1)}), bf16[4,2,128,1,256]{4,1,0,3,2:T(2,128)(2,1)S(1)}, u32[]{:S(2)}, u32[]{:S(2)}) async-start(bf16[4,2,128,1,256]{4,1,0,3,2:T(2,128)(2,1)} %copy.118), calls=%async_computation.4 | async-start | bytes 1048576 | tf_op jit(solution)/shard_map/all_to_all | solution.py:245
  314.1 26.2 %copy-start.15 = (f32[256,1024]{1,0:T(8,128)}, f32[256,1024]{1,0:T(8,128)S(1)}, u32[]{:S(2)}) copy-start(f32[256,1024]{1,0:T(8,128)S(1)} %get-tuple-element.301) | copy-start | bytes 3145732
  315.1 9.5 %copy-start.19 = (bf16[4,1,2,32,1024]{4,3,2,1,0:T(8,128)(2,1)S(1)}, bf16[4,1,2,32,1024]{4,3,2,1,0:T(8,128)(2,1)}, u32[]{:S(2)}) copy-start(bf16[4,1,2,32,1024]{4,3,2,1,0:T(8,128)(2,1)} %param.21) | copy-start | bytes 1572868
  324.6 12.6 %copy-start.67 = (bf16[4,256,4096]{2,1,0:T(8,128)(2,1)S(1)}, bf16[4,256,4096]{2,1,0:T(8,128)(2,1)}, u32[]{:S(2)}) copy-start(bf16[4,256,4096]{2,1,0:T(8,128)(2,1)} %all-gather.22.cloned.1.call-done) | copy-start | bytes 25165828
  345.3 11.4 %all-to-all-start.8 = ((bf16[4,2,32,4,256]{4,2,1,0,3:T(8,128)(2,1)}), bf16[4,2,32,4,256]{4,2,1,0,3:T(8,128)(2,1)S(1)}, u32[]{:S(2)}, u32[]{:S(2)}) async-start(bf16[4,2,32,4,256]{4,2,1,0,3:T(8,128)(2,1)} %copy.121), calls=%async_computation.8 | async-start | bytes 1048576 | tf_op jit(solution)/shard_map/all_to_all | solution.py:273
  348.8 157.0 %reduce-scatter.20.cloned.1.call-start = ((), (), s32[]{:S(2)}) async-start(), calls=%async_computation.37 | async-start | bytes 12582912 | tf_op jit(solution)/shard_map/reduce_scatter | solution.py:129
  356.6 225.3 %reduce-scatter.10.cloned.1.call-start = ((), (), s32[]{:S(2)}) async-start(), calls=%async_computation.31 | async-start | bytes 9437184 | tf_op jit(solution)/shard_map/reduce_scatter | solution.py:282
  357.7 4.1 copy-start.40
  387.2 4.1 copy-start.40
  403.9 3.6 copy-start.10
  416.7 4.1 copy-start.40
  446.1 4.0 copy-start.40
  490.7 130.3 %reduce-scatter.24.cloned.1.call-start = ((), (), s32[]{:S(2)}) async-start(), calls=%async_computation.41 | async-start | bytes 12582912 | tf_op jit(solution)/shard_map/reduce_scatter | solution.py:129
  495.2 4.9 copy-start.20
  505.7 169.2 %reduce-scatter.22.cloned.1.call-start = ((), (), s32[]{:S(2)}) async-start(), calls=%async_computation.38 | async-start | bytes 1310720 | tf_op jit(solution)/shard_map/reduce_scatter | solution.py:135
  556.1 4.4 copy-start.23
  560.4 115.0 %reduce-scatter.16.cloned.1.call-start = ((), (), s32[]{:S(2)}) async-start(), calls=%async_computation.35 | async-start | bytes 3145728 | tf_op jit(solution)/shard_map/reduce_scatter | solution.py:129
  564.8 19.6 %all-to-all-start.9 = ((bf16[4,2,128,1,256]{4,1,0,3,2:T(2,128)(2,1)}), bf16[4,2,128,1,256]{4,1,0,3,2:T(2,128)(2,1)S(1)}, u32[]{:S(2)}, u32[]{:S(2)}) async-start(bf16[4,2,128,1,256]{4,1,0,3,2:T(2,128)(2,1)} %copy.124), calls=%async_computation.9 | async-start | bytes 1048576 | tf_op jit(solution)/shard_map/all_to_all | solution.py:293
  583.1 16.1 %copy-start.46 = (f32[4,2,32]{2,1,0:T(2,128)S(1)}, f32[4,2,32]{2,1,0:T(2,128)}, u32[]{:S(2)}) copy-start(f32[4,2,32]{2,1,0:T(2,128)} %copy-done.45) | copy-start | bytes 3076
  583.1 16.1 %copy-start.14 = (bf16[4,1,2,32,1024]{4,3,2,1,0:T(8,128)(2,1)S(1)}, bf16[4,1,2,32,1024]{4,3,2,1,0:T(8,128)(2,1)}, u32[]{:S(2)}) copy-start(bf16[4,1,2,32,1024]{4,3,2,1,0:T(8,128)(2,1)} %param.20) | copy-start | bytes 1572868
  584.5 10.2 %all-to-all-start.10 = ((bf16[4,2,128,1,256]{4,1,0,3,2:T(2,128)(2,1)}), bf16[4,2,128,1,256]{4,1,0,3,2:T(2,128)(2,1)S(1)}, u32[]{:S(2)}, u32[]{:S(2)}) async-start(bf16[4,2,128,1,256]{4,1,0,3,2:T(2,128)(2,1)} %copy.130), calls=%async_computation.11 | async-start | bytes 1048576 | tf_op jit(solution)/shard_map/all_to_all | solution.py:296
  588.1 12.2 %copy-start.50 = (f32[4,2,32]{2,1,0:T(2,128)S(1)}, f32[4,2,32]{2,1,0:T(2,128)}, u32[]{:S(2)}) copy-start(f32[4,2,32]{2,1,0:T(2,128)} %get-tuple-element.296) | copy-start | bytes 3076
  588.1 12.3 %copy-start.49 = (f32[4,256]{1,0:T(4,128)S(1)}, f32[4,256]{1,0:T(4,128)}, u32[]{:S(2)}) copy-start(f32[4,256]{1,0:T(4,128)} %get-tuple-element.287) | copy-start | bytes 12292
  588.1 12.3 %copy-start.48 = (f32[4,256]{1,0:T(4,128)S(1)}, f32[4,256]{1,0:T(4,128)}, u32[]{:S(2)}) copy-start(f32[4,256]{1,0:T(4,128)} %get-tuple-element.278) | copy-start | bytes 12292
  594.7 4.5 copy-start.32
  594.7 10.8 %all-to-all-start.11 = ((bf16[4,2,128,1,256]{4,1,0,3,2:T(2,128)(2,1)}), bf16[4,2,128,1,256]{4,1,0,3,2:T(2,128)(2,1)}, u32[]{:S(2)}, u32[]{:S(2)}) async-start(bf16[4,2,128,1,256]{4,1,0,3,2:T(2,128)(2,1)} %copy.133), calls=%async_computation.12 | async-start | bytes 1048576 | tf_op jit(solution)/shard_map/all_to_all | solution.py:299
  598.9 90.0 %reduce-scatter.12.cloned.1.call-start = ((), (), s32[]{:S(2)}) async-start(), calls=%async_computation.32 | async-start | bytes 9437184 | tf_op jit(solution)/shard_map/reduce_scatter | solution.py:129
  620.9 85.0 %reduce-scatter.26.cloned.1.call-start = ((), (), s32[]{:S(2)}) async-start(), calls=%async_computation.42 | async-start | bytes 1310720 | tf_op jit(solution)/shard_map/reduce_scatter | solution.py:135
  674.8 59.0 %all-gather.28.cloned.1.call-start = ((), (), s32[]{:S(2)}) async-start(), calls=%async_computation.39 | async-start | bytes 1310720 | tf_op jit(solution)/shard_map/all_gather | solution.py:136
  688.9 34.2 %all-to-all-start.12 = ((bf16[4,128,3072]{2,1,0:T(8,128)(2,1)}), bf16[4,128,3072]{2,1,0:T(8,128)(2,1)}, u32[]{:S(2)}, u32[]{:S(2)}) async-start(bf16[4,128,3072]{2,1,0:T(8,128)(2,1)} %bitcast.305), calls=%async_computation.14 | async-start | bytes 6291456 | tf_op jit(solution)/shard_map/all_to_all | solution.py:131
  693.5 69.1 %all-gather.32.cloned.1.call-start = ((), (), s32[]{:S(2)}) async-start(), calls=%async_computation.43 | async-start | bytes 1310720 | tf_op jit(solution)/shard_map/all_gather | solution.py:136
  705.9 78.3 %reduce-scatter.18.cloned.1.call-start = ((), (), s32[]{:S(2)}) async-start(), calls=%async_computation.36 | async-start | bytes 327680 | tf_op jit(solution)/shard_map/reduce_scatter | solution.py:135
  706.9 102.1 %reduce-scatter.14.cloned.1.call-start = ((), (), s32[]{:S(2)}) async-start(), calls=%async_computation.33 | async-start | bytes 983040 | tf_op jit(solution)/shard_map/reduce_scatter | solution.py:135
  726.6 36.4 %copy-start.47 = (f32[1,2,4,128]{3,2,1,0:T(4,128)S(1)}, f32[1,2,4,128]{3,2,1,0:T(4,128)}, u32[]{:S(2)}) copy-start(f32[1,2,4,128]{3,2,1,0:T(4,128)} %get-tuple-element.281) | copy-start | bytes 12292
  726.6 37.6 %copy-start.69 = (u32[32]{0:T(128)S(1)}, u32[32]{0:T(128)}, u32[]{:S(2)}) copy-start(u32[32]{0:T(128)} %constant.119) | copy-start | bytes 388
  726.7 38.2 %copy-start.68 = (u32[32]{0:T(128)S(1)}, u32[32]{0:T(128)}, u32[]{:S(2)}) copy-start(u32[32]{0:T(128)} %constant.123) | copy-start | bytes 388
  726.7 39.4 %copy-start.53 = (bf16[1024]{0:T(1024)(128)(2,1)S(1)}, bf16[1024]{0:T(1024)(128)(2,1)}, u32[]{:S(2)}) copy-start(bf16[1024]{0:T(1024)(128)(2,1)} %get-tuple-element.244) | copy-start | bytes 6148
  726.7 39.4 %copy-start.57 = (bf16[1024]{0:T(1024)(128)(2,1)S(1)}, bf16[1024]{0:T(1024)(128)(2,1)}, u32[]{:S(2)}) copy-start(bf16[1024]{0:T(1024)(128)(2,1)} %get-tuple-element.199) | copy-start | bytes 6148
  726.7 39.4 %copy-start.56 = (bf16[1024]{0:T(1024)(128)(2,1)S(1)}, bf16[1024]{0:T(1024)(128)(2,1)}, u32[]{:S(2)}) copy-start(bf16[1024]{0:T(1024)(128)(2,1)} %get-tuple-element.203) | copy-start | bytes 6148
  726.7 39.4 %copy-start.54 = (bf16[4096]{0:T(1024)(128)(2,1)S(1)}, bf16[4096]{0:T(1024)(128)(2,1)}, u32[]{:S(2)}) copy-start(bf16[4096]{0:T(1024)(128)(2,1)} %get-tuple-element.306) | copy-start | bytes 24580
  726.7 39.5 %copy-start.16 = (f32[256,1024]{1,0:T(8,128)S(1)}, f32[256,1024]{1,0:T(8,128)}, u32[]{:S(2)}) copy-start(f32[256,1024]{1,0:T(8,128)} %copy-done.15) | copy-start | bytes 3145732
  726.7 147.0 %all-gather.30.cloned.1.call-start = ((), (), s32[]{:S(2)}) async-start(), calls=%async_computation.40 | async-start | bytes 3145728 | tf_op jit(solution)/shard_map/all_gather | solution.py:137
  733.9 143.9 %all-gather.34.cloned.1.call-start = ((), (), s32[]{:S(2)}) async-start(), calls=%async_computation.44 | async-start | bytes 3145728 | tf_op jit(solution)/shard_map/all_gather | solution.py:137
  762.7 119.3 %all-gather.26.cloned.1.call-start = ((), (), s32[]{:S(2)}) async-start(), calls=%async_computation.34 | async-start | bytes 2359296 | tf_op jit(solution)/shard_map/all_gather | solution.py:137
  805.5 66.7 %copy-start.18 = (f32[256,1024]{1,0:T(8,128)S(1)}, f32[256,1024]{1,0:T(8,128)}, u32[]{:S(2)}) copy-start(f32[256,1024]{1,0:T(8,128)} %copy-done.17) | copy-start | bytes 3145732
  805.6 66.7 %copy-start.21 = (bf16[4,1,2,32,1024]{4,3,2,1,0:T(8,128)(2,1)S(1)}, bf16[4,1,2,32,1024]{4,3,2,1,0:T(8,128)(2,1)}, u32[]{:S(2)}) copy-start(bf16[4,1,2,32,1024]{4,3,2,1,0:T(8,128)(2,1)} %param.21) | copy-start | bytes 1572868
  805.6 66.7 %copy-start.25 = (f32[256,1024]{1,0:T(8,128)S(1)}, f32[256,1024]{1,0:T(8,128)}, u32[]{:S(2)}) copy-start(f32[256,1024]{1,0:T(8,128)} %get-tuple-element.305) | copy-start | bytes 3145732
  805.6 66.7 %copy-start.52 = (f32[256]{0:T(256)S(1)}, f32[256]{0:T(256)}, u32[]{:S(2)}) copy-start(f32[256]{0:T(256)} %copy-done.51) | copy-start | bytes 3076
  877.8 7.7 copy-start.1
  (81 other events, 138.4 us)
Sparse Core Ops, SparseCore 0:
  50.9 16.4 all-gather.13
  89.8 46.3 all-gather.15
  138.3 45.6 all-gather.17
  185.4 9.3 all-gather.19
  196.2 21.0 all-gather.21
  239.7 21.2 all-gather.23
  356.7 17.9 reduce-scatter.19
  490.8 91.0 reduce-scatter.9
  584.1 14.8 reduce-scatter.23
  601.1 28.5 reduce-scatter.21
  632.6 8.2 reduce-scatter.15
  643.0 15.3 reduce-scatter.11
  674.9 30.9 reduce-scatter.25
  707.3 26.4 all-gather.27
  735.3 27.3 all-gather.31
  764.8 19.3 reduce-scatter.17
  786.9 22.0 reduce-scatter.13
  810.4 10.0 all-gather.29
  822.1 11.7 all-gather.33
  835.3 10.9 all-gather.25

commit v9 on v8

--- a/solution.py
+++ b/solution.py
@@ -330,12 +330,9 @@
         fc_bias_grad,
         proj_bias_grad,
     )
-    packed = jnp.concatenate(
-        [grad.astype(jnp.bfloat16).reshape(fsdp_size, -1) for grad in vector_grads], axis=1
-    )
-    packed = lax.psum_scatter(packed, "fsdp", scatter_dimension=0, tiled=True).reshape(-1)
-    packed = lax.psum_scatter(packed, CTX, scatter_dimension=0, tiled=True)
-    packed = lax.all_gather(packed, CTX, axis=0, tiled=True).astype(jnp.float32)
+    packed = jnp.concatenate([grad.reshape(fsdp_size, -1) for grad in vector_grads], axis=1)
+    packed = lax.psum(packed.astype(jnp.float32), CTX + ("fsdp",))
+    packed = lax.dynamic_index_in_dim(packed, lax.axis_index("fsdp"), 0, keepdims=False)
     vector_totals = []
     offset = 0
     for grad in vector_grads:

time: 903 us -> 898 us (level)
    psum x0 -> x1, blocking collectives: none -> 39 us  [shards(): packed = lax.psum(packed.astype(jnp.float32), CTX + ('fsdp',))]
    unnamed x2 -> x0, blocking collectives: 30.1 us -> none
    all_gather x1 -> x0, blocking collectives: 12.7 us -> none  [shards(): packed = lax.all_gather(packed, CTX, axis=0, tiled=True).astype(jnp.float32)]
where the time goes in v9:
time: 898 us; the launch traced here: 888 us
  blocking collectives  260 us (29%)
  waiting for transfers between devices  222 us (25%)
  local copies, waits for them, and re-layouts  151 us (17%)
  matrix products  132 us (15%)
  other arithmetic  63.6 us (7%)
  starting transfers between devices  42.4 us (5%)
  between operations  16 us (2%)
    all_to_all x3, blocking collectives, reduce_weight_grad(): lax.all_to_all(grad.reshape((fsdp_size, -1) + grad.shape[1:]), 'fsdp', sp...  113 us
    all_to_all x3, waiting for transfers between devices, gather_weight(): lax.all_to_all(jnp.broadcast_to(piece[None], (fsdp_size,) + piece.shape),...  102 us
    dot_general x52, matrix products, contract_last(): lax.dot_general(left, right, (((1,), (1,)), ((), ())), preferred_element_...  52.5 us
    all_to_all x1, blocking collectives, gather_weight(): lax.all_to_all(jnp.broadcast_to(piece[None], (fsdp_size,) + piece.shape),...  41.7 us
    psum x1, blocking collectives, shards(): packed = lax.psum(packed.astype(jnp.float32), CTX + ('fsdp',))  39 us
    dot_general x36, matrix products, contract_first(): lax.dot_general(left, right, (((0,), (0,)), ((), ())), preferred_element_...  36 us
    all_gather x2, waiting for transfers between devices, reduce_weight_grad(): grad = lax.all_gather(grad, 'zc', axis=0, tiled=True)  35.8 us
    all_gather x2, blocking collectives, reduce_weight_grad(): grad = lax.all_gather(grad, 'zc', axis=0, tiled=True)  33.7 us
  transfers between devices with their start and end apart: 30, of which 15 were waited for; matrix products, arithmetic and copies ran while one was open for 32% of the time, Pallas kernels for 0%

profile of v9, /device:TPU:0, one launch (start us, length us, event | category | flops | bytes accessed | tf_op | source)
XLA Modules:
  0.0 888.4 jit_solution(301184630496174386)
XLA Ops:
  9.0 41.7 %all_to_all.154 = bf16[4,128,3072]{2,1,0:T(8,128)(2,1)} all-to-all(bf16[4,128,3072]{2,1,0:T(8,128)(2,1)S(1)} %broadcast_in_dim.65), channel_id=1, replica_groups=mesh['zc'=4,'core'=2,'fsdp'=4] {'fsdp'}, dimensions={0} | all-to-all | bytes 6291456 | tf_op jit(solution)/shard_map/all_to_all | solution.py:110
  53.2 7.6 all-gather
  62.8 4.6 all-gather.13.cloned.1.call-done
  67.4 4.6 fusion.101
  76.1 12.7 %all_to_all.155 = bf16[4,2,32,4,256]{4,2,1,0,3:T(8,128)(2,1)S(1)} all-to-all(bf16[4,2,32,4,256]{4,2,1,0,3:T(8,128)(2,1)S(1)} %copy.111), channel_id=1, replica_groups=mesh['zc'=4,'core'=2,'fsdp'=4] {'fsdp'}, dimensions={3} | all-to-all | bytes 1048576 | tf_op jit(solution)/shard_map/all_to_all | solution.py:226
  89.7 2.8 fusion.79
  94.0 10.3 %all_to_all.156 = bf16[4,2,32,4,256]{4,2,1,0,3:T(8,128)(2,1)S(1)} all-to-all(bf16[4,2,32,4,256]{4,2,1,0,3:T(8,128)(2,1)S(1)} %copy.114), channel_id=1, replica_groups=mesh['zc'=4,'core'=2,'fsdp'=4] {'fsdp'}, dimensions={3} | all-to-all | bytes 1048576 | tf_op jit(solution)/shard_map/all_to_all | solution.py:227
  106.3 4.3 all-to-all-start.5
  111.7 10.8 %all-to-all-done.5 = bf16[4,128,1024]{2,1,0:T(8,128)(2,1)} async-done(((bf16[4,128,1024]{2,1,0:T(8,128)(2,1)}), bf16[4,128,1024]{2,1,0:T(8,128)(2,1)}, u32[]{:S(2)}, u32[]{:S(2)}) %all-to-all-start.5) | async-done | bytes 1048608 | tf_op jit(solution)/shard_map/all_to_all | solution.py:110
  122.5 3.8 broadcast_in_dim.67
  126.2 4.9 all-to-all-start.6
  131.7 46.3 %all-to-all-done.6 = bf16[4,128,4096]{2,1,0:T(8,128)(2,1)} async-done(((bf16[4,128,4096]{2,1,0:T(8,128)(2,1)}), bf16[4,128,4096]{2,1,0:T(8,128)(2,1)}, u32[]{:S(2)}, u32[]{:S(2)}) %all-to-all-start.6) | async-done | bytes 4194336 | tf_op jit(solution)/shard_map/all_to_all | solution.py:110
  179.7 2.6 broadcast_in_dim.68
  182.3 5.0 all-to-all-start.7
  189.0 45.2 %all-to-all-done.7 = bf16[4,512,1024]{2,1,0:T(8,128)(2,1)} async-done(((bf16[4,512,1024]{2,1,0:T(8,128)(2,1)}), bf16[4,512,1024]{2,1,0:T(8,128)(2,1)}, u32[]{:S(2)}, u32[]{:S(2)}) %all-to-all-start.7) | async-done | bytes 4194336 | tf_op jit(solution)/shard_map/all_to_all | solution.py:110
  234.2 3.5 all-to-all-start.1
  238.3 6.9 all-to-all-done.1
  246.0 5.6 copy.113
  251.6 5.7 copy.116
  257.3 41.3 %while.26 = (s32[]{:T(128)}, bf16[4,256,256]{2,1,0:T(8,128)(2,1)S(1)}, f32[4,256,4]{1,2,0:T(4,128)}, s32[4,2048]{1,0:T(4,128)S(1)}, s32[4,256]{1,0:T(4,128)S(1)}...) while((s32[]{:T(128)}, ...), condition=%wide.region_11.12_spmd, body=%wide.region_2.11_spmd.sunk | while | flops 554240000 | bytes 35092604 | solution.py:242
  300.0 3.7 all-to-all-start.4
  303.9 6.3 all-to-all-done.4
  315.1 9.5 %multiply_convert_fusion.4 = (bf16[256,4096]{1,0:T(8,128)(2,1)}, f32[256,4096]{1,0:T(8,128)}) fusion(f32[4096]{0:T(1024)S(1)} %bitcast.369, bf16[256,1024]{1,0:T(8,128)(2,1)S(1)} %add_convert_fusion.1, bf16[1024,4096]{1,0:T(8,128)(2,1)} %bitcast.383), kind=kOutput, calls=%fused_computation.142 | convolution fusion | flops 2157969408 | bytes 15220736 | tf_op jit(solution)/shard_map/dot_general | solution.py:252
  324.6 12.5 %convert_reduce_fusion = (f32[4096]{0:T(1024)}, bf16[256,4096]{1,0:T(8,128)(2,1)S(1)}) fusion(f32[256,4096]{1,0:T(8,128)} %get-tuple-element.303, bf16[4096,1024]{1,0:T(8,128)(2,1)} %bitcast.381, bf16[256,1024]{1,0:T(8,128)(2,1)S(1)} %bitcast.294), kind=kOutput, calls=%fused_computation.141 | convolution fusion | flops 2170548224 | bytes 15220736 | tf_op jit(solution)/shard_map/dot_general | solution.py:29
  337.1 3.2 multiply_reduce_fusion.4
  345.3 3.5 all-to-all-start.8
  349.4 7.2 convolution_convert_fusion.9
  357.6 118.0 %while.27 = (s32[]{:T(128)}, bf16[4,256,256]{2,1,0:T(8,128)(2,1)}, bf16[4,2048,256]{2,1,0:T(8,128)(2,1)}, bf16[4,2048,256]{2,1,0:T(8,128)(2,1)}, s32[4,2048]{1,0...) while((s32[]{:T(128)}, bf16[4,256,256]{2,1,0:T(8,128)(2,1)}, ...), condition=%wide.region_21.22_spmd, body=%wide.region_16.21_spmd.sunk | while | flops 1370029056 | bytes 166414960 | solution.py:276
  380.3 2.4 constant_dynamic-update-slice_fusion.22
  409.8 2.4 constant_dynamic-update-slice_fusion.22
  439.2 2.4 constant_dynamic-update-slice_fusion.22
  468.6 2.5 constant_dynamic-update-slice_fusion.22
  475.6 7.6 maximum_bitcast_fusion.5
  483.2 7.5 copy.129
  492.3 2.9 reshape.557
  495.3 4.8 copy.140
  500.1 5.6 convolution_convert_fusion.8
  505.9 50.3 %all_to_all.158 = bf16[4,128,4096]{2,1,0:T(8,128)(2,1)} all-to-all(bf16[4,128,4096]{2,1,0:T(8,128)(2,1)} %bitcast.306), channel_id=1, replica_groups=mesh['zc'=4,'core'=2,'fsdp'=4] {'fsdp'}, dimensions={0} | all-to-all | bytes 8388608 | tf_op jit(solution)/shard_map/all_to_all | solution.py:131
  556.2 4.3 reduce_sum.324
  564.9 3.5 all-to-all-start.9
  568.4 13.5 %reduce-scatter.10.cloned.1.call-done = bf16[1024,512]{1,0:T(8,128)(2,1)} async-done(((bf16[8192,512]{1,0:T(8,128)(2,1)}), bf16[1024,512]{1,0:T(8,128)(2,1)}) %reduce-scatter.10.cloned.1.call-update) | async-done | bytes 1048592 | tf_op jit(solution)/shard_map/reduce_scatter | solution.py:282
  584.5 3.7 all-to-all-start.10
  589.6 5.2 all-to-all-done.10
  594.8 4.2 all-to-all-start.11
  603.0 2.6 all-to-all-done.11
  607.5 5.8 fusion.90
  616.5 4.5 convolution_convert_fusion.10
  621.1 49.4 %all_to_all.159 = bf16[4,512,1024]{2,1,0:T(8,128)(2,1)} all-to-all(bf16[4,512,1024]{2,1,0:T(8,128)(2,1)} %bitcast.307), channel_id=1, replica_groups=mesh['zc'=4,'core'=2,'fsdp'=4] {'fsdp'}, dimensions={0} | all-to-all | bytes 8388608 | tf_op jit(solution)/shard_map/all_to_all | solution.py:131
  670.5 4.4 reduce_sum.325
  675.5 13.4 %all_to_all.157 = bf16[4,128,1024]{2,1,0:T(8,128)(2,1)S(1)} all-to-all(bf16[4,128,1024]{2,1,0:T(8,128)(2,1)} %bitcast.337), channel_id=1, replica_groups=mesh['zc'=4,'core'=2,'fsdp'=4] {'fsdp'}, dimensions={0} | all-to-all | bytes 2097152 | tf_op jit(solution)/shard_map/all_to_all | solution.py:131
  688.9 4.7 all-to-all-start.12
  693.6 12.3 %reduce-scatter.26.cloned.1.call-done = bf16[128,1024]{1,0:T(8,128)(2,1)} async-done(((bf16[512,1024]{1,0:T(8,128)(2,1)}), bf16[128,1024]{1,0:T(8,128)(2,1)}) %reduce-scatter.26.cloned.1.call-update) | async-done | bytes 262160 | tf_op jit(solution)/shard_map/reduce_scatter | solution.py:135
  707.0 16.2 %all-to-all-done.12 = bf16[4,128,3072]{2,1,0:T(8,128)(2,1)} async-done(((bf16[4,128,3072]{2,1,0:T(8,128)(2,1)}), bf16[4,128,3072]{2,1,0:T(8,128)(2,1)}, u32[]{:S(2)}, u32[]{:S(2)}) %all-to-all-start.12) | async-done | bytes 3145760 | tf_op jit(solution)/shard_map/all_to_all | solution.py:131
  723.2 3.6 reduce_sum.322
  726.9 7.1 all-gather.27.cloned.1.call-done
  734.0 28.7 %all-gather.31.cloned.1.call-done = bf16[512,1024]{1,0:T(8,128)(2,1)} async-done(((bf16[128,1024]{1,0:T(8,128)(2,1)}), bf16[512,1024]{1,0:T(8,128)(2,1)}) %all-gather.31.cloned.1.call-update) | async-done | bytes 1048592 | tf_op jit(solution)/shard_map/all_gather | solution.py:136
  764.3 7.2 fusion.78
  771.5 12.7 %reduce-scatter.18.cloned.1.call-done = bf16[32,1024]{1,0:T(8,128)(2,1)} async-done(((bf16[128,1024]{1,0:T(8,128)(2,1)}), bf16[32,1024]{1,0:T(8,128)(2,1)}) %reduce-scatter.18.cloned.1.call-update) | async-done | bytes 65552 | tf_op jit(solution)/shard_map/reduce_scatter | solution.py:135
  784.2 15.5 %all_gather.58 = bf16[128,1024]{1,0:T(8,128)(2,1)S(1)} all-gather(bf16[32,1024]{1,0:T(8,128)(2,1)} %reduce-scatter.18.cloned.1.call-done), channel_id=1, replica_groups=mesh['zc'=4,'core'=2,'fsdp'=4] {'zc'}, dimensions={0}, use_global_device_ids=true | all-gather | bytes 327680 | tf_op jit(solution)/shard_map/all_gather | solution.py:136
  809.1 18.2 %all_gather.56 = bf16[128,3072]{1,0:T(8,128)(2,1)} all-gather(bf16[32,3072]{1,0:T(8,128)(2,1)} %reduce-scatter.14.cloned.1.call-done), channel_id=1, replica_groups=mesh['zc'=4,'core'=2,'fsdp'=4] {'zc'}, dimensions={0}, use_global_device_ids=true | all-gather | bytes 983040 | tf_op jit(solution)/shard_map/all_gather | solution.py:136
  827.4 39.0 %psum.7 = f32[4,3072]{1,0:T(4,128)S(1)} all-reduce(f32[4,3072]{1,0:T(4,128)S(1)} %constant_dynamic-update-slice_fusion.7), channel_id=1, replica_groups=mesh['zc'=4,'core'=2,'fsdp'=4] {'zc','core','fsdp'}, use_global_device_ids=true, to_apply=%region_34.35 | all-reduce | flops 12288 | bytes 98304 | tf_op jit(solution)/shard_map/psum | solution.py:334
  869.3 4.1 convert_element_type.314
  873.4 4.2 convert_element_type.316
  877.6 3.4 convert_element_type.310
  (666 shorter events, 216.1 us)
Async XLA Ops:
  7.2 103.4 %copy-start = (bf16[256,4096]{1,0:T(8,128)(2,1)S(1)}, bf16[256,4096]{1,0:T(8,128)(2,1)}, u32[]{:S(2)}) copy-start(bf16[256,4096]{1,0:T(8,128)(2,1)} %param.32) | copy-start | bytes 6291460
  7.2 60.2 %all-gather.13.cloned.1.call-start = ((), (), s32[]{:S(2)}) async-start(), calls=%async_computation.25 | async-start | bytes 9437184 | tf_op jit(solution)/shard_map/all_gather | solution.py:117
  50.7 10.7 %copy-start.13 = (bf16[4,1,2,32,1024]{4,3,2,1,0:T(8,128)(2,1)S(1)}, bf16[4,1,2,32,1024]{4,3,2,1,0:T(8,128)(2,1)}, u32[]{:S(2)}) copy-start(bf16[4,1,2,32,1024]{4,3,2,1,0:T(8,128)(2,1)} %param.20) | copy-start | bytes 1572868
  50.8 195.3 %all-gather.15.cloned.1.call-start = ((), (), s32[]{:S(2)}) async-start(), calls=%async_computation.26 | async-start | bytes 4718592 | tf_op jit(solution)/shard_map/all_gather | solution.py:233
  89.6 162.0 %all-gather.17.cloned.1.call-start = ((), (), s32[]{:S(2)}) async-start(), calls=%async_computation.27 | async-start | bytes 4718592 | tf_op jit(solution)/shard_map/all_gather | solution.py:236
  94.0 11.2 %copy-start.42 = (bf16[256,1024]{1,0:T(8,128)(2,1)S(1)}, bf16[256,1024]{1,0:T(8,128)(2,1)}, u32[]{:S(2)}) copy-start(bf16[256,1024]{1,0:T(8,128)(2,1)} %param.28) | copy-start | bytes 1572868
  106.3 16.1 %all-to-all-start.5 = ((bf16[4,128,1024]{2,1,0:T(8,128)(2,1)}), bf16[4,128,1024]{2,1,0:T(8,128)(2,1)}, u32[]{:S(2)}, u32[]{:S(2)}) async-start(bf16[4,128,1024]{2,1,0:T(8,128)(2,1)} %broadcast_in_dim.66), calls=%async_computation.5 | async-start | bytes 2097152 | tf_op jit(solution)/shard_map/all_to_all | solution.py:110
  126.2 51.8 %all-to-all-start.6 = ((bf16[4,128,4096]{2,1,0:T(8,128)(2,1)}), bf16[4,128,4096]{2,1,0:T(8,128)(2,1)}, u32[]{:S(2)}, u32[]{:S(2)}) async-start(bf16[4,128,4096]{2,1,0:T(8,128)(2,1)} %broadcast_in_dim.67), calls=%async_computation.6 | async-start | bytes 8388608 | tf_op jit(solution)/shard_map/all_to_all | solution.py:110
  131.1 180.6 %all-gather.19.cloned.1.call-start = ((), (), s32[]{:S(2)}) async-start(), calls=%async_computation.28 | async-start | bytes 3145728 | tf_op jit(solution)/shard_map/all_gather | solution.py:117
  131.7 183.4 %all-gather.21.cloned.1.call-start = ((), (), s32[]{:S(2)}) async-start(), calls=%async_computation.29 | async-start | bytes 12582912 | tf_op jit(solution)/shard_map/all_gather | solution.py:117
  182.3 5.0 copy-start.55
  182.3 5.4 copy-start.35
  182.3 51.9 %all-to-all-start.7 = ((bf16[4,512,1024]{2,1,0:T(8,128)(2,1)}), bf16[4,512,1024]{2,1,0:T(8,128)(2,1)}, u32[]{:S(2)}, u32[]{:S(2)}) async-start(bf16[4,512,1024]{2,1,0:T(8,128)(2,1)} %broadcast_in_dim.68), calls=%async_computation.7 | async-start | bytes 8388608 | tf_op jit(solution)/shard_map/all_to_all | solution.py:110
  234.2 11.0 %all-to-all-start.1 = ((bf16[4,2,32,4,256]{4,2,1,0,3:T(8,128)(2,1)}), bf16[4,2,32,4,256]{4,2,1,0,3:T(8,128)(2,1)S(1)}, u32[]{:S(2)}, u32[]{:S(2)}) async-start(bf16[4,2,32,4,256]{4,2,1,0,3:T(8,128)(2,1)} %copy.109), calls=%async_computation.1 | async-start | bytes 1048576 | tf_op jit(solution)/shard_map/all_to_all | solution.py:225
  237.7 86.8 %all-gather.23.cloned.1.call-start = ((), (), s32[]{:S(2)}) async-start(), calls=%async_computation.30 | async-start | bytes 12582912 | tf_op jit(solution)/shard_map/all_gather | solution.py:117
  300.0 10.3 %all-to-all-start.4 = ((bf16[4,2,128,1,256]{4,1,0,3,2:T(2,128)(2,1)}), bf16[4,2,128,1,256]{4,1,0,3,2:T(2,128)(2,1)S(1)}, u32[]{:S(2)}, u32[]{:S(2)}) async-start(bf16[4,2,128,1,256]{4,1,0,3,2:T(2,128)(2,1)} %copy.118), calls=%async_computation.4 | async-start | bytes 1048576 | tf_op jit(solution)/shard_map/all_to_all | solution.py:245
  314.1 26.2 %copy-start.15 = (f32[256,1024]{1,0:T(8,128)}, f32[256,1024]{1,0:T(8,128)S(1)}, u32[]{:S(2)}) copy-start(f32[256,1024]{1,0:T(8,128)S(1)} %get-tuple-element.301) | copy-start | bytes 3145732
  315.1 9.5 %copy-start.19 = (bf16[4,1,2,32,1024]{4,3,2,1,0:T(8,128)(2,1)S(1)}, bf16[4,1,2,32,1024]{4,3,2,1,0:T(8,128)(2,1)}, u32[]{:S(2)}) copy-start(bf16[4,1,2,32,1024]{4,3,2,1,0:T(8,128)(2,1)} %param.21) | copy-start | bytes 1572868
  324.6 12.6 %copy-start.67 = (bf16[4,256,4096]{2,1,0:T(8,128)(2,1)S(1)}, bf16[4,256,4096]{2,1,0:T(8,128)(2,1)}, u32[]{:S(2)}) copy-start(bf16[4,256,4096]{2,1,0:T(8,128)(2,1)} %all-gather.21.cloned.1.call-done) | copy-start | bytes 25165828
  345.3 11.4 %all-to-all-start.8 = ((bf16[4,2,32,4,256]{4,2,1,0,3:T(8,128)(2,1)}), bf16[4,2,32,4,256]{4,2,1,0,3:T(8,128)(2,1)S(1)}, u32[]{:S(2)}, u32[]{:S(2)}) async-start(bf16[4,2,32,4,256]{4,2,1,0,3:T(8,128)(2,1)} %copy.121), calls=%async_computation.8 | async-start | bytes 1048576 | tf_op jit(solution)/shard_map/all_to_all | solution.py:273
  348.8 157.1 %reduce-scatter.20.cloned.1.call-start = ((), (), s32[]{:S(2)}) async-start(), calls=%async_computation.37 | async-start | bytes 12582912 | tf_op jit(solution)/shard_map/reduce_scatter | solution.py:129
  356.6 225.3 %reduce-scatter.10.cloned.1.call-start = ((), (), s32[]{:S(2)}) async-start(), calls=%async_computation.31 | async-start | bytes 9437184 | tf_op jit(solution)/shard_map/reduce_scatter | solution.py:282
  357.8 4.0 copy-start.40
  374.5 3.6 copy-start.10
  387.3 4.0 copy-start.40
  404.0 3.6 copy-start.10
  416.7 4.0 copy-start.40
  433.4 3.6 copy-start.10
  446.1 4.1 copy-start.40
  490.7 130.4 %reduce-scatter.24.cloned.1.call-start = ((), (), s32[]{:S(2)}) async-start(), calls=%async_computation.41 | async-start | bytes 12582912 | tf_op jit(solution)/shard_map/reduce_scatter | solution.py:129
  495.2 4.9 copy-start.20
  505.8 169.2 %reduce-scatter.22.cloned.1.call-start = ((), (), s32[]{:S(2)}) async-start(), calls=%async_computation.38 | async-start | bytes 1310720 | tf_op jit(solution)/shard_map/reduce_scatter | solution.py:135
  556.2 4.4 copy-start.23
  560.5 115.0 %reduce-scatter.16.cloned.1.call-start = ((), (), s32[]{:S(2)}) async-start(), calls=%async_computation.35 | async-start | bytes 3145728 | tf_op jit(solution)/shard_map/reduce_scatter | solution.py:129
  564.9 19.6 %all-to-all-start.9 = ((bf16[4,2,128,1,256]{4,1,0,3,2:T(2,128)(2,1)}), bf16[4,2,128,1,256]{4,1,0,3,2:T(2,128)(2,1)S(1)}, u32[]{:S(2)}, u32[]{:S(2)}) async-start(bf16[4,2,128,1,256]{4,1,0,3,2:T(2,128)(2,1)} %copy.124), calls=%async_computation.9 | async-start | bytes 1048576 | tf_op jit(solution)/shard_map/all_to_all | solution.py:293
  583.2 16.1 %copy-start.46 = (f32[4,2,32]{2,1,0:T(2,128)S(1)}, f32[4,2,32]{2,1,0:T(2,128)}, u32[]{:S(2)}) copy-start(f32[4,2,32]{2,1,0:T(2,128)} %copy-done.45) | copy-start | bytes 3076
  583.2 16.2 %copy-start.14 = (bf16[4,1,2,32,1024]{4,3,2,1,0:T(8,128)(2,1)S(1)}, bf16[4,1,2,32,1024]{4,3,2,1,0:T(8,128)(2,1)}, u32[]{:S(2)}) copy-start(bf16[4,1,2,32,1024]{4,3,2,1,0:T(8,128)(2,1)} %param.20) | copy-start | bytes 1572868
  584.5 10.2 %all-to-all-start.10 = ((bf16[4,2,128,1,256]{4,1,0,3,2:T(2,128)(2,1)}), bf16[4,2,128,1,256]{4,1,0,3,2:T(2,128)(2,1)S(1)}, u32[]{:S(2)}, u32[]{:S(2)}) async-start(bf16[4,2,128,1,256]{4,1,0,3,2:T(2,128)(2,1)} %copy.130), calls=%async_computation.11 | async-start | bytes 1048576 | tf_op jit(solution)/shard_map/all_to_all | solution.py:296
  588.2 12.2 %copy-start.51 = (f32[4,2,32]{2,1,0:T(2,128)S(1)}, f32[4,2,32]{2,1,0:T(2,128)}, u32[]{:S(2)}) copy-start(f32[4,2,32]{2,1,0:T(2,128)} %get-tuple-element.296) | copy-start | bytes 3076
  588.2 12.3 %copy-start.50 = (f32[4,256]{1,0:T(4,128)S(1)}, f32[4,256]{1,0:T(4,128)}, u32[]{:S(2)}) copy-start(f32[4,256]{1,0:T(4,128)} %get-tuple-element.295) | copy-start | bytes 12292
  588.2 12.3 %copy-start.49 = (f32[4,256]{1,0:T(4,128)S(1)}, f32[4,256]{1,0:T(4,128)}, u32[]{:S(2)}) copy-start(f32[4,256]{1,0:T(4,128)} %get-tuple-element.286) | copy-start | bytes 12292
  594.8 4.5 copy-start.30
  594.8 10.8 %all-to-all-start.11 = ((bf16[4,2,128,1,256]{4,1,0,3,2:T(2,128)(2,1)}), bf16[4,2,128,1,256]{4,1,0,3,2:T(2,128)(2,1)}, u32[]{:S(2)}, u32[]{:S(2)}) async-start(bf16[4,2,128,1,256]{4,1,0,3,2:T(2,128)(2,1)} %copy.133), calls=%async_computation.12 | async-start | bytes 1048576 | tf_op jit(solution)/shard_map/all_to_all | solution.py:299
  599.0 89.9 %reduce-scatter.12.cloned.1.call-start = ((), (), s32[]{:S(2)}) async-start(), calls=%async_computation.32 | async-start | bytes 9437184 | tf_op jit(solution)/shard_map/reduce_scatter | solution.py:129
  621.0 84.9 %reduce-scatter.26.cloned.1.call-start = ((), (), s32[]{:S(2)}) async-start(), calls=%async_computation.42 | async-start | bytes 1310720 | tf_op jit(solution)/shard_map/reduce_scatter | solution.py:135
  674.9 59.0 %all-gather.27.cloned.1.call-start = ((), (), s32[]{:S(2)}) async-start(), calls=%async_computation.39 | async-start | bytes 1310720 | tf_op jit(solution)/shard_map/all_gather | solution.py:136
  688.9 34.3 %all-to-all-start.12 = ((bf16[4,128,3072]{2,1,0:T(8,128)(2,1)}), bf16[4,128,3072]{2,1,0:T(8,128)(2,1)}, u32[]{:S(2)}, u32[]{:S(2)}) async-start(bf16[4,128,3072]{2,1,0:T(8,128)(2,1)} %bitcast.311), calls=%async_computation.14 | async-start | bytes 6291456 | tf_op jit(solution)/shard_map/all_to_all | solution.py:131
  693.6 69.1 %all-gather.31.cloned.1.call-start = ((), (), s32[]{:S(2)}) async-start(), calls=%async_computation.43 | async-start | bytes 1310720 | tf_op jit(solution)/shard_map/all_gather | solution.py:136
  706.0 78.2 %reduce-scatter.18.cloned.1.call-start = ((), (), s32[]{:S(2)}) async-start(), calls=%async_computation.36 | async-start | bytes 327680 | tf_op jit(solution)/shard_map/reduce_scatter | solution.py:135
  707.0 102.1 %reduce-scatter.14.cloned.1.call-start = ((), (), s32[]{:S(2)}) async-start(), calls=%async_computation.33 | async-start | bytes 983040 | tf_op jit(solution)/shard_map/reduce_scatter | solution.py:135
  726.8 36.3 %copy-start.48 = (f32[1,2,4,128]{3,2,1,0:T(4,128)S(1)}, f32[1,2,4,128]{3,2,1,0:T(4,128)}, u32[]{:S(2)}) copy-start(f32[1,2,4,128]{3,2,1,0:T(4,128)} %get-tuple-element.289) | copy-start | bytes 12292
  726.8 37.5 %copy-start.47 = (f32[1024]{0:T(1024)S(1)}, f32[1024]{0:T(1024)}, u32[]{:S(2)}) copy-start(f32[1024]{0:T(1024)} %get-tuple-element.244) | copy-start | bytes 12292
  726.8 37.5 %copy-start.57 = (f32[1024]{0:T(1024)S(1)}, f32[1024]{0:T(1024)}, u32[]{:S(2)}) copy-start(f32[1024]{0:T(1024)} %get-tuple-element.199) | copy-start | bytes 12292
  726.8 37.5 %copy-start.56 = (f32[1024]{0:T(1024)S(1)}, f32[1024]{0:T(1024)}, u32[]{:S(2)}) copy-start(f32[1024]{0:T(1024)} %get-tuple-element.203) | copy-start | bytes 12292
  726.8 37.6 %copy-start.52 = (f32[4096]{0:T(1024)S(1)}, f32[4096]{0:T(1024)}, u32[]{:S(2)}) copy-start(f32[4096]{0:T(1024)} %get-tuple-element.306) | copy-start | bytes 49156
  726.8 37.6 %copy-start.16 = (f32[256,1024]{1,0:T(8,128)S(1)}, f32[256,1024]{1,0:T(8,128)}, u32[]{:S(2)}) copy-start(f32[256,1024]{1,0:T(8,128)} %copy-done.15) | copy-start | bytes 3145732
  726.8 142.5 %all-gather.29.cloned.1.call-start = ((), (), s32[]{:S(2)}) async-start(), calls=%async_computation.40 | async-start | bytes 3145728 | tf_op jit(solution)/shard_map/all_gather | solution.py:137
  733.9 139.4 %all-gather.33.cloned.1.call-start = ((), (), s32[]{:S(2)}) async-start(), calls=%async_computation.44 | async-start | bytes 3145728 | tf_op jit(solution)/shard_map/all_gather | solution.py:137
  762.7 114.8 %all-gather.25.cloned.1.call-start = ((), (), s32[]{:S(2)}) async-start(), calls=%async_computation.34 | async-start | bytes 2359296 | tf_op jit(solution)/shard_map/all_gather | solution.py:137
  805.6 62.2 %copy-start.18 = (f32[256,1024]{1,0:T(8,128)S(1)}, f32[256,1024]{1,0:T(8,128)}, u32[]{:S(2)}) copy-start(f32[256,1024]{1,0:T(8,128)} %copy-done.17) | copy-start | bytes 3145732
  805.6 62.2 %copy-start.21 = (bf16[4,1,2,32,1024]{4,3,2,1,0:T(8,128)(2,1)S(1)}, bf16[4,1,2,32,1024]{4,3,2,1,0:T(8,128)(2,1)}, u32[]{:S(2)}) copy-start(bf16[4,1,2,32,1024]{4,3,2,1,0:T(8,128)(2,1)} %param.21) | copy-start | bytes 1572868
  805.6 62.2 %copy-start.25 = (f32[256,1024]{1,0:T(8,128)S(1)}, f32[256,1024]{1,0:T(8,128)}, u32[]{:S(2)}) copy-start(f32[256,1024]{1,0:T(8,128)} %get-tuple-element.305) | copy-start | bytes 3145732
  805.6 62.2 %copy-start.54 = (f32[256]{0:T(256)S(1)}, f32[256]{0:T(256)}, u32[]{:S(2)}) copy-start(f32[256]{0:T(256)} %copy-done.53) | copy-start | bytes 3076
  873.4 7.7 copy-start.1
  (79 other events, 131.2 us)
Sparse Core Ops, SparseCore 0:
  50.9 16.4 all-gather.12
  89.8 46.3 all-gather.14
  138.3 45.6 all-gather.16
  185.4 9.3 all-gather.18
  196.2 21.0 all-gather.20
  239.8 21.2 all-gather.22
  356.7 17.9 reduce-scatter.19
  490.9 90.9 reduce-scatter.9
  584.2 14.8 reduce-scatter.23
  601.2 28.5 reduce-scatter.21
  632.7 8.2 reduce-scatter.15
  643.1 15.3 reduce-scatter.11
  675.0 30.9 reduce-scatter.25
  707.4 26.4 all-gather.26
  735.3 27.3 all-gather.30
  764.8 19.3 reduce-scatter.17
  787.0 22.0 reduce-scatter.13
  810.5 10.1 all-gather.28
  822.1 11.7 all-gather.32
  835.3 10.9 all-gather.24

commit v10 on v9

--- a/solution.py
+++ b/solution.py
@@ -221,22 +221,20 @@
     def to_pairs(array):
         return array.reshape(seq_count, 2, block_len, 1, group_width)
 
-    query_heads, key_heads, value_heads = (
-        lax.all_to_all(to_groups(query), "fsdp", split_axis=3, concat_axis=2, tiled=True),
-        lax.all_to_all(to_groups(keys), "fsdp", split_axis=3, concat_axis=2, tiled=True),
-        lax.all_to_all(to_groups(values), "fsdp", split_axis=3, concat_axis=2, tiled=True),
-    )
-    query_heads = query_heads.reshape(seq_count, pair_len, group_width)
-    own_keys = key_heads.reshape(seq_count, pair_len, group_width)
-    own_values = value_heads.reshape(seq_count, pair_len, group_width)
-    key_all, value_all = (
-        lax.all_gather(
-            own_keys.reshape(seq_count, 1, pair_len, group_width), CTX, axis=1, tiled=True
-        ),
-        lax.all_gather(
-            own_values.reshape(seq_count, 1, pair_len, group_width), CTX, axis=1, tiled=True
-        ),
-    )
+    qkv_heads = lax.all_to_all(
+        jnp.concatenate([to_groups(query), to_groups(keys), to_groups(values)], axis=4),
+        "fsdp",
+        split_axis=3,
+        concat_axis=2,
+        tiled=True,
+    ).reshape(seq_count, pair_len, 3 * group_width)
+    query_heads = qkv_heads[..., :group_width]
+    own_kv = qkv_heads[..., group_width:]
+    kv_all = lax.all_gather(
+        own_kv.reshape(seq_count, 1, pair_len, 2 * group_width), CTX, axis=1, tiled=True
+    )
+    key_all = kv_all[..., :group_width]
+    value_all = kv_all[..., group_width:]
     key_all = key_all.reshape(seq_count, -1, group_width)
     value_all = value_all.reshape(seq_count, -1, group_width)
     attended, summary = lax.map(

time: 898 us -> 889 us (0.990)
    all_gather x2 -> x0, local copies, waits for them, and re-layouts: 11.3 us -> none  [the longest x1 5.68 us: shards(): lax.all_gather(own_values.reshape(seq_count, 1, pair_len, group_width), C...]
    slice x0 -> x3, local copies, waits for them, and re-layouts: none -> 9.45 us  [the longest x1 6.52 us: shards(): value_all = kv_all[..., group_width:]]
    all_to_all x2 -> x1, blocking collectives: 23 us -> 23.9 us  [shards(): lax.all_to_all(jnp.concatenate([to_groups(query), to_groups(keys), to_gro...]
  transfers between devices with their start and end apart: 30 -> 28, of which waited for: 15 -> 14; matrix products, arithmetic and copies ran while one was open for 32% -> 31% of each run, Pallas kernels for 0% -> 0%
where the time goes in v10:
time: 889 us; the launch traced here: 880 us
  blocking collectives  263 us (30%)
  waiting for transfers between devices  216 us (24%)
  local copies, waits for them, and re-layouts  150 us (17%)
  matrix products  132 us (15%)
  other arithmetic  63.4 us (7%)
  starting transfers between devices  38.7 us (4%)
  between operations  15.6 us (2%)
    all_to_all x3, blocking collectives, reduce_weight_grad(): lax.all_to_all(grad.reshape((fsdp_size, -1) + grad.shape[1:]), 'fsdp', sp...  115 us
    all_to_all x3, waiting for transfers between devices, gather_weight(): lax.all_to_all(jnp.broadcast_to(piece[None], (fsdp_size,) + piece.shape),...  104 us
    dot_general x52, matrix products, contract_last(): lax.dot_general(left, right, (((1,), (1,)), ((), ())), preferred_element_...  52.5 us
    all_to_all x1, blocking collectives, gather_weight(): lax.all_to_all(jnp.broadcast_to(piece[None], (fsdp_size,) + piece.shape),...  41.7 us
    psum x1, blocking collectives, shards(): packed = lax.psum(packed.astype(jnp.float32), CTX + ('fsdp',))  39 us
    dot_general x36, matrix products, contract_first(): lax.dot_general(left, right, (((0,), (0,)), ((), ())), preferred_element_...  36 us
    all_gather x2, waiting for transfers between devices, reduce_weight_grad(): grad = lax.all_gather(grad, 'zc', axis=0, tiled=True)  35.7 us
    all_gather x2, blocking collectives, reduce_weight_grad(): grad = lax.all_gather(grad, 'zc', axis=0, tiled=True)  33.7 us
  transfers between devices with their start and end apart: 28, of which 14 were waited for; matrix products, arithmetic and copies ran while one was open for 31% of the time, Pallas kernels for 0%

profile of v10, /device:TPU:0, one launch (start us, length us, event | category | flops | bytes accessed | tf_op | source)
XLA Modules:
  0.0 879.7 jit_solution(5103445620654060094)
XLA Ops:
  9.0 41.7 %all_to_all.124 = bf16[4,128,3072]{2,1,0:T(8,128)(2,1)} all-to-all(bf16[4,128,3072]{2,1,0:T(8,128)(2,1)S(1)} %broadcast_in_dim.65), channel_id=1, replica_groups=mesh['zc'=4,'core'=2,'fsdp'=4] {'fsdp'}, dimensions={0} | all-to-all | bytes 6291456 | tf_op jit(solution)/shard_map/all_to_all | solution.py:110
  53.2 7.6 all-gather
  62.8 4.6 all-gather.13.cloned.1.call-done
  67.4 4.6 fusion.102
  73.3 2.2 reshape.521
  83.4 23.9 %all_to_all.125 = bf16[4,2,32,4,768]{4,2,1,0,3:T(8,128)(2,1)S(1)} all-to-all(bf16[4,2,32,4,768]{4,2,1,0,3:T(8,128)(2,1)S(1)} %pad_maximum_fusion), channel_id=1, replica_groups=mesh['zc'=4,'core'=2,'fsdp'=4] {'fsdp'}, dimensions={3} | all-to-all | bytes 3145728 | tf_op jit(solution)/shard_map/all_to_all | solution.py:224
  110.9 4.3 all-to-all-start.3
  116.2 11.9 %all-to-all-done.3 = bf16[4,128,1024]{2,1,0:T(8,128)(2,1)} async-done(((bf16[4,128,1024]{2,1,0:T(8,128)(2,1)}), bf16[4,128,1024]{2,1,0:T(8,128)(2,1)}, u32[]{:S(2)}, u32[]{:S(2)}) %all-to-all-start.3) | async-done | bytes 1048608 | tf_op jit(solution)/shard_map/all_to_all | solution.py:110
  128.1 3.7 broadcast_in_dim.67
  131.8 4.8 all-to-all-start.4
  137.4 46.1 %all-to-all-done.4 = bf16[4,128,4096]{2,1,0:T(8,128)(2,1)} async-done(((bf16[4,128,4096]{2,1,0:T(8,128)(2,1)}), bf16[4,128,4096]{2,1,0:T(8,128)(2,1)}, u32[]{:S(2)}, u32[]{:S(2)}) %all-to-all-start.4) | async-done | bytes 4194336 | tf_op jit(solution)/shard_map/all_to_all | solution.py:110
  185.2 2.6 broadcast_in_dim.68
  187.9 5.0 all-to-all-start.5
  193.5 46.2 %all-to-all-done.5 = bf16[4,512,1024]{2,1,0:T(8,128)(2,1)} async-done(((bf16[4,512,1024]{2,1,0:T(8,128)(2,1)}), bf16[4,512,1024]{2,1,0:T(8,128)(2,1)}, u32[]{:S(2)}, u32[]{:S(2)}) %all-to-all-start.5) | async-done | bytes 4194336 | tf_op jit(solution)/shard_map/all_to_all | solution.py:110
  241.6 6.5 fusion.98
  248.2 41.8 %while.26 = (s32[]{:T(128)}, bf16[4,256,256]{2,1,0:T(8,128)(2,1)S(1)}, f32[4,256,4]{1,2,0:T(4,128)}, s32[4,2048]{1,0:T(4,128)S(1)}, s32[4,256]{1,0:T(4,128)S(1)}...) while((s32[]{:T(128)}, ...), condition=%wide.region_11.12_spmd, body=%wide.region_2.11_spmd.sunk | while | flops 554240000 | bytes 35092604 | solution.py:240
  248.2 2.1 dynamic-slice_bitcast_fusion.13
  291.3 3.7 all-to-all-start.2
  295.2 6.8 all-to-all-done.2
  303.4 2.4 fusion.101
  306.8 9.5 %multiply_convert_fusion.4 = (bf16[256,4096]{1,0:T(8,128)(2,1)}, f32[256,4096]{1,0:T(8,128)}) fusion(f32[4096]{0:T(1024)S(1)} %bitcast.361, bf16[256,1024]{1,0:T(8,128)(2,1)S(1)} %add_convert_fusion.1, bf16[1024,4096]{1,0:T(8,128)(2,1)} %bitcast.375), kind=kOutput, calls=%fused_computation.142 | convolution fusion | flops 2157969408 | bytes 15220736 | tf_op jit(solution)/shard_map/dot_general | solution.py:250
  316.2 12.6 %convert_reduce_fusion = (f32[4096]{0:T(1024)}, bf16[256,4096]{1,0:T(8,128)(2,1)S(1)}) fusion(f32[256,4096]{1,0:T(8,128)} %get-tuple-element.305, bf16[4096,1024]{1,0:T(8,128)(2,1)} %bitcast.373, bf16[256,1024]{1,0:T(8,128)(2,1)S(1)} %bitcast.285), kind=kOutput, calls=%fused_computation.141 | convolution fusion | flops 2170548224 | bytes 15220736 | tf_op jit(solution)/shard_map/dot_general | solution.py:29
  328.8 3.2 multiply_reduce_fusion.4
  337.1 3.5 all-to-all-start.6
  341.2 7.2 convolution_convert_fusion.9
  349.3 118.0 %while.27 = (s32[]{:T(128)}, bf16[4,256,256]{2,1,0:T(8,128)(2,1)}, bf16[4,2048,256]{2,1,0:T(8,128)(2,1)}, bf16[4,2048,256]{2,1,0:T(8,128)(2,1)}, s32[4,2048]{1,0...) while((s32[]{:T(128)}, bf16[4,256,256]{2,1,0:T(8,128)(2,1)}, ...), condition=%wide.region_21.22_spmd, body=%wide.region_16.21_spmd.sunk | while | flops 1370029056 | bytes 166414960 | solution.py:274
  372.0 2.4 constant_dynamic-update-slice_fusion.22
  401.4 2.4 constant_dynamic-update-slice_fusion.22
  430.9 2.4 constant_dynamic-update-slice_fusion.22
  460.3 2.4 constant_dynamic-update-slice_fusion.22
  467.3 7.6 maximum_bitcast_fusion.5
  474.9 7.5 copy.115
  484.0 2.9 reshape.559
  486.9 4.8 copy.126
  491.8 5.6 convolution_convert_fusion.8
  497.5 51.6 %all_to_all.127 = bf16[4,128,4096]{2,1,0:T(8,128)(2,1)} all-to-all(bf16[4,128,4096]{2,1,0:T(8,128)(2,1)} %bitcast.300), channel_id=1, replica_groups=mesh['zc'=4,'core'=2,'fsdp'=4] {'fsdp'}, dimensions={0} | all-to-all | bytes 8388608 | tf_op jit(solution)/shard_map/all_to_all | solution.py:131
  549.1 4.3 reduce_sum.324
  554.5 2.0 convolution_convert_fusion.11
  557.9 3.5 all-to-all-start.7
  561.4 12.0 %reduce-scatter.10.cloned.1.call-done = bf16[1024,512]{1,0:T(8,128)(2,1)} async-done(((bf16[8192,512]{1,0:T(8,128)(2,1)}), bf16[1024,512]{1,0:T(8,128)(2,1)}) %reduce-scatter.10.cloned.1.call-update) | async-done | bytes 1048592 | tf_op jit(solution)/shard_map/reduce_scatter | solution.py:280
  576.0 3.6 all-to-all-start.8
  581.1 5.2 all-to-all-done.8
  586.3 4.2 all-to-all-start.9
  594.5 2.6 all-to-all-done.9
  599.0 5.8 fusion.90
  607.9 4.5 convolution_convert_fusion.10
  612.5 49.4 %all_to_all.128 = bf16[4,512,1024]{2,1,0:T(8,128)(2,1)} all-to-all(bf16[4,512,1024]{2,1,0:T(8,128)(2,1)} %bitcast.301), channel_id=1, replica_groups=mesh['zc'=4,'core'=2,'fsdp'=4] {'fsdp'}, dimensions={0} | all-to-all | bytes 8388608 | tf_op jit(solution)/shard_map/all_to_all | solution.py:131
  662.0 4.4 reduce_sum.325
  667.2 13.4 %all_to_all.126 = bf16[4,128,1024]{2,1,0:T(8,128)(2,1)S(1)} all-to-all(bf16[4,128,1024]{2,1,0:T(8,128)(2,1)} %bitcast.329), channel_id=1, replica_groups=mesh['zc'=4,'core'=2,'fsdp'=4] {'fsdp'}, dimensions={0} | all-to-all | bytes 2097152 | tf_op jit(solution)/shard_map/all_to_all | solution.py:131
  680.6 4.7 all-to-all-start.10
  685.4 12.1 %reduce-scatter.26.cloned.1.call-done = bf16[128,1024]{1,0:T(8,128)(2,1)} async-done(((bf16[512,1024]{1,0:T(8,128)(2,1)}), bf16[128,1024]{1,0:T(8,128)(2,1)}) %reduce-scatter.26.cloned.1.call-update) | async-done | bytes 262160 | tf_op jit(solution)/shard_map/reduce_scatter | solution.py:135
  698.5 16.4 %all-to-all-done.10 = bf16[4,128,3072]{2,1,0:T(8,128)(2,1)} async-done(((bf16[4,128,3072]{2,1,0:T(8,128)(2,1)}), bf16[4,128,3072]{2,1,0:T(8,128)(2,1)}, u32[]{:S(2)}, u32[]{:S(2)}) %all-to-all-start.10) | async-done | bytes 3145760 | tf_op jit(solution)/shard_map/all_to_all | solution.py:131
  714.9 3.6 reduce_sum.322
  718.6 7.0 all-gather.23.cloned.1.call-done
  725.6 28.7 %all-gather.27.cloned.1.call-done = bf16[512,1024]{1,0:T(8,128)(2,1)} async-done(((bf16[128,1024]{1,0:T(8,128)(2,1)}), bf16[512,1024]{1,0:T(8,128)(2,1)}) %all-gather.27.cloned.1.call-update) | async-done | bytes 1048592 | tf_op jit(solution)/shard_map/all_gather | solution.py:136
  756.0 7.2 fusion.78
  763.2 12.7 %reduce-scatter.18.cloned.1.call-done = bf16[32,1024]{1,0:T(8,128)(2,1)} async-done(((bf16[128,1024]{1,0:T(8,128)(2,1)}), bf16[32,1024]{1,0:T(8,128)(2,1)}) %reduce-scatter.18.cloned.1.call-update) | async-done | bytes 65552 | tf_op jit(solution)/shard_map/reduce_scatter | solution.py:135
  775.9 15.6 %all_gather.54 = bf16[128,1024]{1,0:T(8,128)(2,1)S(1)} all-gather(bf16[32,1024]{1,0:T(8,128)(2,1)} %reduce-scatter.18.cloned.1.call-done), channel_id=1, replica_groups=mesh['zc'=4,'core'=2,'fsdp'=4] {'zc'}, dimensions={0}, use_global_device_ids=true | all-gather | bytes 327680 | tf_op jit(solution)/shard_map/all_gather | solution.py:136
  791.4 2.2 all_gather.55
  800.7 18.2 %all_gather.52 = bf16[128,3072]{1,0:T(8,128)(2,1)} all-gather(bf16[32,3072]{1,0:T(8,128)(2,1)} %reduce-scatter.14.cloned.1.call-done), channel_id=1, replica_groups=mesh['zc'=4,'core'=2,'fsdp'=4] {'zc'}, dimensions={0}, use_global_device_ids=true | all-gather | bytes 983040 | tf_op jit(solution)/shard_map/all_gather | solution.py:136
  819.0 39.0 %psum.7 = f32[4,3072]{1,0:T(4,128)S(1)} all-reduce(f32[4,3072]{1,0:T(4,128)S(1)} %constant_dynamic-update-slice_fusion.7), channel_id=1, replica_groups=mesh['zc'=4,'core'=2,'fsdp'=4] {'zc','core','fsdp'}, use_global_device_ids=true, to_apply=%region_34.35 | all-reduce | flops 12288 | bytes 98304 | tf_op jit(solution)/shard_map/psum | solution.py:332
  860.9 4.1 convert_element_type.314
  865.0 4.2 convert_element_type.316
  869.2 3.4 convert_element_type.310
  (658 shorter events, 211.8 us)
Async XLA Ops:
  7.2 107.9 %copy-start = (bf16[256,4096]{1,0:T(8,128)(2,1)S(1)}, bf16[256,4096]{1,0:T(8,128)(2,1)}, u32[]{:S(2)}) copy-start(bf16[256,4096]{1,0:T(8,128)(2,1)} %param.32) | copy-start | bytes 6291460
  7.2 60.2 %all-gather.13.cloned.1.call-start = ((), (), s32[]{:S(2)}) async-start(), calls=%async_computation.23 | async-start | bytes 9437184 | tf_op jit(solution)/shard_map/all_gather | solution.py:117
  50.7 10.7 %copy-start.13 = (bf16[4,1,2,32,1024]{4,3,2,1,0:T(8,128)(2,1)S(1)}, bf16[4,1,2,32,1024]{4,3,2,1,0:T(8,128)(2,1)}, u32[]{:S(2)}) copy-start(bf16[4,1,2,32,1024]{4,3,2,1,0:T(8,128)(2,1)} %param.20) | copy-start | bytes 1572868
  50.8 190.9 %all-gather.31.cloned.1.call-start = ((), (), s32[]{:S(2)}) async-start(), calls=%async_computation.41 | async-start | bytes 9437184 | tf_op jit(solution)/shard_map/all_gather | solution.py:233
  110.9 17.2 %all-to-all-start.3 = ((bf16[4,128,1024]{2,1,0:T(8,128)(2,1)}), bf16[4,128,1024]{2,1,0:T(8,128)(2,1)}, u32[]{:S(2)}, u32[]{:S(2)}) async-start(bf16[4,128,1024]{2,1,0:T(8,128)(2,1)} %broadcast_in_dim.66), calls=%async_computation.3 | async-start | bytes 2097152 | tf_op jit(solution)/shard_map/all_to_all | solution.py:110
  131.8 51.8 %all-to-all-start.4 = ((bf16[4,128,4096]{2,1,0:T(8,128)(2,1)}), bf16[4,128,4096]{2,1,0:T(8,128)(2,1)}, u32[]{:S(2)}, u32[]{:S(2)}) async-start(bf16[4,128,4096]{2,1,0:T(8,128)(2,1)} %broadcast_in_dim.67), calls=%async_computation.4 | async-start | bytes 8388608 | tf_op jit(solution)/shard_map/all_to_all | solution.py:110
  136.6 166.8 %all-gather.15.cloned.1.call-start = ((), (), s32[]{:S(2)}) async-start(), calls=%async_computation.24 | async-start | bytes 3145728 | tf_op jit(solution)/shard_map/all_gather | solution.py:117
  137.4 169.4 %all-gather.17.cloned.1.call-start = ((), (), s32[]{:S(2)}) async-start(), calls=%async_computation.25 | async-start | bytes 12582912 | tf_op jit(solution)/shard_map/all_gather | solution.py:117
  187.9 5.3 copy-start.54
  187.9 51.9 %all-to-all-start.5 = ((bf16[4,512,1024]{2,1,0:T(8,128)(2,1)}), bf16[4,512,1024]{2,1,0:T(8,128)(2,1)}, u32[]{:S(2)}, u32[]{:S(2)}) async-start(bf16[4,512,1024]{2,1,0:T(8,128)(2,1)} %broadcast_in_dim.68), calls=%async_computation.5 | async-start | bytes 8388608 | tf_op jit(solution)/shard_map/all_to_all | solution.py:110
  192.9 123.4 %all-gather.19.cloned.1.call-start = ((), (), s32[]{:S(2)}) async-start(), calls=%async_computation.26 | async-start | bytes 12582912 | tf_op jit(solution)/shard_map/all_gather | solution.py:117
  291.3 10.7 %all-to-all-start.2 = ((bf16[4,2,128,1,256]{4,1,0,3,2:T(2,128)(2,1)}), bf16[4,2,128,1,256]{4,1,0,3,2:T(2,128)(2,1)S(1)}, u32[]{:S(2)}, u32[]{:S(2)}) async-start(bf16[4,2,128,1,256]{4,1,0,3,2:T(2,128)(2,1)} %copy.104), calls=%async_computation.2 | async-start | bytes 1048576 | tf_op jit(solution)/shard_map/all_to_all | solution.py:243
  305.8 26.2 %copy-start.15 = (f32[256,1024]{1,0:T(8,128)}, f32[256,1024]{1,0:T(8,128)S(1)}, u32[]{:S(2)}) copy-start(f32[256,1024]{1,0:T(8,128)S(1)} %get-tuple-element.303) | copy-start | bytes 3145732
  306.8 9.5 %copy-start.19 = (bf16[4,1,2,32,1024]{4,3,2,1,0:T(8,128)(2,1)S(1)}, bf16[4,1,2,32,1024]{4,3,2,1,0:T(8,128)(2,1)}, u32[]{:S(2)}) copy-start(bf16[4,1,2,32,1024]{4,3,2,1,0:T(8,128)(2,1)} %param.21) | copy-start | bytes 1572868
  316.2 12.6 %copy-start.66 = (bf16[4,256,4096]{2,1,0:T(8,128)(2,1)S(1)}, bf16[4,256,4096]{2,1,0:T(8,128)(2,1)}, u32[]{:S(2)}) copy-start(bf16[4,256,4096]{2,1,0:T(8,128)(2,1)} %all-gather.17.cloned.1.call-done) | copy-start | bytes 25165828
  328.8 3.2 copy-start.35
  332.0 3.0 copy-start.34
  332.4 3.4 copy-start.52
  337.1 11.3 %all-to-all-start.6 = ((bf16[4,2,32,4,256]{4,2,1,0,3:T(8,128)(2,1)}), bf16[4,2,32,4,256]{4,2,1,0,3:T(8,128)(2,1)S(1)}, u32[]{:S(2)}, u32[]{:S(2)}) async-start(bf16[4,2,32,4,256]{4,2,1,0,3:T(8,128)(2,1)} %copy.107), calls=%async_computation.6 | async-start | bytes 1048576 | tf_op jit(solution)/shard_map/all_to_all | solution.py:271
  340.6 156.9 %reduce-scatter.20.cloned.1.call-start = ((), (), s32[]{:S(2)}) async-start(), calls=%async_computation.33 | async-start | bytes 12582912 | tf_op jit(solution)/shard_map/reduce_scatter | solution.py:129
  348.4 225.0 %reduce-scatter.10.cloned.1.call-start = ((), (), s32[]{:S(2)}) async-start(), calls=%async_computation.27 | async-start | bytes 9437184 | tf_op jit(solution)/shard_map/reduce_scatter | solution.py:280
  349.5 4.0 copy-start.39
  366.2 3.6 copy-start.10
  378.9 4.1 copy-start.39
  395.6 3.6 copy-start.10
  408.4 4.0 copy-start.39
  425.1 3.6 copy-start.10
  437.8 4.1 copy-start.39
  454.5 3.6 copy-start.10
  482.4 130.1 %reduce-scatter.24.cloned.1.call-start = ((), (), s32[]{:S(2)}) async-start(), calls=%async_computation.37 | async-start | bytes 12582912 | tf_op jit(solution)/shard_map/reduce_scatter | solution.py:129
  486.9 4.9 copy-start.20
  497.4 169.1 %reduce-scatter.22.cloned.1.call-start = ((), (), s32[]{:S(2)}) async-start(), calls=%async_computation.34 | async-start | bytes 1310720 | tf_op jit(solution)/shard_map/reduce_scatter | solution.py:135
  549.1 4.4 copy-start.24
  553.5 113.7 %reduce-scatter.16.cloned.1.call-start = ((), (), s32[]{:S(2)}) async-start(), calls=%async_computation.31 | async-start | bytes 3145728 | tf_op jit(solution)/shard_map/reduce_scatter | solution.py:129
  557.9 18.1 %all-to-all-start.7 = ((bf16[4,2,128,1,256]{4,1,0,3,2:T(2,128)(2,1)}), bf16[4,2,128,1,256]{4,1,0,3,2:T(2,128)(2,1)S(1)}, u32[]{:S(2)}, u32[]{:S(2)}) async-start(bf16[4,2,128,1,256]{4,1,0,3,2:T(2,128)(2,1)} %copy.110), calls=%async_computation.7 | async-start | bytes 1048576 | tf_op jit(solution)/shard_map/all_to_all | solution.py:291
  574.7 16.1 %copy-start.45 = (f32[4,2,32]{2,1,0:T(2,128)S(1)}, f32[4,2,32]{2,1,0:T(2,128)}, u32[]{:S(2)}) copy-start(f32[4,2,32]{2,1,0:T(2,128)} %copy-done.44) | copy-start | bytes 3076
  574.7 16.1 %copy-start.14 = (bf16[4,1,2,32,1024]{4,3,2,1,0:T(8,128)(2,1)S(1)}, bf16[4,1,2,32,1024]{4,3,2,1,0:T(8,128)(2,1)}, u32[]{:S(2)}) copy-start(bf16[4,1,2,32,1024]{4,3,2,1,0:T(8,128)(2,1)} %param.20) | copy-start | bytes 1572868
  576.0 10.2 %all-to-all-start.8 = ((bf16[4,2,128,1,256]{4,1,0,3,2:T(2,128)(2,1)}), bf16[4,2,128,1,256]{4,1,0,3,2:T(2,128)(2,1)S(1)}, u32[]{:S(2)}, u32[]{:S(2)}) async-start(bf16[4,2,128,1,256]{4,1,0,3,2:T(2,128)(2,1)} %copy.116), calls=%async_computation.9 | async-start | bytes 1048576 | tf_op jit(solution)/shard_map/all_to_all | solution.py:294
  579.7 12.2 %copy-start.50 = (f32[4,2,32]{2,1,0:T(2,128)S(1)}, f32[4,2,32]{2,1,0:T(2,128)}, u32[]{:S(2)}) copy-start(f32[4,2,32]{2,1,0:T(2,128)} %get-tuple-element.298) | copy-start | bytes 3076
  579.7 12.3 %copy-start.49 = (f32[4,256]{1,0:T(4,128)S(1)}, f32[4,256]{1,0:T(4,128)}, u32[]{:S(2)}) copy-start(f32[4,256]{1,0:T(4,128)} %get-tuple-element.297) | copy-start | bytes 12292
  579.7 12.3 %copy-start.48 = (f32[4,256]{1,0:T(4,128)S(1)}, f32[4,256]{1,0:T(4,128)}, u32[]{:S(2)}) copy-start(f32[4,256]{1,0:T(4,128)} %get-tuple-element.288) | copy-start | bytes 12292
  586.3 4.5 copy-start.30
  586.3 10.8 %all-to-all-start.9 = ((bf16[4,2,128,1,256]{4,1,0,3,2:T(2,128)(2,1)}), bf16[4,2,128,1,256]{4,1,0,3,2:T(2,128)(2,1)}, u32[]{:S(2)}, u32[]{:S(2)}) async-start(bf16[4,2,128,1,256]{4,1,0,3,2:T(2,128)(2,1)} %copy.119), calls=%async_computation.10 | async-start | bytes 1048576 | tf_op jit(solution)/shard_map/all_to_all | solution.py:297
  590.4 90.2 %reduce-scatter.12.cloned.1.call-start = ((), (), s32[]{:S(2)}) async-start(), calls=%async_computation.28 | async-start | bytes 9437184 | tf_op jit(solution)/shard_map/reduce_scatter | solution.py:129
  612.5 85.0 %reduce-scatter.26.cloned.1.call-start = ((), (), s32[]{:S(2)}) async-start(), calls=%async_computation.38 | async-start | bytes 1310720 | tf_op jit(solution)/shard_map/reduce_scatter | solution.py:135
  666.4 59.1 %all-gather.23.cloned.1.call-start = ((), (), s32[]{:S(2)}) async-start(), calls=%async_computation.35 | async-start | bytes 1310720 | tf_op jit(solution)/shard_map/all_gather | solution.py:136
  680.6 34.3 %all-to-all-start.10 = ((bf16[4,128,3072]{2,1,0:T(8,128)(2,1)}), bf16[4,128,3072]{2,1,0:T(8,128)(2,1)}, u32[]{:S(2)}, u32[]{:S(2)}) async-start(bf16[4,128,3072]{2,1,0:T(8,128)(2,1)} %bitcast.305), calls=%async_computation.12 | async-start | bytes 6291456 | tf_op jit(solution)/shard_map/all_to_all | solution.py:131
  685.3 69.1 %all-gather.27.cloned.1.call-start = ((), (), s32[]{:S(2)}) async-start(), calls=%async_computation.39 | async-start | bytes 1310720 | tf_op jit(solution)/shard_map/all_gather | solution.py:136
  697.5 78.4 %reduce-scatter.18.cloned.1.call-start = ((), (), s32[]{:S(2)}) async-start(), calls=%async_computation.32 | async-start | bytes 327680 | tf_op jit(solution)/shard_map/reduce_scatter | solution.py:135
  698.5 102.2 %reduce-scatter.14.cloned.1.call-start = ((), (), s32[]{:S(2)}) async-start(), calls=%async_computation.29 | async-start | bytes 983040 | tf_op jit(solution)/shard_map/reduce_scatter | solution.py:135
  718.5 36.2 %copy-start.47 = (f32[1,2,4,128]{3,2,1,0:T(4,128)S(1)}, f32[1,2,4,128]{3,2,1,0:T(4,128)}, u32[]{:S(2)}) copy-start(f32[1,2,4,128]{3,2,1,0:T(4,128)} %get-tuple-element.291) | copy-start | bytes 12292
  718.5 37.4 %copy-start.46 = (f32[1024]{0:T(1024)S(1)}, f32[1024]{0:T(1024)}, u32[]{:S(2)}) copy-start(f32[1024]{0:T(1024)} %get-tuple-element.244) | copy-start | bytes 12292
  718.5 37.4 %copy-start.56 = (f32[1024]{0:T(1024)S(1)}, f32[1024]{0:T(1024)}, u32[]{:S(2)}) copy-start(f32[1024]{0:T(1024)} %get-tuple-element.199) | copy-start | bytes 12292
  718.5 37.5 %copy-start.55 = (f32[1024]{0:T(1024)S(1)}, f32[1024]{0:T(1024)}, u32[]{:S(2)}) copy-start(f32[1024]{0:T(1024)} %get-tuple-element.203) | copy-start | bytes 12292
  718.5 37.5 %copy-start.51 = (f32[4096]{0:T(1024)S(1)}, f32[4096]{0:T(1024)}, u32[]{:S(2)}) copy-start(f32[4096]{0:T(1024)} %get-tuple-element.308) | copy-start | bytes 49156
  718.5 37.5 %copy-start.16 = (f32[256,1024]{1,0:T(8,128)S(1)}, f32[256,1024]{1,0:T(8,128)}, u32[]{:S(2)}) copy-start(f32[256,1024]{1,0:T(8,128)} %copy-done.15) | copy-start | bytes 3145732
  718.5 142.4 %all-gather.25.cloned.1.call-start = ((), (), s32[]{:S(2)}) async-start(), calls=%async_computation.36 | async-start | bytes 3145728 | tf_op jit(solution)/shard_map/all_gather | solution.py:137
  725.6 139.4 %all-gather.29.cloned.1.call-start = ((), (), s32[]{:S(2)}) async-start(), calls=%async_computation.40 | async-start | bytes 3145728 | tf_op jit(solution)/shard_map/all_gather | solution.py:137
  754.4 114.8 %all-gather.21.cloned.1.call-start = ((), (), s32[]{:S(2)}) async-start(), calls=%async_computation.30 | async-start | bytes 2359296 | tf_op jit(solution)/shard_map/all_gather | solution.py:137
  797.3 62.2 %copy-start.18 = (f32[256,1024]{1,0:T(8,128)S(1)}, f32[256,1024]{1,0:T(8,128)}, u32[]{:S(2)}) copy-start(f32[256,1024]{1,0:T(8,128)} %copy-done.17) | copy-start | bytes 3145732
  797.3 62.2 %copy-start.21 = (bf16[4,1,2,32,1024]{4,3,2,1,0:T(8,128)(2,1)S(1)}, bf16[4,1,2,32,1024]{4,3,2,1,0:T(8,128)(2,1)}, u32[]{:S(2)}) copy-start(bf16[4,1,2,32,1024]{4,3,2,1,0:T(8,128)(2,1)} %param.21) | copy-start | bytes 1572868
  797.3 62.2 %copy-start.26 = (f32[256,1024]{1,0:T(8,128)S(1)}, f32[256,1024]{1,0:T(8,128)}, u32[]{:S(2)}) copy-start(f32[256,1024]{1,0:T(8,128)} %get-tuple-element.307) | copy-start | bytes 3145732
  797.3 62.2 %copy-start.53 = (f32[256]{0:T(256)S(1)}, f32[256]{0:T(256)}, u32[]{:S(2)}) copy-start(f32[256]{0:T(256)} %copy-done.52) | copy-start | bytes 3076
  865.0 7.7 copy-start.1
  (76 other events, 119.9 us)
Sparse Core Ops, SparseCore 0:
  50.9 16.4 all-gather.12
  109.8 81.4 all-gather.30
  192.9 9.0 all-gather.14
  203.4 21.0 all-gather.16
  239.9 19.8 all-gather.18
  348.5 17.7 reduce-scatter.19
  482.5 90.8 reduce-scatter.9
  575.7 14.8 reduce-scatter.23
  592.9 28.5 reduce-scatter.21
  624.2 8.2 reduce-scatter.15
  634.8 15.3 reduce-scatter.11
  666.5 30.8 reduce-scatter.25
  699.0 26.4 all-gather.22
  727.0 27.3 all-gather.26
  756.5 19.3 reduce-scatter.17
  778.6 22.0 reduce-scatter.13
  802.1 10.1 all-gather.24
  813.6 11.7 all-gather.28
  827.0 10.9 all-gather.20
